TPU v7x, 512 devices: a whole 4x4x16 slice. The times are simulated.
512 devices in a mesh: band: 256 (over x_hi, y, z, core), pair: 2 (over x_lo).
Axes of the slice: x: 4 (x_hi: 2, x_lo: 2; x = x_hi * 2 + x_lo), y: 4, z: 16, core: 2. Of those that a mesh axis runs over, the one named last changes fastest.
Arguments:
- frame1: bfloat16 [256, 768, 256], P('band', 'pair'), parts along dimension 1, may hold values from -6 to 6, as said below
- frame2: bfloat16 [256, 768, 256], P('band', 'pair'), parts along dimension 1, may hold values from -6 to 6, as said below
- context: bfloat16 [256, 768, 128], P('band', 'pair'), parts along dimension 1, may hold values from -6 to 6
- hidden_init: bfloat16 [256, 768, 128], P('band', 'pair'), parts along dimension 1, may hold values from -1 to 1
- offsets: int32 [2, 256, 768], P(None, 'band', 'pair'), parts along dimension 2, may hold values from -4 to 4
- w_motion: float32 [3, 128], replicated, may hold values from -3.5 to 3.5
- w_row: bfloat16 [5, 384, 384], replicated, may hold values from -0.125 to 0.125
- w_col: bfloat16 [5, 384, 384], replicated, may hold values from -0.125 to 0.125
Outputs:
- hidden: float32 [256, 768, 128], P('band', 'pair'), parts along dimension 1
- flow: float32 [2, 256, 768], P(None, 'band', 'pair'), parts along dimension 2
There are 2 independent parts, one for each index of `pair`. A program takes and returns all parts, laid end to end along the dimension named above; an argument that names none is the same for every part. Nothing has to cross between parts.
Inputs may be any that keep to these rules, and one draw needn't show every extreme that they name: `frame1`: feature vectors. `frame2`: feature vectors. offsets[0] and offsets[1] are each pixel's teacher lookup offsets, in rows and in strips.
All inputs are finite; a program needn't handle non-finite values.
Results may differ from a plain program's by a relative error of at most 0.0041.
Values may be sent and summed in bfloat16 or wider, within the bound.
No kernel may reach another device: no remote copies, remote signals or barrier semaphores. Data moves between devices by JAX's collectives and lax.ppermute only.
A program may use at most 64 MiB of HBM per device.

v0:
```python
import math

import jax
import jax.numpy as jnp
from jax import lax
from jax.sharding import PartitionSpec as P

ITERS = 2


def passed_along(array, axis, by):
    count = lax.axis_size(axis)
    pairs = [(i, i + by) for i in range(count) if 0 <= i + by < count]
    return lax.ppermute(array, axis, pairs)


def pool_strips(frame2):
    band_rows, image_width, channels = frame2.shape
    blocks = frame2.astype(jnp.float32).reshape(band_rows, image_width // 8, 8, channels)
    return (jnp.sum(blocks, axis=2) / 2.0).astype(jnp.bfloat16)


def lookup_targets(offsets, row_first, total_rows, image_width):
    band_rows = offsets.shape[1]
    pixel_row = (
        row_first
        + jnp.arange(band_rows, dtype=jnp.int32)[:, None]
        + jnp.zeros((1, image_width), jnp.int32)
    )
    pixel_col = jnp.arange(image_width, dtype=jnp.int32)[None, :]
    target_row = pixel_row + offsets[0]
    target_col = pixel_col // 8 + offsets[1]
    inside = (
        (target_row >= 0)
        & (target_row < total_rows)
        & (target_col >= 0)
        & (target_col < image_width // 8)
    )
    target_row = jnp.where(inside, target_row, -1)
    target_col = jnp.where(inside, target_col, -1)
    return (target_row, target_col, pixel_row, pixel_col)


def strip_step(
    state, feature_rows, strip_block, row_zero, total_rows, image_width, target_row, target_col
):
    block_rows, grid_cols, channels = strip_block.shape
    scores = jnp.dot(
        feature_rows,
        strip_block.reshape(block_rows * grid_cols, channels).T,
        preferred_element_type=jnp.float32,
    ) / math.sqrt(channels)
    running_max, denominator, acc_row, acc_col, lookup = state
    new_max = jnp.maximum(running_max, jnp.max(scores, axis=1))
    shrink = jnp.exp(running_max - new_max)
    exponent = jnp.exp(scores - new_max[:, None]).reshape(-1, block_rows, grid_cols)
    strip_row = row_zero + jnp.arange(block_rows, dtype=jnp.int32)
    column_ids = jnp.arange(grid_cols, dtype=jnp.int32)
    row_centre = strip_row.astype(jnp.float32) / total_rows
    col_centre = ((8 * column_ids).astype(jnp.float32) + 3.5) / image_width
    row_weight = jnp.sum(exponent, axis=2)
    col_weight = jnp.sum(exponent, axis=1)
    scores_grid = scores.reshape(-1, block_rows, grid_cols)
    hit = (strip_row[None, :, None] == target_row[:, None, None]) & (
        column_ids[None, None, :] == target_col[:, None, None]
    )
    found = jnp.sum(jnp.where(hit, scores_grid, 0.0), axis=(1, 2))
    return (
        new_max,
        denominator * shrink + jnp.sum(row_weight, axis=1),
        acc_row * shrink + jnp.sum(row_weight * row_centre[None, :], axis=1),
        acc_col * shrink + jnp.sum(col_weight * col_centre[None, :], axis=1),
        lookup + found,
    )


def conv_valid(source, weight, conv_axis):
    out_count = source.shape[conv_axis] - 4
    summed = None
    for kernel_tap in range(5):
        tap_slice = lax.slice_in_dim(source, kernel_tap, kernel_tap + out_count, axis=conv_axis)
        tap_term = jnp.dot(
            tap_slice.reshape(-1, tap_slice.shape[-1]),
            weight[kernel_tap],
            preferred_element_type=jnp.float32,
        )
        summed = tap_term if summed is None else summed + tap_term
    out_shape = tuple(tap_slice.shape[:-1]) + (weight.shape[-1],)
    return summed.reshape(out_shape)


def pad_columns(source):
    return jnp.pad(source, ((0, 0), (2, 2), (0, 0)))


def rows_around(source, depth, mover):
    above = [
        mover(source, offset)
        for offset in list(range(depth, 0, -1)) + list(range(-1, -depth - 1, -1))
    ]
    return jnp.concatenate(above[:depth] + [source] + above[depth:], axis=0)


def row_pass(hidden, from_inputs, weight):
    width_h = hidden.shape[-1]
    hidden_half = lax.optimization_barrier(hidden.astype(jnp.bfloat16))
    gate_pair = jax.nn.sigmoid(
        conv_valid(pad_columns(hidden_half), weight[:, :width_h, : 2 * width_h], 1)
        + from_inputs[..., : 2 * width_h]
    )
    update_gate = gate_pair[..., :width_h]
    reset_gate = gate_pair[..., width_h:]
    gated = (reset_gate * hidden_half.astype(jnp.float32)).astype(jnp.bfloat16)
    candidate = jnp.tanh(
        conv_valid(pad_columns(gated), weight[:, :width_h, 2 * width_h :], 1)
        + from_inputs[..., 2 * width_h :]
    )
    return (1.0 - update_gate) * hidden + update_gate * candidate


def column_pass_each(hidden, from_inputs, weight):
    width_h = hidden.shape[-1]
    hidden_half = lax.optimization_barrier(hidden.astype(jnp.bfloat16))
    hidden_ext = rows_around(
        hidden_half, 2, lambda source, offset: passed_along(source, "band", offset)
    )
    gate_pair = jax.nn.sigmoid(
        conv_valid(hidden_ext, weight[:, :width_h, : 2 * width_h], 0)
        + from_inputs[..., : 2 * width_h]
    )
    update_gate = gate_pair[..., :width_h]
    reset_gate = gate_pair[..., width_h:]
    gated = (reset_gate * hidden_half.astype(jnp.float32)).astype(jnp.bfloat16)
    gated_ext = rows_around(gated, 2, lambda source, offset: passed_along(source, "band", offset))
    candidate = jnp.tanh(
        conv_valid(gated_ext, weight[:, :width_h, 2 * width_h :], 0)
        + from_inputs[..., 2 * width_h :]
    )
    return (1.0 - update_gate) * hidden + update_gate * candidate


def per_device(frame1, frame2, context, hidden_init, offsets, w_motion, w_row, w_col):
    band_rows, image_width, channels = frame1.shape
    total_rows = band_rows * lax.axis_size("band")
    row_first = lax.axis_index("band") * band_rows
    strips = pool_strips(frame2)
    target_row, target_col, pixel_row, pixel_col = lookup_targets(
        offsets, row_first, total_rows, image_width
    )
    pixel_count = band_rows * image_width
    features = frame1.reshape(pixel_count, channels)
    rows_target = target_row.reshape(pixel_count)
    cols_target = target_col.reshape(pixel_count)
    zeros_state = jnp.zeros((pixel_count,), jnp.float32)
    initial = (
        jnp.full((pixel_count,), -jnp.inf, jnp.float32),
        zeros_state,
        zeros_state,
        zeros_state,
        zeros_state,
    )
    state = initial
    arriving = lax.all_gather(strips, "band", axis=0, tiled=True)
    arriving_rows = arriving.shape[0]
    step_rows = min(arriving_rows, 16)
    full_steps = arriving_rows // step_rows
    blocks = arriving.reshape((full_steps, step_rows) + arriving.shape[1:])
    starts = step_rows * jnp.arange(full_steps, dtype=jnp.int32)

    def advance(carry, pieces):
        return (
            strip_step(
                carry,
                features,
                pieces[0],
                pieces[1],
                total_rows,
                image_width,
                rows_target,
                cols_target,
            ),
            None,
        )

    state, unused = lax.scan(advance, state, (blocks, starts))
    running_max, denominator, acc_row, acc_col, lookup = state
    flow_row = (acc_row / denominator).reshape(band_rows, image_width) - pixel_row.astype(
        jnp.float32
    ) / total_rows
    flow_col = (acc_col / denominator).reshape(band_rows, image_width) - pixel_col.astype(
        jnp.float32
    ) / image_width
    lookup = lookup.reshape(band_rows, image_width)
    motion = jax.nn.relu(
        flow_row[..., None] * w_motion[0]
        + flow_col[..., None] * w_motion[1]
        + lookup[..., None] * w_motion[2]
    ).astype(jnp.bfloat16)
    inputs = jnp.concatenate([context, motion], axis=-1)
    width_h = hidden_init.shape[-1]
    from_row = conv_valid(pad_columns(inputs), w_row[:, width_h:, :], 1)
    hidden = hidden_init.astype(jnp.float32)
    inputs_ext = rows_around(inputs, 2, lambda source, offset: passed_along(source, "band", offset))
    from_col = conv_valid(inputs_ext, w_col[:, width_h:, :], 0)
    for iteration in range(ITERS):
        hidden = row_pass(hidden, from_row, w_row)
        hidden = column_pass_each(hidden, from_col, w_col)
    return (hidden, jnp.stack([flow_row, flow_col]))


def solution(mesh):
    return jax.shard_map(
        per_device,
        mesh=mesh,
        in_specs=(
            P("band", "pair", None),
            P("band", "pair", None),
            P("band", "pair", None),
            P("band", "pair", None),
            P(None, "band", "pair"),
            P(),
            P(),
            P(),
        ),
        out_specs=(P("band", "pair", None), P(None, "band", "pair")),
        check_vma=False,
    )
```

profile of v0, /device:TPU:7, one launch (start us, length us, event | category | flops | bytes accessed | tf_op | source)
XLA Modules:
  0.0 416.5 jit_solution(839724236668119955)
XLA Ops:
  7.2 1.2 convert_reduce_fusion
  9.1 0.8 slice_bitcast_fusion.2
  11.3 1.1 fusion.158
  12.4 1.1 convolution_add_fusion.17
  14.0 222.3 %all-gather.3.cloned.1.call-done = bf16[12288,256]{1,0:T(8,128)(2,1)} async-done(((bf16[48,256]{1,0:T(8,128)(2,1)}), bf16[12288,256]{1,0:T(8,128)(2,1)}) %all-gather.3.cloned.1.call-update) | async-done | bytes 6291472 | tf_op jit(solution)/shard_map/all_gather | solution.py:163
  236.2 70.1 %while.19 = (s32[]{:T(128)}, f32[384]{0:T(512)S(1)}, f32[384]{0:T(512)S(1)}, f32[384]{0:T(512)S(1)}, f32[384]{0:T(512)S(1)}, /*index=5*/f32[384]{0:T(512)S(1)}, ...) while((s32[]{:T(128)}, f32[384]{0:T(512)S(1)}, ...), condition=%wide.region_9.10_spmd.clone, body=%wide.region_1.9_spmd.clone.sunk | while | flops 153702400 | bytes 6978856 | solution.py:185
  236.2 1.1 constant_dynamic-slice_fusion.2
  240.6 1.0 constant_dynamic-slice_fusion.2
  245.0 1.0 constant_dynamic-slice_fusion.2
  249.4 1.0 constant_dynamic-slice_fusion.2
  253.8 1.0 constant_dynamic-slice_fusion.2
  258.2 1.0 constant_dynamic-slice_fusion.2
  262.5 1.0 constant_dynamic-slice_fusion.2
  266.9 1.0 constant_dynamic-slice_fusion.2
  271.3 1.0 constant_dynamic-slice_fusion.2
  275.7 1.0 constant_dynamic-slice_fusion.2
  280.1 1.0 constant_dynamic-slice_fusion.2
  284.4 1.0 constant_dynamic-slice_fusion.2
  288.8 1.0 constant_dynamic-slice_fusion.2
  293.2 1.0 constant_dynamic-slice_fusion.2
  297.6 1.0 constant_dynamic-slice_fusion.2
  302.0 1.0 constant_dynamic-slice_fusion.2
  309.2 3.3 collective-permute-start.1
  312.5 2.2 collective-permute-start
  314.7 8.8 %collective-permute-start.3 = (bf16[1,384,128]{2,1,0:T(8,128)(2,1)S(1)}, bf16[1,384,128]{2,1,0:T(8,128)(2,1)S(1)}, u32[]{:S(2)}, u32[]{:S(2)}) collective-permute-start(bf16[1,384,128]{2,1,0:T(8,128)(2,1)S(1)} %get-tuple-element.142), channel_id=1, source_target_pairs={{4,0},{6,2},{8,4},{10,6},{12,8},{14,10},{16,12},{18,14},{20,16},{2... | collective-permute-start | bytes 294920 | tf_op jit(solution)/shard_map/ppermute | solution.py:14
  323.5 1.9 collective-permute-start.2
  325.4 3.6 collective-permute-start.5
  330.1 1.9 collective-permute-start.4
  332.3 9.1 %collective-permute-start.7 = (bf16[1,384,256]{2,1,0:T(8,128)(2,1)S(1)}, bf16[1,384,256]{2,1,0:T(8,128)(2,1)S(1)}, u32[]{:S(2)}, u32[]{:S(2)}) collective-permute-start(bf16[1,384,256]{2,1,0:T(8,128)(2,1)S(1)} %pad_maximum_fusion), channel_id=1, source_target_pairs={{4,0},{6,2},{8,4},{10,6},{12,8},{14,10},{16,12},{18,14},{20,16},{2... | collective-permute-start | bytes 589832 | tf_op jit(solution)/shard_map/ppermute | solution.py:14
  341.6 1.9 collective-permute-start.6
  344.2 1.8 collective-permute-done.7
  346.3 2.2 collective-permute-done.6
  349.1 1.9 collective-permute-start.9
  351.2 1.9 collective-permute-start.8
  353.1 9.1 %collective-permute-start.11 = (bf16[1,384,128]{2,1,0:T(8,128)(2,1)S(1)}, bf16[1,384,128]{2,1,0:T(8,128)(2,1)S(1)}, u32[]{:S(2)}, u32[]{:S(2)}) collective-permute-start(bf16[1,384,128]{2,1,0:T(8,128)(2,1)S(1)} %fusion.60), channel_id=1, source_target_pairs={{4,0},{6,2},{8,4},{10,6},{12,8},{14,10},{16,12},{18,14},{20,16},{2... | collective-permute-start | bytes 294920 | tf_op jit(solution)/shard_map/ppermute | solution.py:14
  362.2 3.0 collective-permute-start.10
  365.7 2.5 collective-permute-done.10
  370.3 1.9 collective-permute-start.13
  372.5 1.9 collective-permute-start.12
  374.4 9.1 %collective-permute-start.15 = (bf16[1,384,128]{2,1,0:T(8,128)(2,1)S(1)}, bf16[1,384,128]{2,1,0:T(8,128)(2,1)S(1)}, u32[]{:S(2)}, u32[]{:S(2)}) collective-permute-start(bf16[1,384,128]{2,1,0:T(8,128)(2,1)S(1)} %get-tuple-element.146), channel_id=1, source_target_pairs={{4,0},{6,2},{8,4},{10,6},{12,8},{14,10},{16,12},{18,14},{20,16},{2... | collective-permute-start | bytes 294920 | tf_op jit(solution)/shard_map/ppermute | solution.py:14
  383.5 3.0 collective-permute-start.14
  387.1 2.3 collective-permute-done.14
  389.7 1.9 collective-permute-start.17
  391.8 1.9 collective-permute-start.16
  393.7 9.1 %collective-permute-start.19 = (bf16[1,384,128]{2,1,0:T(8,128)(2,1)S(1)}, bf16[1,384,128]{2,1,0:T(8,128)(2,1)S(1)}, u32[]{:S(2)}, u32[]{:S(2)}) collective-permute-start(bf16[1,384,128]{2,1,0:T(8,128)(2,1)S(1)} %fusion.58), channel_id=1, source_target_pairs={{4,0},{6,2},{8,4},{10,6},{12,8},{14,10},{16,12},{18,14},{20,16},{2... | collective-permute-start | bytes 294920 | tf_op jit(solution)/shard_map/ppermute | solution.py:14
  402.8 3.0 collective-permute-start.18
  406.3 2.4 collective-permute-done.18
  408.8 0.9 multiply_add_fusion
  (365 shorter events, 65.1 us)
Async XLA Ops:
  7.2 6.4 %copy-start.1 = (bf16[1,384,128]{2,1,0:T(8,128)(2,1)S(1)}, bf16[1,384,128]{2,1,0:T(8,128)(2,1)}, u32[]{:S(2)}) copy-start(bf16[1,384,128]{2,1,0:T(8,128)(2,1)} %param.13) | copy-start | bytes 294916
  7.2 6.4 %copy-start.3 = (bf16[5,384,384]{2,1,0:T(8,128)(2,1)S(1)}, bf16[5,384,384]{2,1,0:T(8,128)(2,1)}, u32[]{:S(2)}) copy-start(bf16[5,384,384]{2,1,0:T(8,128)(2,1)} %param.16) | copy-start | bytes 4423684
  7.2 229.0 %all-gather.3.cloned.1.call-start = ((), (), s32[]{:S(2)}) async-start(), calls=%async_computation | async-start | bytes 6316032 | tf_op jit(solution)/shard_map/all_gather | solution.py:163
  12.4 223.8 %copy-start = (bf16[1,384,256]{2,1,0:T(8,128)(2,1)S(1)}, bf16[1,384,256]{2,1,0:T(8,128)(2,1)}, u32[]{:S(2)}) copy-start(bf16[1,384,256]{2,1,0:T(8,128)(2,1)} %param.10) | copy-start | bytes 589828
  236.2 70.3 %copy-start.4 = (bf16[1,384,128]{2,1,0:T(8,128)(2,1)S(1)}, bf16[1,384,128]{2,1,0:T(8,128)(2,1)}, u32[]{:S(2)}) copy-start(bf16[1,384,128]{2,1,0:T(8,128)(2,1)} %param.12) | copy-start | bytes 294916
  308.3 20.8 %copy-start.2 = (bf16[5,384,384]{2,1,0:T(8,128)(2,1)S(1)}, bf16[5,384,384]{2,1,0:T(8,128)(2,1)}, u32[]{:S(2)}) copy-start(bf16[5,384,384]{2,1,0:T(8,128)(2,1)} %param.17) | copy-start | bytes 4423684
  309.2 21.0 %collective-permute-start.1 = (bf16[1,384,128]{2,1,0:T(8,128)(2,1)S(1)}, bf16[1,384,128]{2,1,0:T(8,128)(2,1)S(1)}, u32[]{:S(2)}, u32[]{:S(2)}) collective-permute-start(bf16[1,384,128]{2,1,0:T(8,128)(2,1)S(1)} %get-tuple-element.142), channel_id=1, source_target_pairs={{0,2},{2,4},{4,6},{6,8},{8,10},{10,12},{12,14},{14,16},{16,18},{18... | collective-permute-start | bytes 294920 | tf_op jit(solution)/shard_map/ppermute | solution.py:14
  312.5 19.8 %collective-permute-start = (bf16[1,384,128]{2,1,0:T(8,128)(2,1)S(1)}, bf16[1,384,128]{2,1,0:T(8,128)(2,1)S(1)}, u32[]{:S(2)}, u32[]{:S(2)}) collective-permute-start(bf16[1,384,128]{2,1,0:T(8,128)(2,1)S(1)} %get-tuple-element.142), channel_id=1, source_target_pairs={{0,4},{2,6},{4,8},{6,10},{8,12},{10,14},{12,16},{14,18},{16,20},{1... | collective-permute-start | bytes 294920 | tf_op jit(solution)/shard_map/ppermute | solution.py:14
  314.7 26.8 %collective-permute-start.3 = (bf16[1,384,128]{2,1,0:T(8,128)(2,1)S(1)}, bf16[1,384,128]{2,1,0:T(8,128)(2,1)S(1)}, u32[]{:S(2)}, u32[]{:S(2)}) collective-permute-start(bf16[1,384,128]{2,1,0:T(8,128)(2,1)S(1)} %get-tuple-element.142), channel_id=1, source_target_pairs={{4,0},{6,2},{8,4},{10,6},{12,8},{14,10},{16,12},{18,14},{20,16},{2... | collective-permute-start | bytes 294920 | tf_op jit(solution)/shard_map/ppermute | solution.py:14
  323.5 25.3 %collective-permute-start.2 = (bf16[1,384,128]{2,1,0:T(8,128)(2,1)S(1)}, bf16[1,384,128]{2,1,0:T(8,128)(2,1)S(1)}, u32[]{:S(2)}, u32[]{:S(2)}) collective-permute-start(bf16[1,384,128]{2,1,0:T(8,128)(2,1)S(1)} %get-tuple-element.142), channel_id=1, source_target_pairs={{2,0},{4,2},{6,4},{8,6},{10,8},{12,10},{14,12},{16,14},{18,16},{20... | collective-permute-start | bytes 294920 | tf_op jit(solution)/shard_map/ppermute | solution.py:14
  325.4 18.3 %collective-permute-start.5 = (bf16[1,384,256]{2,1,0:T(8,128)(2,1)S(1)}, bf16[1,384,256]{2,1,0:T(8,128)(2,1)S(1)}, u32[]{:S(2)}, u32[]{:S(2)}) collective-permute-start(bf16[1,384,256]{2,1,0:T(8,128)(2,1)S(1)} %pad_maximum_fusion), channel_id=1, source_target_pairs={{0,2},{2,4},{4,6},{6,8},{8,10},{10,12},{12,14},{14,16},{16,18},{18... | collective-permute-start | bytes 589832 | tf_op jit(solution)/shard_map/ppermute | solution.py:14
  330.1 13.8 %collective-permute-start.4 = (bf16[1,384,256]{2,1,0:T(8,128)(2,1)S(1)}, bf16[1,384,256]{2,1,0:T(8,128)(2,1)S(1)}, u32[]{:S(2)}, u32[]{:S(2)}) collective-permute-start(bf16[1,384,256]{2,1,0:T(8,128)(2,1)S(1)} %pad_maximum_fusion), channel_id=1, source_target_pairs={{0,4},{2,6},{4,8},{6,10},{8,12},{10,14},{12,16},{14,18},{16,20},{1... | collective-permute-start | bytes 589832 | tf_op jit(solution)/shard_map/ppermute | solution.py:14
  332.3 13.8 %collective-permute-start.7 = (bf16[1,384,256]{2,1,0:T(8,128)(2,1)S(1)}, bf16[1,384,256]{2,1,0:T(8,128)(2,1)S(1)}, u32[]{:S(2)}, u32[]{:S(2)}) collective-permute-start(bf16[1,384,256]{2,1,0:T(8,128)(2,1)S(1)} %pad_maximum_fusion), channel_id=1, source_target_pairs={{4,0},{6,2},{8,4},{10,6},{12,8},{14,10},{16,12},{18,14},{20,16},{2... | collective-permute-start | bytes 589832 | tf_op jit(solution)/shard_map/ppermute | solution.py:14
  341.6 7.0 %collective-permute-start.6 = (bf16[1,384,256]{2,1,0:T(8,128)(2,1)S(1)}, bf16[1,384,256]{2,1,0:T(8,128)(2,1)S(1)}, u32[]{:S(2)}, u32[]{:S(2)}) collective-permute-start(bf16[1,384,256]{2,1,0:T(8,128)(2,1)S(1)} %pad_maximum_fusion), channel_id=1, source_target_pairs={{2,0},{4,2},{6,4},{8,6},{10,8},{12,10},{14,12},{16,14},{18,16},{20... | collective-permute-start | bytes 589832 | tf_op jit(solution)/shard_map/ppermute | solution.py:14
  349.1 16.1 %collective-permute-start.9 = (bf16[1,384,128]{2,1,0:T(8,128)(2,1)S(1)}, bf16[1,384,128]{2,1,0:T(8,128)(2,1)S(1)}, u32[]{:S(2)}, u32[]{:S(2)}) collective-permute-start(bf16[1,384,128]{2,1,0:T(8,128)(2,1)S(1)} %fusion.60), channel_id=1, source_target_pairs={{0,2},{2,4},{4,6},{6,8},{8,10},{10,12},{12,14},{14,16},{16,18},{18... | collective-permute-start | bytes 294920 | tf_op jit(solution)/shard_map/ppermute | solution.py:14
  351.2 14.2 %collective-permute-start.8 = (bf16[1,384,128]{2,1,0:T(8,128)(2,1)S(1)}, bf16[1,384,128]{2,1,0:T(8,128)(2,1)S(1)}, u32[]{:S(2)}, u32[]{:S(2)}) collective-permute-start(bf16[1,384,128]{2,1,0:T(8,128)(2,1)S(1)} %fusion.60), channel_id=1, source_target_pairs={{0,4},{2,6},{4,8},{6,10},{8,12},{10,14},{12,16},{14,18},{16,20},{1... | collective-permute-start | bytes 294920 | tf_op jit(solution)/shard_map/ppermute | solution.py:14
  353.1 12.4 %collective-permute-start.11 = (bf16[1,384,128]{2,1,0:T(8,128)(2,1)S(1)}, bf16[1,384,128]{2,1,0:T(8,128)(2,1)S(1)}, u32[]{:S(2)}, u32[]{:S(2)}) collective-permute-start(bf16[1,384,128]{2,1,0:T(8,128)(2,1)S(1)} %fusion.60), channel_id=1, source_target_pairs={{4,0},{6,2},{8,4},{10,6},{12,8},{14,10},{16,12},{18,14},{20,16},{2... | collective-permute-start | bytes 294920 | tf_op jit(solution)/shard_map/ppermute | solution.py:14
  362.2 5.9 %collective-permute-start.10 = (bf16[1,384,128]{2,1,0:T(8,128)(2,1)S(1)}, bf16[1,384,128]{2,1,0:T(8,128)(2,1)S(1)}, u32[]{:S(2)}, u32[]{:S(2)}) collective-permute-start(bf16[1,384,128]{2,1,0:T(8,128)(2,1)S(1)} %fusion.60), channel_id=1, source_target_pairs={{2,0},{4,2},{6,4},{8,6},{10,8},{12,10},{14,12},{16,14},{18,16},{20... | collective-permute-start | bytes 294920 | tf_op jit(solution)/shard_map/ppermute | solution.py:14
  370.3 16.1 %collective-permute-start.13 = (bf16[1,384,128]{2,1,0:T(8,128)(2,1)S(1)}, bf16[1,384,128]{2,1,0:T(8,128)(2,1)S(1)}, u32[]{:S(2)}, u32[]{:S(2)}) collective-permute-start(bf16[1,384,128]{2,1,0:T(8,128)(2,1)S(1)} %get-tuple-element.146), channel_id=1, source_target_pairs={{0,2},{2,4},{4,6},{6,8},{8,10},{10,12},{12,14},{14,16},{16,18},{18... | collective-permute-start | bytes 294920 | tf_op jit(solution)/shard_map/ppermute | solution.py:14
  372.5 14.2 %collective-permute-start.12 = (bf16[1,384,128]{2,1,0:T(8,128)(2,1)S(1)}, bf16[1,384,128]{2,1,0:T(8,128)(2,1)S(1)}, u32[]{:S(2)}, u32[]{:S(2)}) collective-permute-start(bf16[1,384,128]{2,1,0:T(8,128)(2,1)S(1)} %get-tuple-element.146), channel_id=1, source_target_pairs={{0,4},{2,6},{4,8},{6,10},{8,12},{10,14},{12,16},{14,18},{16,20},{1... | collective-permute-start | bytes 294920 | tf_op jit(solution)/shard_map/ppermute | solution.py:14
  374.4 12.5 %collective-permute-start.15 = (bf16[1,384,128]{2,1,0:T(8,128)(2,1)S(1)}, bf16[1,384,128]{2,1,0:T(8,128)(2,1)S(1)}, u32[]{:S(2)}, u32[]{:S(2)}) collective-permute-start(bf16[1,384,128]{2,1,0:T(8,128)(2,1)S(1)} %get-tuple-element.146), channel_id=1, source_target_pairs={{4,0},{6,2},{8,4},{10,6},{12,8},{14,10},{16,12},{18,14},{20,16},{2... | collective-permute-start | bytes 294920 | tf_op jit(solution)/shard_map/ppermute | solution.py:14
  383.5 5.9 %collective-permute-start.14 = (bf16[1,384,128]{2,1,0:T(8,128)(2,1)S(1)}, bf16[1,384,128]{2,1,0:T(8,128)(2,1)S(1)}, u32[]{:S(2)}, u32[]{:S(2)}) collective-permute-start(bf16[1,384,128]{2,1,0:T(8,128)(2,1)S(1)} %get-tuple-element.146), channel_id=1, source_target_pairs={{2,0},{4,2},{6,4},{8,6},{10,8},{12,10},{14,12},{16,14},{18,16},{20... | collective-permute-start | bytes 294920 | tf_op jit(solution)/shard_map/ppermute | solution.py:14
  389.7 16.1 %collective-permute-start.17 = (bf16[1,384,128]{2,1,0:T(8,128)(2,1)S(1)}, bf16[1,384,128]{2,1,0:T(8,128)(2,1)S(1)}, u32[]{:S(2)}, u32[]{:S(2)}) collective-permute-start(bf16[1,384,128]{2,1,0:T(8,128)(2,1)S(1)} %fusion.58), channel_id=1, source_target_pairs={{0,2},{2,4},{4,6},{6,8},{8,10},{10,12},{12,14},{14,16},{16,18},{18... | collective-permute-start | bytes 294920 | tf_op jit(solution)/shard_map/ppermute | solution.py:14
  391.8 14.2 %collective-permute-start.16 = (bf16[1,384,128]{2,1,0:T(8,128)(2,1)S(1)}, bf16[1,384,128]{2,1,0:T(8,128)(2,1)S(1)}, u32[]{:S(2)}, u32[]{:S(2)}) collective-permute-start(bf16[1,384,128]{2,1,0:T(8,128)(2,1)S(1)} %fusion.58), channel_id=1, source_target_pairs={{0,4},{2,6},{4,8},{6,10},{8,12},{10,14},{12,16},{14,18},{16,20},{1... | collective-permute-start | bytes 294920 | tf_op jit(solution)/shard_map/ppermute | solution.py:14
  393.7 12.4 %collective-permute-start.19 = (bf16[1,384,128]{2,1,0:T(8,128)(2,1)S(1)}, bf16[1,384,128]{2,1,0:T(8,128)(2,1)S(1)}, u32[]{:S(2)}, u32[]{:S(2)}) collective-permute-start(bf16[1,384,128]{2,1,0:T(8,128)(2,1)S(1)} %fusion.58), channel_id=1, source_target_pairs={{4,0},{6,2},{8,4},{10,6},{12,8},{14,10},{16,12},{18,14},{20,16},{2... | collective-permute-start | bytes 294920 | tf_op jit(solution)/shard_map/ppermute | solution.py:14
  402.8 5.9 %collective-permute-start.18 = (bf16[1,384,128]{2,1,0:T(8,128)(2,1)S(1)}, bf16[1,384,128]{2,1,0:T(8,128)(2,1)S(1)}, u32[]{:S(2)}, u32[]{:S(2)}) collective-permute-start(bf16[1,384,128]{2,1,0:T(8,128)(2,1)S(1)} %fusion.58), channel_id=1, source_target_pairs={{2,0},{4,2},{6,4},{8,6},{10,8},{12,10},{14,12},{16,14},{18,16},{20... | collective-permute-start | bytes 294920 | tf_op jit(solution)/shard_map/ppermute | solution.py:14
Sparse Core Ops, SparseCore 0:
  13.2 223.0 all-gather.2
where the time goes:
time: 418 us; the launch traced here: 416 us
  waiting for transfers between devices  234 us (56%)
  starting transfers between devices  80.5 us (19%)
  other arithmetic  40.6 us (10%)
  local copies, waits for them, and re-layouts  26.7 us (6%)
  matrix products  19.1 us (5%)
  between operations  14.7 us (4%)
    all_gather x1, waiting for transfers between devices, per_device(): arriving = lax.all_gather(strips, 'band', axis=0, tiled=True)  222 us
    ppermute x20, starting transfers between devices, passed_along(): return lax.ppermute(array, axis, pairs)  80.5 us
    dynamic_slice x32, local copies, waits for them, and re-layouts, per_device(): state, unused = lax.scan(advance, state, (blocks, starts))  25.9 us
    dot_general x50, matrix products, conv_valid(): jnp.dot(tap_slice.reshape(-1, tap_slice.shape[-1]), weight[kernel_tap], p...  12.6 us
    ppermute x20, waiting for transfers between devices, passed_along(): return lax.ppermute(array, axis, pairs)  11.3 us
    div x16, other arithmetic, strip_step(): row_centre = strip_row.astype(jnp.float32) / total_rows  10.4 us
    add x16, other arithmetic, strip_step(): strip_row = row_zero + jnp.arange(block_rows, dtype=jnp.int32)  10.3 us
  transfers between devices with their start and end apart: 21, of which 6 were waited for; matrix products, arithmetic and copies ran while one was open for 2% of the time, Pallas kernels for 0%

commit v1 on v0

--- a/solution.py
+++ b/solution.py
@@ -1,8 +1,11 @@
 import math
+
+import numpy as np
 
 import jax
 import jax.numpy as jnp
 from jax import lax
+from jax.experimental import pallas as pl
 from jax.sharding import PartitionSpec as P
 
 ITERS = 2
@@ -139,57 +142,129 @@
     return (1.0 - update_gate) * hidden + update_gate * candidate
 
 
+GATHER_BITS = (4, 3, 2, 7, 6, 5, 1, 0)
+
+
+def match_kernel(f1_ref, s_ref, w_ref, m_in, a_in, m_out, a_out):
+    @pl.when(pl.program_id(0) == 0)
+    def _():
+        m_out[...] = m_in[...]
+        a_out[...] = a_in[...]
+
+    scores = lax.dot_general(
+        f1_ref[...], s_ref[...], (((1,), (1,)), ((), ())), preferred_element_type=jnp.float32
+    ) / 16.0
+    m_old = m_out[:, 0:1]
+    m_new = jnp.maximum(m_old, jnp.max(scores, axis=1, keepdims=True))
+    p = jnp.exp(scores - m_new)
+    shrink = jnp.exp(m_old - m_new)
+    p_hi = p.astype(jnp.bfloat16)
+    p_lo = (p - p_hi.astype(jnp.float32)).astype(jnp.bfloat16)
+    w = w_ref[...]
+    part = jnp.dot(p_hi, w, preferred_element_type=jnp.float32) + jnp.dot(
+        p_lo, w, preferred_element_type=jnp.float32
+    )
+    a_out[...] = a_out[...] * shrink + part
+    m_out[...] = jnp.broadcast_to(m_new, m_out.shape)
+
+
+def match_block(state, features, block, block_rows, grid_cols):
+    count, channels = block.shape
+    pixels = features.shape[0]
+    tile = min(count, 768)
+    strip_row = jnp.repeat(block_rows, grid_cols).astype(jnp.float32)
+    strip_col = (jnp.arange(count, dtype=jnp.int32) % grid_cols).astype(jnp.float32)
+    weights = jnp.concatenate(
+        [
+            jnp.ones((count, 1), jnp.float32),
+            strip_row[:, None],
+            strip_col[:, None],
+            jnp.zeros((count, 125), jnp.float32),
+        ],
+        axis=1,
+    ).astype(jnp.bfloat16)
+    running_max, acc = state
+    return pl.pallas_call(
+        match_kernel,
+        grid=(count // tile,),
+        in_specs=[
+            pl.BlockSpec((pixels, channels), lambda i: (0, 0)),
+            pl.BlockSpec((tile, channels), lambda i: (i, 0)),
+            pl.BlockSpec((tile, 128), lambda i: (i, 0)),
+            pl.BlockSpec((pixels, 128), lambda i: (0, 0)),
+            pl.BlockSpec((pixels, 128), lambda i: (0, 0)),
+        ],
+        out_specs=[
+            pl.BlockSpec((pixels, 128), lambda i: (0, 0)),
+            pl.BlockSpec((pixels, 128), lambda i: (0, 0)),
+        ],
+        out_shape=[
+            jax.ShapeDtypeStruct((pixels, 128), jnp.float32),
+            jax.ShapeDtypeStruct((pixels, 128), jnp.float32),
+        ],
+    )(features, block, weights, running_max, acc)
+
+
+def deposit_table(bits):
+    table = np.zeros((1 << len(bits),), np.int32)
+    for q in range(table.shape[0]):
+        table[q] = sum(((q >> i) & 1) << b for i, b in enumerate(bits))
+    return table
+
+
 def per_device(frame1, frame2, context, hidden_init, offsets, w_motion, w_row, w_col):
     band_rows, image_width, channels = frame1.shape
-    total_rows = band_rows * lax.axis_size("band")
-    row_first = lax.axis_index("band") * band_rows
+    bands = lax.axis_size("band")
+    total_rows = band_rows * bands
+    band = lax.axis_index("band")
+    row_first = band * band_rows
     strips = pool_strips(frame2)
+    grid_cols = strips.shape[1]
     target_row, target_col, pixel_row, pixel_col = lookup_targets(
         offsets, row_first, total_rows, image_width
     )
     pixel_count = band_rows * image_width
     features = frame1.reshape(pixel_count, channels)
-    rows_target = target_row.reshape(pixel_count)
-    cols_target = target_col.reshape(pixel_count)
-    zeros_state = jnp.zeros((pixel_count,), jnp.float32)
-    initial = (
-        jnp.full((pixel_count,), -jnp.inf, jnp.float32),
-        zeros_state,
-        zeros_state,
-        zeros_state,
-        zeros_state,
-    )
-    state = initial
-    arriving = lax.all_gather(strips, "band", axis=0, tiled=True)
-    arriving_rows = arriving.shape[0]
-    step_rows = min(arriving_rows, 16)
-    full_steps = arriving_rows // step_rows
-    blocks = arriving.reshape((full_steps, step_rows) + arriving.shape[1:])
-    starts = step_rows * jnp.arange(full_steps, dtype=jnp.int32)
-
-    def advance(carry, pieces):
-        return (
-            strip_step(
-                carry,
-                features,
-                pieces[0],
-                pieces[1],
-                total_rows,
-                image_width,
-                rows_target,
-                cols_target,
-            ),
-            None,
-        )
-
-    state, unused = lax.scan(advance, state, (blocks, starts))
-    running_max, denominator, acc_row, acc_col, lookup = state
-    flow_row = (acc_row / denominator).reshape(band_rows, image_width) - pixel_row.astype(
-        jnp.float32
-    ) / total_rows
-    flow_col = (acc_col / denominator).reshape(band_rows, image_width) - pixel_col.astype(
-        jnp.float32
-    ) / image_width
+    deposit = deposit_table(GATHER_BITS)
+    state = (
+        jnp.full((pixel_count, 128), -jnp.inf, jnp.float32),
+        jnp.zeros((pixel_count, 128), jnp.float32),
+    )
+    held = strips.reshape(band_rows * grid_cols, channels)
+    state = match_block(state, features, held, band[None], grid_cols)
+    for step, bit in enumerate(GATHER_BITS):
+        flip = 1 << bit
+        pairs = [(i, i ^ flip) for i in range(bands)]
+        got = lax.ppermute(held, "band", pairs)
+        got_rows = (band ^ flip) ^ jnp.asarray(deposit[: 1 << step])
+        state = match_block(state, features, got, got_rows, grid_cols)
+        if step + 1 < len(GATHER_BITS):
+            held = jnp.concatenate([held, got], axis=0)
+    running_max, acc = state
+    denominator = acc[:, 0]
+    flow_row = (acc[:, 1] / denominator / total_rows).reshape(
+        band_rows, image_width
+    ) - pixel_row.astype(jnp.float32) / total_rows
+    flow_col = (
+        (8.0 * (acc[:, 2] / denominator) + 3.5) / image_width
+    ).reshape(band_rows, image_width) - pixel_col.astype(jnp.float32) / image_width
+    inverse = np.argsort(deposit).astype(np.int32)
+    t_row = target_row.reshape(pixel_count)
+    t_col = target_col.reshape(pixel_count)
+    valid = t_row >= 0
+    place = jnp.asarray(inverse)[jnp.where(valid, t_row ^ band, 0)] * grid_cols + jnp.where(
+        valid, t_col, 0
+    )
+    half = held.shape[0]
+    picked = jnp.where(
+        (place < half)[:, None],
+        jnp.take(held, jnp.minimum(place, half - 1), axis=0),
+        jnp.take(got, jnp.maximum(place - half, 0), axis=0),
+    )
+    found = jnp.sum(
+        features.astype(jnp.float32) * picked.astype(jnp.float32), axis=1
+    ) / math.sqrt(channels)
+    lookup = jnp.where(valid, found, 0.0)
     lookup = lookup.reshape(band_rows, image_width)
     motion = jax.nn.relu(
         flow_row[..., None] * w_motion[0]

time: 418 us -> 314 us (0.75)
  waiting for transfers between devices: 234 us -> 80.9 us
  starting transfers between devices: 80.5 us -> 127 us
  Pallas kernels: 0 us -> 37.5 us
  other arithmetic: 40.6 us -> 19.1 us
  between operations: 14.7 us -> 1.76 us
  matrix products: 19.1 us -> 14.9 us
    all_gather x1 -> x0, waiting for transfers between devices: 222 us -> none  [per_device(): arriving = lax.all_gather(strips, 'band', axis=0, tiled=True)]
    ppermute x0 -> x8, starting transfers between devices: none -> 45.5 us  [per_device(): got = lax.ppermute(held, 'band', pairs)]
    ppermute x0 -> x8, waiting for transfers between devices: none -> 43 us  [per_device(): got = lax.ppermute(held, 'band', pairs)]
    pallas_call x0 -> x9, Pallas kernels: none -> 37.5 us  [match_block(): pl.pallas_call(match_kernel, grid=(count // tile,), in_specs=[pl.BlockSpe...]
    ppermute x20, waiting for transfers between devices: 11.3 us -> 37.9 us  [passed_along(): return lax.ppermute(array, axis, pairs)]
    dynamic_slice x32 -> x0, local copies, waits for them, and re-layouts: 25.9 us -> none  [per_device(): state, unused = lax.scan(advance, state, (blocks, starts))]
    gather x0 -> x3, local copies, waits for them, and re-layouts: none -> 10.8 us  [the longest x1 4.08 us: per_device(): jnp.take(got, jnp.maximum(place - half, 0), axis=0)]
    add x32 -> x0, other arithmetic: 10.7 us -> none  [the longest x16 10.3 us: strip_step(): strip_row = row_zero + jnp.arange(block_rows, dtype=jnp.int32)]
  transfers between devices with their start and end apart: 21 -> 28, of which waited for: 6 -> 13; matrix products, arithmetic and copies ran while one was open for 2% -> 14% of each run, Pallas kernels for 0% -> 9%
where the time goes in v1:
time: 314 us; the launch traced here: 311 us
  starting transfers between devices  127 us (40%)
  waiting for transfers between devices  80.9 us (26%)
  Pallas kernels  37.5 us (12%)
  local copies, waits for them, and re-layouts  29.8 us (9%)
  other arithmetic  19.1 us (6%)
  matrix products  14.9 us (5%)
    ppermute x20, starting transfers between devices, passed_along(): return lax.ppermute(array, axis, pairs)  81.6 us
    ppermute x8, starting transfers between devices, per_device(): got = lax.ppermute(held, 'band', pairs)  45.5 us
    ppermute x8, waiting for transfers between devices, per_device(): got = lax.ppermute(held, 'band', pairs)  43 us
    ppermute x20, waiting for transfers between devices, passed_along(): return lax.ppermute(array, axis, pairs)  37.9 us
    pallas_call x9, Pallas kernels, match_block(): pl.pallas_call(match_kernel, grid=(count // tile,), in_specs=[pl.BlockSpe...  37.5 us
    dot_general x50, matrix products, conv_valid(): jnp.dot(tap_slice.reshape(-1, tap_slice.shape[-1]), weight[kernel_tap], p...  14.9 us
    concatenate x9, other arithmetic, match_block(): jnp.concatenate([jnp.ones((count, 1), jnp.float32), strip_row[:, None], s...  10.4 us
    unnamed x54, local copies, waits for them, and re-layouts  8.27 us
  transfers between devices with their start and end apart: 28, of which 13 were waited for; matrix products, arithmetic and copies ran while one was open for 14% of the time, Pallas kernels for 9%

profile of v1, /device:TPU:7, one launch (start us, length us, event | category | flops | bytes accessed | tf_op | source)
XLA Modules:
  0.0 311.2 jit_solution(13450853179165862989)
XLA Ops:
  2.3 15.4 %collective-permute-start = (bf16[48,256]{1,0:T(8,128)(2,1)S(1)}, bf16[48,256]{1,0:T(8,128)(2,1)S(1)}, u32[]{:S(2)}, u32[]{:S(2)}) collective-permute-start(bf16[48,256]{1,0:T(8,128)(2,1)S(1)} %get-tuple-element.45.s_ref), channel_id=1, source_target_pairs={{0,32},{2,34},{4,36},{6,38},{8,40},{10,42},{12,44},{14,46},{16,48}... | collective-permute-start | bytes 73736 | tf_op jit(solution)/shard_map/ppermute | solution.py:238
  19.1 2.8 gather_fusion
  23.9 4.0 %collective-permute-start.1 = (bf16[96,256]{1,0:T(8,128)(2,1)S(1)}, bf16[96,256]{1,0:T(8,128)(2,1)S(1)}, u32[]{:S(2)}, u32[]{:S(2)}) collective-permute-start(bf16[96,256]{1,0:T(8,128)(2,1)S(1)} %pad_maximum_fusion.3), channel_id=1, source_target_pairs={{0,16},{2,18},{4,20},{6,22},{8,24},{10,26},{12,28},{14,30},{16,0},... | collective-permute-start | bytes 147464 | tf_op jit(solution)/shard_map/ppermute | solution.py:238
  28.6 4.1 %collective-permute-done.1.s_ref = bf16[96,256]{1,0:T(8,128)(2,1)S(1)} collective-permute-done((bf16[96,256]{1,0:T(8,128)(2,1)S(1)}, bf16[96,256]{1,0:T(8,128)(2,1)S(1)}, u32[]{:S(2)}, u32[]{:S(2)}) %collective-permute-start.1) | collective-permute-done | bytes 49184 | tf_op jit(solution)/shard_map/ppermute | solution.py:238
  32.7 3.3 %collective-permute-start.2 = (bf16[192,256]{1,0:T(8,128)(2,1)S(1)}, bf16[192,256]{1,0:T(8,128)(2,1)S(1)}, u32[]{:S(2)}, u32[]{:S(2)}) collective-permute-start(bf16[192,256]{1,0:T(8,128)(2,1)S(1)} %pad_maximum_fusion.2), channel_id=1, source_target_pairs={{0,8},{2,10},{4,12},{6,14},{8,0},{10,2},{12,4},{14,6},{16,24},{18,... | collective-permute-start | bytes 294920 | tf_op jit(solution)/shard_map/ppermute | solution.py:238
  36.6 3.4 %collective-permute-done.2.s_ref = bf16[192,256]{1,0:T(8,128)(2,1)S(1)} collective-permute-done((bf16[192,256]{1,0:T(8,128)(2,1)S(1)}, bf16[192,256]{1,0:T(8,128)(2,1)S(1)}, u32[]{:S(2)}, u32[]{:S(2)}) %collective-permute-start.2) | collective-permute-done | bytes 98336 | tf_op jit(solution)/shard_map/ppermute | solution.py:238
  40.0 3.0 collective-permute-start.3
  44.5 3.5 %collective-permute-done.3.s_ref = bf16[384,256]{1,0:T(8,128)(2,1)S(1)} collective-permute-done((bf16[384,256]{1,0:T(8,128)(2,1)S(1)}, bf16[384,256]{1,0:T(8,128)(2,1)S(1)}, u32[]{:S(2)}, u32[]{:S(2)}) %collective-permute-start.3) | collective-permute-done | bytes 196640 | tf_op jit(solution)/shard_map/ppermute | solution.py:238
  48.8 4.8 %collective-permute-start.4 = (bf16[768,256]{1,0:T(8,128)(2,1)S(1)}, bf16[768,256]{1,0:T(8,128)(2,1)S(1)}, u32[]{:S(2)}, u32[]{:S(2)}) collective-permute-start(bf16[768,256]{1,0:T(8,128)(2,1)S(1)} %get-tuple-element.54), channel_id=1, source_target_pairs={{0,128},{2,130},{4,132},{6,134},{8,136},{10,138},{12,140},{14,142}... | collective-permute-start | bytes 1179656 | tf_op jit(solution)/shard_map/ppermute | solution.py:238
  55.3 3.5 %collective-permute-done.4.s_ref = bf16[768,256]{1,0:T(8,128)(2,1)S(1)} collective-permute-done((bf16[768,256]{1,0:T(8,128)(2,1)S(1)}, bf16[768,256]{1,0:T(8,128)(2,1)S(1)}, u32[]{:S(2)}, u32[]{:S(2)}) %collective-permute-start.4) | collective-permute-done | bytes 393248 | tf_op jit(solution)/shard_map/ppermute | solution.py:238
  59.9 3.2 %collective-permute-start.5 = (bf16[1536,256]{1,0:T(8,128)(2,1)S(1)}, bf16[1536,256]{1,0:T(8,128)(2,1)S(1)}, u32[]{:S(2)}, u32[]{:S(2)}) collective-permute-start(bf16[1536,256]{1,0:T(8,128)(2,1)S(1)} %get-tuple-element.50), channel_id=1, source_target_pairs={{0,64},{2,66},{4,68},{6,70},{8,72},{10,74},{12,76},{14,78},{16,80}... | collective-permute-start | bytes 2359304 | tf_op jit(solution)/shard_map/ppermute | solution.py:238
  65.9 10.3 %collective-permute-done.5.s_ref = bf16[1536,256]{1,0:T(8,128)(2,1)S(1)} collective-permute-done((bf16[1536,256]{1,0:T(8,128)(2,1)S(1)}, bf16[1536,256]{1,0:T(8,128)(2,1)S(1)}, u32[]{:S(2)}, u32[]{:S(2)}) %collective-permute-start.5) | collective-permute-done | bytes 786464 | tf_op jit(solution)/shard_map/ppermute | solution.py:238
  79.6 2.9 convert_element_type.336
  90.3 18.2 %collective-permute-done.6.s_ref = bf16[3072,256]{1,0:T(8,128)(2,1)S(1)} collective-permute-done((bf16[3072,256]{1,0:T(8,128)(2,1)}, bf16[3072,256]{1,0:T(8,128)(2,1)S(1)}, u32[]{:S(2)}, u32[]{:S(2)}) %collective-permute-start.6) | collective-permute-done | bytes 1572896 | tf_op jit(solution)/shard_map/ppermute | solution.py:238
  110.9 9.9 %collective-permute-start.7 = (bf16[6144,256]{1,0:T(8,128)(2,1)}, bf16[6144,256]{1,0:T(8,128)(2,1)S(1)}, u32[]{:S(2)}, u32[]{:S(2)}) collective-permute-start(bf16[6144,256]{1,0:T(8,128)(2,1)} %constant_dynamic-update-slice_fusion.18), channel_id=1, source_target_pairs={{0,2},{2,0},{4,6},{6,4},{8,10},{10,8},{12,14},{14,12},{16,18},{18,... | collective-permute-start | bytes 9437192 | tf_op jit(solution)/shard_map/ppermute | solution.py:238
  122.2 2.5 shard_map.176
  125.4 2.9 maximum_maximum_fusion.1.w_ref
  130.2 2.5 maximum_maximum_fusion.w_ref
  132.7 2.6 shard_map.177
  135.3 2.6 shard_map.178
  137.9 2.6 shard_map.179
  140.5 2.8 shard_map.180
  143.3 3.0 shard_map.181
  146.3 4.2 %shard_map.182 = (f32[384,128]{1,0:T(8,128)}, f32[384,128]{1,0:T(8,128)}) custom-call(bf16[384,256]{1,0:T(8,128)(2,1)} %bitcast.414, bf16[1536,256]{1,0:T(8,128)(2,1)} %copy-done.6, bf16[1536,128]{1,0:T(8,128)(2,1)} %maximum_maximum_fusion.2.w_ref, f32[384,128]{1,0:T(8,128)} %get-tuple-element.30.m_in, f32[384,128]{1,0:T(8,128)} %get-tuple-element.31.a_in), custom_call_target="tpu_custom_call" | custom-call | tf_op jit(solution)/shard_map/pallas_call | solution.py:187
  150.5 4.0 %gather_fusion.1 = bf16[384,256]{1,0:T(8,128)(2,1)S(1)} fusion(bf16[6144,256]{1,0:T(8,128)(2,1)} %constant_dynamic-update-slice_fusion.18, s32[1024]{0:T(1024)S(1)} %get-tuple-element.88), kind=kCustom, calls=%fused_computation.clone | custom fusion | bytes 394752 | tf_op jit(solution)/shard_map/jit(_take)/gather | solution.py:261
  154.5 6.4 %shard_map.183 = (f32[384,128]{1,0:T(8,128)}, f32[384,128]{1,0:T(8,128)}) custom-call(bf16[384,256]{1,0:T(8,128)(2,1)} %bitcast.415, bf16[3072,256]{1,0:T(8,128)(2,1)} %copy-done.3, bf16[3072,128]{1,0:T(8,128)(2,1)} %maximum_maximum_fusion.1.w_ref, f32[384,128]{1,0:T(8,128)} %get-tuple-element.32.m_in, f32[384,128]{1,0:T(8,128)} %get-tuple-element.33.a_in), custom_call_target="tpu_custom_call" | custom-call | tf_op jit(solution)/shard_map/pallas_call | solution.py:187
  162.5 10.8 %shard_map.184 = (f32[384,128]{1,0:T(8,128)}, f32[384,128]{1,0:T(8,128)}) custom-call(bf16[384,256]{1,0:T(8,128)(2,1)} %bitcast.416, bf16[6144,256]{1,0:T(8,128)(2,1)} %copy-done.2, bf16[6144,128]{1,0:T(8,128)(2,1)} %maximum_maximum_fusion.w_ref, f32[384,128]{1,0:T(8,128)} %get-tuple-element.34.m_in, f32[384,128]{1,0:T(8,128)} %get-tuple-element.35.a_in), custom_call_target="tpu_custom_call" | custom-call | tf_op jit(solution)/shard_map/pallas_call | solution.py:187
  174.9 4.1 %gather_fusion.2 = bf16[384,256]{1,0:T(8,128)(2,1)S(1)} fusion(bf16[6144,256]{1,0:T(8,128)(2,1)} %copy-done.2, s32[1024]{0:T(1024)S(1)} %get-tuple-element.87), kind=kCustom, calls=%fused_computation.1.clone | custom fusion | bytes 394752 | tf_op jit(solution)/shard_map/jit(_take)/gather | solution.py:262
  179.8 2.5 collective-permute-start.15
  182.3 3.0 collective-permute-start.13
  185.3 2.6 collective-permute-start.12
  187.9 2.1 collective-permute-start.14
  193.6 3.6 %collective-permute-start.9 = (bf16[1,384,128]{2,1,0:T(8,128)(2,1)S(1)}, bf16[1,384,128]{2,1,0:T(8,128)(2,1)S(1)}, u32[]{:S(2)}, u32[]{:S(2)}) collective-permute-start(bf16[1,384,128]{2,1,0:T(8,128)(2,1)S(1)} %get-tuple-element.81), channel_id=1, source_target_pairs={{0,2},{2,4},{4,6},{6,8},{8,10},{10,12},{12,14},{14,16},{16,18},{18... | collective-permute-start | bytes 294920 | tf_op jit(solution)/shard_map/ppermute | solution.py:17
  197.8 5.4 %collective-permute-done.9 = bf16[1,384,128]{2,1,0:T(8,128)(2,1)S(1)} collective-permute-done((bf16[1,384,128]{2,1,0:T(8,128)(2,1)S(1)}, bf16[1,384,128]{2,1,0:T(8,128)(2,1)S(1)}, u32[]{:S(2)}, u32[]{:S(2)}) %collective-permute-start.9) | collective-permute-done | bytes 98336 | tf_op jit(solution)/shard_map/ppermute | solution.py:17
  205.3 9.7 %collective-permute-done.8 = bf16[1,384,128]{2,1,0:T(8,128)(2,1)S(1)} collective-permute-done((bf16[1,384,128]{2,1,0:T(8,128)(2,1)S(1)}, bf16[1,384,128]{2,1,0:T(8,128)(2,1)S(1)}, u32[]{:S(2)}, u32[]{:S(2)}) %collective-permute-start.8) | collective-permute-done | bytes 98336 | tf_op jit(solution)/shard_map/ppermute | solution.py:17
  215.0 3.4 %collective-permute-start.11 = (bf16[1,384,128]{2,1,0:T(8,128)(2,1)S(1)}, bf16[1,384,128]{2,1,0:T(8,128)(2,1)S(1)}, u32[]{:S(2)}, u32[]{:S(2)}) collective-permute-start(bf16[1,384,128]{2,1,0:T(8,128)(2,1)S(1)} %get-tuple-element.81), channel_id=1, source_target_pairs={{4,0},{6,2},{8,4},{10,6},{12,8},{14,10},{16,12},{18,14},{20,16},{2... | collective-permute-start | bytes 294920 | tf_op jit(solution)/shard_map/ppermute | solution.py:17
  220.4 12.4 %collective-permute-start.10 = (bf16[1,384,128]{2,1,0:T(8,128)(2,1)S(1)}, bf16[1,384,128]{2,1,0:T(8,128)(2,1)S(1)}, u32[]{:S(2)}, u32[]{:S(2)}) collective-permute-start(bf16[1,384,128]{2,1,0:T(8,128)(2,1)S(1)} %get-tuple-element.81), channel_id=1, source_target_pairs={{2,0},{4,2},{6,4},{8,6},{10,8},{12,10},{14,12},{16,14},{18,16},{20... | collective-permute-start | bytes 294920 | tf_op jit(solution)/shard_map/ppermute | solution.py:17
  234.6 9.8 %collective-permute-start.19 = (bf16[1,384,128]{2,1,0:T(8,128)(2,1)S(1)}, bf16[1,384,128]{2,1,0:T(8,128)(2,1)S(1)}, u32[]{:S(2)}, u32[]{:S(2)}) collective-permute-start(bf16[1,384,128]{2,1,0:T(8,128)(2,1)S(1)} %fusion.81), channel_id=1, source_target_pairs={{4,0},{6,2},{8,4},{10,6},{12,8},{14,10},{16,12},{18,14},{20,16},{2... | collective-permute-start | bytes 294920 | tf_op jit(solution)/shard_map/ppermute | solution.py:17
  248.4 2.4 collective-permute-start.18
  250.9 7.0 %collective-permute-done.16 = bf16[1,384,128]{2,1,0:T(8,128)(2,1)S(1)} collective-permute-done((bf16[1,384,128]{2,1,0:T(8,128)(2,1)S(1)}, bf16[1,384,128]{2,1,0:T(8,128)(2,1)S(1)}, u32[]{:S(2)}, u32[]{:S(2)}) %collective-permute-start.16) | collective-permute-done | bytes 98336 | tf_op jit(solution)/shard_map/ppermute | solution.py:17
  260.4 10.8 %collective-permute-start.23 = (bf16[1,384,128]{2,1,0:T(8,128)(2,1)S(1)}, bf16[1,384,128]{2,1,0:T(8,128)(2,1)S(1)}, u32[]{:S(2)}, u32[]{:S(2)}) collective-permute-start(bf16[1,384,128]{2,1,0:T(8,128)(2,1)S(1)} %get-tuple-element.85), channel_id=1, source_target_pairs={{4,0},{6,2},{8,4},{10,6},{12,8},{14,10},{16,12},{18,14},{20,16},{2... | collective-permute-start | bytes 294920 | tf_op jit(solution)/shard_map/ppermute | solution.py:17
  271.3 1.9 collective-permute-start.21
  275.3 2.4 collective-permute-start.22
  277.9 6.9 %collective-permute-done.20 = bf16[1,384,128]{2,1,0:T(8,128)(2,1)S(1)} collective-permute-done((bf16[1,384,128]{2,1,0:T(8,128)(2,1)S(1)}, bf16[1,384,128]{2,1,0:T(8,128)(2,1)S(1)}, u32[]{:S(2)}, u32[]{:S(2)}) %collective-permute-start.20) | collective-permute-done | bytes 98336 | tf_op jit(solution)/shard_map/ppermute | solution.py:17
  285.6 10.8 %collective-permute-start.27 = (bf16[1,384,128]{2,1,0:T(8,128)(2,1)S(1)}, bf16[1,384,128]{2,1,0:T(8,128)(2,1)S(1)}, u32[]{:S(2)}, u32[]{:S(2)}) collective-permute-start(bf16[1,384,128]{2,1,0:T(8,128)(2,1)S(1)} %fusion.79), channel_id=1, source_target_pairs={{4,0},{6,2},{8,4},{10,6},{12,8},{14,10},{16,12},{18,14},{20,16},{2... | collective-permute-start | bytes 294920 | tf_op jit(solution)/shard_map/ppermute | solution.py:17
  296.4 1.9 collective-permute-start.25
  300.4 2.4 collective-permute-start.26
  303.0 7.0 %collective-permute-done.24 = bf16[1,384,128]{2,1,0:T(8,128)(2,1)S(1)} collective-permute-done((bf16[1,384,128]{2,1,0:T(8,128)(2,1)S(1)}, bf16[1,384,128]{2,1,0:T(8,128)(2,1)S(1)}, u32[]{:S(2)}, u32[]{:S(2)}) %collective-permute-start.24) | collective-permute-done | bytes 98336 | tf_op jit(solution)/shard_map/ppermute | solution.py:17
  (197 shorter events, 58.1 us)
Async XLA Ops:
  0.6 18.4 %copy-start = (s32[256]{0:T(256)S(1)}, s32[256]{0:T(256)}, u32[]{:S(2)}) copy-start(s32[256]{0:T(256)} %constant.210.clone) | copy-start | bytes 3076
  2.3 37.7 %copy-start.10 = (bf16[48,256]{1,0:T(8,128)(2,1)}, bf16[48,256]{1,0:T(8,128)(2,1)S(1)}, u32[]{:S(2)}) copy-start(bf16[48,256]{1,0:T(8,128)(2,1)S(1)} %get-tuple-element.45.s_ref) | copy-start | bytes 73732
  2.3 21.6 %collective-permute-start = (bf16[48,256]{1,0:T(8,128)(2,1)S(1)}, bf16[48,256]{1,0:T(8,128)(2,1)S(1)}, u32[]{:S(2)}, u32[]{:S(2)}) collective-permute-start(bf16[48,256]{1,0:T(8,128)(2,1)S(1)} %get-tuple-element.45.s_ref), channel_id=1, source_target_pairs={{0,32},{2,34},{4,36},{6,38},{8,40},{10,42},{12,44},{14,46},{16,48}... | collective-permute-start | bytes 73736 | tf_op jit(solution)/shard_map/ppermute | solution.py:238
  18.5 3.5 %copy-start.17 = (f32[3,128]{1,0:T(4,128)S(1)}, f32[3,128]{1,0:T(4,128)}, u32[]{:S(2)}) copy-start(f32[3,128]{1,0:T(4,128)} %param.24) | copy-start | bytes 4612
  18.5 3.8 %copy-start.23 = (s32[128]{0:T(128)S(1)}, s32[128]{0:T(128)}, u32[]{:S(2)}) copy-start(s32[128]{0:T(128)} %constant.209.clone) | copy-start | bytes 1540
  18.5 3.9 %copy-start.22 = (s32[64]{0:T(128)S(1)}, s32[64]{0:T(128)}, u32[]{:S(2)}) copy-start(s32[64]{0:T(128)} %constant.208.clone) | copy-start | bytes 772
  18.5 3.9 %copy-start.21 = (s32[16]{0:T(128)S(1)}, s32[16]{0:T(128)}, u32[]{:S(2)}) copy-start(s32[16]{0:T(128)} %constant.206.clone) | copy-start | bytes 196
  18.5 3.9 %copy-start.20 = (s32[8]{0:T(128)S(1)}, s32[8]{0:T(128)}, u32[]{:S(2)}) copy-start(s32[8]{0:T(128)} %constant.205.clone) | copy-start | bytes 100
  18.7 5.2 %copy-start.19 = (s32[4]{0:T(128)S(1)}, s32[4]{0:T(128)}, u32[]{:S(2)}) copy-start(s32[4]{0:T(128)} %constant.204.clone) | copy-start | bytes 52
  23.9 30.3 %copy-start.15 = (bf16[48,256]{1,0:T(8,128)(2,1)}, bf16[48,256]{1,0:T(8,128)(2,1)S(1)}, u32[]{:S(2)}) copy-start(bf16[48,256]{1,0:T(8,128)(2,1)S(1)} %collective-permute-done.s_ref) | copy-start | bytes 73732
  23.9 8.8 %collective-permute-start.1 = (bf16[96,256]{1,0:T(8,128)(2,1)S(1)}, bf16[96,256]{1,0:T(8,128)(2,1)S(1)}, u32[]{:S(2)}, u32[]{:S(2)}) collective-permute-start(bf16[96,256]{1,0:T(8,128)(2,1)S(1)} %pad_maximum_fusion.3), channel_id=1, source_target_pairs={{0,16},{2,18},{4,20},{6,22},{8,24},{10,26},{12,28},{14,30},{16,0},... | collective-permute-start | bytes 147464 | tf_op jit(solution)/shard_map/ppermute | solution.py:238
  32.7 21.9 %copy-start.14 = (bf16[96,256]{1,0:T(8,128)(2,1)}, bf16[96,256]{1,0:T(8,128)(2,1)S(1)}, u32[]{:S(2)}) copy-start(bf16[96,256]{1,0:T(8,128)(2,1)S(1)} %collective-permute-done.1.s_ref) | copy-start | bytes 147460
  32.7 7.3 %collective-permute-start.2 = (bf16[192,256]{1,0:T(8,128)(2,1)S(1)}, bf16[192,256]{1,0:T(8,128)(2,1)S(1)}, u32[]{:S(2)}, u32[]{:S(2)}) collective-permute-start(bf16[192,256]{1,0:T(8,128)(2,1)S(1)} %pad_maximum_fusion.2), channel_id=1, source_target_pairs={{0,8},{2,10},{4,12},{6,14},{8,0},{10,2},{12,4},{14,6},{16,24},{18,... | collective-permute-start | bytes 294920 | tf_op jit(solution)/shard_map/ppermute | solution.py:238
  40.0 19.9 %copy-start.12 = (bf16[192,256]{1,0:T(8,128)(2,1)}, bf16[192,256]{1,0:T(8,128)(2,1)S(1)}, u32[]{:S(2)}) copy-start(bf16[192,256]{1,0:T(8,128)(2,1)S(1)} %collective-permute-done.2.s_ref) | copy-start | bytes 294916
  40.0 7.9 %collective-permute-start.3 = (bf16[384,256]{1,0:T(8,128)(2,1)S(1)}, bf16[384,256]{1,0:T(8,128)(2,1)S(1)}, u32[]{:S(2)}, u32[]{:S(2)}) collective-permute-start(bf16[384,256]{1,0:T(8,128)(2,1)S(1)} %pad_maximum_fusion), channel_id=1, source_target_pairs={{0,256},{2,258},{4,260},{6,262},{8,264},{10,266},{12,268},{14,270}... | collective-permute-start | bytes 589832 | tf_op jit(solution)/shard_map/ppermute | solution.py:238
  48.8 10.0 %collective-permute-start.4 = (bf16[768,256]{1,0:T(8,128)(2,1)S(1)}, bf16[768,256]{1,0:T(8,128)(2,1)S(1)}, u32[]{:S(2)}, u32[]{:S(2)}) collective-permute-start(bf16[768,256]{1,0:T(8,128)(2,1)S(1)} %get-tuple-element.54), channel_id=1, source_target_pairs={{0,128},{2,130},{4,132},{6,134},{8,136},{10,138},{12,140},{14,142}... | collective-permute-start | bytes 1179656 | tf_op jit(solution)/shard_map/ppermute | solution.py:238
  54.3 10.6 %copy-start.5 = (bf16[1,384,128]{2,1,0:T(8,128)(2,1)S(1)}, bf16[1,384,128]{2,1,0:T(8,128)(2,1)}, u32[]{:S(2)}) copy-start(bf16[1,384,128]{2,1,0:T(8,128)(2,1)} %param.22) | copy-start | bytes 294916
  58.8 7.1 %copy-start.9 = (bf16[768,256]{1,0:T(8,128)(2,1)}, bf16[768,256]{1,0:T(8,128)(2,1)S(1)}, u32[]{:S(2)}) copy-start(bf16[768,256]{1,0:T(8,128)(2,1)S(1)} %collective-permute-done.4.s_ref) | copy-start | bytes 1179652
  59.9 16.3 %collective-permute-start.5 = (bf16[1536,256]{1,0:T(8,128)(2,1)S(1)}, bf16[1536,256]{1,0:T(8,128)(2,1)S(1)}, u32[]{:S(2)}, u32[]{:S(2)}) collective-permute-start(bf16[1536,256]{1,0:T(8,128)(2,1)S(1)} %get-tuple-element.50), channel_id=1, source_target_pairs={{0,64},{2,66},{4,68},{6,70},{8,72},{10,74},{12,76},{14,78},{16,80}... | collective-permute-start | bytes 2359304 | tf_op jit(solution)/shard_map/ppermute | solution.py:238
  64.8 14.7 %copy-start.18 = (s32[32]{0:T(128)S(1)}, s32[32]{0:T(128)}, u32[]{:S(2)}) copy-start(s32[32]{0:T(128)} %constant.207.clone) | copy-start | bytes 388
  76.2 1.4 copy-start.6
  77.6 30.9 %collective-permute-start.6 = (bf16[3072,256]{1,0:T(8,128)(2,1)}, bf16[3072,256]{1,0:T(8,128)(2,1)S(1)}, u32[]{:S(2)}, u32[]{:S(2)}) collective-permute-start(bf16[3072,256]{1,0:T(8,128)(2,1)} %get-tuple-element.46), channel_id=1, source_target_pairs={{0,4},{2,6},{4,0},{6,2},{8,12},{10,14},{12,8},{14,10},{16,20},{18,... | collective-permute-start | bytes 4718600 | tf_op jit(solution)/shard_map/ppermute | solution.py:238
  110.9 50.0 %collective-permute-start.7 = (bf16[6144,256]{1,0:T(8,128)(2,1)}, bf16[6144,256]{1,0:T(8,128)(2,1)S(1)}, u32[]{:S(2)}, u32[]{:S(2)}) collective-permute-start(bf16[6144,256]{1,0:T(8,128)(2,1)} %constant_dynamic-update-slice_fusion.18), channel_id=1, source_target_pairs={{0,2},{2,0},{4,6},{6,4},{8,10},{10,8},{12,14},{14,12},{16,18},{18,... | collective-permute-start | bytes 9437192 | tf_op jit(solution)/shard_map/ppermute | solution.py:238
  125.4 4.8 %copy-start.4 = (bf16[6144,1]{1,0:T(8,128)(2,1)S(1)}, bf16[6144,1]{1,0:T(8,128)(2,1)}, u32[]{:S(2)}) copy-start(bf16[6144,1]{1,0:T(8,128)(2,1)} %convert_element_type.336) | copy-start | bytes 36868
  160.9 1.6 copy-start.2
  173.3 5.6 %copy-start.1 = (bf16[1,384,256]{2,1,0:T(8,128)(2,1)S(1)}, bf16[1,384,256]{2,1,0:T(8,128)(2,1)}, u32[]{:S(2)}) copy-start(bf16[1,384,256]{2,1,0:T(8,128)(2,1)} %param.19) | copy-start | bytes 589828
  173.3 6.2 %copy-start.11 = (bf16[1,384,128]{2,1,0:T(8,128)(2,1)S(1)}, bf16[1,384,128]{2,1,0:T(8,128)(2,1)}, u32[]{:S(2)}) copy-start(bf16[1,384,128]{2,1,0:T(8,128)(2,1)} %param.21) | copy-start | bytes 294916
  174.8 4.7 %copy-start.8 = (bf16[5,384,384]{2,1,0:T(8,128)(2,1)S(1)}, bf16[5,384,384]{2,1,0:T(8,128)(2,1)}, u32[]{:S(2)}) copy-start(bf16[5,384,384]{2,1,0:T(8,128)(2,1)} %param.25) | copy-start | bytes 4423684
  179.8 53.7 %collective-permute-start.15 = (bf16[1,384,256]{2,1,0:T(8,128)(2,1)S(1)}, bf16[1,384,256]{2,1,0:T(8,128)(2,1)S(1)}, u32[]{:S(2)}, u32[]{:S(2)}) collective-permute-start(bf16[1,384,256]{2,1,0:T(8,128)(2,1)S(1)} %pad_maximum_fusion.1), channel_id=1, source_target_pairs={{4,0},{6,2},{8,4},{10,6},{12,8},{14,10},{16,12},{18,14},{20,16},{2... | collective-permute-start | bytes 589832 | tf_op jit(solution)/shard_map/ppermute | solution.py:17
  182.3 50.7 %collective-permute-start.13 = (bf16[1,384,256]{2,1,0:T(8,128)(2,1)S(1)}, bf16[1,384,256]{2,1,0:T(8,128)(2,1)S(1)}, u32[]{:S(2)}, u32[]{:S(2)}) collective-permute-start(bf16[1,384,256]{2,1,0:T(8,128)(2,1)S(1)} %pad_maximum_fusion.1), channel_id=1, source_target_pairs={{0,2},{2,4},{4,6},{6,8},{8,10},{10,12},{12,14},{14,16},{16,18},{18... | collective-permute-start | bytes 589832 | tf_op jit(solution)/shard_map/ppermute | solution.py:17
  185.3 48.0 %collective-permute-start.12 = (bf16[1,384,256]{2,1,0:T(8,128)(2,1)S(1)}, bf16[1,384,256]{2,1,0:T(8,128)(2,1)S(1)}, u32[]{:S(2)}, u32[]{:S(2)}) collective-permute-start(bf16[1,384,256]{2,1,0:T(8,128)(2,1)S(1)} %pad_maximum_fusion.1), channel_id=1, source_target_pairs={{0,4},{2,6},{4,8},{6,10},{8,12},{10,14},{12,16},{14,18},{16,20},{1... | collective-permute-start | bytes 589832 | tf_op jit(solution)/shard_map/ppermute | solution.py:17
  187.9 45.9 %collective-permute-start.14 = (bf16[1,384,256]{2,1,0:T(8,128)(2,1)S(1)}, bf16[1,384,256]{2,1,0:T(8,128)(2,1)S(1)}, u32[]{:S(2)}, u32[]{:S(2)}) collective-permute-start(bf16[1,384,256]{2,1,0:T(8,128)(2,1)S(1)} %pad_maximum_fusion.1), channel_id=1, source_target_pairs={{2,0},{4,2},{6,4},{8,6},{10,8},{12,10},{14,12},{16,14},{18,16},{20... | collective-permute-start | bytes 589832 | tf_op jit(solution)/shard_map/ppermute | solution.py:17
  193.6 9.6 %collective-permute-start.9 = (bf16[1,384,128]{2,1,0:T(8,128)(2,1)S(1)}, bf16[1,384,128]{2,1,0:T(8,128)(2,1)S(1)}, u32[]{:S(2)}, u32[]{:S(2)}) collective-permute-start(bf16[1,384,128]{2,1,0:T(8,128)(2,1)S(1)} %get-tuple-element.81), channel_id=1, source_target_pairs={{0,2},{2,4},{4,6},{6,8},{8,10},{10,12},{12,14},{14,16},{16,18},{18... | collective-permute-start | bytes 294920 | tf_op jit(solution)/shard_map/ppermute | solution.py:17
  203.2 11.8 %collective-permute-start.8 = (bf16[1,384,128]{2,1,0:T(8,128)(2,1)S(1)}, bf16[1,384,128]{2,1,0:T(8,128)(2,1)S(1)}, u32[]{:S(2)}, u32[]{:S(2)}) collective-permute-start(bf16[1,384,128]{2,1,0:T(8,128)(2,1)S(1)} %get-tuple-element.81), channel_id=1, source_target_pairs={{0,4},{2,6},{4,8},{6,10},{8,12},{10,14},{12,16},{14,18},{16,20},{1... | collective-permute-start | bytes 294920 | tf_op jit(solution)/shard_map/ppermute | solution.py:17
  215.0 5.3 %collective-permute-start.11 = (bf16[1,384,128]{2,1,0:T(8,128)(2,1)S(1)}, bf16[1,384,128]{2,1,0:T(8,128)(2,1)S(1)}, u32[]{:S(2)}, u32[]{:S(2)}) collective-permute-start(bf16[1,384,128]{2,1,0:T(8,128)(2,1)S(1)} %get-tuple-element.81), channel_id=1, source_target_pairs={{4,0},{6,2},{8,4},{10,6},{12,8},{14,10},{16,12},{18,14},{20,16},{2... | collective-permute-start | bytes 294920 | tf_op jit(solution)/shard_map/ppermute | solution.py:17
  220.4 13.9 %collective-permute-start.10 = (bf16[1,384,128]{2,1,0:T(8,128)(2,1)S(1)}, bf16[1,384,128]{2,1,0:T(8,128)(2,1)S(1)}, u32[]{:S(2)}, u32[]{:S(2)}) collective-permute-start(bf16[1,384,128]{2,1,0:T(8,128)(2,1)S(1)} %get-tuple-element.81), channel_id=1, source_target_pairs={{2,0},{4,2},{6,4},{8,6},{10,8},{12,10},{14,12},{16,14},{18,16},{20... | collective-permute-start | bytes 294920 | tf_op jit(solution)/shard_map/ppermute | solution.py:17
  234.6 23.5 %collective-permute-start.19 = (bf16[1,384,128]{2,1,0:T(8,128)(2,1)S(1)}, bf16[1,384,128]{2,1,0:T(8,128)(2,1)S(1)}, u32[]{:S(2)}, u32[]{:S(2)}) collective-permute-start(bf16[1,384,128]{2,1,0:T(8,128)(2,1)S(1)} %fusion.81), channel_id=1, source_target_pairs={{4,0},{6,2},{8,4},{10,6},{12,8},{14,10},{16,12},{18,14},{20,16},{2... | collective-permute-start | bytes 294920 | tf_op jit(solution)/shard_map/ppermute | solution.py:17
  244.4 6.4 %collective-permute-start.17 = (bf16[1,384,128]{2,1,0:T(8,128)(2,1)S(1)}, bf16[1,384,128]{2,1,0:T(8,128)(2,1)S(1)}, u32[]{:S(2)}, u32[]{:S(2)}) collective-permute-start(bf16[1,384,128]{2,1,0:T(8,128)(2,1)S(1)} %fusion.81), channel_id=1, source_target_pairs={{0,2},{2,4},{4,6},{6,8},{8,10},{10,12},{12,14},{14,16},{16,18},{18... | collective-permute-start | bytes 294920 | tf_op jit(solution)/shard_map/ppermute | solution.py:17
  246.4 11.5 %collective-permute-start.16 = (bf16[1,384,128]{2,1,0:T(8,128)(2,1)S(1)}, bf16[1,384,128]{2,1,0:T(8,128)(2,1)S(1)}, u32[]{:S(2)}, u32[]{:S(2)}) collective-permute-start(bf16[1,384,128]{2,1,0:T(8,128)(2,1)S(1)} %fusion.81), channel_id=1, source_target_pairs={{0,4},{2,6},{4,8},{6,10},{8,12},{10,14},{12,16},{14,18},{16,20},{1... | collective-permute-start | bytes 294920 | tf_op jit(solution)/shard_map/ppermute | solution.py:17
  248.4 9.9 %collective-permute-start.18 = (bf16[1,384,128]{2,1,0:T(8,128)(2,1)S(1)}, bf16[1,384,128]{2,1,0:T(8,128)(2,1)S(1)}, u32[]{:S(2)}, u32[]{:S(2)}) collective-permute-start(bf16[1,384,128]{2,1,0:T(8,128)(2,1)S(1)} %fusion.81), channel_id=1, source_target_pairs={{2,0},{4,2},{6,4},{8,6},{10,8},{12,10},{14,12},{16,14},{18,16},{20... | collective-permute-start | bytes 294920 | tf_op jit(solution)/shard_map/ppermute | solution.py:17
  260.4 24.7 %collective-permute-start.23 = (bf16[1,384,128]{2,1,0:T(8,128)(2,1)S(1)}, bf16[1,384,128]{2,1,0:T(8,128)(2,1)S(1)}, u32[]{:S(2)}, u32[]{:S(2)}) collective-permute-start(bf16[1,384,128]{2,1,0:T(8,128)(2,1)S(1)} %get-tuple-element.85), channel_id=1, source_target_pairs={{4,0},{6,2},{8,4},{10,6},{12,8},{14,10},{16,12},{18,14},{20,16},{2... | collective-permute-start | bytes 294920 | tf_op jit(solution)/shard_map/ppermute | solution.py:17
  271.3 6.5 %collective-permute-start.21 = (bf16[1,384,128]{2,1,0:T(8,128)(2,1)S(1)}, bf16[1,384,128]{2,1,0:T(8,128)(2,1)S(1)}, u32[]{:S(2)}, u32[]{:S(2)}) collective-permute-start(bf16[1,384,128]{2,1,0:T(8,128)(2,1)S(1)} %get-tuple-element.85), channel_id=1, source_target_pairs={{0,2},{2,4},{4,6},{6,8},{8,10},{10,12},{12,14},{14,16},{16,18},{18... | collective-permute-start | bytes 294920 | tf_op jit(solution)/shard_map/ppermute | solution.py:17
  273.4 11.5 %collective-permute-start.20 = (bf16[1,384,128]{2,1,0:T(8,128)(2,1)S(1)}, bf16[1,384,128]{2,1,0:T(8,128)(2,1)S(1)}, u32[]{:S(2)}, u32[]{:S(2)}) collective-permute-start(bf16[1,384,128]{2,1,0:T(8,128)(2,1)S(1)} %get-tuple-element.85), channel_id=1, source_target_pairs={{0,4},{2,6},{4,8},{6,10},{8,12},{10,14},{12,16},{14,18},{16,20},{1... | collective-permute-start | bytes 294920 | tf_op jit(solution)/shard_map/ppermute | solution.py:17
  275.3 9.9 %collective-permute-start.22 = (bf16[1,384,128]{2,1,0:T(8,128)(2,1)S(1)}, bf16[1,384,128]{2,1,0:T(8,128)(2,1)S(1)}, u32[]{:S(2)}, u32[]{:S(2)}) collective-permute-start(bf16[1,384,128]{2,1,0:T(8,128)(2,1)S(1)} %get-tuple-element.85), channel_id=1, source_target_pairs={{2,0},{4,2},{6,4},{8,6},{10,8},{12,10},{14,12},{16,14},{18,16},{20... | collective-permute-start | bytes 294920 | tf_op jit(solution)/shard_map/ppermute | solution.py:17
  285.6 24.5 %collective-permute-start.27 = (bf16[1,384,128]{2,1,0:T(8,128)(2,1)S(1)}, bf16[1,384,128]{2,1,0:T(8,128)(2,1)S(1)}, u32[]{:S(2)}, u32[]{:S(2)}) collective-permute-start(bf16[1,384,128]{2,1,0:T(8,128)(2,1)S(1)} %fusion.79), channel_id=1, source_target_pairs={{4,0},{6,2},{8,4},{10,6},{12,8},{14,10},{16,12},{18,14},{20,16},{2... | collective-permute-start | bytes 294920 | tf_op jit(solution)/shard_map/ppermute | solution.py:17
  296.4 6.4 %collective-permute-start.25 = (bf16[1,384,128]{2,1,0:T(8,128)(2,1)S(1)}, bf16[1,384,128]{2,1,0:T(8,128)(2,1)S(1)}, u32[]{:S(2)}, u32[]{:S(2)}) collective-permute-start(bf16[1,384,128]{2,1,0:T(8,128)(2,1)S(1)} %fusion.79), channel_id=1, source_target_pairs={{0,2},{2,4},{4,6},{6,8},{8,10},{10,12},{12,14},{14,16},{16,18},{18... | collective-permute-start | bytes 294920 | tf_op jit(solution)/shard_map/ppermute | solution.py:17
  298.5 11.5 %collective-permute-start.24 = (bf16[1,384,128]{2,1,0:T(8,128)(2,1)S(1)}, bf16[1,384,128]{2,1,0:T(8,128)(2,1)S(1)}, u32[]{:S(2)}, u32[]{:S(2)}) collective-permute-start(bf16[1,384,128]{2,1,0:T(8,128)(2,1)S(1)} %fusion.79), channel_id=1, source_target_pairs={{0,4},{2,6},{4,8},{6,10},{8,12},{10,14},{12,16},{14,18},{16,20},{1... | collective-permute-start | bytes 294920 | tf_op jit(solution)/shard_map/ppermute | solution.py:17
  300.4 9.9 %collective-permute-start.26 = (bf16[1,384,128]{2,1,0:T(8,128)(2,1)S(1)}, bf16[1,384,128]{2,1,0:T(8,128)(2,1)S(1)}, u32[]{:S(2)}, u32[]{:S(2)}) collective-permute-start(bf16[1,384,128]{2,1,0:T(8,128)(2,1)S(1)} %fusion.79), channel_id=1, source_target_pairs={{2,0},{4,2},{6,4},{8,6},{10,8},{12,10},{14,12},{16,14},{18,16},{20... | collective-permute-start | bytes 294920 | tf_op jit(solution)/shard_map/ppermute | solution.py:17
  (4 other events, 4.7 us)

commit v2 on v1

--- a/solution.py
+++ b/solution.py
@@ -21,6 +21,12 @@
     band_rows, image_width, channels = frame2.shape
     blocks = frame2.astype(jnp.float32).reshape(band_rows, image_width // 8, 8, channels)
     return (jnp.sum(blocks, axis=2) / 2.0).astype(jnp.bfloat16)
+
+
+def scaled_strips(frame2, scale):
+    band_rows, image_width, channels = frame2.shape
+    blocks = frame2.astype(jnp.float32).reshape(band_rows, image_width // 8, 8, channels)
+    return (jnp.sum(blocks, axis=2) / (2.0 * scale)).astype(jnp.bfloat16)
 
 
 def lookup_targets(offsets, row_first, total_rows, image_width):
@@ -153,7 +159,7 @@
 
     scores = lax.dot_general(
         f1_ref[...], s_ref[...], (((1,), (1,)), ((), ())), preferred_element_type=jnp.float32
-    ) / 16.0
+    )
     m_old = m_out[:, 0:1]
     m_new = jnp.maximum(m_old, jnp.max(scores, axis=1, keepdims=True))
     p = jnp.exp(scores - m_new)
@@ -202,6 +208,11 @@
             jax.ShapeDtypeStruct((pixels, 128), jnp.float32),
             jax.ShapeDtypeStruct((pixels, 128), jnp.float32),
         ],
+        cost_estimate=pl.CostEstimate(
+            flops=2 * pixels * count * (channels + 256),
+            transcendentals=pixels * count,
+            bytes_accessed=2 * count * (channels + 128) + 2 * pixels * channels + 16 * pixels * 128,
+        ),
     )(features, block, weights, running_max, acc)
 
 
@@ -218,7 +229,7 @@
     total_rows = band_rows * bands
     band = lax.axis_index("band")
     row_first = band * band_rows
-    strips = pool_strips(frame2)
+    strips = scaled_strips(frame2, math.sqrt(channels))
     grid_cols = strips.shape[1]
     target_row, target_col, pixel_row, pixel_col = lookup_targets(
         offsets, row_first, total_rows, image_width
@@ -237,9 +248,11 @@
         pairs = [(i, i ^ flip) for i in range(bands)]
         got = lax.ppermute(held, "band", pairs)
         got_rows = (band ^ flip) ^ jnp.asarray(deposit[: 1 << step])
+        settled = state
         state = match_block(state, features, got, got_rows, grid_cols)
         if step + 1 < len(GATHER_BITS):
             held = jnp.concatenate([held, got], axis=0)
+            held, settled = lax.optimization_barrier((held, settled))
     running_max, acc = state
     denominator = acc[:, 0]
     flow_row = (acc[:, 1] / denominator / total_rows).reshape(
@@ -261,9 +274,7 @@
         jnp.take(held, jnp.minimum(place, half - 1), axis=0),
         jnp.take(got, jnp.maximum(place - half, 0), axis=0),
     )
-    found = jnp.sum(
-        features.astype(jnp.float32) * picked.astype(jnp.float32), axis=1
-    ) / math.sqrt(channels)
+    found = jnp.sum(features.astype(jnp.float32) * picked.astype(jnp.float32), axis=1)
     lookup = jnp.where(valid, found, 0.0)
     lookup = lookup.reshape(band_rows, image_width)
     motion = jax.nn.relu(

time: 314 us -> 289 us (0.920)
  waiting for transfers between devices: 80.9 us -> 64.7 us
  local copies, waits for them, and re-layouts: 29.8 us -> 18.2 us
  other arithmetic: 19.1 us -> 22.9 us
    ppermute x8, waiting for transfers between devices: 43 us -> 28.7 us  [per_device(): got = lax.ppermute(held, 'band', pairs)]
    unnamed x54 -> x48, local copies, waits for them, and re-layouts: 8.27 us -> 0.55 us
    concatenate x3 -> x7, other arithmetic: 0.03 us -> 4.24 us  [per_device(): held = jnp.concatenate([held, got], axis=0)]
  transfers between devices with their start and end apart: 28 -> 28, of which waited for: 13 -> 13; matrix products, arithmetic and copies ran while one was open for 14% -> 15% of each run, Pallas kernels for 9% -> 9%
where the time goes in v2:
time: 289 us; the launch traced here: 288 us
  starting transfers between devices  127 us (44%)
  waiting for transfers between devices  64.7 us (22%)
  Pallas kernels  37.3 us (13%)
  other arithmetic  22.9 us (8%)
  local copies, waits for them, and re-layouts  18.2 us (6%)
  matrix products  16.4 us (6%)
    ppermute x20, starting transfers between devices, passed_along(): return lax.ppermute(array, axis, pairs)  80.7 us
    ppermute x8, starting transfers between devices, per_device(): got = lax.ppermute(held, 'band', pairs)  45.9 us
    pallas_call x9, Pallas kernels, match_block(): pl.pallas_call(match_kernel, grid=(count // tile,), in_specs=[pl.BlockSpe...  37.3 us
    ppermute x20, waiting for transfers between devices, passed_along(): return lax.ppermute(array, axis, pairs)  36 us
    ppermute x8, waiting for transfers between devices, per_device(): got = lax.ppermute(held, 'band', pairs)  28.7 us
    dot_general x50, matrix products, conv_valid(): jnp.dot(tap_slice.reshape(-1, tap_slice.shape[-1]), weight[kernel_tap], p...  16.4 us
    concatenate x9, other arithmetic, match_block(): jnp.concatenate([jnp.ones((count, 1), jnp.float32), strip_row[:, None], s...  8.97 us
  transfers between devices with their start and end apart: 28, of which 13 were waited for; matrix products, arithmetic and copies ran while one was open for 15% of the time, Pallas kernels for 9%

profile of v2, /device:TPU:7, one launch (start us, length us, event | category | flops | bytes accessed | tf_op | source)
XLA Modules:
  0.0 287.8 jit_solution(16121991456803688168)
XLA Ops:
  1.7 15.4 %collective-permute-start = (bf16[48,256]{1,0:T(8,128)(2,1)S(1)}, bf16[48,256]{1,0:T(8,128)(2,1)S(1)}, u32[]{:S(2)}, u32[]{:S(2)}) collective-permute-start(bf16[48,256]{1,0:T(8,128)(2,1)S(1)} %multiply_convert_fusion.s_ref), channel_id=1, source_target_pairs={{0,32},{2,34},{4,36},{6,38},{8,40},{10,42},{12,44},{14,46},{16,48}... | collective-permute-start | bytes 73736 | tf_op jit(solution)/shard_map/ppermute | solution.py:249
  20.6 2.8 gather_fusion
  27.0 2.5 shard_map.176
  30.3 4.0 %collective-permute-start.1 = (bf16[96,256]{1,0:T(8,128)(2,1)S(1)}, bf16[96,256]{1,0:T(8,128)(2,1)S(1)}, u32[]{:S(2)}, u32[]{:S(2)}) collective-permute-start(bf16[96,256]{1,0:T(8,128)(2,1)S(1)} %pad_maximum_fusion.7), channel_id=1, source_target_pairs={{0,16},{2,18},{4,20},{6,22},{8,24},{10,26},{12,28},{14,30},{16,0},... | collective-permute-start | bytes 147464 | tf_op jit(solution)/shard_map/ppermute | solution.py:249
  34.4 2.5 shard_map.177
  36.9 2.2 collective-permute-done.1.s_ref
  39.1 3.3 %collective-permute-start.2 = (bf16[192,256]{1,0:T(8,128)(2,1)S(1)}, bf16[192,256]{1,0:T(8,128)(2,1)S(1)}, u32[]{:S(2)}, u32[]{:S(2)}) collective-permute-start(bf16[192,256]{1,0:T(8,128)(2,1)S(1)} %pad_maximum_fusion.6), channel_id=1, source_target_pairs={{0,8},{2,10},{4,12},{6,14},{8,0},{10,2},{12,4},{14,6},{16,24},{18,... | collective-permute-start | bytes 294920 | tf_op jit(solution)/shard_map/ppermute | solution.py:249
  42.4 2.6 shard_map.178
  46.4 3.0 %collective-permute-start.3 = (bf16[384,256]{1,0:T(8,128)(2,1)S(1)}, bf16[384,256]{1,0:T(8,128)(2,1)S(1)}, u32[]{:S(2)}, u32[]{:S(2)}) collective-permute-start(bf16[384,256]{1,0:T(8,128)(2,1)S(1)} %pad_maximum_fusion.4), channel_id=1, source_target_pairs={{0,256},{2,258},{4,260},{6,262},{8,264},{10,266},{12,268},{14,270}... | collective-permute-start | bytes 589832 | tf_op jit(solution)/shard_map/ppermute | solution.py:249
  49.5 2.6 shard_map.179
  52.1 2.2 collective-permute-done.3.s_ref
  54.4 4.8 %collective-permute-start.4 = (bf16[768,256]{1,0:T(8,128)(2,1)S(1)}, bf16[768,256]{1,0:T(8,128)(2,1)S(1)}, u32[]{:S(2)}, u32[]{:S(2)}) collective-permute-start(bf16[768,256]{1,0:T(8,128)(2,1)S(1)} %pad_maximum_fusion.3), channel_id=1, source_target_pairs={{0,128},{2,130},{4,132},{6,134},{8,136},{10,138},{12,140},{14,142}... | collective-permute-start | bytes 1179656 | tf_op jit(solution)/shard_map/ppermute | solution.py:249
  60.4 2.8 shard_map.180
  64.4 3.2 %collective-permute-start.5 = (bf16[1536,256]{1,0:T(8,128)(2,1)S(1)}, bf16[1536,256]{1,0:T(8,128)(2,1)}, u32[]{:S(2)}, u32[]{:S(2)}) collective-permute-start(bf16[1536,256]{1,0:T(8,128)(2,1)S(1)} %pad_maximum_fusion.2), channel_id=1, source_target_pairs={{0,64},{2,66},{4,68},{6,70},{8,72},{10,74},{12,76},{14,78},{16,80}... | collective-permute-start | bytes 2359304 | tf_op jit(solution)/shard_map/ppermute | solution.py:249
  70.4 2.9 %convert_element_type.341 = bf16[6144,1]{1,0:T(8,128)(2,1)} reshape(bf16[128,48]{1,0:T(8,128)(2,1)S(1)} %broadcast_in_dim.140) | data formatting | bytes 24576 | tf_op jit(solution)/shard_map/convert_element_type | solution.py:181
  76.3 3.0 %shard_map.181 = (f32[384,128]{1,0:T(8,128)}, f32[384,128]{1,0:T(8,128)}) custom-call(bf16[384,256]{1,0:T(8,128)(2,1)} %bitcast.413, bf16[768,256]{1,0:T(8,128)(2,1)} %copy-done.9, bf16[768,128]{1,0:T(8,128)(2,1)} %maximum_maximum_fusion.3.w_ref, f32[384,128]{1,0:T(8,128)} %get-tuple-element.39.m_in, f32[384,128]{1,0:T(8,128)} %get-tuple-element.40.a_in), custom_call_target="tpu_custom_call" | custom-call | flops 301989888 | bytes 1572864 | tf_op jit(solution)/shard_map/pallas_call | solution.py:193
  79.3 2.6 collective-permute-done.5.s_ref
  83.1 1.9 collective-permute-start.6
  90.6 4.2 %shard_map.182 = (f32[384,128]{1,0:T(8,128)}, f32[384,128]{1,0:T(8,128)}) custom-call(bf16[384,256]{1,0:T(8,128)(2,1)} %bitcast.414, bf16[1536,256]{1,0:T(8,128)(2,1)} %collective-permute-done.5.s_ref, bf16[1536,128]{1,0:T(8,128)(2,1)} %maximum_maximum_fusion.2.w_ref, f32[384,128]{1,0:T(8,128)} %get-tuple-element.42.m_in, f32[384,128]{1,0:T(8,128)} %get-tuple-element.43.a_in), custom_call_target="tpu_custom_call" | custom-call | flops 603979776 | bytes 2162688 | tf_op jit(solution)/shard_map/pallas_call | solution.py:193
  94.8 19.1 %collective-permute-done.6.s_ref = bf16[3072,256]{1,0:T(8,128)(2,1)} collective-permute-done((bf16[3072,256]{1,0:T(8,128)(2,1)S(1)}, bf16[3072,256]{1,0:T(8,128)(2,1)}, u32[]{:S(2)}, u32[]{:S(2)}) %collective-permute-start.6) | collective-permute-done | bytes 1572896 | tf_op jit(solution)/shard_map/ppermute | solution.py:249
  113.9 2.2 pad_maximum_fusion
  116.1 10.2 %collective-permute-start.7 = (bf16[6144,256]{1,0:T(8,128)(2,1)S(1)}, bf16[6144,256]{1,0:T(8,128)(2,1)}, u32[]{:S(2)}, u32[]{:S(2)}) collective-permute-start(bf16[6144,256]{1,0:T(8,128)(2,1)S(1)} %pad_maximum_fusion), channel_id=1, source_target_pairs={{0,2},{2,0},{4,6},{6,4},{8,10},{10,8},{12,14},{14,12},{16,18},{18,... | collective-permute-start | bytes 9437192 | tf_op jit(solution)/shard_map/ppermute | solution.py:249
  131.6 2.5 maximum_maximum_fusion.w_ref
  134.1 2.0 gather_fusion.1
  136.1 6.3 %shard_map.183 = (f32[384,128]{1,0:T(8,128)}, f32[384,128]{1,0:T(8,128)}) custom-call(bf16[384,256]{1,0:T(8,128)(2,1)} %bitcast.415, bf16[3072,256]{1,0:T(8,128)(2,1)} %collective-permute-done.6.s_ref, bf16[3072,128]{1,0:T(8,128)(2,1)} %maximum_maximum_fusion.1.w_ref, f32[384,128]{1,0:T(8,128)} %get-tuple-element.45.m_in, f32[384,128]{1,0:T(8,128)} %get-tuple-element.46.a_in), custom_call_target="tpu_custom_call" | custom-call | flops 1207959552 | bytes 3342336 | tf_op jit(solution)/shard_map/pallas_call | solution.py:193
  142.5 10.7 %shard_map.184 = (f32[384,128]{1,0:T(8,128)}, f32[384,128]{1,0:T(8,128)}) custom-call(bf16[384,256]{1,0:T(8,128)(2,1)} %bitcast.416, bf16[6144,256]{1,0:T(8,128)(2,1)} %collective-permute-done.7.s_ref, bf16[6144,128]{1,0:T(8,128)(2,1)} %maximum_maximum_fusion.w_ref, f32[384,128]{1,0:T(8,128)} %get-tuple-element.48.m_in, f32[384,128]{1,0:T(8,128)} %get-tuple-element.49.a_in), custom_call_target="tpu_custom_call" | custom-call | flops 2415919104 | bytes 5701632 | tf_op jit(solution)/shard_map/pallas_call | solution.py:193
  154.8 4.1 %gather_fusion.2 = bf16[384,256]{1,0:T(8,128)(2,1)S(1)} fusion(bf16[6144,256]{1,0:T(8,128)(2,1)} %collective-permute-done.7.s_ref, s32[1024]{0:T(1024)S(1)} %get-tuple-element.77), kind=kCustom, calls=%fused_computation.1.clone | custom fusion | bytes 394752 | tf_op jit(solution)/shard_map/jit(_take)/gather | solution.py:275
  159.5 14.4 %collective-permute-start.15 = (bf16[1,384,256]{2,1,0:T(8,128)(2,1)S(1)}, bf16[1,384,256]{2,1,0:T(8,128)(2,1)S(1)}, u32[]{:S(2)}, u32[]{:S(2)}) collective-permute-start(bf16[1,384,256]{2,1,0:T(8,128)(2,1)S(1)} %pad_maximum_fusion.5), channel_id=1, source_target_pairs={{4,0},{6,2},{8,4},{10,6},{12,8},{14,10},{16,12},{18,14},{20,16},{2... | collective-permute-start | bytes 589832 | tf_op jit(solution)/shard_map/ppermute | solution.py:17
  173.9 2.2 collective-permute-start.14
  176.1 3.4 %collective-permute-start.13 = (bf16[1,384,256]{2,1,0:T(8,128)(2,1)S(1)}, bf16[1,384,256]{2,1,0:T(8,128)(2,1)S(1)}, u32[]{:S(2)}, u32[]{:S(2)}) collective-permute-start(bf16[1,384,256]{2,1,0:T(8,128)(2,1)S(1)} %pad_maximum_fusion.5), channel_id=1, source_target_pairs={{0,2},{2,4},{4,6},{6,8},{8,10},{10,12},{12,14},{14,16},{16,18},{18... | collective-permute-start | bytes 589832 | tf_op jit(solution)/shard_map/ppermute | solution.py:17
  179.5 1.9 collective-permute-start.12
  184.4 1.9 collective-permute-start.9
  190.1 9.2 %collective-permute-done.8 = bf16[1,384,128]{2,1,0:T(8,128)(2,1)S(1)} collective-permute-done((bf16[1,384,128]{2,1,0:T(8,128)(2,1)S(1)}, bf16[1,384,128]{2,1,0:T(8,128)(2,1)S(1)}, u32[]{:S(2)}, u32[]{:S(2)}) %collective-permute-start.8) | collective-permute-done | bytes 98336 | tf_op jit(solution)/shard_map/ppermute | solution.py:17
  199.3 3.4 %collective-permute-start.11 = (bf16[1,384,128]{2,1,0:T(8,128)(2,1)S(1)}, bf16[1,384,128]{2,1,0:T(8,128)(2,1)S(1)}, u32[]{:S(2)}, u32[]{:S(2)}) collective-permute-start(bf16[1,384,128]{2,1,0:T(8,128)(2,1)S(1)} %get-tuple-element.69), channel_id=1, source_target_pairs={{4,0},{6,2},{8,4},{10,6},{12,8},{14,10},{16,12},{18,14},{20,16},{2... | collective-permute-start | bytes 294920 | tf_op jit(solution)/shard_map/ppermute | solution.py:17
  204.7 12.4 %collective-permute-start.10 = (bf16[1,384,128]{2,1,0:T(8,128)(2,1)S(1)}, bf16[1,384,128]{2,1,0:T(8,128)(2,1)S(1)}, u32[]{:S(2)}, u32[]{:S(2)}) collective-permute-start(bf16[1,384,128]{2,1,0:T(8,128)(2,1)S(1)} %get-tuple-element.69), channel_id=1, source_target_pairs={{2,0},{4,2},{6,4},{8,6},{10,8},{12,10},{14,12},{16,14},{18,16},{20... | collective-permute-start | bytes 294920 | tf_op jit(solution)/shard_map/ppermute | solution.py:17
  218.9 9.8 %collective-permute-start.19 = (bf16[1,384,128]{2,1,0:T(8,128)(2,1)S(1)}, bf16[1,384,128]{2,1,0:T(8,128)(2,1)S(1)}, u32[]{:S(2)}, u32[]{:S(2)}) collective-permute-start(bf16[1,384,128]{2,1,0:T(8,128)(2,1)S(1)} %fusion.81), channel_id=1, source_target_pairs={{4,0},{6,2},{8,4},{10,6},{12,8},{14,10},{16,12},{18,14},{20,16},{2... | collective-permute-start | bytes 294920 | tf_op jit(solution)/shard_map/ppermute | solution.py:17
  228.7 1.9 collective-permute-start.18
  230.6 3.6 %collective-permute-start.17 = (bf16[1,384,128]{2,1,0:T(8,128)(2,1)S(1)}, bf16[1,384,128]{2,1,0:T(8,128)(2,1)S(1)}, u32[]{:S(2)}, u32[]{:S(2)}) collective-permute-start(bf16[1,384,128]{2,1,0:T(8,128)(2,1)S(1)} %fusion.81), channel_id=1, source_target_pairs={{0,2},{2,4},{4,6},{6,8},{8,10},{10,12},{12,14},{14,16},{16,18},{18... | collective-permute-start | bytes 294920 | tf_op jit(solution)/shard_map/ppermute | solution.py:17
  234.3 2.1 collective-permute-start.16
  236.7 8.9 %collective-permute-done.16 = bf16[1,384,128]{2,1,0:T(8,128)(2,1)S(1)} collective-permute-done((bf16[1,384,128]{2,1,0:T(8,128)(2,1)S(1)}, bf16[1,384,128]{2,1,0:T(8,128)(2,1)S(1)}, u32[]{:S(2)}, u32[]{:S(2)}) %collective-permute-start.16) | collective-permute-done | bytes 98336 | tf_op jit(solution)/shard_map/ppermute | solution.py:17
  248.2 1.9 collective-permute-start.23
  250.1 1.9 collective-permute-start.22
  252.0 3.6 %collective-permute-start.21 = (bf16[1,384,128]{2,1,0:T(8,128)(2,1)S(1)}, bf16[1,384,128]{2,1,0:T(8,128)(2,1)S(1)}, u32[]{:S(2)}, u32[]{:S(2)}) collective-permute-start(bf16[1,384,128]{2,1,0:T(8,128)(2,1)S(1)} %get-tuple-element.73), channel_id=1, source_target_pairs={{0,2},{2,4},{4,6},{6,8},{8,10},{10,12},{12,14},{14,16},{16,18},{18... | collective-permute-start | bytes 294920 | tf_op jit(solution)/shard_map/ppermute | solution.py:17
  255.7 3.4 %collective-permute-start.20 = (bf16[1,384,128]{2,1,0:T(8,128)(2,1)S(1)}, bf16[1,384,128]{2,1,0:T(8,128)(2,1)S(1)}, u32[]{:S(2)}, u32[]{:S(2)}) collective-permute-start(bf16[1,384,128]{2,1,0:T(8,128)(2,1)S(1)} %get-tuple-element.73), channel_id=1, source_target_pairs={{0,4},{2,6},{4,8},{6,10},{8,12},{10,14},{12,16},{14,18},{16,20},{1... | collective-permute-start | bytes 294920 | tf_op jit(solution)/shard_map/ppermute | solution.py:17
  259.4 7.6 %collective-permute-done.20 = bf16[1,384,128]{2,1,0:T(8,128)(2,1)S(1)} collective-permute-done((bf16[1,384,128]{2,1,0:T(8,128)(2,1)S(1)}, bf16[1,384,128]{2,1,0:T(8,128)(2,1)S(1)}, u32[]{:S(2)}, u32[]{:S(2)}) %collective-permute-start.20) | collective-permute-done | bytes 98336 | tf_op jit(solution)/shard_map/ppermute | solution.py:17
  271.6 3.6 %collective-permute-start.25 = (bf16[1,384,128]{2,1,0:T(8,128)(2,1)S(1)}, bf16[1,384,128]{2,1,0:T(8,128)(2,1)S(1)}, u32[]{:S(2)}, u32[]{:S(2)}) collective-permute-start(bf16[1,384,128]{2,1,0:T(8,128)(2,1)S(1)} %fusion.79), channel_id=1, source_target_pairs={{0,2},{2,4},{4,6},{6,8},{8,10},{10,12},{12,14},{14,16},{16,18},{18... | collective-permute-start | bytes 294920 | tf_op jit(solution)/shard_map/ppermute | solution.py:17
  275.3 3.4 %collective-permute-start.24 = (bf16[1,384,128]{2,1,0:T(8,128)(2,1)S(1)}, bf16[1,384,128]{2,1,0:T(8,128)(2,1)S(1)}, u32[]{:S(2)}, u32[]{:S(2)}) collective-permute-start(bf16[1,384,128]{2,1,0:T(8,128)(2,1)S(1)} %fusion.79), channel_id=1, source_target_pairs={{0,4},{2,6},{4,8},{6,10},{8,12},{10,14},{12,16},{14,18},{16,20},{1... | collective-permute-start | bytes 294920 | tf_op jit(solution)/shard_map/ppermute | solution.py:17
  278.9 7.7 %collective-permute-done.24 = bf16[1,384,128]{2,1,0:T(8,128)(2,1)S(1)} collective-permute-done((bf16[1,384,128]{2,1,0:T(8,128)(2,1)S(1)}, bf16[1,384,128]{2,1,0:T(8,128)(2,1)S(1)}, u32[]{:S(2)}, u32[]{:S(2)}) %collective-permute-start.24) | collective-permute-done | bytes 98336 | tf_op jit(solution)/shard_map/ppermute | solution.py:17
  (193 shorter events, 51.9 us)
Async XLA Ops:
  0.6 19.9 %copy-start = (s32[256]{0:T(256)S(1)}, s32[256]{0:T(256)}, u32[]{:S(2)}) copy-start(s32[256]{0:T(256)} %constant.207.clone) | copy-start | bytes 3076
  1.7 21.7 %copy-start.16 = (bf16[48,256]{1,0:T(8,128)(2,1)}, bf16[48,256]{1,0:T(8,128)(2,1)S(1)}, u32[]{:S(2)}) copy-start(bf16[48,256]{1,0:T(8,128)(2,1)S(1)} %multiply_convert_fusion.s_ref) | copy-start | bytes 73732
  1.7 27.9 %collective-permute-start = (bf16[48,256]{1,0:T(8,128)(2,1)S(1)}, bf16[48,256]{1,0:T(8,128)(2,1)S(1)}, u32[]{:S(2)}, u32[]{:S(2)}) collective-permute-start(bf16[48,256]{1,0:T(8,128)(2,1)S(1)} %multiply_convert_fusion.s_ref), channel_id=1, source_target_pairs={{0,32},{2,34},{4,36},{6,38},{8,40},{10,42},{12,44},{14,46},{16,48}... | collective-permute-start | bytes 73736 | tf_op jit(solution)/shard_map/ppermute | solution.py:249
  20.0 3.4 %copy-start.23 = (s32[128]{0:T(128)S(1)}, s32[128]{0:T(128)}, u32[]{:S(2)}) copy-start(s32[128]{0:T(128)} %constant.206.clone) | copy-start | bytes 1540
  20.2 5.5 %copy-start.22 = (s32[64]{0:T(128)S(1)}, s32[64]{0:T(128)}, u32[]{:S(2)}) copy-start(s32[64]{0:T(128)} %constant.205.clone) | copy-start | bytes 772
  20.5 13.8 %copy-start.21 = (s32[32]{0:T(128)S(1)}, s32[32]{0:T(128)}, u32[]{:S(2)}) copy-start(s32[32]{0:T(128)} %constant.204.clone) | copy-start | bytes 388
  23.4 19.0 %copy-start.20 = (s32[16]{0:T(128)S(1)}, s32[16]{0:T(128)}, u32[]{:S(2)}) copy-start(s32[16]{0:T(128)} %constant.203.clone) | copy-start | bytes 196
  25.6 23.8 %copy-start.19 = (s32[8]{0:T(128)S(1)}, s32[8]{0:T(128)}, u32[]{:S(2)}) copy-start(s32[8]{0:T(128)} %constant.202.clone) | copy-start | bytes 100
  29.6 4.8 %copy-start.18 = (bf16[48,256]{1,0:T(8,128)(2,1)}, bf16[48,256]{1,0:T(8,128)(2,1)S(1)}, u32[]{:S(2)}) copy-start(bf16[48,256]{1,0:T(8,128)(2,1)S(1)} %collective-permute-done.s_ref) | copy-start | bytes 73732
  30.3 8.7 %collective-permute-start.1 = (bf16[96,256]{1,0:T(8,128)(2,1)S(1)}, bf16[96,256]{1,0:T(8,128)(2,1)S(1)}, u32[]{:S(2)}, u32[]{:S(2)}) collective-permute-start(bf16[96,256]{1,0:T(8,128)(2,1)S(1)} %pad_maximum_fusion.7), channel_id=1, source_target_pairs={{0,16},{2,18},{4,20},{6,22},{8,24},{10,26},{12,28},{14,30},{16,0},... | collective-permute-start | bytes 147464 | tf_op jit(solution)/shard_map/ppermute | solution.py:249
  39.1 7.3 %collective-permute-start.2 = (bf16[192,256]{1,0:T(8,128)(2,1)S(1)}, bf16[192,256]{1,0:T(8,128)(2,1)S(1)}, u32[]{:S(2)}, u32[]{:S(2)}) collective-permute-start(bf16[192,256]{1,0:T(8,128)(2,1)S(1)} %pad_maximum_fusion.6), channel_id=1, source_target_pairs={{0,8},{2,10},{4,12},{6,14},{8,0},{10,2},{12,4},{14,6},{16,24},{18,... | collective-permute-start | bytes 294920 | tf_op jit(solution)/shard_map/ppermute | solution.py:249
  46.4 7.9 %collective-permute-start.3 = (bf16[384,256]{1,0:T(8,128)(2,1)S(1)}, bf16[384,256]{1,0:T(8,128)(2,1)S(1)}, u32[]{:S(2)}, u32[]{:S(2)}) collective-permute-start(bf16[384,256]{1,0:T(8,128)(2,1)S(1)} %pad_maximum_fusion.4), channel_id=1, source_target_pairs={{0,256},{2,258},{4,260},{6,262},{8,264},{10,266},{12,268},{14,270}... | collective-permute-start | bytes 589832 | tf_op jit(solution)/shard_map/ppermute | solution.py:249
  54.3 6.1 %copy-start.13 = (bf16[384,256]{1,0:T(8,128)(2,1)}, bf16[384,256]{1,0:T(8,128)(2,1)S(1)}, u32[]{:S(2)}) copy-start(bf16[384,256]{1,0:T(8,128)(2,1)S(1)} %collective-permute-done.3.s_ref) | copy-start | bytes 589828
  54.4 10.0 %collective-permute-start.4 = (bf16[768,256]{1,0:T(8,128)(2,1)S(1)}, bf16[768,256]{1,0:T(8,128)(2,1)S(1)}, u32[]{:S(2)}, u32[]{:S(2)}) collective-permute-start(bf16[768,256]{1,0:T(8,128)(2,1)S(1)} %pad_maximum_fusion.3), channel_id=1, source_target_pairs={{0,128},{2,130},{4,132},{6,134},{8,136},{10,138},{12,140},{14,142}... | collective-permute-start | bytes 1179656 | tf_op jit(solution)/shard_map/ppermute | solution.py:249
  64.4 5.9 %copy-start.9 = (bf16[768,256]{1,0:T(8,128)(2,1)}, bf16[768,256]{1,0:T(8,128)(2,1)S(1)}, u32[]{:S(2)}) copy-start(bf16[768,256]{1,0:T(8,128)(2,1)S(1)} %collective-permute-done.4.s_ref) | copy-start | bytes 1179652
  64.4 17.4 %collective-permute-start.5 = (bf16[1536,256]{1,0:T(8,128)(2,1)S(1)}, bf16[1536,256]{1,0:T(8,128)(2,1)}, u32[]{:S(2)}, u32[]{:S(2)}) collective-permute-start(bf16[1536,256]{1,0:T(8,128)(2,1)S(1)} %pad_maximum_fusion.2), channel_id=1, source_target_pairs={{0,64},{2,66},{4,68},{6,70},{8,72},{10,74},{12,76},{14,78},{16,80}... | collective-permute-start | bytes 2359304 | tf_op jit(solution)/shard_map/ppermute | solution.py:249
  68.5 5.6 %copy-start.4 = (bf16[1,384,128]{2,1,0:T(8,128)(2,1)S(1)}, bf16[1,384,128]{2,1,0:T(8,128)(2,1)}, u32[]{:S(2)}) copy-start(bf16[1,384,128]{2,1,0:T(8,128)(2,1)} %param.22) | copy-start | bytes 294916
  79.3 5.8 %copy-start.10 = (f32[384,256]{1,0:T(8,128)S(1)}, f32[384,256]{1,0:T(8,128)}, u32[]{:S(2)}) copy-start(f32[384,256]{1,0:T(8,128)} %fusion.185) | copy-start | bytes 1179652
  83.1 7.5 %copy-start.3 = (bf16[3072,256]{1,0:T(8,128)(2,1)}, bf16[3072,256]{1,0:T(8,128)(2,1)S(1)}, u32[]{:S(2)}) copy-start(bf16[3072,256]{1,0:T(8,128)(2,1)S(1)} %pad_maximum_fusion.1) | copy-start | bytes 4718596
  83.1 30.8 %collective-permute-start.6 = (bf16[3072,256]{1,0:T(8,128)(2,1)S(1)}, bf16[3072,256]{1,0:T(8,128)(2,1)}, u32[]{:S(2)}, u32[]{:S(2)}) collective-permute-start(bf16[3072,256]{1,0:T(8,128)(2,1)S(1)} %pad_maximum_fusion.1), channel_id=1, source_target_pairs={{0,4},{2,6},{4,0},{6,2},{8,12},{10,14},{12,8},{14,10},{16,20},{18,... | collective-permute-start | bytes 4718600 | tf_op jit(solution)/shard_map/ppermute | solution.py:249
  94.8 31.6 %copy-start.11 = (f32[384,256]{1,0:T(8,128)S(1)}, f32[384,256]{1,0:T(8,128)}, u32[]{:S(2)}) copy-start(f32[384,256]{1,0:T(8,128)} %convolution_add_fusion.16) | copy-start | bytes 1179652
  113.9 14.2 %copy-start.6 = (bf16[3072,1]{1,0:T(8,128)(2,1)S(1)}, bf16[3072,1]{1,0:T(8,128)(2,1)}, u32[]{:S(2)}) copy-start(bf16[3072,1]{1,0:T(8,128)(2,1)} %fusion.6) | copy-start | bytes 18436
  116.1 12.1 %copy-start.5 = (bf16[3072,1]{1,0:T(8,128)(2,1)S(1)}, bf16[3072,1]{1,0:T(8,128)(2,1)}, u32[]{:S(2)}) copy-start(bf16[3072,1]{1,0:T(8,128)(2,1)} %convert_element_type.342) | copy-start | bytes 18436
  116.1 26.4 %collective-permute-start.7 = (bf16[6144,256]{1,0:T(8,128)(2,1)S(1)}, bf16[6144,256]{1,0:T(8,128)(2,1)}, u32[]{:S(2)}, u32[]{:S(2)}) collective-permute-start(bf16[6144,256]{1,0:T(8,128)(2,1)S(1)} %pad_maximum_fusion), channel_id=1, source_target_pairs={{0,2},{2,0},{4,6},{6,4},{8,10},{10,8},{12,14},{14,12},{16,18},{18,... | collective-permute-start | bytes 9437192 | tf_op jit(solution)/shard_map/ppermute | solution.py:249
  128.1 3.4 %copy-start.2 = (bf16[6144,1]{1,0:T(8,128)(2,1)S(1)}, bf16[6144,1]{1,0:T(8,128)(2,1)}, u32[]{:S(2)}) copy-start(bf16[6144,1]{1,0:T(8,128)(2,1)} %convert_element_type.341) | copy-start | bytes 36868
  153.2 5.6 %copy-start.1 = (bf16[1,384,256]{2,1,0:T(8,128)(2,1)S(1)}, bf16[1,384,256]{2,1,0:T(8,128)(2,1)}, u32[]{:S(2)}) copy-start(bf16[1,384,256]{2,1,0:T(8,128)(2,1)} %param.19) | copy-start | bytes 589828
  153.2 6.2 %copy-start.12 = (bf16[1,384,128]{2,1,0:T(8,128)(2,1)S(1)}, bf16[1,384,128]{2,1,0:T(8,128)(2,1)}, u32[]{:S(2)}) copy-start(bf16[1,384,128]{2,1,0:T(8,128)(2,1)} %param.21) | copy-start | bytes 294916
  154.7 26.7 %copy-start.8 = (bf16[5,384,384]{2,1,0:T(8,128)(2,1)S(1)}, bf16[5,384,384]{2,1,0:T(8,128)(2,1)}, u32[]{:S(2)}) copy-start(bf16[5,384,384]{2,1,0:T(8,128)(2,1)} %param.25) | copy-start | bytes 4423684
  159.5 58.4 %collective-permute-start.15 = (bf16[1,384,256]{2,1,0:T(8,128)(2,1)S(1)}, bf16[1,384,256]{2,1,0:T(8,128)(2,1)S(1)}, u32[]{:S(2)}, u32[]{:S(2)}) collective-permute-start(bf16[1,384,256]{2,1,0:T(8,128)(2,1)S(1)} %pad_maximum_fusion.5), channel_id=1, source_target_pairs={{4,0},{6,2},{8,4},{10,6},{12,8},{14,10},{16,12},{18,14},{20,16},{2... | collective-permute-start | bytes 589832 | tf_op jit(solution)/shard_map/ppermute | solution.py:17
  173.9 44.2 %collective-permute-start.14 = (bf16[1,384,256]{2,1,0:T(8,128)(2,1)S(1)}, bf16[1,384,256]{2,1,0:T(8,128)(2,1)S(1)}, u32[]{:S(2)}, u32[]{:S(2)}) collective-permute-start(bf16[1,384,256]{2,1,0:T(8,128)(2,1)S(1)} %pad_maximum_fusion.5), channel_id=1, source_target_pairs={{2,0},{4,2},{6,4},{8,6},{10,8},{12,10},{14,12},{16,14},{18,16},{20... | collective-permute-start | bytes 589832 | tf_op jit(solution)/shard_map/ppermute | solution.py:17
  176.1 41.2 %collective-permute-start.13 = (bf16[1,384,256]{2,1,0:T(8,128)(2,1)S(1)}, bf16[1,384,256]{2,1,0:T(8,128)(2,1)S(1)}, u32[]{:S(2)}, u32[]{:S(2)}) collective-permute-start(bf16[1,384,256]{2,1,0:T(8,128)(2,1)S(1)} %pad_maximum_fusion.5), channel_id=1, source_target_pairs={{0,2},{2,4},{4,6},{6,8},{8,10},{10,12},{12,14},{14,16},{16,18},{18... | collective-permute-start | bytes 589832 | tf_op jit(solution)/shard_map/ppermute | solution.py:17
  179.5 38.1 %collective-permute-start.12 = (bf16[1,384,256]{2,1,0:T(8,128)(2,1)S(1)}, bf16[1,384,256]{2,1,0:T(8,128)(2,1)S(1)}, u32[]{:S(2)}, u32[]{:S(2)}) collective-permute-start(bf16[1,384,256]{2,1,0:T(8,128)(2,1)S(1)} %pad_maximum_fusion.5), channel_id=1, source_target_pairs={{0,4},{2,6},{4,8},{6,10},{8,12},{10,14},{12,16},{14,18},{16,20},{1... | collective-permute-start | bytes 589832 | tf_op jit(solution)/shard_map/ppermute | solution.py:17
  184.4 3.5 %collective-permute-start.9 = (bf16[1,384,128]{2,1,0:T(8,128)(2,1)S(1)}, bf16[1,384,128]{2,1,0:T(8,128)(2,1)S(1)}, u32[]{:S(2)}, u32[]{:S(2)}) collective-permute-start(bf16[1,384,128]{2,1,0:T(8,128)(2,1)S(1)} %get-tuple-element.69), channel_id=1, source_target_pairs={{0,2},{2,4},{4,6},{6,8},{8,10},{10,12},{12,14},{14,16},{16,18},{18... | collective-permute-start | bytes 294920 | tf_op jit(solution)/shard_map/ppermute | solution.py:17
  188.0 11.4 %collective-permute-start.8 = (bf16[1,384,128]{2,1,0:T(8,128)(2,1)S(1)}, bf16[1,384,128]{2,1,0:T(8,128)(2,1)S(1)}, u32[]{:S(2)}, u32[]{:S(2)}) collective-permute-start(bf16[1,384,128]{2,1,0:T(8,128)(2,1)S(1)} %get-tuple-element.69), channel_id=1, source_target_pairs={{0,4},{2,6},{4,8},{6,10},{8,12},{10,14},{12,16},{14,18},{16,20},{1... | collective-permute-start | bytes 294920 | tf_op jit(solution)/shard_map/ppermute | solution.py:17
  199.3 5.3 %collective-permute-start.11 = (bf16[1,384,128]{2,1,0:T(8,128)(2,1)S(1)}, bf16[1,384,128]{2,1,0:T(8,128)(2,1)S(1)}, u32[]{:S(2)}, u32[]{:S(2)}) collective-permute-start(bf16[1,384,128]{2,1,0:T(8,128)(2,1)S(1)} %get-tuple-element.69), channel_id=1, source_target_pairs={{4,0},{6,2},{8,4},{10,6},{12,8},{14,10},{16,12},{18,14},{20,16},{2... | collective-permute-start | bytes 294920 | tf_op jit(solution)/shard_map/ppermute | solution.py:17
  204.7 13.9 %collective-permute-start.10 = (bf16[1,384,128]{2,1,0:T(8,128)(2,1)S(1)}, bf16[1,384,128]{2,1,0:T(8,128)(2,1)S(1)}, u32[]{:S(2)}, u32[]{:S(2)}) collective-permute-start(bf16[1,384,128]{2,1,0:T(8,128)(2,1)S(1)} %get-tuple-element.69), channel_id=1, source_target_pairs={{2,0},{4,2},{6,4},{8,6},{10,8},{12,10},{14,12},{16,14},{18,16},{20... | collective-permute-start | bytes 294920 | tf_op jit(solution)/shard_map/ppermute | solution.py:17
  218.9 26.9 %collective-permute-start.19 = (bf16[1,384,128]{2,1,0:T(8,128)(2,1)S(1)}, bf16[1,384,128]{2,1,0:T(8,128)(2,1)S(1)}, u32[]{:S(2)}, u32[]{:S(2)}) collective-permute-start(bf16[1,384,128]{2,1,0:T(8,128)(2,1)S(1)} %fusion.81), channel_id=1, source_target_pairs={{4,0},{6,2},{8,4},{10,6},{12,8},{14,10},{16,12},{18,14},{20,16},{2... | collective-permute-start | bytes 294920 | tf_op jit(solution)/shard_map/ppermute | solution.py:17
  228.7 17.3 %collective-permute-start.18 = (bf16[1,384,128]{2,1,0:T(8,128)(2,1)S(1)}, bf16[1,384,128]{2,1,0:T(8,128)(2,1)S(1)}, u32[]{:S(2)}, u32[]{:S(2)}) collective-permute-start(bf16[1,384,128]{2,1,0:T(8,128)(2,1)S(1)} %fusion.81), channel_id=1, source_target_pairs={{2,0},{4,2},{6,4},{8,6},{10,8},{12,10},{14,12},{16,14},{18,16},{20... | collective-permute-start | bytes 294920 | tf_op jit(solution)/shard_map/ppermute | solution.py:17
  230.6 6.0 %collective-permute-start.17 = (bf16[1,384,128]{2,1,0:T(8,128)(2,1)S(1)}, bf16[1,384,128]{2,1,0:T(8,128)(2,1)S(1)}, u32[]{:S(2)}, u32[]{:S(2)}) collective-permute-start(bf16[1,384,128]{2,1,0:T(8,128)(2,1)S(1)} %fusion.81), channel_id=1, source_target_pairs={{0,2},{2,4},{4,6},{6,8},{8,10},{10,12},{12,14},{14,16},{16,18},{18... | collective-permute-start | bytes 294920 | tf_op jit(solution)/shard_map/ppermute | solution.py:17
  234.3 11.4 %collective-permute-start.16 = (bf16[1,384,128]{2,1,0:T(8,128)(2,1)S(1)}, bf16[1,384,128]{2,1,0:T(8,128)(2,1)S(1)}, u32[]{:S(2)}, u32[]{:S(2)}) collective-permute-start(bf16[1,384,128]{2,1,0:T(8,128)(2,1)S(1)} %fusion.81), channel_id=1, source_target_pairs={{0,4},{2,6},{4,8},{6,10},{8,12},{10,14},{12,16},{14,18},{16,20},{1... | collective-permute-start | bytes 294920 | tf_op jit(solution)/shard_map/ppermute | solution.py:17
  248.2 19.1 %collective-permute-start.23 = (bf16[1,384,128]{2,1,0:T(8,128)(2,1)S(1)}, bf16[1,384,128]{2,1,0:T(8,128)(2,1)S(1)}, u32[]{:S(2)}, u32[]{:S(2)}) collective-permute-start(bf16[1,384,128]{2,1,0:T(8,128)(2,1)S(1)} %get-tuple-element.73), channel_id=1, source_target_pairs={{4,0},{6,2},{8,4},{10,6},{12,8},{14,10},{16,12},{18,14},{20,16},{2... | collective-permute-start | bytes 294920 | tf_op jit(solution)/shard_map/ppermute | solution.py:17
  250.1 17.4 %collective-permute-start.22 = (bf16[1,384,128]{2,1,0:T(8,128)(2,1)S(1)}, bf16[1,384,128]{2,1,0:T(8,128)(2,1)S(1)}, u32[]{:S(2)}, u32[]{:S(2)}) collective-permute-start(bf16[1,384,128]{2,1,0:T(8,128)(2,1)S(1)} %get-tuple-element.73), channel_id=1, source_target_pairs={{2,0},{4,2},{6,4},{8,6},{10,8},{12,10},{14,12},{16,14},{18,16},{20... | collective-permute-start | bytes 294920 | tf_op jit(solution)/shard_map/ppermute | solution.py:17
  252.0 7.2 %collective-permute-start.21 = (bf16[1,384,128]{2,1,0:T(8,128)(2,1)S(1)}, bf16[1,384,128]{2,1,0:T(8,128)(2,1)S(1)}, u32[]{:S(2)}, u32[]{:S(2)}) collective-permute-start(bf16[1,384,128]{2,1,0:T(8,128)(2,1)S(1)} %get-tuple-element.73), channel_id=1, source_target_pairs={{0,2},{2,4},{4,6},{6,8},{8,10},{10,12},{12,14},{14,16},{16,18},{18... | collective-permute-start | bytes 294920 | tf_op jit(solution)/shard_map/ppermute | solution.py:17
  255.7 11.4 %collective-permute-start.20 = (bf16[1,384,128]{2,1,0:T(8,128)(2,1)S(1)}, bf16[1,384,128]{2,1,0:T(8,128)(2,1)S(1)}, u32[]{:S(2)}, u32[]{:S(2)}) collective-permute-start(bf16[1,384,128]{2,1,0:T(8,128)(2,1)S(1)} %get-tuple-element.73), channel_id=1, source_target_pairs={{0,4},{2,6},{4,8},{6,10},{8,12},{10,14},{12,16},{14,18},{16,20},{1... | collective-permute-start | bytes 294920 | tf_op jit(solution)/shard_map/ppermute | solution.py:17
  267.7 19.0 %collective-permute-start.27 = (bf16[1,384,128]{2,1,0:T(8,128)(2,1)S(1)}, bf16[1,384,128]{2,1,0:T(8,128)(2,1)S(1)}, u32[]{:S(2)}, u32[]{:S(2)}) collective-permute-start(bf16[1,384,128]{2,1,0:T(8,128)(2,1)S(1)} %fusion.79), channel_id=1, source_target_pairs={{4,0},{6,2},{8,4},{10,6},{12,8},{14,10},{16,12},{18,14},{20,16},{2... | collective-permute-start | bytes 294920 | tf_op jit(solution)/shard_map/ppermute | solution.py:17
  269.7 17.3 %collective-permute-start.26 = (bf16[1,384,128]{2,1,0:T(8,128)(2,1)S(1)}, bf16[1,384,128]{2,1,0:T(8,128)(2,1)S(1)}, u32[]{:S(2)}, u32[]{:S(2)}) collective-permute-start(bf16[1,384,128]{2,1,0:T(8,128)(2,1)S(1)} %fusion.79), channel_id=1, source_target_pairs={{2,0},{4,2},{6,4},{8,6},{10,8},{12,10},{14,12},{16,14},{18,16},{20... | collective-permute-start | bytes 294920 | tf_op jit(solution)/shard_map/ppermute | solution.py:17
  271.6 7.2 %collective-permute-start.25 = (bf16[1,384,128]{2,1,0:T(8,128)(2,1)S(1)}, bf16[1,384,128]{2,1,0:T(8,128)(2,1)S(1)}, u32[]{:S(2)}, u32[]{:S(2)}) collective-permute-start(bf16[1,384,128]{2,1,0:T(8,128)(2,1)S(1)} %fusion.79), channel_id=1, source_target_pairs={{0,2},{2,4},{4,6},{6,8},{8,10},{10,12},{12,14},{14,16},{16,18},{18... | collective-permute-start | bytes 294920 | tf_op jit(solution)/shard_map/ppermute | solution.py:17
  275.3 11.4 %collective-permute-start.24 = (bf16[1,384,128]{2,1,0:T(8,128)(2,1)S(1)}, bf16[1,384,128]{2,1,0:T(8,128)(2,1)S(1)}, u32[]{:S(2)}, u32[]{:S(2)}) collective-permute-start(bf16[1,384,128]{2,1,0:T(8,128)(2,1)S(1)} %fusion.79), channel_id=1, source_target_pairs={{0,4},{2,6},{4,8},{6,10},{8,12},{10,14},{12,16},{14,18},{16,20},{1... | collective-permute-start | bytes 294920 | tf_op jit(solution)/shard_map/ppermute | solution.py:17
  (4 other events, 10.2 us)

commit v3 on v2

--- a/solution.py
+++ b/solution.py
@@ -127,12 +127,16 @@
     return (1.0 - update_gate) * hidden + update_gate * candidate
 
 
-def column_pass_each(hidden, from_inputs, weight):
+def column_pass_each(hidden, from_inputs, weight, inputs=None):
     width_h = hidden.shape[-1]
     hidden_half = lax.optimization_barrier(hidden.astype(jnp.bfloat16))
-    hidden_ext = rows_around(
-        hidden_half, 2, lambda source, offset: passed_along(source, "band", offset)
-    )
+    mover = lambda source, offset: passed_along(source, "band", offset)
+    if inputs is None:
+        hidden_ext = rows_around(hidden_half, 2, mover)
+    else:
+        joined_ext = rows_around(jnp.concatenate([hidden_half, inputs], axis=-1), 2, mover)
+        hidden_ext = joined_ext[..., :width_h]
+        from_inputs = conv_valid(joined_ext[..., width_h:], weight[:, width_h:, :], 0)
     gate_pair = jax.nn.sigmoid(
         conv_valid(hidden_ext, weight[:, :width_h, : 2 * width_h], 0)
         + from_inputs[..., : 2 * width_h]
@@ -140,12 +144,12 @@
     update_gate = gate_pair[..., :width_h]
     reset_gate = gate_pair[..., width_h:]
     gated = (reset_gate * hidden_half.astype(jnp.float32)).astype(jnp.bfloat16)
-    gated_ext = rows_around(gated, 2, lambda source, offset: passed_along(source, "band", offset))
+    gated_ext = rows_around(gated, 2, mover)
     candidate = jnp.tanh(
         conv_valid(gated_ext, weight[:, :width_h, 2 * width_h :], 0)
         + from_inputs[..., 2 * width_h :]
     )
-    return (1.0 - update_gate) * hidden + update_gate * candidate
+    return ((1.0 - update_gate) * hidden + update_gate * candidate, from_inputs)
 
 
 GATHER_BITS = (4, 3, 2, 7, 6, 5, 1, 0)
@@ -286,11 +290,12 @@
     width_h = hidden_init.shape[-1]
     from_row = conv_valid(pad_columns(inputs), w_row[:, width_h:, :], 1)
     hidden = hidden_init.astype(jnp.float32)
-    inputs_ext = rows_around(inputs, 2, lambda source, offset: passed_along(source, "band", offset))
-    from_col = conv_valid(inputs_ext, w_col[:, width_h:, :], 0)
+    from_col = None
     for iteration in range(ITERS):
         hidden = row_pass(hidden, from_row, w_row)
-        hidden = column_pass_each(hidden, from_col, w_col)
+        hidden, from_col = column_pass_each(
+            hidden, from_col, w_col, inputs if iteration == 0 else None
+        )
     return (hidden, jnp.stack([flow_row, flow_col]))
 
 

time: 289 us -> 263 us (0.910)
  starting transfers between devices: 127 us -> 101 us
    ppermute x20 -> x16, starting transfers between devices: 80.7 us -> 54.7 us  [passed_along(): return lax.ppermute(array, axis, pairs)]
    ppermute x20 -> x16, waiting for transfers between devices: 36 us -> 35.6 us  [passed_along(): return lax.ppermute(array, axis, pairs)]
  transfers between devices with their start and end apart: 28 -> 24, of which waited for: 13 -> 11; matrix products, arithmetic and copies ran while one was open for 15% -> 15% of each run, Pallas kernels for 9% -> 10%
where the time goes in v3:
time: 263 us; the launch traced here: 261 us
  starting transfers between devices  101 us (38%)
  waiting for transfers between devices  64.3 us (24%)
  Pallas kernels  37.3 us (14%)
  other arithmetic  22.9 us (9%)
  local copies, waits for them, and re-layouts  18.2 us (7%)
  matrix products  16.3 us (6%)
    ppermute x16, starting transfers between devices, passed_along(): return lax.ppermute(array, axis, pairs)  54.7 us
    ppermute x8, starting transfers between devices, per_device(): got = lax.ppermute(held, 'band', pairs)  45.9 us
    pallas_call x9, Pallas kernels, match_block(): pl.pallas_call(match_kernel, grid=(count // tile,), in_specs=[pl.BlockSpe...  37.3 us
    ppermute x16, waiting for transfers between devices, passed_along(): return lax.ppermute(array, axis, pairs)  35.6 us
    ppermute x8, waiting for transfers between devices, per_device(): got = lax.ppermute(held, 'band', pairs)  28.7 us
    dot_general x50, matrix products, conv_valid(): jnp.dot(tap_slice.reshape(-1, tap_slice.shape[-1]), weight[kernel_tap], p...  16.3 us
    concatenate x9, other arithmetic, match_block(): jnp.concatenate([jnp.ones((count, 1), jnp.float32), strip_row[:, None], s...  8.99 us
    convert_element_type x7, local copies, waits for them, and re-layouts, match_block(): strip_row = jnp.repeat(block_rows, grid_cols).astype(jnp.float32)  5.71 us
  transfers between devices with their start and end apart: 24, of which 11 were waited for; matrix products, arithmetic and copies ran while one was open for 15% of the time, Pallas kernels for 10%

profile of v3, /device:TPU:7, one launch (start us, length us, event | category | flops | bytes accessed | tf_op | source)
XLA Modules:
  0.0 261.4 jit_solution(16506212470352605597)
XLA Ops:
  1.7 15.4 %collective-permute-start = (bf16[48,256]{1,0:T(8,128)(2,1)S(1)}, bf16[48,256]{1,0:T(8,128)(2,1)S(1)}, u32[]{:S(2)}, u32[]{:S(2)}) collective-permute-start(bf16[48,256]{1,0:T(8,128)(2,1)S(1)} %multiply_convert_fusion.s_ref), channel_id=1, source_target_pairs={{0,32},{2,34},{4,36},{6,38},{8,40},{10,42},{12,44},{14,46},{16,48}... | collective-permute-start | bytes 73736 | tf_op jit(solution)/shard_map/ppermute | solution.py:253
  20.6 2.8 %gather_fusion = s32[384]{0:T(512)S(1)} fusion(s32[256]{0:T(256)S(1)} %copy-done, s32[1024]{0:T(1024)S(1)} %pad_clamp_fusion.2), kind=kCustom, calls=%fused_computation.2 | custom fusion | bytes 4608 | tf_op jit(solution)/shard_map/gather | solution.py:272
  27.0 2.5 shard_map.176
  30.3 4.0 %collective-permute-start.1 = (bf16[96,256]{1,0:T(8,128)(2,1)S(1)}, bf16[96,256]{1,0:T(8,128)(2,1)S(1)}, u32[]{:S(2)}, u32[]{:S(2)}) collective-permute-start(bf16[96,256]{1,0:T(8,128)(2,1)S(1)} %pad_maximum_fusion.8), channel_id=1, source_target_pairs={{0,16},{2,18},{4,20},{6,22},{8,24},{10,26},{12,28},{14,30},{16,0},... | collective-permute-start | bytes 147464 | tf_op jit(solution)/shard_map/ppermute | solution.py:253
  34.4 2.5 shard_map.177
  36.9 2.2 collective-permute-done.1.s_ref
  39.1 3.3 %collective-permute-start.2 = (bf16[192,256]{1,0:T(8,128)(2,1)S(1)}, bf16[192,256]{1,0:T(8,128)(2,1)S(1)}, u32[]{:S(2)}, u32[]{:S(2)}) collective-permute-start(bf16[192,256]{1,0:T(8,128)(2,1)S(1)} %pad_maximum_fusion.7), channel_id=1, source_target_pairs={{0,8},{2,10},{4,12},{6,14},{8,0},{10,2},{12,4},{14,6},{16,24},{18,... | collective-permute-start | bytes 294920 | tf_op jit(solution)/shard_map/ppermute | solution.py:253
  42.4 2.6 shard_map.178
  46.4 3.0 %collective-permute-start.3 = (bf16[384,256]{1,0:T(8,128)(2,1)S(1)}, bf16[384,256]{1,0:T(8,128)(2,1)S(1)}, u32[]{:S(2)}, u32[]{:S(2)}) collective-permute-start(bf16[384,256]{1,0:T(8,128)(2,1)S(1)} %pad_maximum_fusion.5), channel_id=1, source_target_pairs={{0,256},{2,258},{4,260},{6,262},{8,264},{10,266},{12,268},{14,270}... | collective-permute-start | bytes 589832 | tf_op jit(solution)/shard_map/ppermute | solution.py:253
  49.5 2.6 shard_map.179
  52.1 2.2 collective-permute-done.3.s_ref
  54.4 4.8 %collective-permute-start.4 = (bf16[768,256]{1,0:T(8,128)(2,1)S(1)}, bf16[768,256]{1,0:T(8,128)(2,1)S(1)}, u32[]{:S(2)}, u32[]{:S(2)}) collective-permute-start(bf16[768,256]{1,0:T(8,128)(2,1)S(1)} %pad_maximum_fusion.3), channel_id=1, source_target_pairs={{0,128},{2,130},{4,132},{6,134},{8,136},{10,138},{12,140},{14,142}... | collective-permute-start | bytes 1179656 | tf_op jit(solution)/shard_map/ppermute | solution.py:253
  60.4 2.8 %shard_map.180 = (f32[384,128]{1,0:T(8,128)}, f32[384,128]{1,0:T(8,128)}) custom-call(bf16[384,256]{1,0:T(8,128)(2,1)} %bitcast.412, bf16[384,256]{1,0:T(8,128)(2,1)} %copy-done.13, bf16[384,128]{1,0:T(8,128)(2,1)} %maximum_maximum_fusion.4.w_ref, f32[384,128]{1,0:T(8,128)} %get-tuple-element.36.m_in, f32[384,128]{1,0:T(8,128)} %get-tuple-element.37.a_in), custom_call_target="tpu_custom_call" | custom-call | flops 150994944 | bytes 1277952 | tf_op jit(solution)/shard_map/pallas_call | solution.py:197
  64.4 3.2 %collective-permute-start.5 = (bf16[1536,256]{1,0:T(8,128)(2,1)S(1)}, bf16[1536,256]{1,0:T(8,128)(2,1)}, u32[]{:S(2)}, u32[]{:S(2)}) collective-permute-start(bf16[1536,256]{1,0:T(8,128)(2,1)S(1)} %pad_maximum_fusion.2), channel_id=1, source_target_pairs={{0,64},{2,66},{4,68},{6,70},{8,72},{10,74},{12,76},{14,78},{16,80}... | collective-permute-start | bytes 2359304 | tf_op jit(solution)/shard_map/ppermute | solution.py:253
  70.4 2.9 %convert_element_type.341 = bf16[6144,1]{1,0:T(8,128)(2,1)} reshape(bf16[128,48]{1,0:T(8,128)(2,1)S(1)} %broadcast_in_dim.140) | data formatting | bytes 24576 | tf_op jit(solution)/shard_map/convert_element_type | solution.py:185
  76.3 3.0 %shard_map.181 = (f32[384,128]{1,0:T(8,128)}, f32[384,128]{1,0:T(8,128)}) custom-call(bf16[384,256]{1,0:T(8,128)(2,1)} %bitcast.413, bf16[768,256]{1,0:T(8,128)(2,1)} %copy-done.9, bf16[768,128]{1,0:T(8,128)(2,1)} %maximum_maximum_fusion.3.w_ref, f32[384,128]{1,0:T(8,128)} %get-tuple-element.39.m_in, f32[384,128]{1,0:T(8,128)} %get-tuple-element.40.a_in), custom_call_target="tpu_custom_call" | custom-call | flops 301989888 | bytes 1572864 | tf_op jit(solution)/shard_map/pallas_call | solution.py:197
  79.3 2.5 collective-permute-done.5.s_ref
  83.1 1.9 collective-permute-start.6
  90.6 4.2 %shard_map.182 = (f32[384,128]{1,0:T(8,128)}, f32[384,128]{1,0:T(8,128)}) custom-call(bf16[384,256]{1,0:T(8,128)(2,1)} %bitcast.414, bf16[1536,256]{1,0:T(8,128)(2,1)} %collective-permute-done.5.s_ref, bf16[1536,128]{1,0:T(8,128)(2,1)} %maximum_maximum_fusion.2.w_ref, f32[384,128]{1,0:T(8,128)} %get-tuple-element.42.m_in, f32[384,128]{1,0:T(8,128)} %get-tuple-element.43.a_in), custom_call_target="tpu_custom_call" | custom-call | flops 603979776 | bytes 2162688 | tf_op jit(solution)/shard_map/pallas_call | solution.py:197
  94.8 19.1 %collective-permute-done.6.s_ref = bf16[3072,256]{1,0:T(8,128)(2,1)} collective-permute-done((bf16[3072,256]{1,0:T(8,128)(2,1)S(1)}, bf16[3072,256]{1,0:T(8,128)(2,1)}, u32[]{:S(2)}, u32[]{:S(2)}) %collective-permute-start.6) | collective-permute-done | bytes 1572896 | tf_op jit(solution)/shard_map/ppermute | solution.py:253
  113.9 2.2 pad_maximum_fusion
  116.1 10.2 %collective-permute-start.7 = (bf16[6144,256]{1,0:T(8,128)(2,1)S(1)}, bf16[6144,256]{1,0:T(8,128)(2,1)}, u32[]{:S(2)}, u32[]{:S(2)}) collective-permute-start(bf16[6144,256]{1,0:T(8,128)(2,1)S(1)} %pad_maximum_fusion), channel_id=1, source_target_pairs={{0,2},{2,0},{4,6},{6,4},{8,10},{10,8},{12,14},{14,12},{16,18},{18,... | collective-permute-start | bytes 9437192 | tf_op jit(solution)/shard_map/ppermute | solution.py:253
  129.7 1.9 fusion.1
  131.6 2.5 maximum_maximum_fusion.w_ref
  134.1 2.0 gather_fusion.1
  136.1 6.3 %shard_map.183 = (f32[384,128]{1,0:T(8,128)}, f32[384,128]{1,0:T(8,128)}) custom-call(bf16[384,256]{1,0:T(8,128)(2,1)} %bitcast.415, bf16[3072,256]{1,0:T(8,128)(2,1)} %collective-permute-done.6.s_ref, bf16[3072,128]{1,0:T(8,128)(2,1)} %maximum_maximum_fusion.1.w_ref, f32[384,128]{1,0:T(8,128)} %get-tuple-element.45.m_in, f32[384,128]{1,0:T(8,128)} %get-tuple-element.46.a_in), custom_call_target="tpu_custom_call" | custom-call | flops 1207959552 | bytes 3342336 | tf_op jit(solution)/shard_map/pallas_call | solution.py:197
  142.5 10.8 %shard_map.184 = (f32[384,128]{1,0:T(8,128)}, f32[384,128]{1,0:T(8,128)}) custom-call(bf16[384,256]{1,0:T(8,128)(2,1)} %bitcast.416, bf16[6144,256]{1,0:T(8,128)(2,1)} %collective-permute-done.7.s_ref, bf16[6144,128]{1,0:T(8,128)(2,1)} %maximum_maximum_fusion.w_ref, f32[384,128]{1,0:T(8,128)} %get-tuple-element.48.m_in, f32[384,128]{1,0:T(8,128)} %get-tuple-element.49.a_in), custom_call_target="tpu_custom_call" | custom-call | flops 2415919104 | bytes 5701632 | tf_op jit(solution)/shard_map/pallas_call | solution.py:197
  154.8 4.1 %gather_fusion.2 = bf16[384,256]{1,0:T(8,128)(2,1)S(1)} fusion(bf16[6144,256]{1,0:T(8,128)(2,1)} %collective-permute-done.7.s_ref, s32[1024]{0:T(1024)S(1)} %get-tuple-element.77), kind=kCustom, calls=%fused_computation.1.clone | custom fusion | bytes 394752 | tf_op jit(solution)/shard_map/jit(_take)/gather | solution.py:279
  162.5 14.4 %collective-permute-start.11 = (bf16[1,384,384]{2,1,0:T(8,128)(2,1)S(1)}, bf16[1,384,384]{2,1,0:T(8,128)(2,1)S(1)}, u32[]{:S(2)}, u32[]{:S(2)}) collective-permute-start(bf16[1,384,384]{2,1,0:T(8,128)(2,1)S(1)} %pad_maximum_fusion.4), channel_id=1, source_target_pairs={{4,0},{6,2},{8,4},{10,6},{12,8},{14,10},{16,12},{18,14},{20,16},{2... | collective-permute-start | bytes 884744 | tf_op jit(solution)/shard_map/ppermute | solution.py:17
  177.0 2.2 collective-permute-start.10
  179.2 3.4 %collective-permute-start.9 = (bf16[1,384,384]{2,1,0:T(8,128)(2,1)S(1)}, bf16[1,384,384]{2,1,0:T(8,128)(2,1)S(1)}, u32[]{:S(2)}, u32[]{:S(2)}) collective-permute-start(bf16[1,384,384]{2,1,0:T(8,128)(2,1)S(1)} %pad_maximum_fusion.4), channel_id=1, source_target_pairs={{0,2},{2,4},{4,6},{6,8},{8,10},{10,12},{12,14},{14,16},{16,18},{18... | collective-permute-start | bytes 884744 | tf_op jit(solution)/shard_map/ppermute | solution.py:17
  182.5 1.9 collective-permute-start.8
  187.6 11.1 %collective-permute-done.8 = bf16[1,384,384]{2,1,0:T(8,128)(2,1)S(1)} collective-permute-done((bf16[1,384,384]{2,1,0:T(8,128)(2,1)S(1)}, bf16[1,384,384]{2,1,0:T(8,128)(2,1)S(1)}, u32[]{:S(2)}, u32[]{:S(2)}) %collective-permute-start.8) | collective-permute-done | bytes 294944 | tf_op jit(solution)/shard_map/ppermute | solution.py:17
  199.9 1.9 collective-permute-start.15
  201.8 2.3 collective-permute-start.14
  204.2 3.5 %collective-permute-start.13 = (bf16[1,384,128]{2,1,0:T(8,128)(2,1)S(1)}, bf16[1,384,128]{2,1,0:T(8,128)(2,1)S(1)}, u32[]{:S(2)}, u32[]{:S(2)}) collective-permute-start(bf16[1,384,128]{2,1,0:T(8,128)(2,1)S(1)} %fusion.82), channel_id=1, source_target_pairs={{0,2},{2,4},{4,6},{6,8},{8,10},{10,12},{12,14},{14,16},{16,18},{18... | collective-permute-start | bytes 294920 | tf_op jit(solution)/shard_map/ppermute | solution.py:17
  207.7 3.3 %collective-permute-start.12 = (bf16[1,384,128]{2,1,0:T(8,128)(2,1)S(1)}, bf16[1,384,128]{2,1,0:T(8,128)(2,1)S(1)}, u32[]{:S(2)}, u32[]{:S(2)}) collective-permute-start(bf16[1,384,128]{2,1,0:T(8,128)(2,1)S(1)} %fusion.82), channel_id=1, source_target_pairs={{0,4},{2,6},{4,8},{6,10},{8,12},{10,14},{12,16},{14,18},{16,20},{1... | collective-permute-start | bytes 294920 | tf_op jit(solution)/shard_map/ppermute | solution.py:17
  211.3 7.8 %collective-permute-done.12 = bf16[1,384,128]{2,1,0:T(8,128)(2,1)S(1)} collective-permute-done((bf16[1,384,128]{2,1,0:T(8,128)(2,1)S(1)}, bf16[1,384,128]{2,1,0:T(8,128)(2,1)S(1)}, u32[]{:S(2)}, u32[]{:S(2)}) %collective-permute-start.12) | collective-permute-done | bytes 98336 | tf_op jit(solution)/shard_map/ppermute | solution.py:17
  221.7 1.9 collective-permute-start.19
  223.6 1.9 collective-permute-start.18
  225.6 3.6 %collective-permute-start.17 = (bf16[1,384,128]{2,1,0:T(8,128)(2,1)S(1)}, bf16[1,384,128]{2,1,0:T(8,128)(2,1)S(1)}, u32[]{:S(2)}, u32[]{:S(2)}) collective-permute-start(bf16[1,384,128]{2,1,0:T(8,128)(2,1)S(1)} %get-tuple-element.73), channel_id=1, source_target_pairs={{0,2},{2,4},{4,6},{6,8},{8,10},{10,12},{12,14},{14,16},{16,18},{18... | collective-permute-start | bytes 294920 | tf_op jit(solution)/shard_map/ppermute | solution.py:17
  229.2 3.4 %collective-permute-start.16 = (bf16[1,384,128]{2,1,0:T(8,128)(2,1)S(1)}, bf16[1,384,128]{2,1,0:T(8,128)(2,1)S(1)}, u32[]{:S(2)}, u32[]{:S(2)}) collective-permute-start(bf16[1,384,128]{2,1,0:T(8,128)(2,1)S(1)} %get-tuple-element.73), channel_id=1, source_target_pairs={{0,4},{2,6},{4,8},{6,10},{8,12},{10,14},{12,16},{14,18},{16,20},{1... | collective-permute-start | bytes 294920 | tf_op jit(solution)/shard_map/ppermute | solution.py:17
  233.0 7.6 %collective-permute-done.16 = bf16[1,384,128]{2,1,0:T(8,128)(2,1)S(1)} collective-permute-done((bf16[1,384,128]{2,1,0:T(8,128)(2,1)S(1)}, bf16[1,384,128]{2,1,0:T(8,128)(2,1)S(1)}, u32[]{:S(2)}, u32[]{:S(2)}) %collective-permute-start.16) | collective-permute-done | bytes 98336 | tf_op jit(solution)/shard_map/ppermute | solution.py:17
  241.3 1.9 collective-permute-start.23
  243.2 1.9 collective-permute-start.22
  245.2 3.6 %collective-permute-start.21 = (bf16[1,384,128]{2,1,0:T(8,128)(2,1)S(1)}, bf16[1,384,128]{2,1,0:T(8,128)(2,1)S(1)}, u32[]{:S(2)}, u32[]{:S(2)}) collective-permute-start(bf16[1,384,128]{2,1,0:T(8,128)(2,1)S(1)} %fusion.80), channel_id=1, source_target_pairs={{0,2},{2,4},{4,6},{6,8},{8,10},{10,12},{12,14},{14,16},{16,18},{18... | collective-permute-start | bytes 294920 | tf_op jit(solution)/shard_map/ppermute | solution.py:17
  248.8 3.4 %collective-permute-start.20 = (bf16[1,384,128]{2,1,0:T(8,128)(2,1)S(1)}, bf16[1,384,128]{2,1,0:T(8,128)(2,1)S(1)}, u32[]{:S(2)}, u32[]{:S(2)}) collective-permute-start(bf16[1,384,128]{2,1,0:T(8,128)(2,1)S(1)} %fusion.80), channel_id=1, source_target_pairs={{0,4},{2,6},{4,8},{6,10},{8,12},{10,14},{12,16},{14,18},{16,20},{1... | collective-permute-start | bytes 294920 | tf_op jit(solution)/shard_map/ppermute | solution.py:17
  252.5 7.7 %collective-permute-done.20 = bf16[1,384,128]{2,1,0:T(8,128)(2,1)S(1)} collective-permute-done((bf16[1,384,128]{2,1,0:T(8,128)(2,1)S(1)}, bf16[1,384,128]{2,1,0:T(8,128)(2,1)S(1)}, u32[]{:S(2)}, u32[]{:S(2)}) %collective-permute-start.20) | collective-permute-done | bytes 98336 | tf_op jit(solution)/shard_map/ppermute | solution.py:17
  (186 shorter events, 43.1 us)
Async XLA Ops:
  0.6 19.9 %copy-start = (s32[256]{0:T(256)S(1)}, s32[256]{0:T(256)}, u32[]{:S(2)}) copy-start(s32[256]{0:T(256)} %constant.207.clone) | copy-start | bytes 3076
  1.7 21.7 %copy-start.16 = (bf16[48,256]{1,0:T(8,128)(2,1)}, bf16[48,256]{1,0:T(8,128)(2,1)S(1)}, u32[]{:S(2)}) copy-start(bf16[48,256]{1,0:T(8,128)(2,1)S(1)} %multiply_convert_fusion.s_ref) | copy-start | bytes 73732
  1.7 27.8 %collective-permute-start = (bf16[48,256]{1,0:T(8,128)(2,1)S(1)}, bf16[48,256]{1,0:T(8,128)(2,1)S(1)}, u32[]{:S(2)}, u32[]{:S(2)}) collective-permute-start(bf16[48,256]{1,0:T(8,128)(2,1)S(1)} %multiply_convert_fusion.s_ref), channel_id=1, source_target_pairs={{0,32},{2,34},{4,36},{6,38},{8,40},{10,42},{12,44},{14,46},{16,48}... | collective-permute-start | bytes 73736 | tf_op jit(solution)/shard_map/ppermute | solution.py:253
  20.0 3.4 %copy-start.23 = (s32[128]{0:T(128)S(1)}, s32[128]{0:T(128)}, u32[]{:S(2)}) copy-start(s32[128]{0:T(128)} %constant.206.clone) | copy-start | bytes 1540
  20.2 5.5 %copy-start.22 = (s32[64]{0:T(128)S(1)}, s32[64]{0:T(128)}, u32[]{:S(2)}) copy-start(s32[64]{0:T(128)} %constant.205.clone) | copy-start | bytes 772
  20.5 13.8 %copy-start.21 = (s32[32]{0:T(128)S(1)}, s32[32]{0:T(128)}, u32[]{:S(2)}) copy-start(s32[32]{0:T(128)} %constant.204.clone) | copy-start | bytes 388
  23.4 19.0 %copy-start.20 = (s32[16]{0:T(128)S(1)}, s32[16]{0:T(128)}, u32[]{:S(2)}) copy-start(s32[16]{0:T(128)} %constant.203.clone) | copy-start | bytes 196
  25.6 23.8 %copy-start.19 = (s32[8]{0:T(128)S(1)}, s32[8]{0:T(128)}, u32[]{:S(2)}) copy-start(s32[8]{0:T(128)} %constant.202.clone) | copy-start | bytes 100
  29.6 4.8 %copy-start.18 = (bf16[48,256]{1,0:T(8,128)(2,1)}, bf16[48,256]{1,0:T(8,128)(2,1)S(1)}, u32[]{:S(2)}) copy-start(bf16[48,256]{1,0:T(8,128)(2,1)S(1)} %collective-permute-done.s_ref) | copy-start | bytes 73732
  30.3 8.7 %collective-permute-start.1 = (bf16[96,256]{1,0:T(8,128)(2,1)S(1)}, bf16[96,256]{1,0:T(8,128)(2,1)S(1)}, u32[]{:S(2)}, u32[]{:S(2)}) collective-permute-start(bf16[96,256]{1,0:T(8,128)(2,1)S(1)} %pad_maximum_fusion.8), channel_id=1, source_target_pairs={{0,16},{2,18},{4,20},{6,22},{8,24},{10,26},{12,28},{14,30},{16,0},... | collective-permute-start | bytes 147464 | tf_op jit(solution)/shard_map/ppermute | solution.py:253
  39.1 3.3 %copy-start.17 = (bf16[96,256]{1,0:T(8,128)(2,1)}, bf16[96,256]{1,0:T(8,128)(2,1)S(1)}, u32[]{:S(2)}) copy-start(bf16[96,256]{1,0:T(8,128)(2,1)S(1)} %collective-permute-done.1.s_ref) | copy-start | bytes 147460
  39.1 7.3 %collective-permute-start.2 = (bf16[192,256]{1,0:T(8,128)(2,1)S(1)}, bf16[192,256]{1,0:T(8,128)(2,1)S(1)}, u32[]{:S(2)}, u32[]{:S(2)}) collective-permute-start(bf16[192,256]{1,0:T(8,128)(2,1)S(1)} %pad_maximum_fusion.7), channel_id=1, source_target_pairs={{0,8},{2,10},{4,12},{6,14},{8,0},{10,2},{12,4},{14,6},{16,24},{18,... | collective-permute-start | bytes 294920 | tf_op jit(solution)/shard_map/ppermute | solution.py:253
  46.4 3.1 %copy-start.15 = (bf16[192,256]{1,0:T(8,128)(2,1)}, bf16[192,256]{1,0:T(8,128)(2,1)S(1)}, u32[]{:S(2)}) copy-start(bf16[192,256]{1,0:T(8,128)(2,1)S(1)} %collective-permute-done.2.s_ref) | copy-start | bytes 294916
  46.4 7.9 %collective-permute-start.3 = (bf16[384,256]{1,0:T(8,128)(2,1)S(1)}, bf16[384,256]{1,0:T(8,128)(2,1)S(1)}, u32[]{:S(2)}, u32[]{:S(2)}) collective-permute-start(bf16[384,256]{1,0:T(8,128)(2,1)S(1)} %pad_maximum_fusion.5), channel_id=1, source_target_pairs={{0,256},{2,258},{4,260},{6,262},{8,264},{10,266},{12,268},{14,270}... | collective-permute-start | bytes 589832 | tf_op jit(solution)/shard_map/ppermute | solution.py:253
  54.3 6.1 %copy-start.13 = (bf16[384,256]{1,0:T(8,128)(2,1)}, bf16[384,256]{1,0:T(8,128)(2,1)S(1)}, u32[]{:S(2)}) copy-start(bf16[384,256]{1,0:T(8,128)(2,1)S(1)} %collective-permute-done.3.s_ref) | copy-start | bytes 589828
  54.4 10.0 %collective-permute-start.4 = (bf16[768,256]{1,0:T(8,128)(2,1)S(1)}, bf16[768,256]{1,0:T(8,128)(2,1)S(1)}, u32[]{:S(2)}, u32[]{:S(2)}) collective-permute-start(bf16[768,256]{1,0:T(8,128)(2,1)S(1)} %pad_maximum_fusion.3), channel_id=1, source_target_pairs={{0,128},{2,130},{4,132},{6,134},{8,136},{10,138},{12,140},{14,142}... | collective-permute-start | bytes 1179656 | tf_op jit(solution)/shard_map/ppermute | solution.py:253
  64.4 5.9 %copy-start.9 = (bf16[768,256]{1,0:T(8,128)(2,1)}, bf16[768,256]{1,0:T(8,128)(2,1)S(1)}, u32[]{:S(2)}) copy-start(bf16[768,256]{1,0:T(8,128)(2,1)S(1)} %collective-permute-done.4.s_ref) | copy-start | bytes 1179652
  64.4 17.4 %collective-permute-start.5 = (bf16[1536,256]{1,0:T(8,128)(2,1)S(1)}, bf16[1536,256]{1,0:T(8,128)(2,1)}, u32[]{:S(2)}, u32[]{:S(2)}) collective-permute-start(bf16[1536,256]{1,0:T(8,128)(2,1)S(1)} %pad_maximum_fusion.2), channel_id=1, source_target_pairs={{0,64},{2,66},{4,68},{6,70},{8,72},{10,74},{12,76},{14,78},{16,80}... | collective-permute-start | bytes 2359304 | tf_op jit(solution)/shard_map/ppermute | solution.py:253
  68.5 5.6 %copy-start.4 = (bf16[1,384,128]{2,1,0:T(8,128)(2,1)S(1)}, bf16[1,384,128]{2,1,0:T(8,128)(2,1)}, u32[]{:S(2)}) copy-start(bf16[1,384,128]{2,1,0:T(8,128)(2,1)} %param.22) | copy-start | bytes 294916
  79.3 5.7 %copy-start.10 = (f32[384,256]{1,0:T(8,128)S(1)}, f32[384,256]{1,0:T(8,128)}, u32[]{:S(2)}) copy-start(f32[384,256]{1,0:T(8,128)} %fusion.178) | copy-start | bytes 1179652
  83.1 7.5 %copy-start.3 = (bf16[3072,256]{1,0:T(8,128)(2,1)}, bf16[3072,256]{1,0:T(8,128)(2,1)S(1)}, u32[]{:S(2)}) copy-start(bf16[3072,256]{1,0:T(8,128)(2,1)S(1)} %pad_maximum_fusion.1) | copy-start | bytes 4718596
  83.1 30.8 %collective-permute-start.6 = (bf16[3072,256]{1,0:T(8,128)(2,1)S(1)}, bf16[3072,256]{1,0:T(8,128)(2,1)}, u32[]{:S(2)}, u32[]{:S(2)}) collective-permute-start(bf16[3072,256]{1,0:T(8,128)(2,1)S(1)} %pad_maximum_fusion.1), channel_id=1, source_target_pairs={{0,4},{2,6},{4,0},{6,2},{8,12},{10,14},{12,8},{14,10},{16,20},{18,... | collective-permute-start | bytes 4718600 | tf_op jit(solution)/shard_map/ppermute | solution.py:253
  94.7 31.6 %copy-start.11 = (f32[384,256]{1,0:T(8,128)S(1)}, f32[384,256]{1,0:T(8,128)}, u32[]{:S(2)}) copy-start(f32[384,256]{1,0:T(8,128)} %convolution_add_fusion.16) | copy-start | bytes 1179652
  113.9 14.2 %copy-start.6 = (bf16[3072,1]{1,0:T(8,128)(2,1)S(1)}, bf16[3072,1]{1,0:T(8,128)(2,1)}, u32[]{:S(2)}) copy-start(bf16[3072,1]{1,0:T(8,128)(2,1)} %fusion.6) | copy-start | bytes 18436
  116.1 12.1 %copy-start.5 = (bf16[3072,1]{1,0:T(8,128)(2,1)S(1)}, bf16[3072,1]{1,0:T(8,128)(2,1)}, u32[]{:S(2)}) copy-start(bf16[3072,1]{1,0:T(8,128)(2,1)} %convert_element_type.342) | copy-start | bytes 18436
  116.1 26.4 %collective-permute-start.7 = (bf16[6144,256]{1,0:T(8,128)(2,1)S(1)}, bf16[6144,256]{1,0:T(8,128)(2,1)}, u32[]{:S(2)}, u32[]{:S(2)}) collective-permute-start(bf16[6144,256]{1,0:T(8,128)(2,1)S(1)} %pad_maximum_fusion), channel_id=1, source_target_pairs={{0,2},{2,0},{4,6},{6,4},{8,10},{10,8},{12,14},{14,12},{16,18},{18,... | collective-permute-start | bytes 9437192 | tf_op jit(solution)/shard_map/ppermute | solution.py:253
  128.1 3.4 %copy-start.2 = (bf16[6144,1]{1,0:T(8,128)(2,1)S(1)}, bf16[6144,1]{1,0:T(8,128)(2,1)}, u32[]{:S(2)}) copy-start(bf16[6144,1]{1,0:T(8,128)(2,1)} %convert_element_type.341) | copy-start | bytes 36868
  153.2 5.6 %copy-start.1 = (bf16[1,384,256]{2,1,0:T(8,128)(2,1)S(1)}, bf16[1,384,256]{2,1,0:T(8,128)(2,1)}, u32[]{:S(2)}) copy-start(bf16[1,384,256]{2,1,0:T(8,128)(2,1)} %param.19) | copy-start | bytes 589828
  153.2 6.2 %copy-start.12 = (bf16[1,384,128]{2,1,0:T(8,128)(2,1)S(1)}, bf16[1,384,128]{2,1,0:T(8,128)(2,1)}, u32[]{:S(2)}) copy-start(bf16[1,384,128]{2,1,0:T(8,128)(2,1)} %param.21) | copy-start | bytes 294916
  154.7 4.7 %copy-start.8 = (bf16[5,384,384]{2,1,0:T(8,128)(2,1)S(1)}, bf16[5,384,384]{2,1,0:T(8,128)(2,1)}, u32[]{:S(2)}) copy-start(bf16[5,384,384]{2,1,0:T(8,128)(2,1)} %param.25) | copy-start | bytes 4423684
  160.3 1.0 copy-start.14
  161.9 22.5 %copy-start.7 = (bf16[5,384,384]{2,1,0:T(8,128)(2,1)S(1)}, bf16[5,384,384]{2,1,0:T(8,128)(2,1)}, u32[]{:S(2)}) copy-start(bf16[5,384,384]{2,1,0:T(8,128)(2,1)} %param.26) | copy-start | bytes 4423684
  162.5 24.8 %collective-permute-start.11 = (bf16[1,384,384]{2,1,0:T(8,128)(2,1)S(1)}, bf16[1,384,384]{2,1,0:T(8,128)(2,1)S(1)}, u32[]{:S(2)}, u32[]{:S(2)}) collective-permute-start(bf16[1,384,384]{2,1,0:T(8,128)(2,1)S(1)} %pad_maximum_fusion.4), channel_id=1, source_target_pairs={{4,0},{6,2},{8,4},{10,6},{12,8},{14,10},{16,12},{18,14},{20,16},{2... | collective-permute-start | bytes 884744 | tf_op jit(solution)/shard_map/ppermute | solution.py:17
  177.0 22.4 %collective-permute-start.10 = (bf16[1,384,384]{2,1,0:T(8,128)(2,1)S(1)}, bf16[1,384,384]{2,1,0:T(8,128)(2,1)S(1)}, u32[]{:S(2)}, u32[]{:S(2)}) collective-permute-start(bf16[1,384,384]{2,1,0:T(8,128)(2,1)S(1)} %pad_maximum_fusion.4), channel_id=1, source_target_pairs={{2,0},{4,2},{6,4},{8,6},{10,8},{12,10},{14,12},{16,14},{18,16},{20... | collective-permute-start | bytes 884744 | tf_op jit(solution)/shard_map/ppermute | solution.py:17
  179.2 7.7 %collective-permute-start.9 = (bf16[1,384,384]{2,1,0:T(8,128)(2,1)S(1)}, bf16[1,384,384]{2,1,0:T(8,128)(2,1)S(1)}, u32[]{:S(2)}, u32[]{:S(2)}) collective-permute-start(bf16[1,384,384]{2,1,0:T(8,128)(2,1)S(1)} %pad_maximum_fusion.4), channel_id=1, source_target_pairs={{0,2},{2,4},{4,6},{6,8},{8,10},{10,12},{12,14},{14,16},{16,18},{18... | collective-permute-start | bytes 884744 | tf_op jit(solution)/shard_map/ppermute | solution.py:17
  182.5 16.2 %collective-permute-start.8 = (bf16[1,384,384]{2,1,0:T(8,128)(2,1)S(1)}, bf16[1,384,384]{2,1,0:T(8,128)(2,1)S(1)}, u32[]{:S(2)}, u32[]{:S(2)}) collective-permute-start(bf16[1,384,384]{2,1,0:T(8,128)(2,1)S(1)} %pad_maximum_fusion.4), channel_id=1, source_target_pairs={{0,4},{2,6},{4,8},{6,10},{8,12},{10,14},{12,16},{14,18},{16,20},{1... | collective-permute-start | bytes 884744 | tf_op jit(solution)/shard_map/ppermute | solution.py:17
  199.9 19.4 %collective-permute-start.15 = (bf16[1,384,128]{2,1,0:T(8,128)(2,1)S(1)}, bf16[1,384,128]{2,1,0:T(8,128)(2,1)S(1)}, u32[]{:S(2)}, u32[]{:S(2)}) collective-permute-start(bf16[1,384,128]{2,1,0:T(8,128)(2,1)S(1)} %fusion.82), channel_id=1, source_target_pairs={{4,0},{6,2},{8,4},{10,6},{12,8},{14,10},{16,12},{18,14},{20,16},{2... | collective-permute-start | bytes 294920 | tf_op jit(solution)/shard_map/ppermute | solution.py:17
  201.8 17.7 %collective-permute-start.14 = (bf16[1,384,128]{2,1,0:T(8,128)(2,1)S(1)}, bf16[1,384,128]{2,1,0:T(8,128)(2,1)S(1)}, u32[]{:S(2)}, u32[]{:S(2)}) collective-permute-start(bf16[1,384,128]{2,1,0:T(8,128)(2,1)S(1)} %fusion.82), channel_id=1, source_target_pairs={{2,0},{4,2},{6,4},{8,6},{10,8},{12,10},{14,12},{16,14},{18,16},{20... | collective-permute-start | bytes 294920 | tf_op jit(solution)/shard_map/ppermute | solution.py:17
  204.2 7.0 %collective-permute-start.13 = (bf16[1,384,128]{2,1,0:T(8,128)(2,1)S(1)}, bf16[1,384,128]{2,1,0:T(8,128)(2,1)S(1)}, u32[]{:S(2)}, u32[]{:S(2)}) collective-permute-start(bf16[1,384,128]{2,1,0:T(8,128)(2,1)S(1)} %fusion.82), channel_id=1, source_target_pairs={{0,2},{2,4},{4,6},{6,8},{8,10},{10,12},{12,14},{14,16},{16,18},{18... | collective-permute-start | bytes 294920 | tf_op jit(solution)/shard_map/ppermute | solution.py:17
  207.7 11.5 %collective-permute-start.12 = (bf16[1,384,128]{2,1,0:T(8,128)(2,1)S(1)}, bf16[1,384,128]{2,1,0:T(8,128)(2,1)S(1)}, u32[]{:S(2)}, u32[]{:S(2)}) collective-permute-start(bf16[1,384,128]{2,1,0:T(8,128)(2,1)S(1)} %fusion.82), channel_id=1, source_target_pairs={{0,4},{2,6},{4,8},{6,10},{8,12},{10,14},{12,16},{14,18},{16,20},{1... | collective-permute-start | bytes 294920 | tf_op jit(solution)/shard_map/ppermute | solution.py:17
  221.7 19.1 %collective-permute-start.19 = (bf16[1,384,128]{2,1,0:T(8,128)(2,1)S(1)}, bf16[1,384,128]{2,1,0:T(8,128)(2,1)S(1)}, u32[]{:S(2)}, u32[]{:S(2)}) collective-permute-start(bf16[1,384,128]{2,1,0:T(8,128)(2,1)S(1)} %get-tuple-element.73), channel_id=1, source_target_pairs={{4,0},{6,2},{8,4},{10,6},{12,8},{14,10},{16,12},{18,14},{20,16},{2... | collective-permute-start | bytes 294920 | tf_op jit(solution)/shard_map/ppermute | solution.py:17
  223.6 17.4 %collective-permute-start.18 = (bf16[1,384,128]{2,1,0:T(8,128)(2,1)S(1)}, bf16[1,384,128]{2,1,0:T(8,128)(2,1)S(1)}, u32[]{:S(2)}, u32[]{:S(2)}) collective-permute-start(bf16[1,384,128]{2,1,0:T(8,128)(2,1)S(1)} %get-tuple-element.73), channel_id=1, source_target_pairs={{2,0},{4,2},{6,4},{8,6},{10,8},{12,10},{14,12},{16,14},{18,16},{20... | collective-permute-start | bytes 294920 | tf_op jit(solution)/shard_map/ppermute | solution.py:17
  225.6 7.2 %collective-permute-start.17 = (bf16[1,384,128]{2,1,0:T(8,128)(2,1)S(1)}, bf16[1,384,128]{2,1,0:T(8,128)(2,1)S(1)}, u32[]{:S(2)}, u32[]{:S(2)}) collective-permute-start(bf16[1,384,128]{2,1,0:T(8,128)(2,1)S(1)} %get-tuple-element.73), channel_id=1, source_target_pairs={{0,2},{2,4},{4,6},{6,8},{8,10},{10,12},{12,14},{14,16},{16,18},{18... | collective-permute-start | bytes 294920 | tf_op jit(solution)/shard_map/ppermute | solution.py:17
  229.2 11.4 %collective-permute-start.16 = (bf16[1,384,128]{2,1,0:T(8,128)(2,1)S(1)}, bf16[1,384,128]{2,1,0:T(8,128)(2,1)S(1)}, u32[]{:S(2)}, u32[]{:S(2)}) collective-permute-start(bf16[1,384,128]{2,1,0:T(8,128)(2,1)S(1)} %get-tuple-element.73), channel_id=1, source_target_pairs={{0,4},{2,6},{4,8},{6,10},{8,12},{10,14},{12,16},{14,18},{16,20},{1... | collective-permute-start | bytes 294920 | tf_op jit(solution)/shard_map/ppermute | solution.py:17
  241.3 19.0 %collective-permute-start.23 = (bf16[1,384,128]{2,1,0:T(8,128)(2,1)S(1)}, bf16[1,384,128]{2,1,0:T(8,128)(2,1)S(1)}, u32[]{:S(2)}, u32[]{:S(2)}) collective-permute-start(bf16[1,384,128]{2,1,0:T(8,128)(2,1)S(1)} %fusion.80), channel_id=1, source_target_pairs={{4,0},{6,2},{8,4},{10,6},{12,8},{14,10},{16,12},{18,14},{20,16},{2... | collective-permute-start | bytes 294920 | tf_op jit(solution)/shard_map/ppermute | solution.py:17
  243.2 17.3 %collective-permute-start.22 = (bf16[1,384,128]{2,1,0:T(8,128)(2,1)S(1)}, bf16[1,384,128]{2,1,0:T(8,128)(2,1)S(1)}, u32[]{:S(2)}, u32[]{:S(2)}) collective-permute-start(bf16[1,384,128]{2,1,0:T(8,128)(2,1)S(1)} %fusion.80), channel_id=1, source_target_pairs={{2,0},{4,2},{6,4},{8,6},{10,8},{12,10},{14,12},{16,14},{18,16},{20... | collective-permute-start | bytes 294920 | tf_op jit(solution)/shard_map/ppermute | solution.py:17
  245.2 7.2 %collective-permute-start.21 = (bf16[1,384,128]{2,1,0:T(8,128)(2,1)S(1)}, bf16[1,384,128]{2,1,0:T(8,128)(2,1)S(1)}, u32[]{:S(2)}, u32[]{:S(2)}) collective-permute-start(bf16[1,384,128]{2,1,0:T(8,128)(2,1)S(1)} %fusion.80), channel_id=1, source_target_pairs={{0,2},{2,4},{4,6},{6,8},{8,10},{10,12},{12,14},{14,16},{16,18},{18... | collective-permute-start | bytes 294920 | tf_op jit(solution)/shard_map/ppermute | solution.py:17
  248.8 11.4 %collective-permute-start.20 = (bf16[1,384,128]{2,1,0:T(8,128)(2,1)S(1)}, bf16[1,384,128]{2,1,0:T(8,128)(2,1)S(1)}, u32[]{:S(2)}, u32[]{:S(2)}) collective-permute-start(bf16[1,384,128]{2,1,0:T(8,128)(2,1)S(1)} %fusion.80), channel_id=1, source_target_pairs={{0,4},{2,6},{4,8},{6,10},{8,12},{10,14},{12,16},{14,18},{16,20},{1... | collective-permute-start | bytes 294920 | tf_op jit(solution)/shard_map/ppermute | solution.py:17

commit v4 on v3

--- a/solution.py
+++ b/solution.py
@@ -152,7 +152,7 @@
     return ((1.0 - update_gate) * hidden + update_gate * candidate, from_inputs)
 
 
-GATHER_BITS = (4, 3, 2, 7, 6, 5, 1, 0)
+GATHER_BITS = (4, 3, 2, 7, 6, 1, 5, 0)
 
 
 def match_kernel(f1_ref, s_ref, w_ref, m_in, a_in, m_out, a_out):
@@ -247,16 +247,25 @@
     )
     held = strips.reshape(band_rows * grid_cols, channels)
     state = match_block(state, features, held, band[None], grid_cols)
+    last = len(GATHER_BITS) - 1
     for step, bit in enumerate(GATHER_BITS):
         flip = 1 << bit
         pairs = [(i, i ^ flip) for i in range(bands)]
-        got = lax.ppermute(held, "band", pairs)
         got_rows = (band ^ flip) ^ jnp.asarray(deposit[: 1 << step])
-        settled = state
-        state = match_block(state, features, got, got_rows, grid_cols)
-        if step + 1 < len(GATHER_BITS):
+        if step < last:
+            got = lax.ppermute(held, "band", pairs)
+            settled = state
+            state = match_block(state, features, got, got_rows, grid_cols)
             held = jnp.concatenate([held, got], axis=0)
             held, settled = lax.optimization_barrier((held, settled))
+        else:
+            split = held.shape[0] // 2
+            first = lax.ppermute(held[:split], "band", pairs)
+            second = lax.ppermute(held[split:], "band", pairs)
+            half_rows = got_rows.shape[0] // 2
+            state = match_block(state, features, first, got_rows[:half_rows], grid_cols)
+            state = match_block(state, features, second, got_rows[half_rows:], grid_cols)
+    pieces = [held, first, second]
     running_max, acc = state
     denominator = acc[:, 0]
     flow_row = (acc[:, 1] / denominator / total_rows).reshape(
@@ -265,20 +274,30 @@
     flow_col = (
         (8.0 * (acc[:, 2] / denominator) + 3.5) / image_width
     ).reshape(band_rows, image_width) - pixel_col.astype(jnp.float32) / image_width
-    inverse = np.argsort(deposit).astype(np.int32)
+    inverse = jnp.asarray(np.argsort(deposit).astype(np.int32))
+    reach = 4
+    window = []
+    for shift in range(-reach, reach + 1):
+        block = inverse[jnp.clip(band + shift, 0, total_rows - 1) ^ band]
+        chosen = None
+        first_block = 0
+        for piece in pieces:
+            count = piece.shape[0] // grid_cols
+            local = jnp.clip(block - first_block, 0, count - 1)
+            part = lax.dynamic_slice_in_dim(piece, local * grid_cols, grid_cols, 0)
+            chosen = part if chosen is None else jnp.where(block >= first_block, part, chosen)
+            first_block += count
+        window.append(chosen)
+    window = jnp.concatenate(window, axis=0)
+    near = lax.dot_general(
+        features, window, (((1,), (1,)), ((), ())), preferred_element_type=jnp.float32
+    )
     t_row = target_row.reshape(pixel_count)
     t_col = target_col.reshape(pixel_count)
     valid = t_row >= 0
-    place = jnp.asarray(inverse)[jnp.where(valid, t_row ^ band, 0)] * grid_cols + jnp.where(
-        valid, t_col, 0
-    )
-    half = held.shape[0]
-    picked = jnp.where(
-        (place < half)[:, None],
-        jnp.take(held, jnp.minimum(place, half - 1), axis=0),
-        jnp.take(got, jnp.maximum(place - half, 0), axis=0),
-    )
-    found = jnp.sum(features.astype(jnp.float32) * picked.astype(jnp.float32), axis=1)
+    slot = (t_row - band + reach) * grid_cols + t_col
+    hit = jnp.arange(near.shape[1], dtype=jnp.int32)[None, :] == slot[:, None]
+    found = jnp.sum(jnp.where(hit, near, 0.0), axis=1)
     lookup = jnp.where(valid, found, 0.0)
     lookup = lookup.reshape(band_rows, image_width)
     motion = jax.nn.relu(

time: 263 us -> 283 us (1.076)
  between operations: 1.72 us -> 30.7 us
  waiting for transfers between devices: 64.3 us -> 41.8 us
  starting transfers between devices: 101 us -> 115 us
  local copies, waits for them, and re-layouts: 18.2 us -> 12.3 us
    ppermute x16, waiting for transfers between devices: 35.6 us -> 10.8 us  [passed_along(): return lax.ppermute(array, axis, pairs)]
    ppermute x0 -> x2, starting transfers between devices: none -> 13 us  [the longest x1 10.9 us: per_device(): first = lax.ppermute(held[:split], 'band', pairs)]
    ppermute x16, starting transfers between devices: 54.7 us -> 65.9 us  [passed_along(): return lax.ppermute(array, axis, pairs)]
    ppermute x8 -> x7, starting transfers between devices: 45.9 us -> 35.7 us  [per_device(): got = lax.ppermute(held, 'band', pairs)]
    gather x3 -> x0, local copies, waits for them, and re-layouts: 8.93 us -> none  [the longest x1 4.07 us: per_device(): jnp.take(got, jnp.maximum(place - half, 0), axis=0)]
    unnamed x0 -> x8, other arithmetic: none -> 6.23 us
    ppermute x8 -> x7, waiting for transfers between devices: 28.7 us -> 30.9 us  [per_device(): got = lax.ppermute(held, 'band', pairs)]
    pallas_call x9 -> x10, Pallas kernels: 37.3 us -> 39.1 us  [match_block(): pl.pallas_call(match_kernel, grid=(count // tile,), in_specs=[pl.BlockSpe...]
  transfers between devices with their start and end apart: 24 -> 25, of which waited for: 11 -> 11; matrix products, arithmetic and copies ran while one was open for 15% -> 11% of each run, Pallas kernels for 10% -> 12%
where the time goes in v4:
time: 283 us; the launch traced here: 280 us
  starting transfers between devices  115 us (41%)
  waiting for transfers between devices  41.8 us (15%)
  Pallas kernels  39.1 us (14%)
  between operations  30.7 us (11%)
  other arithmetic  25.4 us (9%)
  matrix products  16.2 us (6%)
  local copies, waits for them, and re-layouts  12.3 us (4%)
    ppermute x16, starting transfers between devices, passed_along(): return lax.ppermute(array, axis, pairs)  65.9 us
    pallas_call x10, Pallas kernels, match_block(): pl.pallas_call(match_kernel, grid=(count // tile,), in_specs=[pl.BlockSpe...  39.1 us
    ppermute x7, starting transfers between devices, per_device(): got = lax.ppermute(held, 'band', pairs)  35.7 us
    ppermute x7, waiting for transfers between devices, per_device(): got = lax.ppermute(held, 'band', pairs)  30.9 us
    dot_general x50, matrix products, conv_valid(): jnp.dot(tap_slice.reshape(-1, tap_slice.shape[-1]), weight[kernel_tap], p...  15.9 us
    ppermute x1, starting transfers between devices, per_device(): first = lax.ppermute(held[:split], 'band', pairs)  10.9 us
    ppermute x16, waiting for transfers between devices, passed_along(): return lax.ppermute(array, axis, pairs)  10.8 us
    concatenate x8, other arithmetic, match_block(): jnp.concatenate([jnp.ones((count, 1), jnp.float32), strip_row[:, None], s...  8.95 us
  transfers between devices with their start and end apart: 25, of which 11 were waited for; matrix products, arithmetic and copies ran while one was open for 11% of the time, Pallas kernels for 12%

profile of v4, /device:TPU:7, one launch (start us, length us, event | category | flops | bytes accessed | tf_op | source)
XLA Modules:
  0.0 280.1 jit_solution(3589459505518482218)
XLA Ops:
  1.7 15.4 %collective-permute-start = (bf16[48,256]{1,0:T(8,128)(2,1)S(1)}, bf16[48,256]{1,0:T(8,128)(2,1)S(1)}, u32[]{:S(2)}, u32[]{:S(2)}) collective-permute-start(bf16[48,256]{1,0:T(8,128)(2,1)S(1)} %multiply_convert_fusion.s_ref), channel_id=1, source_target_pairs={{0,32},{2,34},{4,36},{6,38},{8,40},{10,42},{12,44},{14,46},{16,48}... | collective-permute-start | bytes 73736 | tf_op jit(solution)/shard_map/ppermute | solution.py:256
  22.7 2.5 shard_map.176
  26.0 4.0 %collective-permute-start.1 = (bf16[96,256]{1,0:T(8,128)(2,1)S(1)}, bf16[96,256]{1,0:T(8,128)(2,1)S(1)}, u32[]{:S(2)}, u32[]{:S(2)}) collective-permute-start(bf16[96,256]{1,0:T(8,128)(2,1)S(1)} %pad_maximum_fusion.8), channel_id=1, source_target_pairs={{0,16},{2,18},{4,20},{6,22},{8,24},{10,26},{12,28},{14,30},{16,0},... | collective-permute-start | bytes 147464 | tf_op jit(solution)/shard_map/ppermute | solution.py:256
  30.1 2.5 shard_map.177
  32.6 2.1 collective-permute-done.1.s_ref
  34.8 3.3 %collective-permute-start.2 = (bf16[192,256]{1,0:T(8,128)(2,1)S(1)}, bf16[192,256]{1,0:T(8,128)(2,1)S(1)}, u32[]{:S(2)}, u32[]{:S(2)}) collective-permute-start(bf16[192,256]{1,0:T(8,128)(2,1)S(1)} %pad_maximum_fusion.7), channel_id=1, source_target_pairs={{0,8},{2,10},{4,12},{6,14},{8,0},{10,2},{12,4},{14,6},{16,24},{18,... | collective-permute-start | bytes 294920 | tf_op jit(solution)/shard_map/ppermute | solution.py:256
  38.1 2.6 shard_map.178
  42.1 3.0 %collective-permute-start.3 = (bf16[384,256]{1,0:T(8,128)(2,1)S(1)}, bf16[384,256]{1,0:T(8,128)(2,1)S(1)}, u32[]{:S(2)}, u32[]{:S(2)}) collective-permute-start(bf16[384,256]{1,0:T(8,128)(2,1)S(1)} %pad_maximum_fusion.5), channel_id=1, source_target_pairs={{0,256},{2,258},{4,260},{6,262},{8,264},{10,266},{12,268},{14,270}... | collective-permute-start | bytes 589832 | tf_op jit(solution)/shard_map/ppermute | solution.py:256
  45.2 2.6 shard_map.179
  47.8 2.2 collective-permute-done.3.s_ref
  50.0 4.8 %collective-permute-start.4 = (bf16[768,256]{1,0:T(8,128)(2,1)S(1)}, bf16[768,256]{1,0:T(8,128)(2,1)S(1)}, u32[]{:S(2)}, u32[]{:S(2)}) collective-permute-start(bf16[768,256]{1,0:T(8,128)(2,1)S(1)} %pad_maximum_fusion.3), channel_id=1, source_target_pairs={{0,128},{2,130},{4,132},{6,134},{8,136},{10,138},{12,140},{14,142}... | collective-permute-start | bytes 1179656 | tf_op jit(solution)/shard_map/ppermute | solution.py:256
  56.4 2.8 shard_map.180
  60.1 1.9 collective-permute-start.5
  63.0 3.0 %shard_map.181 = (f32[384,128]{1,0:T(8,128)}, f32[384,128]{1,0:T(8,128)}) custom-call(bf16[384,256]{1,0:T(8,128)(2,1)} %bitcast.461, bf16[768,256]{1,0:T(8,128)(2,1)} %copy-done.7, bf16[768,128]{1,0:T(8,128)(2,1)} %maximum_maximum_fusion.4.w_ref, f32[384,128]{1,0:T(8,128)} %get-tuple-element.40.m_in, f32[384,128]{1,0:T(8,128)} %get-tuple-element.41.a_in), custom_call_target="tpu_custom_call" | custom-call | flops 301989888 | bytes 1572864 | tf_op jit(solution)/shard_map/pallas_call | solution.py:197
  66.0 7.8 %collective-permute-done.5.s_ref = bf16[1536,256]{1,0:T(8,128)(2,1)S(1)} collective-permute-done((bf16[1536,256]{1,0:T(8,128)(2,1)S(1)}, bf16[1536,256]{1,0:T(8,128)(2,1)S(1)}, u32[]{:S(2)}, u32[]{:S(2)}) %collective-permute-start.5) | collective-permute-done | bytes 786464 | tf_op jit(solution)/shard_map/ppermute | solution.py:256
  74.7 3.2 %collective-permute-start.6 = (bf16[3072,256]{1,0:T(8,128)(2,1)S(1)}, bf16[3072,256]{1,0:T(8,128)(2,1)}, u32[]{:S(2)}, u32[]{:S(2)}) collective-permute-start(bf16[3072,256]{1,0:T(8,128)(2,1)S(1)} %pad_maximum_fusion.1), channel_id=1, source_target_pairs={{0,64},{2,66},{4,68},{6,70},{8,72},{10,74},{12,76},{14,78},{16,80}... | collective-permute-start | bytes 4718600 | tf_op jit(solution)/shard_map/ppermute | solution.py:256
  83.8 4.1 %shard_map.182 = (f32[384,128]{1,0:T(8,128)}, f32[384,128]{1,0:T(8,128)}) custom-call(bf16[384,256]{1,0:T(8,128)(2,1)} %bitcast.462, bf16[1536,256]{1,0:T(8,128)(2,1)} %copy-done.10, bf16[1536,128]{1,0:T(8,128)(2,1)} %maximum_maximum_fusion.3.w_ref, f32[384,128]{1,0:T(8,128)} %get-tuple-element.43.m_in, f32[384,128]{1,0:T(8,128)} %get-tuple-element.44.a_in), custom_call_target="tpu_custom_call" | custom-call | flops 603979776 | bytes 2162688 | tf_op jit(solution)/shard_map/pallas_call | solution.py:197
  88.0 16.5 %collective-permute-done.6.s_ref = bf16[3072,256]{1,0:T(8,128)(2,1)} collective-permute-done((bf16[3072,256]{1,0:T(8,128)(2,1)S(1)}, bf16[3072,256]{1,0:T(8,128)(2,1)}, u32[]{:S(2)}, u32[]{:S(2)}) %collective-permute-start.6) | collective-permute-done | bytes 1572896 | tf_op jit(solution)/shard_map/ppermute | solution.py:256
  104.4 2.1 pad_maximum_fusion
  106.6 1.9 fusion.317
  108.4 10.9 %collective-permute-start.8 = (bf16[3072,256]{1,0:T(8,128)(2,1)}, bf16[3072,256]{1,0:T(8,128)(2,1)}, u32[]{:S(2)}, u32[]{:S(2)}) collective-permute-start(bf16[3072,256]{1,0:T(8,128)(2,1)} %get-tuple-element.59), channel_id=1, source_target_pairs={{0,2},{2,0},{4,6},{6,4},{8,10},{10,8},{12,14},{14,12},{16,18},{18,... | collective-permute-start | bytes 4718600 | tf_op jit(solution)/shard_map/ppermute | solution.py:263
  119.4 2.1 collective-permute-start.7
  154.9 1.8 convert_element_type.347
  156.7 2.1 convolution_add_fusion.15
  159.5 4.0 %maximum_maximum_fusion.2 = (bf16[3072,128]{1,0:T(8,128)(2,1)}, bf16[3072,128]{1,0:T(8,128)(2,1)}, bf16[3072,128]{1,0:T(8,128)(2,1)}) fusion(bf16[3072,1]{1,0:T(8,128)(2,1)} %convert_element_type.347, bf16[3072,1]{1,0:T(8,128)(2,1)S(1)} %fusion.1, bf16[128]{0:T(256)(128)(2,1)S(1)} %pad.80.clone, bf16[128]{0:T(256)(128)(2,1)S(1)} %pad.77.clone, ...), kind=kLoop, calls=%fused_computation.102 | loop fusion | flops 7077888 | bytes 2384384 | tf_op jit(solution)/shard_map/concatenate | solution.py:187
  163.5 6.3 %shard_map.183 = (f32[384,128]{1,0:T(8,128)}, f32[384,128]{1,0:T(8,128)}) custom-call(bf16[384,256]{1,0:T(8,128)(2,1)} %bitcast.463, bf16[3072,256]{1,0:T(8,128)(2,1)} %collective-permute-done.6.s_ref, bf16[3072,128]{1,0:T(8,128)(2,1)} %get-tuple-element.60.w_ref, f32[384,128]{1,0:T(8,128)} %get-tuple-element.46.m_in, f32[384,128]{1,0:T(8,128)} %get-tuple-element.47.a_in), custom_call_target="tpu_custom_call" | custom-call | flops 1207959552 | bytes 3342336 | tf_op jit(solution)/shard_map/pallas_call | solution.py:197
  169.9 6.3 %shard_map.184 = (f32[384,128]{1,0:T(8,128)}, f32[384,128]{1,0:T(8,128)}) custom-call(bf16[384,256]{1,0:T(8,128)(2,1)} %bitcast.464, bf16[3072,256]{1,0:T(8,128)(2,1)} %collective-permute-done.8.s_ref, bf16[3072,128]{1,0:T(8,128)(2,1)} %get-tuple-element.61.w_ref, f32[384,128]{1,0:T(8,128)} %get-tuple-element.49.m_in, f32[384,128]{1,0:T(8,128)} %get-tuple-element.50.a_in), custom_call_target="tpu_custom_call" | custom-call | flops 1207959552 | bytes 3342336 | tf_op jit(solution)/shard_map/pallas_call | solution.py:197
  176.2 6.3 %shard_map.185 = (f32[384,128]{1,0:T(8,128)}, f32[384,128]{1,0:T(8,128)}) custom-call(bf16[384,256]{1,0:T(8,128)(2,1)} %bitcast.465, bf16[3072,256]{1,0:T(8,128)(2,1)} %collective-permute-done.7.s_ref, bf16[3072,128]{1,0:T(8,128)(2,1)} %get-tuple-element.62.w_ref, f32[384,128]{1,0:T(8,128)} %get-tuple-element.51.m_in, f32[384,128]{1,0:T(8,128)} %get-tuple-element.52.a_in), custom_call_target="tpu_custom_call" | custom-call | flops 1207959552 | bytes 3342336 | tf_op jit(solution)/shard_map/pallas_call | solution.py:197
  194.8 2.6 collective-permute-start.10
  197.4 5.9 %collective-permute-start.9 = (bf16[1,384,384]{2,1,0:T(8,128)(2,1)S(1)}, bf16[1,384,384]{2,1,0:T(8,128)(2,1)S(1)}, u32[]{:S(2)}, u32[]{:S(2)}) collective-permute-start(bf16[1,384,384]{2,1,0:T(8,128)(2,1)S(1)} %pad_maximum_fusion.4), channel_id=1, source_target_pairs={{0,4},{2,6},{4,8},{6,10},{8,12},{10,14},{12,16},{14,18},{16,20},{1... | collective-permute-start | bytes 884744 | tf_op jit(solution)/shard_map/ppermute | solution.py:17
  203.3 5.1 %collective-permute-start.12 = (bf16[1,384,384]{2,1,0:T(8,128)(2,1)S(1)}, bf16[1,384,384]{2,1,0:T(8,128)(2,1)S(1)}, u32[]{:S(2)}, u32[]{:S(2)}) collective-permute-start(bf16[1,384,384]{2,1,0:T(8,128)(2,1)S(1)} %pad_maximum_fusion.4), channel_id=1, source_target_pairs={{4,0},{6,2},{8,4},{10,6},{12,8},{14,10},{16,12},{18,14},{20,16},{2... | collective-permute-start | bytes 884744 | tf_op jit(solution)/shard_map/ppermute | solution.py:17
  208.4 2.3 collective-permute-start.11
  212.3 2.4 collective-permute-done.12
  217.0 1.9 collective-permute-start.14
  219.1 3.9 %collective-permute-start.13 = (bf16[1,384,128]{2,1,0:T(8,128)(2,1)S(1)}, bf16[1,384,128]{2,1,0:T(8,128)(2,1)S(1)}, u32[]{:S(2)}, u32[]{:S(2)}) collective-permute-start(bf16[1,384,128]{2,1,0:T(8,128)(2,1)S(1)} %fusion.75), channel_id=1, source_target_pairs={{0,4},{2,6},{4,8},{6,10},{8,12},{10,14},{12,16},{14,18},{16,20},{1... | collective-permute-start | bytes 294920 | tf_op jit(solution)/shard_map/ppermute | solution.py:17
  223.0 9.5 %collective-permute-start.16 = (bf16[1,384,128]{2,1,0:T(8,128)(2,1)S(1)}, bf16[1,384,128]{2,1,0:T(8,128)(2,1)S(1)}, u32[]{:S(2)}, u32[]{:S(2)}) collective-permute-start(bf16[1,384,128]{2,1,0:T(8,128)(2,1)S(1)} %fusion.75), channel_id=1, source_target_pairs={{4,0},{6,2},{8,4},{10,6},{12,8},{14,10},{16,12},{18,14},{20,16},{2... | collective-permute-start | bytes 294920 | tf_op jit(solution)/shard_map/ppermute | solution.py:17
  232.5 2.9 %collective-permute-start.15 = (bf16[1,384,128]{2,1,0:T(8,128)(2,1)S(1)}, bf16[1,384,128]{2,1,0:T(8,128)(2,1)S(1)}, u32[]{:S(2)}, u32[]{:S(2)}) collective-permute-start(bf16[1,384,128]{2,1,0:T(8,128)(2,1)S(1)} %fusion.75), channel_id=1, source_target_pairs={{2,0},{4,2},{6,4},{8,6},{10,8},{12,10},{14,12},{16,14},{18,16},{20... | collective-permute-start | bytes 294920 | tf_op jit(solution)/shard_map/ppermute | solution.py:17
  235.9 2.7 collective-permute-done.15
  240.8 1.9 collective-permute-start.18
  242.9 1.9 collective-permute-start.17
  244.9 9.1 %collective-permute-start.20 = (bf16[1,384,128]{2,1,0:T(8,128)(2,1)S(1)}, bf16[1,384,128]{2,1,0:T(8,128)(2,1)S(1)}, u32[]{:S(2)}, u32[]{:S(2)}) collective-permute-start(bf16[1,384,128]{2,1,0:T(8,128)(2,1)S(1)} %get-tuple-element.83), channel_id=1, source_target_pairs={{4,0},{6,2},{8,4},{10,6},{12,8},{14,10},{16,12},{18,14},{20,16},{2... | collective-permute-start | bytes 294920 | tf_op jit(solution)/shard_map/ppermute | solution.py:17
  254.0 3.0 %collective-permute-start.19 = (bf16[1,384,128]{2,1,0:T(8,128)(2,1)S(1)}, bf16[1,384,128]{2,1,0:T(8,128)(2,1)S(1)}, u32[]{:S(2)}, u32[]{:S(2)}) collective-permute-start(bf16[1,384,128]{2,1,0:T(8,128)(2,1)S(1)} %get-tuple-element.83), channel_id=1, source_target_pairs={{2,0},{4,2},{6,4},{8,6},{10,8},{12,10},{14,12},{16,14},{18,16},{20... | collective-permute-start | bytes 294920 | tf_op jit(solution)/shard_map/ppermute | solution.py:17
  257.5 2.4 collective-permute-done.19
  260.2 1.9 collective-permute-start.22
  262.3 1.9 collective-permute-start.21
  264.2 9.1 %collective-permute-start.24 = (bf16[1,384,128]{2,1,0:T(8,128)(2,1)S(1)}, bf16[1,384,128]{2,1,0:T(8,128)(2,1)S(1)}, u32[]{:S(2)}, u32[]{:S(2)}) collective-permute-start(bf16[1,384,128]{2,1,0:T(8,128)(2,1)S(1)} %fusion.73), channel_id=1, source_target_pairs={{4,0},{6,2},{8,4},{10,6},{12,8},{14,10},{16,12},{18,14},{20,16},{2... | collective-permute-start | bytes 294920 | tf_op jit(solution)/shard_map/ppermute | solution.py:17
  273.3 3.0 %collective-permute-start.23 = (bf16[1,384,128]{2,1,0:T(8,128)(2,1)S(1)}, bf16[1,384,128]{2,1,0:T(8,128)(2,1)S(1)}, u32[]{:S(2)}, u32[]{:S(2)}) collective-permute-start(bf16[1,384,128]{2,1,0:T(8,128)(2,1)S(1)} %fusion.73), channel_id=1, source_target_pairs={{2,0},{4,2},{6,4},{8,6},{10,8},{12,10},{14,12},{16,14},{18,16},{20... | collective-permute-start | bytes 294920 | tf_op jit(solution)/shard_map/ppermute | solution.py:17
  276.8 2.5 collective-permute-done.23
  (189 shorter events, 45.2 us)
Async XLA Ops:
  0.6 37.4 %copy-start.22 = (s32[8]{0:T(128)S(1)}, s32[8]{0:T(128)}, u32[]{:S(2)}) copy-start(s32[8]{0:T(128)} %constant.338.clone) | copy-start | bytes 100
  1.7 21.0 %copy-start.13 = (bf16[48,256]{1,0:T(8,128)(2,1)}, bf16[48,256]{1,0:T(8,128)(2,1)S(1)}, u32[]{:S(2)}) copy-start(bf16[48,256]{1,0:T(8,128)(2,1)S(1)} %multiply_convert_fusion.s_ref) | copy-start | bytes 73732
  1.7 23.5 %collective-permute-start = (bf16[48,256]{1,0:T(8,128)(2,1)S(1)}, bf16[48,256]{1,0:T(8,128)(2,1)S(1)}, u32[]{:S(2)}, u32[]{:S(2)}) collective-permute-start(bf16[48,256]{1,0:T(8,128)(2,1)S(1)} %multiply_convert_fusion.s_ref), channel_id=1, source_target_pairs={{0,32},{2,34},{4,36},{6,38},{8,40},{10,42},{12,44},{14,46},{16,48}... | collective-permute-start | bytes 73736 | tf_op jit(solution)/shard_map/ppermute | solution.py:256
  21.3 23.8 %copy-start.21 = (s32[16]{0:T(128)S(1)}, s32[16]{0:T(128)}, u32[]{:S(2)}) copy-start(s32[16]{0:T(128)} %constant.339.clone) | copy-start | bytes 196
  25.2 4.8 %copy-start.15 = (bf16[48,256]{1,0:T(8,128)(2,1)}, bf16[48,256]{1,0:T(8,128)(2,1)S(1)}, u32[]{:S(2)}) copy-start(bf16[48,256]{1,0:T(8,128)(2,1)S(1)} %collective-permute-done.s_ref) | copy-start | bytes 73732
  26.0 8.7 %collective-permute-start.1 = (bf16[96,256]{1,0:T(8,128)(2,1)S(1)}, bf16[96,256]{1,0:T(8,128)(2,1)S(1)}, u32[]{:S(2)}, u32[]{:S(2)}) collective-permute-start(bf16[96,256]{1,0:T(8,128)(2,1)S(1)} %pad_maximum_fusion.8), channel_id=1, source_target_pairs={{0,16},{2,18},{4,20},{6,22},{8,24},{10,26},{12,28},{14,30},{16,0},... | collective-permute-start | bytes 147464 | tf_op jit(solution)/shard_map/ppermute | solution.py:256
  34.7 3.3 %copy-start.14 = (bf16[96,256]{1,0:T(8,128)(2,1)}, bf16[96,256]{1,0:T(8,128)(2,1)S(1)}, u32[]{:S(2)}) copy-start(bf16[96,256]{1,0:T(8,128)(2,1)S(1)} %collective-permute-done.1.s_ref) | copy-start | bytes 147460
  34.8 7.3 %collective-permute-start.2 = (bf16[192,256]{1,0:T(8,128)(2,1)S(1)}, bf16[192,256]{1,0:T(8,128)(2,1)S(1)}, u32[]{:S(2)}, u32[]{:S(2)}) collective-permute-start(bf16[192,256]{1,0:T(8,128)(2,1)S(1)} %pad_maximum_fusion.7), channel_id=1, source_target_pairs={{0,8},{2,10},{4,12},{6,14},{8,0},{10,2},{12,4},{14,6},{16,24},{18,... | collective-permute-start | bytes 294920 | tf_op jit(solution)/shard_map/ppermute | solution.py:256
  42.1 3.1 %copy-start.12 = (bf16[192,256]{1,0:T(8,128)(2,1)}, bf16[192,256]{1,0:T(8,128)(2,1)S(1)}, u32[]{:S(2)}) copy-start(bf16[192,256]{1,0:T(8,128)(2,1)S(1)} %collective-permute-done.2.s_ref) | copy-start | bytes 294916
  42.1 7.9 %collective-permute-start.3 = (bf16[384,256]{1,0:T(8,128)(2,1)S(1)}, bf16[384,256]{1,0:T(8,128)(2,1)S(1)}, u32[]{:S(2)}, u32[]{:S(2)}) collective-permute-start(bf16[384,256]{1,0:T(8,128)(2,1)S(1)} %pad_maximum_fusion.5), channel_id=1, source_target_pairs={{0,256},{2,258},{4,260},{6,262},{8,264},{10,266},{12,268},{14,270}... | collective-permute-start | bytes 589832 | tf_op jit(solution)/shard_map/ppermute | solution.py:256
  50.0 6.4 %copy-start.9 = (bf16[384,256]{1,0:T(8,128)(2,1)}, bf16[384,256]{1,0:T(8,128)(2,1)S(1)}, u32[]{:S(2)}) copy-start(bf16[384,256]{1,0:T(8,128)(2,1)S(1)} %collective-permute-done.3.s_ref) | copy-start | bytes 589828
  50.0 10.0 %collective-permute-start.4 = (bf16[768,256]{1,0:T(8,128)(2,1)S(1)}, bf16[768,256]{1,0:T(8,128)(2,1)S(1)}, u32[]{:S(2)}, u32[]{:S(2)}) collective-permute-start(bf16[768,256]{1,0:T(8,128)(2,1)S(1)} %pad_maximum_fusion.3), channel_id=1, source_target_pairs={{0,128},{2,130},{4,132},{6,134},{8,136},{10,138},{12,140},{14,142}... | collective-permute-start | bytes 1179656 | tf_op jit(solution)/shard_map/ppermute | solution.py:256
  55.5 6.6 %copy-start.17 = (s32[2,1,384]{2,1,0:T(1,128)S(1)}, s32[2,1,384]{2,1,0:T(1,128)}, u32[]{:S(2)}) copy-start(s32[2,1,384]{2,1,0:T(1,128)} %param.21) | copy-start | bytes 9220
  55.5 6.6 %copy-start.18 = (f32[3,128]{1,0:T(4,128)S(1)}, f32[3,128]{1,0:T(4,128)}, u32[]{:S(2)}) copy-start(f32[3,128]{1,0:T(4,128)} %param.22) | copy-start | bytes 4612
  60.1 2.9 %copy-start.7 = (bf16[768,256]{1,0:T(8,128)(2,1)}, bf16[768,256]{1,0:T(8,128)(2,1)S(1)}, u32[]{:S(2)}) copy-start(bf16[768,256]{1,0:T(8,128)(2,1)S(1)} %collective-permute-done.4.s_ref) | copy-start | bytes 1179652
  60.1 13.7 %collective-permute-start.5 = (bf16[1536,256]{1,0:T(8,128)(2,1)S(1)}, bf16[1536,256]{1,0:T(8,128)(2,1)S(1)}, u32[]{:S(2)}, u32[]{:S(2)}) collective-permute-start(bf16[1536,256]{1,0:T(8,128)(2,1)S(1)} %pad_maximum_fusion.2), channel_id=1, source_target_pairs={{0,4},{2,6},{4,0},{6,2},{8,12},{10,14},{12,8},{14,10},{16,20},{18,... | collective-permute-start | bytes 2359304 | tf_op jit(solution)/shard_map/ppermute | solution.py:256
  66.0 11.9 %copy-start.20 = (s32[32]{0:T(128)S(1)}, s32[32]{0:T(128)}, u32[]{:S(2)}) copy-start(s32[32]{0:T(128)} %constant.340.clone) | copy-start | bytes 388
  66.0 12.5 %copy-start.2 = (bf16[1,384,128]{2,1,0:T(8,128)(2,1)S(1)}, bf16[1,384,128]{2,1,0:T(8,128)(2,1)}, u32[]{:S(2)}) copy-start(bf16[1,384,128]{2,1,0:T(8,128)(2,1)} %param.20) | copy-start | bytes 294916
  73.8 0.9 copy-start.10
  74.7 8.1 %copy-start.1 = (bf16[3072,256]{1,0:T(8,128)(2,1)}, bf16[3072,256]{1,0:T(8,128)(2,1)S(1)}, u32[]{:S(2)}) copy-start(bf16[3072,256]{1,0:T(8,128)(2,1)S(1)} %pad_maximum_fusion.1) | copy-start | bytes 4718596
  74.7 29.8 %collective-permute-start.6 = (bf16[3072,256]{1,0:T(8,128)(2,1)S(1)}, bf16[3072,256]{1,0:T(8,128)(2,1)}, u32[]{:S(2)}, u32[]{:S(2)}) collective-permute-start(bf16[3072,256]{1,0:T(8,128)(2,1)S(1)} %pad_maximum_fusion.1), channel_id=1, source_target_pairs={{0,64},{2,66},{4,68},{6,70},{8,72},{10,74},{12,76},{14,78},{16,80}... | collective-permute-start | bytes 4718600 | tf_op jit(solution)/shard_map/ppermute | solution.py:256
  106.5 12.8 %copy-start.19 = (s32[64]{0:T(128)S(1)}, s32[64]{0:T(128)}, u32[]{:S(2)}) copy-start(s32[64]{0:T(128)} %constant.341.clone) | copy-start | bytes 772
  106.5 15.0 %copy-start.16 = (s32[256]{0:T(256)S(1)}, s32[256]{0:T(256)}, u32[]{:S(2)}) copy-start(s32[256]{0:T(256)} %constant.343.clone) | copy-start | bytes 3076
  108.4 61.4 %collective-permute-start.8 = (bf16[3072,256]{1,0:T(8,128)(2,1)}, bf16[3072,256]{1,0:T(8,128)(2,1)}, u32[]{:S(2)}, u32[]{:S(2)}) collective-permute-start(bf16[3072,256]{1,0:T(8,128)(2,1)} %get-tuple-element.59), channel_id=1, source_target_pairs={{0,2},{2,0},{4,6},{6,4},{8,10},{10,8},{12,14},{14,12},{16,18},{18,... | collective-permute-start | bytes 4718600 | tf_op jit(solution)/shard_map/ppermute | solution.py:263
  119.4 56.8 %collective-permute-start.7 = (bf16[3072,256]{1,0:T(8,128)(2,1)}, bf16[3072,256]{1,0:T(8,128)(2,1)}, u32[]{:S(2)}, u32[]{:S(2)}) collective-permute-start(bf16[3072,256]{1,0:T(8,128)(2,1)} %get-tuple-element.58), channel_id=1, source_target_pairs={{0,2},{2,0},{4,6},{6,4},{8,10},{10,8},{12,14},{14,12},{16,18},{18,... | collective-permute-start | bytes 4718600 | tf_op jit(solution)/shard_map/ppermute | solution.py:264
  156.7 2.8 copy-start.3
  156.7 2.8 copy-start.4
  182.5 8.6 %copy-start = (bf16[1,384,256]{2,1,0:T(8,128)(2,1)S(1)}, bf16[1,384,256]{2,1,0:T(8,128)(2,1)}, u32[]{:S(2)}) copy-start(bf16[1,384,256]{2,1,0:T(8,128)(2,1)} %param.17) | copy-start | bytes 589828
  182.5 9.2 %copy-start.8 = (bf16[1,384,128]{2,1,0:T(8,128)(2,1)S(1)}, bf16[1,384,128]{2,1,0:T(8,128)(2,1)}, u32[]{:S(2)}) copy-start(bf16[1,384,128]{2,1,0:T(8,128)(2,1)} %param.19) | copy-start | bytes 294916
  182.5 9.2 %copy-start.6 = (bf16[5,384,384]{2,1,0:T(8,128)(2,1)S(1)}, bf16[5,384,384]{2,1,0:T(8,128)(2,1)}, u32[]{:S(2)}) copy-start(bf16[5,384,384]{2,1,0:T(8,128)(2,1)} %param.23) | copy-start | bytes 4423684
  192.6 1.0 copy-start.11
  194.2 16.5 %copy-start.5 = (bf16[5,384,384]{2,1,0:T(8,128)(2,1)S(1)}, bf16[5,384,384]{2,1,0:T(8,128)(2,1)}, u32[]{:S(2)}) copy-start(bf16[5,384,384]{2,1,0:T(8,128)(2,1)} %param.24) | copy-start | bytes 4423684
  194.8 17.0 %collective-permute-start.10 = (bf16[1,384,384]{2,1,0:T(8,128)(2,1)S(1)}, bf16[1,384,384]{2,1,0:T(8,128)(2,1)S(1)}, u32[]{:S(2)}, u32[]{:S(2)}) collective-permute-start(bf16[1,384,384]{2,1,0:T(8,128)(2,1)S(1)} %pad_maximum_fusion.4), channel_id=1, source_target_pairs={{0,2},{2,4},{4,6},{6,8},{8,10},{10,12},{12,14},{14,16},{16,18},{18... | collective-permute-start | bytes 884744 | tf_op jit(solution)/shard_map/ppermute | solution.py:17
  197.4 17.5 %collective-permute-start.9 = (bf16[1,384,384]{2,1,0:T(8,128)(2,1)S(1)}, bf16[1,384,384]{2,1,0:T(8,128)(2,1)S(1)}, u32[]{:S(2)}, u32[]{:S(2)}) collective-permute-start(bf16[1,384,384]{2,1,0:T(8,128)(2,1)S(1)} %pad_maximum_fusion.4), channel_id=1, source_target_pairs={{0,4},{2,6},{4,8},{6,10},{8,12},{10,14},{12,16},{14,18},{16,20},{1... | collective-permute-start | bytes 884744 | tf_op jit(solution)/shard_map/ppermute | solution.py:17
  203.3 11.3 %collective-permute-start.12 = (bf16[1,384,384]{2,1,0:T(8,128)(2,1)S(1)}, bf16[1,384,384]{2,1,0:T(8,128)(2,1)S(1)}, u32[]{:S(2)}, u32[]{:S(2)}) collective-permute-start(bf16[1,384,384]{2,1,0:T(8,128)(2,1)S(1)} %pad_maximum_fusion.4), channel_id=1, source_target_pairs={{4,0},{6,2},{8,4},{10,6},{12,8},{14,10},{16,12},{18,14},{20,16},{2... | collective-permute-start | bytes 884744 | tf_op jit(solution)/shard_map/ppermute | solution.py:17
  208.4 8.0 %collective-permute-start.11 = (bf16[1,384,384]{2,1,0:T(8,128)(2,1)S(1)}, bf16[1,384,384]{2,1,0:T(8,128)(2,1)S(1)}, u32[]{:S(2)}, u32[]{:S(2)}) collective-permute-start(bf16[1,384,384]{2,1,0:T(8,128)(2,1)S(1)} %pad_maximum_fusion.4), channel_id=1, source_target_pairs={{2,0},{4,2},{6,4},{8,6},{10,8},{12,10},{14,12},{16,14},{18,16},{20... | collective-permute-start | bytes 884744 | tf_op jit(solution)/shard_map/ppermute | solution.py:17
  217.0 18.4 %collective-permute-start.14 = (bf16[1,384,128]{2,1,0:T(8,128)(2,1)S(1)}, bf16[1,384,128]{2,1,0:T(8,128)(2,1)S(1)}, u32[]{:S(2)}, u32[]{:S(2)}) collective-permute-start(bf16[1,384,128]{2,1,0:T(8,128)(2,1)S(1)} %fusion.75), channel_id=1, source_target_pairs={{0,2},{2,4},{4,6},{6,8},{8,10},{10,12},{12,14},{14,16},{16,18},{18... | collective-permute-start | bytes 294920 | tf_op jit(solution)/shard_map/ppermute | solution.py:17
  219.1 16.5 %collective-permute-start.13 = (bf16[1,384,128]{2,1,0:T(8,128)(2,1)S(1)}, bf16[1,384,128]{2,1,0:T(8,128)(2,1)S(1)}, u32[]{:S(2)}, u32[]{:S(2)}) collective-permute-start(bf16[1,384,128]{2,1,0:T(8,128)(2,1)S(1)} %fusion.75), channel_id=1, source_target_pairs={{0,4},{2,6},{4,8},{6,10},{8,12},{10,14},{12,16},{14,18},{16,20},{1... | collective-permute-start | bytes 294920 | tf_op jit(solution)/shard_map/ppermute | solution.py:17
  223.0 12.8 %collective-permute-start.16 = (bf16[1,384,128]{2,1,0:T(8,128)(2,1)S(1)}, bf16[1,384,128]{2,1,0:T(8,128)(2,1)S(1)}, u32[]{:S(2)}, u32[]{:S(2)}) collective-permute-start(bf16[1,384,128]{2,1,0:T(8,128)(2,1)S(1)} %fusion.75), channel_id=1, source_target_pairs={{4,0},{6,2},{8,4},{10,6},{12,8},{14,10},{16,12},{18,14},{20,16},{2... | collective-permute-start | bytes 294920 | tf_op jit(solution)/shard_map/ppermute | solution.py:17
  232.5 6.2 %collective-permute-start.15 = (bf16[1,384,128]{2,1,0:T(8,128)(2,1)S(1)}, bf16[1,384,128]{2,1,0:T(8,128)(2,1)S(1)}, u32[]{:S(2)}, u32[]{:S(2)}) collective-permute-start(bf16[1,384,128]{2,1,0:T(8,128)(2,1)S(1)} %fusion.75), channel_id=1, source_target_pairs={{2,0},{4,2},{6,4},{8,6},{10,8},{12,10},{14,12},{16,14},{18,16},{20... | collective-permute-start | bytes 294920 | tf_op jit(solution)/shard_map/ppermute | solution.py:17
  240.8 16.1 %collective-permute-start.18 = (bf16[1,384,128]{2,1,0:T(8,128)(2,1)S(1)}, bf16[1,384,128]{2,1,0:T(8,128)(2,1)S(1)}, u32[]{:S(2)}, u32[]{:S(2)}) collective-permute-start(bf16[1,384,128]{2,1,0:T(8,128)(2,1)S(1)} %get-tuple-element.83), channel_id=1, source_target_pairs={{0,2},{2,4},{4,6},{6,8},{8,10},{10,12},{12,14},{14,16},{16,18},{18... | collective-permute-start | bytes 294920 | tf_op jit(solution)/shard_map/ppermute | solution.py:17
  242.9 14.2 %collective-permute-start.17 = (bf16[1,384,128]{2,1,0:T(8,128)(2,1)S(1)}, bf16[1,384,128]{2,1,0:T(8,128)(2,1)S(1)}, u32[]{:S(2)}, u32[]{:S(2)}) collective-permute-start(bf16[1,384,128]{2,1,0:T(8,128)(2,1)S(1)} %get-tuple-element.83), channel_id=1, source_target_pairs={{0,4},{2,6},{4,8},{6,10},{8,12},{10,14},{12,16},{14,18},{16,20},{1... | collective-permute-start | bytes 294920 | tf_op jit(solution)/shard_map/ppermute | solution.py:17
  244.9 12.5 %collective-permute-start.20 = (bf16[1,384,128]{2,1,0:T(8,128)(2,1)S(1)}, bf16[1,384,128]{2,1,0:T(8,128)(2,1)S(1)}, u32[]{:S(2)}, u32[]{:S(2)}) collective-permute-start(bf16[1,384,128]{2,1,0:T(8,128)(2,1)S(1)} %get-tuple-element.83), channel_id=1, source_target_pairs={{4,0},{6,2},{8,4},{10,6},{12,8},{14,10},{16,12},{18,14},{20,16},{2... | collective-permute-start | bytes 294920 | tf_op jit(solution)/shard_map/ppermute | solution.py:17
  254.0 5.9 %collective-permute-start.19 = (bf16[1,384,128]{2,1,0:T(8,128)(2,1)S(1)}, bf16[1,384,128]{2,1,0:T(8,128)(2,1)S(1)}, u32[]{:S(2)}, u32[]{:S(2)}) collective-permute-start(bf16[1,384,128]{2,1,0:T(8,128)(2,1)S(1)} %get-tuple-element.83), channel_id=1, source_target_pairs={{2,0},{4,2},{6,4},{8,6},{10,8},{12,10},{14,12},{16,14},{18,16},{20... | collective-permute-start | bytes 294920 | tf_op jit(solution)/shard_map/ppermute | solution.py:17
  260.2 16.1 %collective-permute-start.22 = (bf16[1,384,128]{2,1,0:T(8,128)(2,1)S(1)}, bf16[1,384,128]{2,1,0:T(8,128)(2,1)S(1)}, u32[]{:S(2)}, u32[]{:S(2)}) collective-permute-start(bf16[1,384,128]{2,1,0:T(8,128)(2,1)S(1)} %fusion.73), channel_id=1, source_target_pairs={{0,2},{2,4},{4,6},{6,8},{8,10},{10,12},{12,14},{14,16},{16,18},{18... | collective-permute-start | bytes 294920 | tf_op jit(solution)/shard_map/ppermute | solution.py:17
  262.3 14.2 %collective-permute-start.21 = (bf16[1,384,128]{2,1,0:T(8,128)(2,1)S(1)}, bf16[1,384,128]{2,1,0:T(8,128)(2,1)S(1)}, u32[]{:S(2)}, u32[]{:S(2)}) collective-permute-start(bf16[1,384,128]{2,1,0:T(8,128)(2,1)S(1)} %fusion.73), channel_id=1, source_target_pairs={{0,4},{2,6},{4,8},{6,10},{8,12},{10,14},{12,16},{14,18},{16,20},{1... | collective-permute-start | bytes 294920 | tf_op jit(solution)/shard_map/ppermute | solution.py:17
  264.2 12.4 %collective-permute-start.24 = (bf16[1,384,128]{2,1,0:T(8,128)(2,1)S(1)}, bf16[1,384,128]{2,1,0:T(8,128)(2,1)S(1)}, u32[]{:S(2)}, u32[]{:S(2)}) collective-permute-start(bf16[1,384,128]{2,1,0:T(8,128)(2,1)S(1)} %fusion.73), channel_id=1, source_target_pairs={{4,0},{6,2},{8,4},{10,6},{12,8},{14,10},{16,12},{18,14},{20,16},{2... | collective-permute-start | bytes 294920 | tf_op jit(solution)/shard_map/ppermute | solution.py:17
  273.3 5.9 %collective-permute-start.23 = (bf16[1,384,128]{2,1,0:T(8,128)(2,1)S(1)}, bf16[1,384,128]{2,1,0:T(8,128)(2,1)S(1)}, u32[]{:S(2)}, u32[]{:S(2)}) collective-permute-start(bf16[1,384,128]{2,1,0:T(8,128)(2,1)S(1)} %fusion.73), channel_id=1, source_target_pairs={{2,0},{4,2},{6,4},{8,6},{10,8},{12,10},{14,12},{16,14},{18,16},{20... | collective-permute-start | bytes 294920 | tf_op jit(solution)/shard_map/ppermute | solution.py:17

commit v5 on v4

--- a/solution.py
+++ b/solution.py
@@ -168,12 +168,7 @@
     m_new = jnp.maximum(m_old, jnp.max(scores, axis=1, keepdims=True))
     p = jnp.exp(scores - m_new)
     shrink = jnp.exp(m_old - m_new)
-    p_hi = p.astype(jnp.bfloat16)
-    p_lo = (p - p_hi.astype(jnp.float32)).astype(jnp.bfloat16)
-    w = w_ref[...]
-    part = jnp.dot(p_hi, w, preferred_element_type=jnp.float32) + jnp.dot(
-        p_lo, w, preferred_element_type=jnp.float32
-    )
+    part = jnp.dot(p.astype(jnp.bfloat16), w_ref[...], preferred_element_type=jnp.float32)
     a_out[...] = a_out[...] * shrink + part
     m_out[...] = jnp.broadcast_to(m_new, m_out.shape)
 
@@ -247,25 +242,16 @@
     )
     held = strips.reshape(band_rows * grid_cols, channels)
     state = match_block(state, features, held, band[None], grid_cols)
-    last = len(GATHER_BITS) - 1
     for step, bit in enumerate(GATHER_BITS):
         flip = 1 << bit
         pairs = [(i, i ^ flip) for i in range(bands)]
+        got = lax.ppermute(held, "band", pairs)
         got_rows = (band ^ flip) ^ jnp.asarray(deposit[: 1 << step])
-        if step < last:
-            got = lax.ppermute(held, "band", pairs)
-            settled = state
-            state = match_block(state, features, got, got_rows, grid_cols)
+        settled = state
+        state = match_block(state, features, got, got_rows, grid_cols)
+        if step + 1 < len(GATHER_BITS):
             held = jnp.concatenate([held, got], axis=0)
             held, settled = lax.optimization_barrier((held, settled))
-        else:
-            split = held.shape[0] // 2
-            first = lax.ppermute(held[:split], "band", pairs)
-            second = lax.ppermute(held[split:], "band", pairs)
-            half_rows = got_rows.shape[0] // 2
-            state = match_block(state, features, first, got_rows[:half_rows], grid_cols)
-            state = match_block(state, features, second, got_rows[half_rows:], grid_cols)
-    pieces = [held, first, second]
     running_max, acc = state
     denominator = acc[:, 0]
     flow_row = (acc[:, 1] / denominator / total_rows).reshape(
@@ -274,6 +260,7 @@
     flow_col = (
         (8.0 * (acc[:, 2] / denominator) + 3.5) / image_width
     ).reshape(band_rows, image_width) - pixel_col.astype(jnp.float32) / image_width
+    pieces = [held, got]
     inverse = jnp.asarray(np.argsort(deposit).astype(np.int32))
     reach = 4
     window = []

time: 283 us -> 272 us (0.961)
  waiting for transfers between devices: 41.8 us -> 62.5 us
  starting transfers between devices: 115 us -> 97.1 us
  between operations: 30.7 us -> 18.4 us
  other arithmetic: 25.4 us -> 32.2 us
  local copies, waits for them, and re-layouts: 12.3 us -> 8.17 us
  Pallas kernels: 39.1 us -> 35.7 us
    ppermute x16, waiting for transfers between devices: 10.8 us -> 36.9 us  [passed_along(): return lax.ppermute(array, axis, pairs)]
    ppermute x16, starting transfers between devices: 65.9 us -> 51 us  [passed_along(): return lax.ppermute(array, axis, pairs)]
    ppermute x2 -> x0, starting transfers between devices: 13 us -> none  [the longest x1 10.9 us: per_device(): first = lax.ppermute(held[:split], 'band', pairs)]
    ppermute x7 -> x8, starting transfers between devices: 35.7 us -> 46.2 us  [per_device(): got = lax.ppermute(held, 'band', pairs)]
    ppermute x7 -> x8, waiting for transfers between devices: 30.9 us -> 25.6 us  [per_device(): got = lax.ppermute(held, 'band', pairs)]
    another operation x14 -> x15, other arithmetic: 2.13 us -> 6.22 us
    pallas_call x10 -> x9, Pallas kernels: 39.1 us -> 35.7 us  [match_block(): pl.pallas_call(match_kernel, grid=(count // tile,), in_specs=[pl.BlockSpe...]
    convert_element_type x8 -> x7, local copies, waits for them, and re-layouts: 6.38 us -> 5.39 us  [match_block(): strip_row = jnp.repeat(block_rows, grid_cols).astype(jnp.float32)]
  transfers between devices with their start and end apart: 25 -> 24, of which waited for: 11 -> 10; matrix products, arithmetic and copies ran while one was open for 11% -> 13% of each run, Pallas kernels for 12% -> 9%
where the time goes in v5:
time: 272 us; the launch traced here: 270 us
  starting transfers between devices  97.1 us (36%)
  waiting for transfers between devices  62.5 us (23%)
  Pallas kernels  35.7 us (13%)
  other arithmetic  32.2 us (12%)
  between operations  18.4 us (7%)
  matrix products  15.9 us (6%)
  local copies, waits for them, and re-layouts  8.17 us (3%)
    ppermute x16, starting transfers between devices, passed_along(): return lax.ppermute(array, axis, pairs)  51 us
    ppermute x8, starting transfers between devices, per_device(): got = lax.ppermute(held, 'band', pairs)  46.2 us
    ppermute x16, waiting for transfers between devices, passed_along(): return lax.ppermute(array, axis, pairs)  36.9 us
    pallas_call x9, Pallas kernels, match_block(): pl.pallas_call(match_kernel, grid=(count // tile,), in_specs=[pl.BlockSpe...  35.7 us
    ppermute x8, waiting for transfers between devices, per_device(): got = lax.ppermute(held, 'band', pairs)  25.6 us
    dot_general x50, matrix products, conv_valid(): jnp.dot(tap_slice.reshape(-1, tap_slice.shape[-1]), weight[kernel_tap], p...  15.5 us
    concatenate x9, other arithmetic, match_block(): jnp.concatenate([jnp.ones((count, 1), jnp.float32), strip_row[:, None], s...  9.04 us
    another operation x15, other arithmetic  6.22 us
  transfers between devices with their start and end apart: 24, of which 10 were waited for; matrix products, arithmetic and copies ran while one was open for 13% of the time, Pallas kernels for 9%

profile of v5, /device:TPU:7, one launch (start us, length us, event | category | flops | bytes accessed | tf_op | source)
XLA Modules:
  0.0 270.0 jit_solution(3580488689705017022)
XLA Ops:
  1.7 15.4 %collective-permute-start = (bf16[48,256]{1,0:T(8,128)(2,1)S(1)}, bf16[48,256]{1,0:T(8,128)(2,1)S(1)}, u32[]{:S(2)}, u32[]{:S(2)}) collective-permute-start(bf16[48,256]{1,0:T(8,128)(2,1)S(1)} %multiply_convert_fusion.s_ref), channel_id=1, source_target_pairs={{0,32},{2,34},{4,36},{6,38},{8,40},{10,42},{12,44},{14,46},{16,48}... | collective-permute-start | bytes 73736 | tf_op jit(solution)/shard_map/ppermute | solution.py:248
  23.5 2.3 shard_map.176
  26.5 4.0 %collective-permute-start.1 = (bf16[96,256]{1,0:T(8,128)(2,1)S(1)}, bf16[96,256]{1,0:T(8,128)(2,1)S(1)}, u32[]{:S(2)}, u32[]{:S(2)}) collective-permute-start(bf16[96,256]{1,0:T(8,128)(2,1)S(1)} %pad_maximum_fusion.8), channel_id=1, source_target_pairs={{0,16},{2,18},{4,20},{6,22},{8,24},{10,26},{12,28},{14,30},{16,0},... | collective-permute-start | bytes 147464 | tf_op jit(solution)/shard_map/ppermute | solution.py:248
  30.6 2.3 shard_map.177
  32.9 2.4 collective-permute-done.1.s_ref
  35.3 3.3 %collective-permute-start.2 = (bf16[192,256]{1,0:T(8,128)(2,1)S(1)}, bf16[192,256]{1,0:T(8,128)(2,1)S(1)}, u32[]{:S(2)}, u32[]{:S(2)}) collective-permute-start(bf16[192,256]{1,0:T(8,128)(2,1)S(1)} %pad_maximum_fusion.7), channel_id=1, source_target_pairs={{0,8},{2,10},{4,12},{6,14},{8,0},{10,2},{12,4},{14,6},{16,24},{18,... | collective-permute-start | bytes 294920 | tf_op jit(solution)/shard_map/ppermute | solution.py:248
  38.6 2.3 shard_map.178
  40.9 1.7 collective-permute-done.2.s_ref
  42.6 3.0 %collective-permute-start.3 = (bf16[384,256]{1,0:T(8,128)(2,1)S(1)}, bf16[384,256]{1,0:T(8,128)(2,1)S(1)}, u32[]{:S(2)}, u32[]{:S(2)}) collective-permute-start(bf16[384,256]{1,0:T(8,128)(2,1)S(1)} %pad_maximum_fusion.5), channel_id=1, source_target_pairs={{0,256},{2,258},{4,260},{6,262},{8,264},{10,266},{12,268},{14,270}... | collective-permute-start | bytes 589832 | tf_op jit(solution)/shard_map/ppermute | solution.py:248
  45.7 2.6 shard_map.179
  48.3 2.2 collective-permute-done.3.s_ref
  50.6 4.8 %collective-permute-start.4 = (bf16[768,256]{1,0:T(8,128)(2,1)S(1)}, bf16[768,256]{1,0:T(8,128)(2,1)S(1)}, u32[]{:S(2)}, u32[]{:S(2)}) collective-permute-start(bf16[768,256]{1,0:T(8,128)(2,1)S(1)} %pad_maximum_fusion.3), channel_id=1, source_target_pairs={{0,128},{2,130},{4,132},{6,134},{8,136},{10,138},{12,140},{14,142}... | collective-permute-start | bytes 1179656 | tf_op jit(solution)/shard_map/ppermute | solution.py:248
  56.5 2.7 shard_map.180
  60.7 1.9 collective-permute-start.5
  81.8 1.8 convert_element_type.334
  83.7 1.8 convert_element_type.333
  86.4 1.8 fusion.175
  89.3 2.9 %shard_map.181 = (f32[384,128]{1,0:T(8,128)}, f32[384,128]{1,0:T(8,128)}) custom-call(bf16[384,256]{1,0:T(8,128)(2,1)} %bitcast.444, bf16[768,256]{1,0:T(8,128)(2,1)} %copy-done.9, bf16[768,128]{1,0:T(8,128)(2,1)} %maximum_maximum_fusion.3.w_ref, f32[384,128]{1,0:T(8,128)} %get-tuple-element.38.m_in, f32[384,128]{1,0:T(8,128)} %get-tuple-element.39.a_in), custom_call_target="tpu_custom_call" | custom-call | flops 301989888 | bytes 1572864 | tf_op jit(solution)/shard_map/pallas_call | solution.py:192
  93.8 3.3 %collective-permute-start.6 = (bf16[3072,256]{1,0:T(8,128)(2,1)S(1)}, bf16[3072,256]{1,0:T(8,128)(2,1)}, u32[]{:S(2)}, u32[]{:S(2)}) collective-permute-start(bf16[3072,256]{1,0:T(8,128)(2,1)S(1)} %pad_maximum_fusion.1), channel_id=1, source_target_pairs={{0,64},{2,66},{4,68},{6,70},{8,72},{10,74},{12,76},{14,78},{16,80}... | collective-permute-start | bytes 4718600 | tf_op jit(solution)/shard_map/ppermute | solution.py:248
  98.2 1.8 convolution_add_fusion.16
  102.7 4.0 %shard_map.182 = (f32[384,128]{1,0:T(8,128)}, f32[384,128]{1,0:T(8,128)}) custom-call(bf16[384,256]{1,0:T(8,128)(2,1)} %bitcast.445, bf16[1536,256]{1,0:T(8,128)(2,1)} %collective-permute-done.5.s_ref, bf16[1536,128]{1,0:T(8,128)(2,1)} %maximum_maximum_fusion.2.w_ref, f32[384,128]{1,0:T(8,128)} %get-tuple-element.41.m_in, f32[384,128]{1,0:T(8,128)} %get-tuple-element.42.a_in), custom_call_target="tpu_custom_call" | custom-call | flops 603979776 | bytes 2162688 | tf_op jit(solution)/shard_map/pallas_call | solution.py:192
  106.7 17.9 %collective-permute-done.6.s_ref = bf16[3072,256]{1,0:T(8,128)(2,1)} collective-permute-done((bf16[3072,256]{1,0:T(8,128)(2,1)S(1)}, bf16[3072,256]{1,0:T(8,128)(2,1)}, u32[]{:S(2)}, u32[]{:S(2)}) %collective-permute-start.6) | collective-permute-done | bytes 1572896 | tf_op jit(solution)/shard_map/ppermute | solution.py:248
  124.6 3.3 %pad_maximum_fusion = bf16[6144,256]{1,0:T(8,128)(2,1)} fusion(bf16[3072,256]{1,0:T(8,128)(2,1)} %collective-permute-done.6.s_ref, bf16[3072,256]{1,0:T(8,128)(2,1)S(1)} %pad_maximum_fusion.1), kind=kLoop, calls=%fused_computation.3 | loop fusion | flops 6291456 | bytes 6291456 | tf_op jit(solution)/shard_map/concatenate | solution.py:253
  127.9 10.4 %collective-permute-start.7 = (bf16[6144,256]{1,0:T(8,128)(2,1)}, bf16[6144,256]{1,0:T(8,128)(2,1)}, u32[]{:S(2)}, u32[]{:S(2)}) collective-permute-start(bf16[6144,256]{1,0:T(8,128)(2,1)} %pad_maximum_fusion), channel_id=1, source_target_pairs={{0,2},{2,0},{4,6},{6,4},{8,10},{10,8},{12,14},{14,12},{16,18},{18,... | collective-permute-start | bytes 9437192 | tf_op jit(solution)/shard_map/ppermute | solution.py:248
  141.0 1.9 fusion.1
  142.8 2.5 maximum_maximum_fusion.w_ref
  145.4 6.1 %shard_map.183 = (f32[384,128]{1,0:T(8,128)}, f32[384,128]{1,0:T(8,128)}) custom-call(bf16[384,256]{1,0:T(8,128)(2,1)} %bitcast.446, bf16[3072,256]{1,0:T(8,128)(2,1)} %collective-permute-done.6.s_ref, bf16[3072,128]{1,0:T(8,128)(2,1)} %maximum_maximum_fusion.1.w_ref, f32[384,128]{1,0:T(8,128)} %get-tuple-element.44.m_in, f32[384,128]{1,0:T(8,128)} %get-tuple-element.45.a_in), custom_call_target="tpu_custom_call" | custom-call | flops 1207959552 | bytes 3342336 | tf_op jit(solution)/shard_map/pallas_call | solution.py:192
  151.5 10.3 %shard_map.184 = (f32[384,128]{1,0:T(8,128)}, f32[384,128]{1,0:T(8,128)}) custom-call(bf16[384,256]{1,0:T(8,128)(2,1)} %bitcast.447, bf16[6144,256]{1,0:T(8,128)(2,1)} %collective-permute-done.7.s_ref, bf16[6144,128]{1,0:T(8,128)(2,1)} %maximum_maximum_fusion.w_ref, f32[384,128]{1,0:T(8,128)} %get-tuple-element.47.m_in, f32[384,128]{1,0:T(8,128)} %get-tuple-element.48.a_in), custom_call_target="tpu_custom_call" | custom-call | flops 2415919104 | bytes 5701632 | tf_op jit(solution)/shard_map/pallas_call | solution.py:192
  173.5 11.0 %collective-permute-start.11 = (bf16[1,384,384]{2,1,0:T(8,128)(2,1)S(1)}, bf16[1,384,384]{2,1,0:T(8,128)(2,1)S(1)}, u32[]{:S(2)}, u32[]{:S(2)}) collective-permute-start(bf16[1,384,384]{2,1,0:T(8,128)(2,1)S(1)} %pad_maximum_fusion.4), channel_id=1, source_target_pairs={{4,0},{6,2},{8,4},{10,6},{12,8},{14,10},{16,12},{18,14},{20,16},{2... | collective-permute-start | bytes 884744 | tf_op jit(solution)/shard_map/ppermute | solution.py:17
  184.5 2.2 collective-permute-start.10
  186.7 3.3 %collective-permute-start.9 = (bf16[1,384,384]{2,1,0:T(8,128)(2,1)S(1)}, bf16[1,384,384]{2,1,0:T(8,128)(2,1)S(1)}, u32[]{:S(2)}, u32[]{:S(2)}) collective-permute-start(bf16[1,384,384]{2,1,0:T(8,128)(2,1)S(1)} %pad_maximum_fusion.4), channel_id=1, source_target_pairs={{0,2},{2,4},{4,6},{6,8},{8,10},{10,12},{12,14},{14,16},{16,18},{18... | collective-permute-start | bytes 884744 | tf_op jit(solution)/shard_map/ppermute | solution.py:17
  190.1 1.9 collective-permute-start.8
  195.1 12.6 %collective-permute-done.8 = bf16[1,384,384]{2,1,0:T(8,128)(2,1)S(1)} collective-permute-done((bf16[1,384,384]{2,1,0:T(8,128)(2,1)S(1)}, bf16[1,384,384]{2,1,0:T(8,128)(2,1)S(1)}, u32[]{:S(2)}, u32[]{:S(2)}) %collective-permute-start.8) | collective-permute-done | bytes 294944 | tf_op jit(solution)/shard_map/ppermute | solution.py:17
  208.9 1.9 collective-permute-start.15
  210.9 1.9 collective-permute-start.14
  212.8 3.6 %collective-permute-start.13 = (bf16[1,384,128]{2,1,0:T(8,128)(2,1)S(1)}, bf16[1,384,128]{2,1,0:T(8,128)(2,1)S(1)}, u32[]{:S(2)}, u32[]{:S(2)}) collective-permute-start(bf16[1,384,128]{2,1,0:T(8,128)(2,1)S(1)} %fusion.80), channel_id=1, source_target_pairs={{0,2},{2,4},{4,6},{6,8},{8,10},{10,12},{12,14},{14,16},{16,18},{18... | collective-permute-start | bytes 294920 | tf_op jit(solution)/shard_map/ppermute | solution.py:17
  216.4 3.4 %collective-permute-start.12 = (bf16[1,384,128]{2,1,0:T(8,128)(2,1)S(1)}, bf16[1,384,128]{2,1,0:T(8,128)(2,1)S(1)}, u32[]{:S(2)}, u32[]{:S(2)}) collective-permute-start(bf16[1,384,128]{2,1,0:T(8,128)(2,1)S(1)} %fusion.80), channel_id=1, source_target_pairs={{0,4},{2,6},{4,8},{6,10},{8,12},{10,14},{12,16},{14,18},{16,20},{1... | collective-permute-start | bytes 294920 | tf_op jit(solution)/shard_map/ppermute | solution.py:17
  220.1 7.7 %collective-permute-done.12 = bf16[1,384,128]{2,1,0:T(8,128)(2,1)S(1)} collective-permute-done((bf16[1,384,128]{2,1,0:T(8,128)(2,1)S(1)}, bf16[1,384,128]{2,1,0:T(8,128)(2,1)S(1)}, u32[]{:S(2)}, u32[]{:S(2)}) %collective-permute-start.12) | collective-permute-done | bytes 98336 | tf_op jit(solution)/shard_map/ppermute | solution.py:17
  230.3 1.9 collective-permute-start.19
  232.3 1.9 collective-permute-start.18
  234.2 3.6 %collective-permute-start.17 = (bf16[1,384,128]{2,1,0:T(8,128)(2,1)S(1)}, bf16[1,384,128]{2,1,0:T(8,128)(2,1)S(1)}, u32[]{:S(2)}, u32[]{:S(2)}) collective-permute-start(bf16[1,384,128]{2,1,0:T(8,128)(2,1)S(1)} %get-tuple-element.72), channel_id=1, source_target_pairs={{0,2},{2,4},{4,6},{6,8},{8,10},{10,12},{12,14},{14,16},{16,18},{18... | collective-permute-start | bytes 294920 | tf_op jit(solution)/shard_map/ppermute | solution.py:17
  237.8 3.4 %collective-permute-start.16 = (bf16[1,384,128]{2,1,0:T(8,128)(2,1)S(1)}, bf16[1,384,128]{2,1,0:T(8,128)(2,1)S(1)}, u32[]{:S(2)}, u32[]{:S(2)}) collective-permute-start(bf16[1,384,128]{2,1,0:T(8,128)(2,1)S(1)} %get-tuple-element.72), channel_id=1, source_target_pairs={{0,4},{2,6},{4,8},{6,10},{8,12},{10,14},{12,16},{14,18},{16,20},{1... | collective-permute-start | bytes 294920 | tf_op jit(solution)/shard_map/ppermute | solution.py:17
  241.6 7.6 %collective-permute-done.16 = bf16[1,384,128]{2,1,0:T(8,128)(2,1)S(1)} collective-permute-done((bf16[1,384,128]{2,1,0:T(8,128)(2,1)S(1)}, bf16[1,384,128]{2,1,0:T(8,128)(2,1)S(1)}, u32[]{:S(2)}, u32[]{:S(2)}) %collective-permute-start.16) | collective-permute-done | bytes 98336 | tf_op jit(solution)/shard_map/ppermute | solution.py:17
  249.9 1.9 collective-permute-start.23
  251.8 1.9 collective-permute-start.22
  253.8 3.6 %collective-permute-start.21 = (bf16[1,384,128]{2,1,0:T(8,128)(2,1)S(1)}, bf16[1,384,128]{2,1,0:T(8,128)(2,1)S(1)}, u32[]{:S(2)}, u32[]{:S(2)}) collective-permute-start(bf16[1,384,128]{2,1,0:T(8,128)(2,1)S(1)} %fusion.78), channel_id=1, source_target_pairs={{0,2},{2,4},{4,6},{6,8},{8,10},{10,12},{12,14},{14,16},{16,18},{18... | collective-permute-start | bytes 294920 | tf_op jit(solution)/shard_map/ppermute | solution.py:17
  257.4 3.4 %collective-permute-start.20 = (bf16[1,384,128]{2,1,0:T(8,128)(2,1)S(1)}, bf16[1,384,128]{2,1,0:T(8,128)(2,1)S(1)}, u32[]{:S(2)}, u32[]{:S(2)}) collective-permute-start(bf16[1,384,128]{2,1,0:T(8,128)(2,1)S(1)} %fusion.78), channel_id=1, source_target_pairs={{0,4},{2,6},{4,8},{6,10},{8,12},{10,14},{12,16},{14,18},{16,20},{1... | collective-permute-start | bytes 294920 | tf_op jit(solution)/shard_map/ppermute | solution.py:17
  261.1 7.7 %collective-permute-done.20 = bf16[1,384,128]{2,1,0:T(8,128)(2,1)S(1)} collective-permute-done((bf16[1,384,128]{2,1,0:T(8,128)(2,1)S(1)}, bf16[1,384,128]{2,1,0:T(8,128)(2,1)S(1)}, u32[]{:S(2)}, u32[]{:S(2)}) %collective-permute-start.20) | collective-permute-done | bytes 98336 | tf_op jit(solution)/shard_map/ppermute | solution.py:17
  (186 shorter events, 44.1 us)
Async XLA Ops:
  0.6 29.9 %copy-start.23 = (s32[64]{0:T(128)S(1)}, s32[64]{0:T(128)}, u32[]{:S(2)}) copy-start(s32[64]{0:T(128)} %constant.282.clone) | copy-start | bytes 772
  0.6 37.9 %copy-start.22 = (s32[32]{0:T(128)S(1)}, s32[32]{0:T(128)}, u32[]{:S(2)}) copy-start(s32[32]{0:T(128)} %constant.281.clone) | copy-start | bytes 388
  1.7 21.7 %copy-start.15 = (bf16[48,256]{1,0:T(8,128)(2,1)}, bf16[48,256]{1,0:T(8,128)(2,1)S(1)}, u32[]{:S(2)}) copy-start(bf16[48,256]{1,0:T(8,128)(2,1)S(1)} %multiply_convert_fusion.s_ref) | copy-start | bytes 73732
  1.7 24.0 %collective-permute-start = (bf16[48,256]{1,0:T(8,128)(2,1)S(1)}, bf16[48,256]{1,0:T(8,128)(2,1)S(1)}, u32[]{:S(2)}, u32[]{:S(2)}) collective-permute-start(bf16[48,256]{1,0:T(8,128)(2,1)S(1)} %multiply_convert_fusion.s_ref), channel_id=1, source_target_pairs={{0,32},{2,34},{4,36},{6,38},{8,40},{10,42},{12,44},{14,46},{16,48}... | collective-permute-start | bytes 73736 | tf_op jit(solution)/shard_map/ppermute | solution.py:248
  22.1 23.6 %copy-start.21 = (s32[16]{0:T(128)S(1)}, s32[16]{0:T(128)}, u32[]{:S(2)}) copy-start(s32[16]{0:T(128)} %constant.280.clone) | copy-start | bytes 196
  25.8 4.8 %copy-start.17 = (bf16[48,256]{1,0:T(8,128)(2,1)}, bf16[48,256]{1,0:T(8,128)(2,1)S(1)}, u32[]{:S(2)}) copy-start(bf16[48,256]{1,0:T(8,128)(2,1)S(1)} %collective-permute-done.s_ref) | copy-start | bytes 73732
  26.5 8.7 %collective-permute-start.1 = (bf16[96,256]{1,0:T(8,128)(2,1)S(1)}, bf16[96,256]{1,0:T(8,128)(2,1)S(1)}, u32[]{:S(2)}, u32[]{:S(2)}) collective-permute-start(bf16[96,256]{1,0:T(8,128)(2,1)S(1)} %pad_maximum_fusion.8), channel_id=1, source_target_pairs={{0,16},{2,18},{4,20},{6,22},{8,24},{10,26},{12,28},{14,30},{16,0},... | collective-permute-start | bytes 147464 | tf_op jit(solution)/shard_map/ppermute | solution.py:248
  32.9 22.5 %copy-start.20 = (s32[8]{0:T(128)S(1)}, s32[8]{0:T(128)}, u32[]{:S(2)}) copy-start(s32[8]{0:T(128)} %constant.279.clone) | copy-start | bytes 100
  35.3 3.3 %copy-start.16 = (bf16[96,256]{1,0:T(8,128)(2,1)}, bf16[96,256]{1,0:T(8,128)(2,1)S(1)}, u32[]{:S(2)}) copy-start(bf16[96,256]{1,0:T(8,128)(2,1)S(1)} %collective-permute-done.1.s_ref) | copy-start | bytes 147460
  35.3 7.3 %collective-permute-start.2 = (bf16[192,256]{1,0:T(8,128)(2,1)S(1)}, bf16[192,256]{1,0:T(8,128)(2,1)S(1)}, u32[]{:S(2)}, u32[]{:S(2)}) collective-permute-start(bf16[192,256]{1,0:T(8,128)(2,1)S(1)} %pad_maximum_fusion.7), channel_id=1, source_target_pairs={{0,8},{2,10},{4,12},{6,14},{8,0},{10,2},{12,4},{14,6},{16,24},{18,... | collective-permute-start | bytes 294920 | tf_op jit(solution)/shard_map/ppermute | solution.py:248
  42.6 3.1 %copy-start.14 = (bf16[192,256]{1,0:T(8,128)(2,1)}, bf16[192,256]{1,0:T(8,128)(2,1)S(1)}, u32[]{:S(2)}) copy-start(bf16[192,256]{1,0:T(8,128)(2,1)S(1)} %collective-permute-done.2.s_ref) | copy-start | bytes 294916
  42.6 7.9 %collective-permute-start.3 = (bf16[384,256]{1,0:T(8,128)(2,1)S(1)}, bf16[384,256]{1,0:T(8,128)(2,1)S(1)}, u32[]{:S(2)}, u32[]{:S(2)}) collective-permute-start(bf16[384,256]{1,0:T(8,128)(2,1)S(1)} %pad_maximum_fusion.5), channel_id=1, source_target_pairs={{0,256},{2,258},{4,260},{6,262},{8,264},{10,266},{12,268},{14,270}... | collective-permute-start | bytes 589832 | tf_op jit(solution)/shard_map/ppermute | solution.py:248
  50.5 6.0 %copy-start.13 = (bf16[384,256]{1,0:T(8,128)(2,1)}, bf16[384,256]{1,0:T(8,128)(2,1)S(1)}, u32[]{:S(2)}) copy-start(bf16[384,256]{1,0:T(8,128)(2,1)S(1)} %collective-permute-done.3.s_ref) | copy-start | bytes 589828
  50.6 10.0 %collective-permute-start.4 = (bf16[768,256]{1,0:T(8,128)(2,1)S(1)}, bf16[768,256]{1,0:T(8,128)(2,1)S(1)}, u32[]{:S(2)}, u32[]{:S(2)}) collective-permute-start(bf16[768,256]{1,0:T(8,128)(2,1)S(1)} %pad_maximum_fusion.3), channel_id=1, source_target_pairs={{0,128},{2,130},{4,132},{6,134},{8,136},{10,138},{12,140},{14,142}... | collective-permute-start | bytes 1179656 | tf_op jit(solution)/shard_map/ppermute | solution.py:248
  55.7 7.1 %copy-start.18 = (s32[256]{0:T(256)S(1)}, s32[256]{0:T(256)}, u32[]{:S(2)}) copy-start(s32[256]{0:T(256)} %constant.284.clone) | copy-start | bytes 3076
  60.6 23.0 %copy-start.9 = (bf16[768,256]{1,0:T(8,128)(2,1)}, bf16[768,256]{1,0:T(8,128)(2,1)S(1)}, u32[]{:S(2)}) copy-start(bf16[768,256]{1,0:T(8,128)(2,1)S(1)} %collective-permute-done.4.s_ref) | copy-start | bytes 1179652
  60.7 24.8 %copy-start.2 = (bf16[1536,256]{1,0:T(8,128)(2,1)}, bf16[1536,256]{1,0:T(8,128)(2,1)S(1)}, u32[]{:S(2)}) copy-start(bf16[1536,256]{1,0:T(8,128)(2,1)S(1)} %pad_maximum_fusion.2) | copy-start | bytes 2359300
  60.7 31.6 %collective-permute-start.5 = (bf16[1536,256]{1,0:T(8,128)(2,1)S(1)}, bf16[1536,256]{1,0:T(8,128)(2,1)}, u32[]{:S(2)}, u32[]{:S(2)}) collective-permute-start(bf16[1536,256]{1,0:T(8,128)(2,1)S(1)} %pad_maximum_fusion.2), channel_id=1, source_target_pairs={{0,4},{2,6},{4,0},{6,2},{8,12},{10,14},{12,8},{14,10},{16,20},{18,... | collective-permute-start | bytes 2359304 | tf_op jit(solution)/shard_map/ppermute | solution.py:248
  81.8 4.7 %copy-start.1 = (bf16[1,384,128]{2,1,0:T(8,128)(2,1)S(1)}, bf16[1,384,128]{2,1,0:T(8,128)(2,1)}, u32[]{:S(2)}) copy-start(bf16[1,384,128]{2,1,0:T(8,128)(2,1)} %param.20) | copy-start | bytes 294916
  92.3 4.9 %copy-start.19 = (f32[3,128]{1,0:T(4,128)S(1)}, f32[3,128]{1,0:T(4,128)}, u32[]{:S(2)}) copy-start(f32[3,128]{1,0:T(4,128)} %param.22) | copy-start | bytes 4612
  92.3 4.9 %copy-start.10 = (f32[384,256]{1,0:T(8,128)S(1)}, f32[384,256]{1,0:T(8,128)}, u32[]{:S(2)}) copy-start(f32[384,256]{1,0:T(8,128)} %fusion.175) | copy-start | bytes 1179652
  93.8 7.8 %copy-start.7 = (bf16[1536,1]{1,0:T(8,128)(2,1)S(1)}, bf16[1536,1]{1,0:T(8,128)(2,1)}, u32[]{:S(2)}) copy-start(bf16[1536,1]{1,0:T(8,128)(2,1)} %convert_element_type.332) | copy-start | bytes 9220
  93.8 7.8 %copy-start.8 = (bf16[1536,1]{1,0:T(8,128)(2,1)S(1)}, bf16[1536,1]{1,0:T(8,128)(2,1)}, u32[]{:S(2)}) copy-start(bf16[1536,1]{1,0:T(8,128)(2,1)} %fusion.67) | copy-start | bytes 9220
  93.8 30.8 %collective-permute-start.6 = (bf16[3072,256]{1,0:T(8,128)(2,1)S(1)}, bf16[3072,256]{1,0:T(8,128)(2,1)}, u32[]{:S(2)}, u32[]{:S(2)}) collective-permute-start(bf16[3072,256]{1,0:T(8,128)(2,1)S(1)} %pad_maximum_fusion.1), channel_id=1, source_target_pairs={{0,64},{2,66},{4,68},{6,70},{8,72},{10,74},{12,76},{14,78},{16,80}... | collective-permute-start | bytes 4718600 | tf_op jit(solution)/shard_map/ppermute | solution.py:248
  106.7 31.6 %copy-start.11 = (f32[384,256]{1,0:T(8,128)S(1)}, f32[384,256]{1,0:T(8,128)}, u32[]{:S(2)}) copy-start(f32[384,256]{1,0:T(8,128)} %convolution_add_fusion.16) | copy-start | bytes 1179652
  124.6 14.8 %copy-start.4 = (bf16[3072,1]{1,0:T(8,128)(2,1)S(1)}, bf16[3072,1]{1,0:T(8,128)(2,1)}, u32[]{:S(2)}) copy-start(bf16[3072,1]{1,0:T(8,128)(2,1)} %fusion.6) | copy-start | bytes 18436
  127.9 11.5 %copy-start.3 = (bf16[3072,1]{1,0:T(8,128)(2,1)S(1)}, bf16[3072,1]{1,0:T(8,128)(2,1)}, u32[]{:S(2)}) copy-start(bf16[3072,1]{1,0:T(8,128)(2,1)} %convert_element_type.334) | copy-start | bytes 18436
  127.9 23.6 %collective-permute-start.7 = (bf16[6144,256]{1,0:T(8,128)(2,1)}, bf16[6144,256]{1,0:T(8,128)(2,1)}, u32[]{:S(2)}, u32[]{:S(2)}) collective-permute-start(bf16[6144,256]{1,0:T(8,128)(2,1)} %pad_maximum_fusion), channel_id=1, source_target_pairs={{0,2},{2,0},{4,6},{6,4},{8,10},{10,8},{12,14},{14,12},{16,18},{18,... | collective-permute-start | bytes 9437192 | tf_op jit(solution)/shard_map/ppermute | solution.py:248
  151.5 18.8 %copy-start = (bf16[1,384,256]{2,1,0:T(8,128)(2,1)S(1)}, bf16[1,384,256]{2,1,0:T(8,128)(2,1)}, u32[]{:S(2)}) copy-start(bf16[1,384,256]{2,1,0:T(8,128)(2,1)} %param.17) | copy-start | bytes 589828
  161.9 9.1 %copy-start.12 = (bf16[1,384,128]{2,1,0:T(8,128)(2,1)S(1)}, bf16[1,384,128]{2,1,0:T(8,128)(2,1)}, u32[]{:S(2)}) copy-start(bf16[1,384,128]{2,1,0:T(8,128)(2,1)} %param.19) | copy-start | bytes 294916
  161.9 9.1 %copy-start.6 = (bf16[5,384,384]{2,1,0:T(8,128)(2,1)S(1)}, bf16[5,384,384]{2,1,0:T(8,128)(2,1)}, u32[]{:S(2)}) copy-start(bf16[5,384,384]{2,1,0:T(8,128)(2,1)} %param.23) | copy-start | bytes 4423684
  172.9 19.1 %copy-start.5 = (bf16[5,384,384]{2,1,0:T(8,128)(2,1)S(1)}, bf16[5,384,384]{2,1,0:T(8,128)(2,1)}, u32[]{:S(2)}) copy-start(bf16[5,384,384]{2,1,0:T(8,128)(2,1)} %param.24) | copy-start | bytes 4423684
  173.5 21.3 %collective-permute-start.11 = (bf16[1,384,384]{2,1,0:T(8,128)(2,1)S(1)}, bf16[1,384,384]{2,1,0:T(8,128)(2,1)S(1)}, u32[]{:S(2)}, u32[]{:S(2)}) collective-permute-start(bf16[1,384,384]{2,1,0:T(8,128)(2,1)S(1)} %pad_maximum_fusion.4), channel_id=1, source_target_pairs={{4,0},{6,2},{8,4},{10,6},{12,8},{14,10},{16,12},{18,14},{20,16},{2... | collective-permute-start | bytes 884744 | tf_op jit(solution)/shard_map/ppermute | solution.py:17
  184.5 23.8 %collective-permute-start.10 = (bf16[1,384,384]{2,1,0:T(8,128)(2,1)S(1)}, bf16[1,384,384]{2,1,0:T(8,128)(2,1)S(1)}, u32[]{:S(2)}, u32[]{:S(2)}) collective-permute-start(bf16[1,384,384]{2,1,0:T(8,128)(2,1)S(1)} %pad_maximum_fusion.4), channel_id=1, source_target_pairs={{2,0},{4,2},{6,4},{8,6},{10,8},{12,10},{14,12},{16,14},{18,16},{20... | collective-permute-start | bytes 884744 | tf_op jit(solution)/shard_map/ppermute | solution.py:17
  186.7 7.7 %collective-permute-start.9 = (bf16[1,384,384]{2,1,0:T(8,128)(2,1)S(1)}, bf16[1,384,384]{2,1,0:T(8,128)(2,1)S(1)}, u32[]{:S(2)}, u32[]{:S(2)}) collective-permute-start(bf16[1,384,384]{2,1,0:T(8,128)(2,1)S(1)} %pad_maximum_fusion.4), channel_id=1, source_target_pairs={{0,2},{2,4},{4,6},{6,8},{8,10},{10,12},{12,14},{14,16},{16,18},{18... | collective-permute-start | bytes 884744 | tf_op jit(solution)/shard_map/ppermute | solution.py:17
  190.1 17.6 %collective-permute-start.8 = (bf16[1,384,384]{2,1,0:T(8,128)(2,1)S(1)}, bf16[1,384,384]{2,1,0:T(8,128)(2,1)S(1)}, u32[]{:S(2)}, u32[]{:S(2)}) collective-permute-start(bf16[1,384,384]{2,1,0:T(8,128)(2,1)S(1)} %pad_maximum_fusion.4), channel_id=1, source_target_pairs={{0,4},{2,6},{4,8},{6,10},{8,12},{10,14},{12,16},{14,18},{16,20},{1... | collective-permute-start | bytes 884744 | tf_op jit(solution)/shard_map/ppermute | solution.py:17
  208.9 19.1 %collective-permute-start.15 = (bf16[1,384,128]{2,1,0:T(8,128)(2,1)S(1)}, bf16[1,384,128]{2,1,0:T(8,128)(2,1)S(1)}, u32[]{:S(2)}, u32[]{:S(2)}) collective-permute-start(bf16[1,384,128]{2,1,0:T(8,128)(2,1)S(1)} %fusion.80), channel_id=1, source_target_pairs={{4,0},{6,2},{8,4},{10,6},{12,8},{14,10},{16,12},{18,14},{20,16},{2... | collective-permute-start | bytes 294920 | tf_op jit(solution)/shard_map/ppermute | solution.py:17
  210.9 17.3 %collective-permute-start.14 = (bf16[1,384,128]{2,1,0:T(8,128)(2,1)S(1)}, bf16[1,384,128]{2,1,0:T(8,128)(2,1)S(1)}, u32[]{:S(2)}, u32[]{:S(2)}) collective-permute-start(bf16[1,384,128]{2,1,0:T(8,128)(2,1)S(1)} %fusion.80), channel_id=1, source_target_pairs={{2,0},{4,2},{6,4},{8,6},{10,8},{12,10},{14,12},{16,14},{18,16},{20... | collective-permute-start | bytes 294920 | tf_op jit(solution)/shard_map/ppermute | solution.py:17
  212.8 7.2 %collective-permute-start.13 = (bf16[1,384,128]{2,1,0:T(8,128)(2,1)S(1)}, bf16[1,384,128]{2,1,0:T(8,128)(2,1)S(1)}, u32[]{:S(2)}, u32[]{:S(2)}) collective-permute-start(bf16[1,384,128]{2,1,0:T(8,128)(2,1)S(1)} %fusion.80), channel_id=1, source_target_pairs={{0,2},{2,4},{4,6},{6,8},{8,10},{10,12},{12,14},{14,16},{16,18},{18... | collective-permute-start | bytes 294920 | tf_op jit(solution)/shard_map/ppermute | solution.py:17
  216.4 11.4 %collective-permute-start.12 = (bf16[1,384,128]{2,1,0:T(8,128)(2,1)S(1)}, bf16[1,384,128]{2,1,0:T(8,128)(2,1)S(1)}, u32[]{:S(2)}, u32[]{:S(2)}) collective-permute-start(bf16[1,384,128]{2,1,0:T(8,128)(2,1)S(1)} %fusion.80), channel_id=1, source_target_pairs={{0,4},{2,6},{4,8},{6,10},{8,12},{10,14},{12,16},{14,18},{16,20},{1... | collective-permute-start | bytes 294920 | tf_op jit(solution)/shard_map/ppermute | solution.py:17
  230.3 19.1 %collective-permute-start.19 = (bf16[1,384,128]{2,1,0:T(8,128)(2,1)S(1)}, bf16[1,384,128]{2,1,0:T(8,128)(2,1)S(1)}, u32[]{:S(2)}, u32[]{:S(2)}) collective-permute-start(bf16[1,384,128]{2,1,0:T(8,128)(2,1)S(1)} %get-tuple-element.72), channel_id=1, source_target_pairs={{4,0},{6,2},{8,4},{10,6},{12,8},{14,10},{16,12},{18,14},{20,16},{2... | collective-permute-start | bytes 294920 | tf_op jit(solution)/shard_map/ppermute | solution.py:17
  232.3 17.4 %collective-permute-start.18 = (bf16[1,384,128]{2,1,0:T(8,128)(2,1)S(1)}, bf16[1,384,128]{2,1,0:T(8,128)(2,1)S(1)}, u32[]{:S(2)}, u32[]{:S(2)}) collective-permute-start(bf16[1,384,128]{2,1,0:T(8,128)(2,1)S(1)} %get-tuple-element.72), channel_id=1, source_target_pairs={{2,0},{4,2},{6,4},{8,6},{10,8},{12,10},{14,12},{16,14},{18,16},{20... | collective-permute-start | bytes 294920 | tf_op jit(solution)/shard_map/ppermute | solution.py:17
  234.2 7.2 %collective-permute-start.17 = (bf16[1,384,128]{2,1,0:T(8,128)(2,1)S(1)}, bf16[1,384,128]{2,1,0:T(8,128)(2,1)S(1)}, u32[]{:S(2)}, u32[]{:S(2)}) collective-permute-start(bf16[1,384,128]{2,1,0:T(8,128)(2,1)S(1)} %get-tuple-element.72), channel_id=1, source_target_pairs={{0,2},{2,4},{4,6},{6,8},{8,10},{10,12},{12,14},{14,16},{16,18},{18... | collective-permute-start | bytes 294920 | tf_op jit(solution)/shard_map/ppermute | solution.py:17
  237.8 11.4 %collective-permute-start.16 = (bf16[1,384,128]{2,1,0:T(8,128)(2,1)S(1)}, bf16[1,384,128]{2,1,0:T(8,128)(2,1)S(1)}, u32[]{:S(2)}, u32[]{:S(2)}) collective-permute-start(bf16[1,384,128]{2,1,0:T(8,128)(2,1)S(1)} %get-tuple-element.72), channel_id=1, source_target_pairs={{0,4},{2,6},{4,8},{6,10},{8,12},{10,14},{12,16},{14,18},{16,20},{1... | collective-permute-start | bytes 294920 | tf_op jit(solution)/shard_map/ppermute | solution.py:17
  249.9 19.0 %collective-permute-start.23 = (bf16[1,384,128]{2,1,0:T(8,128)(2,1)S(1)}, bf16[1,384,128]{2,1,0:T(8,128)(2,1)S(1)}, u32[]{:S(2)}, u32[]{:S(2)}) collective-permute-start(bf16[1,384,128]{2,1,0:T(8,128)(2,1)S(1)} %fusion.78), channel_id=1, source_target_pairs={{4,0},{6,2},{8,4},{10,6},{12,8},{14,10},{16,12},{18,14},{20,16},{2... | collective-permute-start | bytes 294920 | tf_op jit(solution)/shard_map/ppermute | solution.py:17
  251.8 17.3 %collective-permute-start.22 = (bf16[1,384,128]{2,1,0:T(8,128)(2,1)S(1)}, bf16[1,384,128]{2,1,0:T(8,128)(2,1)S(1)}, u32[]{:S(2)}, u32[]{:S(2)}) collective-permute-start(bf16[1,384,128]{2,1,0:T(8,128)(2,1)S(1)} %fusion.78), channel_id=1, source_target_pairs={{2,0},{4,2},{6,4},{8,6},{10,8},{12,10},{14,12},{16,14},{18,16},{20... | collective-permute-start | bytes 294920 | tf_op jit(solution)/shard_map/ppermute | solution.py:17
  253.8 7.2 %collective-permute-start.21 = (bf16[1,384,128]{2,1,0:T(8,128)(2,1)S(1)}, bf16[1,384,128]{2,1,0:T(8,128)(2,1)S(1)}, u32[]{:S(2)}, u32[]{:S(2)}) collective-permute-start(bf16[1,384,128]{2,1,0:T(8,128)(2,1)S(1)} %fusion.78), channel_id=1, source_target_pairs={{0,2},{2,4},{4,6},{6,8},{8,10},{10,12},{12,14},{14,16},{16,18},{18... | collective-permute-start | bytes 294920 | tf_op jit(solution)/shard_map/ppermute | solution.py:17
  257.4 11.4 %collective-permute-start.20 = (bf16[1,384,128]{2,1,0:T(8,128)(2,1)S(1)}, bf16[1,384,128]{2,1,0:T(8,128)(2,1)S(1)}, u32[]{:S(2)}, u32[]{:S(2)}) collective-permute-start(bf16[1,384,128]{2,1,0:T(8,128)(2,1)S(1)} %fusion.78), channel_id=1, source_target_pairs={{0,4},{2,6},{4,8},{6,10},{8,12},{10,14},{12,16},{14,18},{16,20},{1... | collective-permute-start | bytes 294920 | tf_op jit(solution)/shard_map/ppermute | solution.py:17

commit v6 on v3

--- a/solution.py
+++ b/solution.py
@@ -220,11 +220,25 @@
     )(features, block, weights, running_max, acc)
 
 
-def deposit_table(bits):
-    table = np.zeros((1 << len(bits),), np.int32)
-    for q in range(table.shape[0]):
-        table[q] = sum(((q >> i) & 1) << b for i, b in enumerate(bits))
-    return table
+def gather_partner(device, step, where):
+    bit = GATHER_BITS[step]
+    if bit != 1:
+        return device ^ (1 << bit)
+    z = (device >> 1) & 15
+    shifted = ((((z + 15) % 16) ^ 1) + 1) % 16
+    partner_z = where((device & 1) == 0, z ^ 1, shifted)
+    return device - (z << 1) + (partner_z << 1)
+
+
+def gather_tables(bands):
+    devices = np.arange(bands, dtype=np.int64)
+    rows = devices[:, None]
+    for step in range(len(GATHER_BITS)):
+        rows = np.concatenate([rows, rows[gather_partner(devices, step, np.where)]], axis=1)
+    places = np.zeros_like(rows)
+    for device in range(bands):
+        places[device, rows[device]] = np.arange(rows.shape[1])
+    return rows.astype(np.int16), places.astype(np.int16)
 
 
 def per_device(frame1, frame2, context, hidden_init, offsets, w_motion, w_row, w_col):
@@ -240,7 +254,7 @@
     )
     pixel_count = band_rows * image_width
     features = frame1.reshape(pixel_count, channels)
-    deposit = deposit_table(GATHER_BITS)
+    row_table, place_table = gather_tables(bands)
     state = (
         jnp.full((pixel_count, 128), -jnp.inf, jnp.float32),
         jnp.zeros((pixel_count, 128), jnp.float32),
@@ -248,10 +262,12 @@
     held = strips.reshape(band_rows * grid_cols, channels)
     state = match_block(state, features, held, band[None], grid_cols)
     for step, bit in enumerate(GATHER_BITS):
-        flip = 1 << bit
-        pairs = [(i, i ^ flip) for i in range(bands)]
+        pairs = [(i, int(gather_partner(i, step, np.where))) for i in range(bands)]
         got = lax.ppermute(held, "band", pairs)
-        got_rows = (band ^ flip) ^ jnp.asarray(deposit[: 1 << step])
+        partner = gather_partner(band, step, jnp.where)
+        got_rows = lax.dynamic_index_in_dim(
+            jnp.asarray(row_table[:, : 1 << step]), partner, 0, keepdims=False
+        ).astype(jnp.int32)
         settled = state
         state = match_block(state, features, got, got_rows, grid_cols)
         if step + 1 < len(GATHER_BITS):
@@ -265,11 +281,11 @@
     flow_col = (
         (8.0 * (acc[:, 2] / denominator) + 3.5) / image_width
     ).reshape(band_rows, image_width) - pixel_col.astype(jnp.float32) / image_width
-    inverse = np.argsort(deposit).astype(np.int32)
+    places = lax.dynamic_index_in_dim(jnp.asarray(place_table), band, 0, keepdims=False)
     t_row = target_row.reshape(pixel_count)
     t_col = target_col.reshape(pixel_count)
     valid = t_row >= 0
-    place = jnp.asarray(inverse)[jnp.where(valid, t_row ^ band, 0)] * grid_cols + jnp.where(
+    place = places.astype(jnp.int32)[jnp.where(valid, t_row, 0)] * grid_cols + jnp.where(
         valid, t_col, 0
     )
     half = held.shape[0]

time: 263 us -> 253 us (0.962)
  waiting for transfers between devices: 64.3 us -> 50.8 us
  other arithmetic: 22.9 us -> 28.9 us
  starting transfers between devices: 101 us -> 98.2 us
    ppermute x8, waiting for transfers between devices: 28.7 us -> 15.2 us  [per_device(): got = lax.ppermute(held, 'band', pairs)]
    another operation x15, other arithmetic: 4.85 us -> 9.01 us
    ppermute x16, starting transfers between devices: 54.7 us -> 50.6 us  [passed_along(): return lax.ppermute(array, axis, pairs)]
  transfers between devices with their start and end apart: 24 -> 24, of which waited for: 11 -> 11; matrix products, arithmetic and copies ran while one was open for 15% -> 18% of each run, Pallas kernels for 10% -> 11%
where the time goes in v6:
time: 253 us; the launch traced here: 251 us
  starting transfers between devices  98.2 us (39%)
  waiting for transfers between devices  50.8 us (20%)
  Pallas kernels  37.2 us (15%)
  other arithmetic  28.9 us (11%)
  local copies, waits for them, and re-layouts  17.4 us (7%)
  matrix products  16.3 us (6%)
    ppermute x16, starting transfers between devices, passed_along(): return lax.ppermute(array, axis, pairs)  50.6 us
    ppermute x8, starting transfers between devices, per_device(): got = lax.ppermute(held, 'band', pairs)  47.6 us
    pallas_call x9, Pallas kernels, match_block(): pl.pallas_call(match_kernel, grid=(count // tile,), in_specs=[pl.BlockSpe...  37.2 us
    ppermute x16, waiting for transfers between devices, passed_along(): return lax.ppermute(array, axis, pairs)  35.6 us
    dot_general x50, matrix products, conv_valid(): jnp.dot(tap_slice.reshape(-1, tap_slice.shape[-1]), weight[kernel_tap], p...  16.3 us
    ppermute x8, waiting for transfers between devices, per_device(): got = lax.ppermute(held, 'band', pairs)  15.2 us
    another operation x15, other arithmetic  9.01 us
    concatenate x9, other arithmetic, match_block(): jnp.concatenate([jnp.ones((count, 1), jnp.float32), strip_row[:, None], s...  8.97 us
  transfers between devices with their start and end apart: 24, of which 11 were waited for; matrix products, arithmetic and copies ran while one was open for 18% of the time, Pallas kernels for 11%

profile of v6, /device:TPU:7, one launch (start us, length us, event | category | flops | bytes accessed | tf_op | source)
XLA Modules:
  0.0 251.2 jit_solution(10052094234931261413)
XLA Ops:
  1.7 15.4 %collective-permute-start = (bf16[48,256]{1,0:T(8,128)(2,1)S(1)}, bf16[48,256]{1,0:T(8,128)(2,1)S(1)}, u32[]{:S(2)}, u32[]{:S(2)}) collective-permute-start(bf16[48,256]{1,0:T(8,128)(2,1)S(1)} %multiply_convert_fusion.s_ref), channel_id=1, source_target_pairs={{0,32},{2,34},{4,36},{6,38},{8,40},{10,42},{12,44},{14,46},{16,48}... | collective-permute-start | bytes 73736 | tf_op jit(solution)/shard_map/ppermute | solution.py:266
  23.1 2.8 %gather_fusion = s32[384]{0:T(512)S(1)} fusion(s32[256]{0:T(256)S(1)} %bitcast.425, s32[1024]{0:T(1024)S(1)} %pad_clamp_fusion.2), kind=kCustom, calls=%fused_computation.2 | custom fusion | bytes 4608 | tf_op jit(solution)/shard_map/gather | solution.py:288
  30.2 2.5 %shard_map.176 = (f32[384,128]{1,0:T(8,128)}, f32[384,128]{1,0:T(8,128)}) custom-call(bf16[384,256]{1,0:T(8,128)(2,1)} %bitcast.426, bf16[48,256]{1,0:T(8,128)(2,1)} %copy-done.15, bf16[48,128]{1,0:T(8,128)(2,1)} %get-tuple-element.59.w_ref, f32[384,128]{1,0:T(8,128)} %broadcast_in_dim.122.m_in, f32[384,128]{1,0:T(8,128)} %broadcast_in_dim.123.a_in), custom_call_target="tpu_custom_call" | custom-call | flops 18874368 | bytes 1019904 | tf_op jit(solution)/shard_map/pallas_call | solution.py:197
  33.5 4.0 %collective-permute-start.1 = (bf16[96,256]{1,0:T(8,128)(2,1)S(1)}, bf16[96,256]{1,0:T(8,128)(2,1)S(1)}, u32[]{:S(2)}, u32[]{:S(2)}) collective-permute-start(bf16[96,256]{1,0:T(8,128)(2,1)S(1)} %pad_maximum_fusion.8), channel_id=1, source_target_pairs={{0,16},{2,18},{4,20},{6,22},{8,24},{10,26},{12,28},{14,30},{16,0},... | collective-permute-start | bytes 147464 | tf_op jit(solution)/shard_map/ppermute | solution.py:266
  38.2 2.5 %shard_map.177 = (f32[384,128]{1,0:T(8,128)}, f32[384,128]{1,0:T(8,128)}) custom-call(bf16[384,256]{1,0:T(8,128)(2,1)} %bitcast.427, bf16[48,256]{1,0:T(8,128)(2,1)} %copy-done.17, bf16[48,128]{1,0:T(8,128)(2,1)} %get-tuple-element.58.w_ref, f32[384,128]{1,0:T(8,128)} %get-tuple-element.27.m_in, f32[384,128]{1,0:T(8,128)} %get-tuple-element.28.a_in), custom_call_target="tpu_custom_call" | custom-call | flops 18874368 | bytes 1019904 | tf_op jit(solution)/shard_map/pallas_call | solution.py:197
  42.2 3.3 %collective-permute-start.2 = (bf16[192,256]{1,0:T(8,128)(2,1)S(1)}, bf16[192,256]{1,0:T(8,128)(2,1)S(1)}, u32[]{:S(2)}, u32[]{:S(2)}) collective-permute-start(bf16[192,256]{1,0:T(8,128)(2,1)S(1)} %pad_maximum_fusion.7), channel_id=1, source_target_pairs={{0,8},{2,10},{4,12},{6,14},{8,0},{10,2},{12,4},{14,6},{16,24},{18,... | collective-permute-start | bytes 294920 | tf_op jit(solution)/shard_map/ppermute | solution.py:266
  46.2 2.6 %shard_map.178 = (f32[384,128]{1,0:T(8,128)}, f32[384,128]{1,0:T(8,128)}) custom-call(bf16[384,256]{1,0:T(8,128)(2,1)} %bitcast.428, bf16[96,256]{1,0:T(8,128)(2,1)} %copy-done.16, bf16[96,128]{1,0:T(8,128)(2,1)} %maximum_maximum_fusion.6.w_ref, f32[384,128]{1,0:T(8,128)} %get-tuple-element.30.m_in, f32[384,128]{1,0:T(8,128)} %get-tuple-element.31.a_in), custom_call_target="tpu_custom_call" | custom-call | flops 37748736 | bytes 1056768 | tf_op jit(solution)/shard_map/pallas_call | solution.py:197
  49.6 3.0 %collective-permute-start.3 = (bf16[384,256]{1,0:T(8,128)(2,1)S(1)}, bf16[384,256]{1,0:T(8,128)(2,1)S(1)}, u32[]{:S(2)}, u32[]{:S(2)}) collective-permute-start(bf16[384,256]{1,0:T(8,128)(2,1)S(1)} %pad_maximum_fusion.5), channel_id=1, source_target_pairs={{0,256},{2,258},{4,260},{6,262},{8,264},{10,266},{12,268},{14,270}... | collective-permute-start | bytes 589832 | tf_op jit(solution)/shard_map/ppermute | solution.py:266
  52.6 2.6 %shard_map.179 = (f32[384,128]{1,0:T(8,128)}, f32[384,128]{1,0:T(8,128)}) custom-call(bf16[384,256]{1,0:T(8,128)(2,1)} %bitcast.429, bf16[192,256]{1,0:T(8,128)(2,1)} %copy-done.14, bf16[192,128]{1,0:T(8,128)(2,1)} %maximum_maximum_fusion.5.w_ref, f32[384,128]{1,0:T(8,128)} %get-tuple-element.33.m_in, f32[384,128]{1,0:T(8,128)} %get-tuple-element.34.a_in), custom_call_target="tpu_custom_call" | custom-call | flops 75497472 | bytes 1130496 | tf_op jit(solution)/shard_map/pallas_call | solution.py:197
  55.3 2.2 collective-permute-done.3.s_ref
  57.5 4.8 %collective-permute-start.4 = (bf16[768,256]{1,0:T(8,128)(2,1)S(1)}, bf16[768,256]{1,0:T(8,128)(2,1)S(1)}, u32[]{:S(2)}, u32[]{:S(2)}) collective-permute-start(bf16[768,256]{1,0:T(8,128)(2,1)S(1)} %pad_maximum_fusion.3), channel_id=1, source_target_pairs={{0,128},{2,130},{4,132},{6,134},{8,136},{10,138},{12,140},{14,142}... | collective-permute-start | bytes 1179656 | tf_op jit(solution)/shard_map/ppermute | solution.py:266
  64.2 2.7 %shard_map.180 = (f32[384,128]{1,0:T(8,128)}, f32[384,128]{1,0:T(8,128)}) custom-call(bf16[384,256]{1,0:T(8,128)(2,1)} %bitcast.430, bf16[384,256]{1,0:T(8,128)(2,1)} %copy-done.12, bf16[384,128]{1,0:T(8,128)(2,1)} %maximum_maximum_fusion.4.w_ref, f32[384,128]{1,0:T(8,128)} %get-tuple-element.36.m_in, f32[384,128]{1,0:T(8,128)} %get-tuple-element.37.a_in), custom_call_target="tpu_custom_call" | custom-call | flops 150994944 | bytes 1277952 | tf_op jit(solution)/shard_map/pallas_call | solution.py:197
  67.6 3.2 %collective-permute-start.5 = (bf16[1536,256]{1,0:T(8,128)(2,1)S(1)}, bf16[1536,256]{1,0:T(8,128)(2,1)}, u32[]{:S(2)}, u32[]{:S(2)}) collective-permute-start(bf16[1536,256]{1,0:T(8,128)(2,1)S(1)} %pad_maximum_fusion.2), channel_id=1, source_target_pairs={{0,64},{2,66},{4,68},{6,70},{8,72},{10,74},{12,76},{14,78},{16,80}... | collective-permute-start | bytes 2359304 | tf_op jit(solution)/shard_map/ppermute | solution.py:266
  74.2 2.9 %convert_element_type.418 = bf16[6144,1]{1,0:T(8,128)(2,1)} reshape(bf16[128,48]{1,0:T(8,128)(2,1)S(1)} %broadcast_in_dim.140) | data formatting | bytes 24576 | tf_op jit(solution)/shard_map/convert_element_type | solution.py:185
  80.1 3.0 %shard_map.181 = (f32[384,128]{1,0:T(8,128)}, f32[384,128]{1,0:T(8,128)}) custom-call(bf16[384,256]{1,0:T(8,128)(2,1)} %bitcast.431, bf16[768,256]{1,0:T(8,128)(2,1)} %copy-done.8, bf16[768,128]{1,0:T(8,128)(2,1)} %maximum_maximum_fusion.3.w_ref, f32[384,128]{1,0:T(8,128)} %get-tuple-element.39.m_in, f32[384,128]{1,0:T(8,128)} %get-tuple-element.40.a_in), custom_call_target="tpu_custom_call" | custom-call | flops 301989888 | bytes 1572864 | tf_op jit(solution)/shard_map/pallas_call | solution.py:197
  83.1 1.9 collective-permute-done.5.s_ref
  86.3 11.1 %collective-permute-start.6 = (bf16[3072,256]{1,0:T(8,128)(2,1)S(1)}, bf16[3072,256]{1,0:T(8,128)(2,1)}, u32[]{:S(2)}, u32[]{:S(2)}) collective-permute-start(bf16[3072,256]{1,0:T(8,128)(2,1)S(1)} %pad_maximum_fusion.1), channel_id=1, source_target_pairs={{0,4},{2,62},{4,0},{6,10},{8,12},{10,6},{12,8},{14,18},{16,20},{18... | collective-permute-start | bytes 4718600 | tf_op jit(solution)/shard_map/ppermute | solution.py:266
  103.0 4.1 %shard_map.182 = (f32[384,128]{1,0:T(8,128)}, f32[384,128]{1,0:T(8,128)}) custom-call(bf16[384,256]{1,0:T(8,128)(2,1)} %bitcast.432, bf16[1536,256]{1,0:T(8,128)(2,1)} %collective-permute-done.5.s_ref, bf16[1536,128]{1,0:T(8,128)(2,1)} %maximum_maximum_fusion.2.w_ref, f32[384,128]{1,0:T(8,128)} %get-tuple-element.42.m_in, f32[384,128]{1,0:T(8,128)} %get-tuple-element.43.a_in), custom_call_target="tpu_custom_call" | custom-call | flops 603979776 | bytes 2162688 | tf_op jit(solution)/shard_map/pallas_call | solution.py:197
  107.1 8.2 %collective-permute-done.6.s_ref = bf16[3072,256]{1,0:T(8,128)(2,1)} collective-permute-done((bf16[3072,256]{1,0:T(8,128)(2,1)S(1)}, bf16[3072,256]{1,0:T(8,128)(2,1)}, u32[]{:S(2)}, u32[]{:S(2)}) %collective-permute-start.6) | collective-permute-done | bytes 1572896 | tf_op jit(solution)/shard_map/ppermute | solution.py:266
  115.3 2.2 pad_maximum_fusion
  117.5 2.7 %collective-permute-start.7 = (bf16[6144,256]{1,0:T(8,128)(2,1)S(1)}, bf16[6144,256]{1,0:T(8,128)(2,1)}, u32[]{:S(2)}, u32[]{:S(2)}) collective-permute-start(bf16[6144,256]{1,0:T(8,128)(2,1)S(1)} %pad_maximum_fusion), channel_id=1, source_target_pairs={{0,2},{2,0},{4,6},{6,4},{8,10},{10,8},{12,14},{14,12},{16,18},{18,... | collective-permute-start | bytes 9437192 | tf_op jit(solution)/shard_map/ppermute | solution.py:266
  120.2 1.8 convolution_add_fusion.15
  123.6 1.9 fusion.1
  125.5 2.5 %maximum_maximum_fusion.w_ref = bf16[6144,128]{1,0:T(8,128)(2,1)} fusion(bf16[6144,1]{1,0:T(8,128)(2,1)S(1)} %fusion.1, bf16[6144,1]{1,0:T(8,128)(2,1)S(1)} %copy-done.1, bf16[128]{0:T(256)(128)(2,1)S(1)} %pad.76.clone, bf16[128]{0:T(256)(128)(2,1)S(1)} %pad.73.clone), kind=kLoop, calls=%fused_computation.15 | loop fusion | flops 6291456 | bytes 1597952 | tf_op jit(solution)/shard_map/concatenate | solution.py:187
  128.0 2.0 gather_fusion.1
  130.0 6.3 %shard_map.183 = (f32[384,128]{1,0:T(8,128)}, f32[384,128]{1,0:T(8,128)}) custom-call(bf16[384,256]{1,0:T(8,128)(2,1)} %bitcast.433, bf16[3072,256]{1,0:T(8,128)(2,1)} %collective-permute-done.6.s_ref, bf16[3072,128]{1,0:T(8,128)(2,1)} %maximum_maximum_fusion.1.w_ref, f32[384,128]{1,0:T(8,128)} %get-tuple-element.45.m_in, f32[384,128]{1,0:T(8,128)} %get-tuple-element.46.a_in), custom_call_target="tpu_custom_call" | custom-call | flops 1207959552 | bytes 3342336 | tf_op jit(solution)/shard_map/pallas_call | solution.py:197
  136.4 10.7 %shard_map.184 = (f32[384,128]{1,0:T(8,128)}, f32[384,128]{1,0:T(8,128)}) custom-call(bf16[384,256]{1,0:T(8,128)(2,1)} %bitcast.434, bf16[6144,256]{1,0:T(8,128)(2,1)} %collective-permute-done.7.s_ref, bf16[6144,128]{1,0:T(8,128)(2,1)} %maximum_maximum_fusion.w_ref, f32[384,128]{1,0:T(8,128)} %get-tuple-element.48.m_in, f32[384,128]{1,0:T(8,128)} %get-tuple-element.49.a_in), custom_call_target="tpu_custom_call" | custom-call | flops 2415919104 | bytes 5701632 | tf_op jit(solution)/shard_map/pallas_call | solution.py:197
  148.6 4.1 %gather_fusion.2 = bf16[384,256]{1,0:T(8,128)(2,1)S(1)} fusion(bf16[6144,256]{1,0:T(8,128)(2,1)} %collective-permute-done.7.s_ref, s32[1024]{0:T(1024)S(1)} %get-tuple-element.77), kind=kCustom, calls=%fused_computation.1.clone | custom fusion | bytes 394752 | tf_op jit(solution)/shard_map/jit(_take)/gather | solution.py:295
  156.4 10.3 %collective-permute-start.11 = (bf16[1,384,384]{2,1,0:T(8,128)(2,1)S(1)}, bf16[1,384,384]{2,1,0:T(8,128)(2,1)S(1)}, u32[]{:S(2)}, u32[]{:S(2)}) collective-permute-start(bf16[1,384,384]{2,1,0:T(8,128)(2,1)S(1)} %pad_maximum_fusion.4), channel_id=1, source_target_pairs={{4,0},{6,2},{8,4},{10,6},{12,8},{14,10},{16,12},{18,14},{20,16},{2... | collective-permute-start | bytes 884744 | tf_op jit(solution)/shard_map/ppermute | solution.py:17
  166.7 2.2 collective-permute-start.10
  168.9 3.4 %collective-permute-start.9 = (bf16[1,384,384]{2,1,0:T(8,128)(2,1)S(1)}, bf16[1,384,384]{2,1,0:T(8,128)(2,1)S(1)}, u32[]{:S(2)}, u32[]{:S(2)}) collective-permute-start(bf16[1,384,384]{2,1,0:T(8,128)(2,1)S(1)} %pad_maximum_fusion.4), channel_id=1, source_target_pairs={{0,2},{2,4},{4,6},{6,8},{8,10},{10,12},{12,14},{14,16},{16,18},{18... | collective-permute-start | bytes 884744 | tf_op jit(solution)/shard_map/ppermute | solution.py:17
  172.3 1.9 collective-permute-start.8
  177.3 11.1 %collective-permute-done.8 = bf16[1,384,384]{2,1,0:T(8,128)(2,1)S(1)} collective-permute-done((bf16[1,384,384]{2,1,0:T(8,128)(2,1)S(1)}, bf16[1,384,384]{2,1,0:T(8,128)(2,1)S(1)}, u32[]{:S(2)}, u32[]{:S(2)}) %collective-permute-start.8) | collective-permute-done | bytes 294944 | tf_op jit(solution)/shard_map/ppermute | solution.py:17
  189.7 1.9 collective-permute-start.15
  191.6 2.3 collective-permute-start.14
  193.9 3.5 %collective-permute-start.13 = (bf16[1,384,128]{2,1,0:T(8,128)(2,1)S(1)}, bf16[1,384,128]{2,1,0:T(8,128)(2,1)S(1)}, u32[]{:S(2)}, u32[]{:S(2)}) collective-permute-start(bf16[1,384,128]{2,1,0:T(8,128)(2,1)S(1)} %fusion.82), channel_id=1, source_target_pairs={{0,2},{2,4},{4,6},{6,8},{8,10},{10,12},{12,14},{14,16},{16,18},{18... | collective-permute-start | bytes 294920 | tf_op jit(solution)/shard_map/ppermute | solution.py:17
  197.5 3.3 %collective-permute-start.12 = (bf16[1,384,128]{2,1,0:T(8,128)(2,1)S(1)}, bf16[1,384,128]{2,1,0:T(8,128)(2,1)S(1)}, u32[]{:S(2)}, u32[]{:S(2)}) collective-permute-start(bf16[1,384,128]{2,1,0:T(8,128)(2,1)S(1)} %fusion.82), channel_id=1, source_target_pairs={{0,4},{2,6},{4,8},{6,10},{8,12},{10,14},{12,16},{14,18},{16,20},{1... | collective-permute-start | bytes 294920 | tf_op jit(solution)/shard_map/ppermute | solution.py:17
  201.1 7.8 %collective-permute-done.12 = bf16[1,384,128]{2,1,0:T(8,128)(2,1)S(1)} collective-permute-done((bf16[1,384,128]{2,1,0:T(8,128)(2,1)S(1)}, bf16[1,384,128]{2,1,0:T(8,128)(2,1)S(1)}, u32[]{:S(2)}, u32[]{:S(2)}) %collective-permute-start.12) | collective-permute-done | bytes 98336 | tf_op jit(solution)/shard_map/ppermute | solution.py:17
  211.5 1.9 collective-permute-start.19
  213.4 1.9 collective-permute-start.18
  215.4 3.6 %collective-permute-start.17 = (bf16[1,384,128]{2,1,0:T(8,128)(2,1)S(1)}, bf16[1,384,128]{2,1,0:T(8,128)(2,1)S(1)}, u32[]{:S(2)}, u32[]{:S(2)}) collective-permute-start(bf16[1,384,128]{2,1,0:T(8,128)(2,1)S(1)} %get-tuple-element.73), channel_id=1, source_target_pairs={{0,2},{2,4},{4,6},{6,8},{8,10},{10,12},{12,14},{14,16},{16,18},{18... | collective-permute-start | bytes 294920 | tf_op jit(solution)/shard_map/ppermute | solution.py:17
  219.0 3.4 %collective-permute-start.16 = (bf16[1,384,128]{2,1,0:T(8,128)(2,1)S(1)}, bf16[1,384,128]{2,1,0:T(8,128)(2,1)S(1)}, u32[]{:S(2)}, u32[]{:S(2)}) collective-permute-start(bf16[1,384,128]{2,1,0:T(8,128)(2,1)S(1)} %get-tuple-element.73), channel_id=1, source_target_pairs={{0,4},{2,6},{4,8},{6,10},{8,12},{10,14},{12,16},{14,18},{16,20},{1... | collective-permute-start | bytes 294920 | tf_op jit(solution)/shard_map/ppermute | solution.py:17
  222.7 7.6 %collective-permute-done.16 = bf16[1,384,128]{2,1,0:T(8,128)(2,1)S(1)} collective-permute-done((bf16[1,384,128]{2,1,0:T(8,128)(2,1)S(1)}, bf16[1,384,128]{2,1,0:T(8,128)(2,1)S(1)}, u32[]{:S(2)}, u32[]{:S(2)}) %collective-permute-start.16) | collective-permute-done | bytes 98336 | tf_op jit(solution)/shard_map/ppermute | solution.py:17
  231.1 1.9 collective-permute-start.23
  233.0 1.9 collective-permute-start.22
  234.9 3.6 %collective-permute-start.21 = (bf16[1,384,128]{2,1,0:T(8,128)(2,1)S(1)}, bf16[1,384,128]{2,1,0:T(8,128)(2,1)S(1)}, u32[]{:S(2)}, u32[]{:S(2)}) collective-permute-start(bf16[1,384,128]{2,1,0:T(8,128)(2,1)S(1)} %fusion.80), channel_id=1, source_target_pairs={{0,2},{2,4},{4,6},{6,8},{8,10},{10,12},{12,14},{14,16},{16,18},{18... | collective-permute-start | bytes 294920 | tf_op jit(solution)/shard_map/ppermute | solution.py:17
  238.6 3.4 %collective-permute-start.20 = (bf16[1,384,128]{2,1,0:T(8,128)(2,1)S(1)}, bf16[1,384,128]{2,1,0:T(8,128)(2,1)S(1)}, u32[]{:S(2)}, u32[]{:S(2)}) collective-permute-start(bf16[1,384,128]{2,1,0:T(8,128)(2,1)S(1)} %fusion.80), channel_id=1, source_target_pairs={{0,4},{2,6},{4,8},{6,10},{8,12},{10,14},{12,16},{14,18},{16,20},{1... | collective-permute-start | bytes 294920 | tf_op jit(solution)/shard_map/ppermute | solution.py:17
  242.3 7.7 %collective-permute-done.20 = bf16[1,384,128]{2,1,0:T(8,128)(2,1)S(1)} collective-permute-done((bf16[1,384,128]{2,1,0:T(8,128)(2,1)S(1)}, bf16[1,384,128]{2,1,0:T(8,128)(2,1)S(1)}, u32[]{:S(2)}, u32[]{:S(2)}) %collective-permute-start.20) | collective-permute-done | bytes 98336 | tf_op jit(solution)/shard_map/ppermute | solution.py:17
  (178 shorter events, 46.7 us)
Async XLA Ops:
  1.7 24.2 %copy-start.15 = (bf16[48,256]{1,0:T(8,128)(2,1)}, bf16[48,256]{1,0:T(8,128)(2,1)S(1)}, u32[]{:S(2)}) copy-start(bf16[48,256]{1,0:T(8,128)(2,1)S(1)} %multiply_convert_fusion.s_ref) | copy-start | bytes 73732
  1.7 31.0 %collective-permute-start = (bf16[48,256]{1,0:T(8,128)(2,1)S(1)}, bf16[48,256]{1,0:T(8,128)(2,1)S(1)}, u32[]{:S(2)}, u32[]{:S(2)}) collective-permute-start(bf16[48,256]{1,0:T(8,128)(2,1)S(1)} %multiply_convert_fusion.s_ref), channel_id=1, source_target_pairs={{0,32},{2,34},{4,36},{6,38},{8,40},{10,42},{12,44},{14,46},{16,48}... | collective-permute-start | bytes 73736 | tf_op jit(solution)/shard_map/ppermute | solution.py:266
  28.8 23.8 %copy-start.18 = (f32[3,128]{1,0:T(4,128)S(1)}, f32[3,128]{1,0:T(4,128)}, u32[]{:S(2)}) copy-start(f32[3,128]{1,0:T(4,128)} %param.24) | copy-start | bytes 4612
  32.7 5.5 %copy-start.17 = (bf16[48,256]{1,0:T(8,128)(2,1)}, bf16[48,256]{1,0:T(8,128)(2,1)S(1)}, u32[]{:S(2)}) copy-start(bf16[48,256]{1,0:T(8,128)(2,1)S(1)} %collective-permute-done.s_ref) | copy-start | bytes 73732
  33.5 8.7 %collective-permute-start.1 = (bf16[96,256]{1,0:T(8,128)(2,1)S(1)}, bf16[96,256]{1,0:T(8,128)(2,1)S(1)}, u32[]{:S(2)}, u32[]{:S(2)}) collective-permute-start(bf16[96,256]{1,0:T(8,128)(2,1)S(1)} %pad_maximum_fusion.8), channel_id=1, source_target_pairs={{0,16},{2,18},{4,20},{6,22},{8,24},{10,26},{12,28},{14,30},{16,0},... | collective-permute-start | bytes 147464 | tf_op jit(solution)/shard_map/ppermute | solution.py:266
  42.2 4.0 %copy-start.16 = (bf16[96,256]{1,0:T(8,128)(2,1)}, bf16[96,256]{1,0:T(8,128)(2,1)S(1)}, u32[]{:S(2)}) copy-start(bf16[96,256]{1,0:T(8,128)(2,1)S(1)} %collective-permute-done.1.s_ref) | copy-start | bytes 147460
  42.2 7.3 %collective-permute-start.2 = (bf16[192,256]{1,0:T(8,128)(2,1)S(1)}, bf16[192,256]{1,0:T(8,128)(2,1)S(1)}, u32[]{:S(2)}, u32[]{:S(2)}) collective-permute-start(bf16[192,256]{1,0:T(8,128)(2,1)S(1)} %pad_maximum_fusion.7), channel_id=1, source_target_pairs={{0,8},{2,10},{4,12},{6,14},{8,0},{10,2},{12,4},{14,6},{16,24},{18,... | collective-permute-start | bytes 294920 | tf_op jit(solution)/shard_map/ppermute | solution.py:266
  49.6 3.1 %copy-start.14 = (bf16[192,256]{1,0:T(8,128)(2,1)}, bf16[192,256]{1,0:T(8,128)(2,1)S(1)}, u32[]{:S(2)}) copy-start(bf16[192,256]{1,0:T(8,128)(2,1)S(1)} %collective-permute-done.2.s_ref) | copy-start | bytes 294916
  49.6 7.9 %collective-permute-start.3 = (bf16[384,256]{1,0:T(8,128)(2,1)S(1)}, bf16[384,256]{1,0:T(8,128)(2,1)S(1)}, u32[]{:S(2)}, u32[]{:S(2)}) collective-permute-start(bf16[384,256]{1,0:T(8,128)(2,1)S(1)} %pad_maximum_fusion.5), channel_id=1, source_target_pairs={{0,256},{2,258},{4,260},{6,262},{8,264},{10,266},{12,268},{14,270}... | collective-permute-start | bytes 589832 | tf_op jit(solution)/shard_map/ppermute | solution.py:266
  57.5 6.7 %copy-start.12 = (bf16[384,256]{1,0:T(8,128)(2,1)}, bf16[384,256]{1,0:T(8,128)(2,1)S(1)}, u32[]{:S(2)}) copy-start(bf16[384,256]{1,0:T(8,128)(2,1)S(1)} %collective-permute-done.3.s_ref) | copy-start | bytes 589828
  57.5 10.0 %collective-permute-start.4 = (bf16[768,256]{1,0:T(8,128)(2,1)S(1)}, bf16[768,256]{1,0:T(8,128)(2,1)S(1)}, u32[]{:S(2)}, u32[]{:S(2)}) collective-permute-start(bf16[768,256]{1,0:T(8,128)(2,1)S(1)} %pad_maximum_fusion.3), channel_id=1, source_target_pairs={{0,128},{2,130},{4,132},{6,134},{8,136},{10,138},{12,140},{14,142}... | collective-permute-start | bytes 1179656 | tf_op jit(solution)/shard_map/ppermute | solution.py:266
  67.6 6.6 %copy-start.8 = (bf16[768,256]{1,0:T(8,128)(2,1)}, bf16[768,256]{1,0:T(8,128)(2,1)S(1)}, u32[]{:S(2)}) copy-start(bf16[768,256]{1,0:T(8,128)(2,1)S(1)} %collective-permute-done.4.s_ref) | copy-start | bytes 1179652
  67.6 17.4 %collective-permute-start.5 = (bf16[1536,256]{1,0:T(8,128)(2,1)S(1)}, bf16[1536,256]{1,0:T(8,128)(2,1)}, u32[]{:S(2)}, u32[]{:S(2)}) collective-permute-start(bf16[1536,256]{1,0:T(8,128)(2,1)S(1)} %pad_maximum_fusion.2), channel_id=1, source_target_pairs={{0,64},{2,66},{4,68},{6,70},{8,72},{10,74},{12,76},{14,78},{16,80}... | collective-permute-start | bytes 2359304 | tf_op jit(solution)/shard_map/ppermute | solution.py:266
  72.4 5.6 %copy-start.3 = (bf16[1,384,128]{2,1,0:T(8,128)(2,1)S(1)}, bf16[1,384,128]{2,1,0:T(8,128)(2,1)}, u32[]{:S(2)}) copy-start(bf16[1,384,128]{2,1,0:T(8,128)(2,1)} %param.22) | copy-start | bytes 294916
  83.1 14.3 %copy-start.9 = (f32[384,256]{1,0:T(8,128)S(1)}, f32[384,256]{1,0:T(8,128)}, u32[]{:S(2)}) copy-start(f32[384,256]{1,0:T(8,128)} %fusion.178) | copy-start | bytes 1179652
  86.3 16.7 %copy-start.2 = (bf16[3072,256]{1,0:T(8,128)(2,1)}, bf16[3072,256]{1,0:T(8,128)(2,1)S(1)}, u32[]{:S(2)}) copy-start(bf16[3072,256]{1,0:T(8,128)(2,1)S(1)} %pad_maximum_fusion.1) | copy-start | bytes 4718596
  86.3 29.1 %collective-permute-start.6 = (bf16[3072,256]{1,0:T(8,128)(2,1)S(1)}, bf16[3072,256]{1,0:T(8,128)(2,1)}, u32[]{:S(2)}, u32[]{:S(2)}) collective-permute-start(bf16[3072,256]{1,0:T(8,128)(2,1)S(1)} %pad_maximum_fusion.1), channel_id=1, source_target_pairs={{0,4},{2,62},{4,0},{6,10},{8,12},{10,6},{12,8},{14,18},{16,20},{18... | collective-permute-start | bytes 4718600 | tf_op jit(solution)/shard_map/ppermute | solution.py:266
  107.1 13.1 %copy-start.10 = (f32[384,256]{1,0:T(8,128)S(1)}, f32[384,256]{1,0:T(8,128)}, u32[]{:S(2)}) copy-start(f32[384,256]{1,0:T(8,128)} %convolution_add_fusion.16) | copy-start | bytes 1179652
  115.3 6.7 %copy-start.5 = (bf16[3072,1]{1,0:T(8,128)(2,1)S(1)}, bf16[3072,1]{1,0:T(8,128)(2,1)}, u32[]{:S(2)}) copy-start(bf16[3072,1]{1,0:T(8,128)(2,1)} %fusion.6) | copy-start | bytes 18436
  117.5 4.6 %copy-start.4 = (bf16[3072,1]{1,0:T(8,128)(2,1)S(1)}, bf16[3072,1]{1,0:T(8,128)(2,1)}, u32[]{:S(2)}) copy-start(bf16[3072,1]{1,0:T(8,128)(2,1)} %convert_element_type.419) | copy-start | bytes 18436
  117.5 18.9 %collective-permute-start.7 = (bf16[6144,256]{1,0:T(8,128)(2,1)S(1)}, bf16[6144,256]{1,0:T(8,128)(2,1)}, u32[]{:S(2)}, u32[]{:S(2)}) collective-permute-start(bf16[6144,256]{1,0:T(8,128)(2,1)S(1)} %pad_maximum_fusion), channel_id=1, source_target_pairs={{0,2},{2,0},{4,6},{6,4},{8,10},{10,8},{12,14},{14,12},{16,18},{18,... | collective-permute-start | bytes 9437192 | tf_op jit(solution)/shard_map/ppermute | solution.py:266
  122.0 3.4 %copy-start.1 = (bf16[6144,1]{1,0:T(8,128)(2,1)S(1)}, bf16[6144,1]{1,0:T(8,128)(2,1)}, u32[]{:S(2)}) copy-start(bf16[6144,1]{1,0:T(8,128)(2,1)} %convert_element_type.418) | copy-start | bytes 36868
  147.1 5.6 %copy-start = (bf16[1,384,256]{2,1,0:T(8,128)(2,1)S(1)}, bf16[1,384,256]{2,1,0:T(8,128)(2,1)}, u32[]{:S(2)}) copy-start(bf16[1,384,256]{2,1,0:T(8,128)(2,1)} %param.19) | copy-start | bytes 589828
  147.1 6.2 %copy-start.11 = (bf16[1,384,128]{2,1,0:T(8,128)(2,1)S(1)}, bf16[1,384,128]{2,1,0:T(8,128)(2,1)}, u32[]{:S(2)}) copy-start(bf16[1,384,128]{2,1,0:T(8,128)(2,1)} %param.21) | copy-start | bytes 294916
  148.6 4.7 %copy-start.7 = (bf16[5,384,384]{2,1,0:T(8,128)(2,1)S(1)}, bf16[5,384,384]{2,1,0:T(8,128)(2,1)}, u32[]{:S(2)}) copy-start(bf16[5,384,384]{2,1,0:T(8,128)(2,1)} %param.25) | copy-start | bytes 4423684
  154.1 1.0 copy-start.13
  155.8 18.5 %copy-start.6 = (bf16[5,384,384]{2,1,0:T(8,128)(2,1)S(1)}, bf16[5,384,384]{2,1,0:T(8,128)(2,1)}, u32[]{:S(2)}) copy-start(bf16[5,384,384]{2,1,0:T(8,128)(2,1)} %param.26) | copy-start | bytes 4423684
  156.4 20.7 %collective-permute-start.11 = (bf16[1,384,384]{2,1,0:T(8,128)(2,1)S(1)}, bf16[1,384,384]{2,1,0:T(8,128)(2,1)S(1)}, u32[]{:S(2)}, u32[]{:S(2)}) collective-permute-start(bf16[1,384,384]{2,1,0:T(8,128)(2,1)S(1)} %pad_maximum_fusion.4), channel_id=1, source_target_pairs={{4,0},{6,2},{8,4},{10,6},{12,8},{14,10},{16,12},{18,14},{20,16},{2... | collective-permute-start | bytes 884744 | tf_op jit(solution)/shard_map/ppermute | solution.py:17
  166.7 22.4 %collective-permute-start.10 = (bf16[1,384,384]{2,1,0:T(8,128)(2,1)S(1)}, bf16[1,384,384]{2,1,0:T(8,128)(2,1)S(1)}, u32[]{:S(2)}, u32[]{:S(2)}) collective-permute-start(bf16[1,384,384]{2,1,0:T(8,128)(2,1)S(1)} %pad_maximum_fusion.4), channel_id=1, source_target_pairs={{2,0},{4,2},{6,4},{8,6},{10,8},{12,10},{14,12},{16,14},{18,16},{20... | collective-permute-start | bytes 884744 | tf_op jit(solution)/shard_map/ppermute | solution.py:17
  168.9 7.7 %collective-permute-start.9 = (bf16[1,384,384]{2,1,0:T(8,128)(2,1)S(1)}, bf16[1,384,384]{2,1,0:T(8,128)(2,1)S(1)}, u32[]{:S(2)}, u32[]{:S(2)}) collective-permute-start(bf16[1,384,384]{2,1,0:T(8,128)(2,1)S(1)} %pad_maximum_fusion.4), channel_id=1, source_target_pairs={{0,2},{2,4},{4,6},{6,8},{8,10},{10,12},{12,14},{14,16},{16,18},{18... | collective-permute-start | bytes 884744 | tf_op jit(solution)/shard_map/ppermute | solution.py:17
  172.3 16.2 %collective-permute-start.8 = (bf16[1,384,384]{2,1,0:T(8,128)(2,1)S(1)}, bf16[1,384,384]{2,1,0:T(8,128)(2,1)S(1)}, u32[]{:S(2)}, u32[]{:S(2)}) collective-permute-start(bf16[1,384,384]{2,1,0:T(8,128)(2,1)S(1)} %pad_maximum_fusion.4), channel_id=1, source_target_pairs={{0,4},{2,6},{4,8},{6,10},{8,12},{10,14},{12,16},{14,18},{16,20},{1... | collective-permute-start | bytes 884744 | tf_op jit(solution)/shard_map/ppermute | solution.py:17
  189.7 19.4 %collective-permute-start.15 = (bf16[1,384,128]{2,1,0:T(8,128)(2,1)S(1)}, bf16[1,384,128]{2,1,0:T(8,128)(2,1)S(1)}, u32[]{:S(2)}, u32[]{:S(2)}) collective-permute-start(bf16[1,384,128]{2,1,0:T(8,128)(2,1)S(1)} %fusion.82), channel_id=1, source_target_pairs={{4,0},{6,2},{8,4},{10,6},{12,8},{14,10},{16,12},{18,14},{20,16},{2... | collective-permute-start | bytes 294920 | tf_op jit(solution)/shard_map/ppermute | solution.py:17
  191.6 17.7 %collective-permute-start.14 = (bf16[1,384,128]{2,1,0:T(8,128)(2,1)S(1)}, bf16[1,384,128]{2,1,0:T(8,128)(2,1)S(1)}, u32[]{:S(2)}, u32[]{:S(2)}) collective-permute-start(bf16[1,384,128]{2,1,0:T(8,128)(2,1)S(1)} %fusion.82), channel_id=1, source_target_pairs={{2,0},{4,2},{6,4},{8,6},{10,8},{12,10},{14,12},{16,14},{18,16},{20... | collective-permute-start | bytes 294920 | tf_op jit(solution)/shard_map/ppermute | solution.py:17
  193.9 7.0 %collective-permute-start.13 = (bf16[1,384,128]{2,1,0:T(8,128)(2,1)S(1)}, bf16[1,384,128]{2,1,0:T(8,128)(2,1)S(1)}, u32[]{:S(2)}, u32[]{:S(2)}) collective-permute-start(bf16[1,384,128]{2,1,0:T(8,128)(2,1)S(1)} %fusion.82), channel_id=1, source_target_pairs={{0,2},{2,4},{4,6},{6,8},{8,10},{10,12},{12,14},{14,16},{16,18},{18... | collective-permute-start | bytes 294920 | tf_op jit(solution)/shard_map/ppermute | solution.py:17
  197.5 11.5 %collective-permute-start.12 = (bf16[1,384,128]{2,1,0:T(8,128)(2,1)S(1)}, bf16[1,384,128]{2,1,0:T(8,128)(2,1)S(1)}, u32[]{:S(2)}, u32[]{:S(2)}) collective-permute-start(bf16[1,384,128]{2,1,0:T(8,128)(2,1)S(1)} %fusion.82), channel_id=1, source_target_pairs={{0,4},{2,6},{4,8},{6,10},{8,12},{10,14},{12,16},{14,18},{16,20},{1... | collective-permute-start | bytes 294920 | tf_op jit(solution)/shard_map/ppermute | solution.py:17
  211.5 19.1 %collective-permute-start.19 = (bf16[1,384,128]{2,1,0:T(8,128)(2,1)S(1)}, bf16[1,384,128]{2,1,0:T(8,128)(2,1)S(1)}, u32[]{:S(2)}, u32[]{:S(2)}) collective-permute-start(bf16[1,384,128]{2,1,0:T(8,128)(2,1)S(1)} %get-tuple-element.73), channel_id=1, source_target_pairs={{4,0},{6,2},{8,4},{10,6},{12,8},{14,10},{16,12},{18,14},{20,16},{2... | collective-permute-start | bytes 294920 | tf_op jit(solution)/shard_map/ppermute | solution.py:17
  213.4 17.4 %collective-permute-start.18 = (bf16[1,384,128]{2,1,0:T(8,128)(2,1)S(1)}, bf16[1,384,128]{2,1,0:T(8,128)(2,1)S(1)}, u32[]{:S(2)}, u32[]{:S(2)}) collective-permute-start(bf16[1,384,128]{2,1,0:T(8,128)(2,1)S(1)} %get-tuple-element.73), channel_id=1, source_target_pairs={{2,0},{4,2},{6,4},{8,6},{10,8},{12,10},{14,12},{16,14},{18,16},{20... | collective-permute-start | bytes 294920 | tf_op jit(solution)/shard_map/ppermute | solution.py:17
  215.4 7.2 %collective-permute-start.17 = (bf16[1,384,128]{2,1,0:T(8,128)(2,1)S(1)}, bf16[1,384,128]{2,1,0:T(8,128)(2,1)S(1)}, u32[]{:S(2)}, u32[]{:S(2)}) collective-permute-start(bf16[1,384,128]{2,1,0:T(8,128)(2,1)S(1)} %get-tuple-element.73), channel_id=1, source_target_pairs={{0,2},{2,4},{4,6},{6,8},{8,10},{10,12},{12,14},{14,16},{16,18},{18... | collective-permute-start | bytes 294920 | tf_op jit(solution)/shard_map/ppermute | solution.py:17
  219.0 11.4 %collective-permute-start.16 = (bf16[1,384,128]{2,1,0:T(8,128)(2,1)S(1)}, bf16[1,384,128]{2,1,0:T(8,128)(2,1)S(1)}, u32[]{:S(2)}, u32[]{:S(2)}) collective-permute-start(bf16[1,384,128]{2,1,0:T(8,128)(2,1)S(1)} %get-tuple-element.73), channel_id=1, source_target_pairs={{0,4},{2,6},{4,8},{6,10},{8,12},{10,14},{12,16},{14,18},{16,20},{1... | collective-permute-start | bytes 294920 | tf_op jit(solution)/shard_map/ppermute | solution.py:17
  231.1 19.0 %collective-permute-start.23 = (bf16[1,384,128]{2,1,0:T(8,128)(2,1)S(1)}, bf16[1,384,128]{2,1,0:T(8,128)(2,1)S(1)}, u32[]{:S(2)}, u32[]{:S(2)}) collective-permute-start(bf16[1,384,128]{2,1,0:T(8,128)(2,1)S(1)} %fusion.80), channel_id=1, source_target_pairs={{4,0},{6,2},{8,4},{10,6},{12,8},{14,10},{16,12},{18,14},{20,16},{2... | collective-permute-start | bytes 294920 | tf_op jit(solution)/shard_map/ppermute | solution.py:17
  233.0 17.3 %collective-permute-start.22 = (bf16[1,384,128]{2,1,0:T(8,128)(2,1)S(1)}, bf16[1,384,128]{2,1,0:T(8,128)(2,1)S(1)}, u32[]{:S(2)}, u32[]{:S(2)}) collective-permute-start(bf16[1,384,128]{2,1,0:T(8,128)(2,1)S(1)} %fusion.80), channel_id=1, source_target_pairs={{2,0},{4,2},{6,4},{8,6},{10,8},{12,10},{14,12},{16,14},{18,16},{20... | collective-permute-start | bytes 294920 | tf_op jit(solution)/shard_map/ppermute | solution.py:17
  234.9 7.2 %collective-permute-start.21 = (bf16[1,384,128]{2,1,0:T(8,128)(2,1)S(1)}, bf16[1,384,128]{2,1,0:T(8,128)(2,1)S(1)}, u32[]{:S(2)}, u32[]{:S(2)}) collective-permute-start(bf16[1,384,128]{2,1,0:T(8,128)(2,1)S(1)} %fusion.80), channel_id=1, source_target_pairs={{0,2},{2,4},{4,6},{6,8},{8,10},{10,12},{12,14},{14,16},{16,18},{18... | collective-permute-start | bytes 294920 | tf_op jit(solution)/shard_map/ppermute | solution.py:17
  238.6 11.4 %collective-permute-start.20 = (bf16[1,384,128]{2,1,0:T(8,128)(2,1)S(1)}, bf16[1,384,128]{2,1,0:T(8,128)(2,1)S(1)}, u32[]{:S(2)}, u32[]{:S(2)}) collective-permute-start(bf16[1,384,128]{2,1,0:T(8,128)(2,1)S(1)} %fusion.80), channel_id=1, source_target_pairs={{0,4},{2,6},{4,8},{6,10},{8,12},{10,14},{12,16},{14,18},{16,20},{1... | collective-permute-start | bytes 294920 | tf_op jit(solution)/shard_map/ppermute | solution.py:17

commit v7 on v6

--- a/solution.py
+++ b/solution.py
@@ -181,7 +181,7 @@
 def match_block(state, features, block, block_rows, grid_cols):
     count, channels = block.shape
     pixels = features.shape[0]
-    tile = min(count, 768)
+    tile = min(count, 1536)
     strip_row = jnp.repeat(block_rows, grid_cols).astype(jnp.float32)
     strip_col = (jnp.arange(count, dtype=jnp.int32) % grid_cols).astype(jnp.float32)
     weights = jnp.concatenate(

time: 253 us -> 250 us (0.988)
  Pallas kernels: 37.2 us -> 33.9 us
    pallas_call x9, Pallas kernels: 37.2 us -> 33.9 us  [match_block(): pl.pallas_call(match_kernel, grid=(count // tile,), in_specs=[pl.BlockSpe...]
  transfers between devices with their start and end apart: 24 -> 24, of which waited for: 11 -> 11; matrix products, arithmetic and copies ran while one was open for 18% -> 18% of each run, Pallas kernels for 11% -> 10%
where the time goes in v7:
time: 250 us; the launch traced here: 248 us
  starting transfers between devices  98.2 us (39%)
  waiting for transfers between devices  51 us (20%)
  Pallas kernels  33.9 us (14%)
  other arithmetic  28.9 us (12%)
  local copies, waits for them, and re-layouts  17.4 us (7%)
  matrix products  16.3 us (7%)
    ppermute x16, starting transfers between devices, passed_along(): return lax.ppermute(array, axis, pairs)  50.6 us
    ppermute x8, starting transfers between devices, per_device(): got = lax.ppermute(held, 'band', pairs)  47.6 us
    ppermute x16, waiting for transfers between devices, passed_along(): return lax.ppermute(array, axis, pairs)  35.6 us
    pallas_call x9, Pallas kernels, match_block(): pl.pallas_call(match_kernel, grid=(count // tile,), in_specs=[pl.BlockSpe...  33.9 us
    dot_general x50, matrix products, conv_valid(): jnp.dot(tap_slice.reshape(-1, tap_slice.shape[-1]), weight[kernel_tap], p...  16.3 us
    ppermute x8, waiting for transfers between devices, per_device(): got = lax.ppermute(held, 'band', pairs)  15.4 us
    another operation x15, other arithmetic  9.01 us
    concatenate x9, other arithmetic, match_block(): jnp.concatenate([jnp.ones((count, 1), jnp.float32), strip_row[:, None], s...  8.97 us
  transfers between devices with their start and end apart: 24, of which 11 were waited for; matrix products, arithmetic and copies ran while one was open for 18% of the time, Pallas kernels for 10%

profile of v7, /device:TPU:7, one launch (start us, length us, event | category | flops | bytes accessed | tf_op | source)
XLA Modules:
  0.0 248.1 jit_solution(13754599315073054026)
XLA Ops:
  1.7 15.4 %collective-permute-start = (bf16[48,256]{1,0:T(8,128)(2,1)S(1)}, bf16[48,256]{1,0:T(8,128)(2,1)S(1)}, u32[]{:S(2)}, u32[]{:S(2)}) collective-permute-start(bf16[48,256]{1,0:T(8,128)(2,1)S(1)} %multiply_convert_fusion.s_ref), channel_id=1, source_target_pairs={{0,32},{2,34},{4,36},{6,38},{8,40},{10,42},{12,44},{14,46},{16,48}... | collective-permute-start | bytes 73736 | tf_op jit(solution)/shard_map/ppermute | solution.py:266
  23.1 2.8 %gather_fusion = s32[384]{0:T(512)S(1)} fusion(s32[256]{0:T(256)S(1)} %bitcast.425, s32[1024]{0:T(1024)S(1)} %pad_clamp_fusion.2), kind=kCustom, calls=%fused_computation.2 | custom fusion | bytes 4608 | tf_op jit(solution)/shard_map/gather | solution.py:288
  30.2 2.5 %shard_map.176 = (f32[384,128]{1,0:T(8,128)}, f32[384,128]{1,0:T(8,128)}) custom-call(bf16[384,256]{1,0:T(8,128)(2,1)} %bitcast.426, bf16[48,256]{1,0:T(8,128)(2,1)} %copy-done.15, bf16[48,128]{1,0:T(8,128)(2,1)} %get-tuple-element.59.w_ref, f32[384,128]{1,0:T(8,128)} %broadcast_in_dim.122.m_in, f32[384,128]{1,0:T(8,128)} %broadcast_in_dim.123.a_in), custom_call_target="tpu_custom_call" | custom-call | flops 18874368 | bytes 1019904 | tf_op jit(solution)/shard_map/pallas_call | solution.py:197
  33.5 4.0 %collective-permute-start.1 = (bf16[96,256]{1,0:T(8,128)(2,1)S(1)}, bf16[96,256]{1,0:T(8,128)(2,1)S(1)}, u32[]{:S(2)}, u32[]{:S(2)}) collective-permute-start(bf16[96,256]{1,0:T(8,128)(2,1)S(1)} %pad_maximum_fusion.8), channel_id=1, source_target_pairs={{0,16},{2,18},{4,20},{6,22},{8,24},{10,26},{12,28},{14,30},{16,0},... | collective-permute-start | bytes 147464 | tf_op jit(solution)/shard_map/ppermute | solution.py:266
  38.2 2.5 %shard_map.177 = (f32[384,128]{1,0:T(8,128)}, f32[384,128]{1,0:T(8,128)}) custom-call(bf16[384,256]{1,0:T(8,128)(2,1)} %bitcast.427, bf16[48,256]{1,0:T(8,128)(2,1)} %copy-done.17, bf16[48,128]{1,0:T(8,128)(2,1)} %get-tuple-element.58.w_ref, f32[384,128]{1,0:T(8,128)} %get-tuple-element.27.m_in, f32[384,128]{1,0:T(8,128)} %get-tuple-element.28.a_in), custom_call_target="tpu_custom_call" | custom-call | flops 18874368 | bytes 1019904 | tf_op jit(solution)/shard_map/pallas_call | solution.py:197
  42.2 3.3 %collective-permute-start.2 = (bf16[192,256]{1,0:T(8,128)(2,1)S(1)}, bf16[192,256]{1,0:T(8,128)(2,1)S(1)}, u32[]{:S(2)}, u32[]{:S(2)}) collective-permute-start(bf16[192,256]{1,0:T(8,128)(2,1)S(1)} %pad_maximum_fusion.7), channel_id=1, source_target_pairs={{0,8},{2,10},{4,12},{6,14},{8,0},{10,2},{12,4},{14,6},{16,24},{18,... | collective-permute-start | bytes 294920 | tf_op jit(solution)/shard_map/ppermute | solution.py:266
  46.2 2.6 %shard_map.178 = (f32[384,128]{1,0:T(8,128)}, f32[384,128]{1,0:T(8,128)}) custom-call(bf16[384,256]{1,0:T(8,128)(2,1)} %bitcast.428, bf16[96,256]{1,0:T(8,128)(2,1)} %copy-done.16, bf16[96,128]{1,0:T(8,128)(2,1)} %maximum_maximum_fusion.6.w_ref, f32[384,128]{1,0:T(8,128)} %get-tuple-element.30.m_in, f32[384,128]{1,0:T(8,128)} %get-tuple-element.31.a_in), custom_call_target="tpu_custom_call" | custom-call | flops 37748736 | bytes 1056768 | tf_op jit(solution)/shard_map/pallas_call | solution.py:197
  49.6 3.0 %collective-permute-start.3 = (bf16[384,256]{1,0:T(8,128)(2,1)S(1)}, bf16[384,256]{1,0:T(8,128)(2,1)S(1)}, u32[]{:S(2)}, u32[]{:S(2)}) collective-permute-start(bf16[384,256]{1,0:T(8,128)(2,1)S(1)} %pad_maximum_fusion.5), channel_id=1, source_target_pairs={{0,256},{2,258},{4,260},{6,262},{8,264},{10,266},{12,268},{14,270}... | collective-permute-start | bytes 589832 | tf_op jit(solution)/shard_map/ppermute | solution.py:266
  52.6 2.6 %shard_map.179 = (f32[384,128]{1,0:T(8,128)}, f32[384,128]{1,0:T(8,128)}) custom-call(bf16[384,256]{1,0:T(8,128)(2,1)} %bitcast.429, bf16[192,256]{1,0:T(8,128)(2,1)} %copy-done.14, bf16[192,128]{1,0:T(8,128)(2,1)} %maximum_maximum_fusion.5.w_ref, f32[384,128]{1,0:T(8,128)} %get-tuple-element.33.m_in, f32[384,128]{1,0:T(8,128)} %get-tuple-element.34.a_in), custom_call_target="tpu_custom_call" | custom-call | flops 75497472 | bytes 1130496 | tf_op jit(solution)/shard_map/pallas_call | solution.py:197
  55.3 2.2 collective-permute-done.3.s_ref
  57.5 4.8 %collective-permute-start.4 = (bf16[768,256]{1,0:T(8,128)(2,1)S(1)}, bf16[768,256]{1,0:T(8,128)(2,1)S(1)}, u32[]{:S(2)}, u32[]{:S(2)}) collective-permute-start(bf16[768,256]{1,0:T(8,128)(2,1)S(1)} %pad_maximum_fusion.3), channel_id=1, source_target_pairs={{0,128},{2,130},{4,132},{6,134},{8,136},{10,138},{12,140},{14,142}... | collective-permute-start | bytes 1179656 | tf_op jit(solution)/shard_map/ppermute | solution.py:266
  64.2 2.7 %shard_map.180 = (f32[384,128]{1,0:T(8,128)}, f32[384,128]{1,0:T(8,128)}) custom-call(bf16[384,256]{1,0:T(8,128)(2,1)} %bitcast.430, bf16[384,256]{1,0:T(8,128)(2,1)} %copy-done.12, bf16[384,128]{1,0:T(8,128)(2,1)} %maximum_maximum_fusion.4.w_ref, f32[384,128]{1,0:T(8,128)} %get-tuple-element.36.m_in, f32[384,128]{1,0:T(8,128)} %get-tuple-element.37.a_in), custom_call_target="tpu_custom_call" | custom-call | flops 150994944 | bytes 1277952 | tf_op jit(solution)/shard_map/pallas_call | solution.py:197
  67.6 3.2 %collective-permute-start.5 = (bf16[1536,256]{1,0:T(8,128)(2,1)S(1)}, bf16[1536,256]{1,0:T(8,128)(2,1)}, u32[]{:S(2)}, u32[]{:S(2)}) collective-permute-start(bf16[1536,256]{1,0:T(8,128)(2,1)S(1)} %pad_maximum_fusion.2), channel_id=1, source_target_pairs={{0,64},{2,66},{4,68},{6,70},{8,72},{10,74},{12,76},{14,78},{16,80}... | collective-permute-start | bytes 2359304 | tf_op jit(solution)/shard_map/ppermute | solution.py:266
  74.2 2.9 %convert_element_type.418 = bf16[6144,1]{1,0:T(8,128)(2,1)} reshape(bf16[128,48]{1,0:T(8,128)(2,1)S(1)} %broadcast_in_dim.140) | data formatting | bytes 24576 | tf_op jit(solution)/shard_map/convert_element_type | solution.py:185
  80.1 3.0 %shard_map.181 = (f32[384,128]{1,0:T(8,128)}, f32[384,128]{1,0:T(8,128)}) custom-call(bf16[384,256]{1,0:T(8,128)(2,1)} %bitcast.431, bf16[768,256]{1,0:T(8,128)(2,1)} %copy-done.8, bf16[768,128]{1,0:T(8,128)(2,1)} %maximum_maximum_fusion.3.w_ref, f32[384,128]{1,0:T(8,128)} %get-tuple-element.39.m_in, f32[384,128]{1,0:T(8,128)} %get-tuple-element.40.a_in), custom_call_target="tpu_custom_call" | custom-call | flops 301989888 | bytes 1572864 | tf_op jit(solution)/shard_map/pallas_call | solution.py:197
  83.1 1.9 collective-permute-done.5.s_ref
  86.3 11.3 %collective-permute-start.6 = (bf16[3072,256]{1,0:T(8,128)(2,1)S(1)}, bf16[3072,256]{1,0:T(8,128)(2,1)}, u32[]{:S(2)}, u32[]{:S(2)}) collective-permute-start(bf16[3072,256]{1,0:T(8,128)(2,1)S(1)} %pad_maximum_fusion.1), channel_id=1, source_target_pairs={{0,4},{2,62},{4,0},{6,10},{8,12},{10,6},{12,8},{14,18},{16,20},{18... | collective-permute-start | bytes 4718600 | tf_op jit(solution)/shard_map/ppermute | solution.py:266
  98.7 1.8 convolution_add_fusion.16
  103.1 3.7 %shard_map.182 = (f32[384,128]{1,0:T(8,128)}, f32[384,128]{1,0:T(8,128)}) custom-call(bf16[384,256]{1,0:T(8,128)(2,1)} %bitcast.432, bf16[1536,256]{1,0:T(8,128)(2,1)} %collective-permute-done.5.s_ref, bf16[1536,128]{1,0:T(8,128)(2,1)} %maximum_maximum_fusion.2.w_ref, f32[384,128]{1,0:T(8,128)} %get-tuple-element.42.m_in, f32[384,128]{1,0:T(8,128)} %get-tuple-element.43.a_in), custom_call_target="tpu_custom_call" | custom-call | flops 603979776 | bytes 2162688 | tf_op jit(solution)/shard_map/pallas_call | solution.py:197
  106.9 8.5 %collective-permute-done.6.s_ref = bf16[3072,256]{1,0:T(8,128)(2,1)} collective-permute-done((bf16[3072,256]{1,0:T(8,128)(2,1)S(1)}, bf16[3072,256]{1,0:T(8,128)(2,1)}, u32[]{:S(2)}, u32[]{:S(2)}) %collective-permute-start.6) | collective-permute-done | bytes 1572896 | tf_op jit(solution)/shard_map/ppermute | solution.py:266
  115.3 2.2 pad_maximum_fusion
  117.5 2.6 %collective-permute-start.7 = (bf16[6144,256]{1,0:T(8,128)(2,1)S(1)}, bf16[6144,256]{1,0:T(8,128)(2,1)}, u32[]{:S(2)}, u32[]{:S(2)}) collective-permute-start(bf16[6144,256]{1,0:T(8,128)(2,1)S(1)} %pad_maximum_fusion), channel_id=1, source_target_pairs={{0,2},{2,0},{4,6},{6,4},{8,10},{10,8},{12,14},{14,12},{16,18},{18,... | collective-permute-start | bytes 9437192 | tf_op jit(solution)/shard_map/ppermute | solution.py:266
  123.4 1.9 fusion.1
  125.3 2.5 %maximum_maximum_fusion.w_ref = bf16[6144,128]{1,0:T(8,128)(2,1)} fusion(bf16[6144,1]{1,0:T(8,128)(2,1)S(1)} %fusion.1, bf16[6144,1]{1,0:T(8,128)(2,1)S(1)} %copy-done.1, bf16[128]{0:T(256)(128)(2,1)S(1)} %pad.76.clone, bf16[128]{0:T(256)(128)(2,1)S(1)} %pad.73.clone), kind=kLoop, calls=%fused_computation.15 | loop fusion | flops 6291456 | bytes 1597952 | tf_op jit(solution)/shard_map/concatenate | solution.py:187
  127.8 2.0 gather_fusion.1
  129.9 5.4 %shard_map.183 = (f32[384,128]{1,0:T(8,128)}, f32[384,128]{1,0:T(8,128)}) custom-call(bf16[384,256]{1,0:T(8,128)(2,1)} %bitcast.433, bf16[3072,256]{1,0:T(8,128)(2,1)} %collective-permute-done.6.s_ref, bf16[3072,128]{1,0:T(8,128)(2,1)} %maximum_maximum_fusion.1.w_ref, f32[384,128]{1,0:T(8,128)} %get-tuple-element.45.m_in, f32[384,128]{1,0:T(8,128)} %get-tuple-element.46.a_in), custom_call_target="tpu_custom_call" | custom-call | flops 1207959552 | bytes 3342336 | tf_op jit(solution)/shard_map/pallas_call | solution.py:197
  135.3 8.7 %shard_map.184 = (f32[384,128]{1,0:T(8,128)}, f32[384,128]{1,0:T(8,128)}) custom-call(bf16[384,256]{1,0:T(8,128)(2,1)} %bitcast.434, bf16[6144,256]{1,0:T(8,128)(2,1)} %collective-permute-done.7.s_ref, bf16[6144,128]{1,0:T(8,128)(2,1)} %maximum_maximum_fusion.w_ref, f32[384,128]{1,0:T(8,128)} %get-tuple-element.48.m_in, f32[384,128]{1,0:T(8,128)} %get-tuple-element.49.a_in), custom_call_target="tpu_custom_call" | custom-call | flops 2415919104 | bytes 5701632 | tf_op jit(solution)/shard_map/pallas_call | solution.py:197
  145.6 4.1 %gather_fusion.2 = bf16[384,256]{1,0:T(8,128)(2,1)S(1)} fusion(bf16[6144,256]{1,0:T(8,128)(2,1)} %collective-permute-done.7.s_ref, s32[1024]{0:T(1024)S(1)} %get-tuple-element.77), kind=kCustom, calls=%fused_computation.1.clone | custom fusion | bytes 394752 | tf_op jit(solution)/shard_map/jit(_take)/gather | solution.py:295
  153.3 10.3 %collective-permute-start.11 = (bf16[1,384,384]{2,1,0:T(8,128)(2,1)S(1)}, bf16[1,384,384]{2,1,0:T(8,128)(2,1)S(1)}, u32[]{:S(2)}, u32[]{:S(2)}) collective-permute-start(bf16[1,384,384]{2,1,0:T(8,128)(2,1)S(1)} %pad_maximum_fusion.4), channel_id=1, source_target_pairs={{4,0},{6,2},{8,4},{10,6},{12,8},{14,10},{16,12},{18,14},{20,16},{2... | collective-permute-start | bytes 884744 | tf_op jit(solution)/shard_map/ppermute | solution.py:17
  163.6 2.2 collective-permute-start.10
  165.9 3.4 %collective-permute-start.9 = (bf16[1,384,384]{2,1,0:T(8,128)(2,1)S(1)}, bf16[1,384,384]{2,1,0:T(8,128)(2,1)S(1)}, u32[]{:S(2)}, u32[]{:S(2)}) collective-permute-start(bf16[1,384,384]{2,1,0:T(8,128)(2,1)S(1)} %pad_maximum_fusion.4), channel_id=1, source_target_pairs={{0,2},{2,4},{4,6},{6,8},{8,10},{10,12},{12,14},{14,16},{16,18},{18... | collective-permute-start | bytes 884744 | tf_op jit(solution)/shard_map/ppermute | solution.py:17
  169.2 2.1 collective-permute-start.8
  174.2 11.1 %collective-permute-done.8 = bf16[1,384,384]{2,1,0:T(8,128)(2,1)S(1)} collective-permute-done((bf16[1,384,384]{2,1,0:T(8,128)(2,1)S(1)}, bf16[1,384,384]{2,1,0:T(8,128)(2,1)S(1)}, u32[]{:S(2)}, u32[]{:S(2)}) %collective-permute-start.8) | collective-permute-done | bytes 294944 | tf_op jit(solution)/shard_map/ppermute | solution.py:17
  186.6 1.9 collective-permute-start.15
  188.5 2.3 collective-permute-start.14
  190.9 3.5 %collective-permute-start.13 = (bf16[1,384,128]{2,1,0:T(8,128)(2,1)S(1)}, bf16[1,384,128]{2,1,0:T(8,128)(2,1)S(1)}, u32[]{:S(2)}, u32[]{:S(2)}) collective-permute-start(bf16[1,384,128]{2,1,0:T(8,128)(2,1)S(1)} %fusion.82), channel_id=1, source_target_pairs={{0,2},{2,4},{4,6},{6,8},{8,10},{10,12},{12,14},{14,16},{16,18},{18... | collective-permute-start | bytes 294920 | tf_op jit(solution)/shard_map/ppermute | solution.py:17
  194.4 3.1 %collective-permute-start.12 = (bf16[1,384,128]{2,1,0:T(8,128)(2,1)S(1)}, bf16[1,384,128]{2,1,0:T(8,128)(2,1)S(1)}, u32[]{:S(2)}, u32[]{:S(2)}) collective-permute-start(bf16[1,384,128]{2,1,0:T(8,128)(2,1)S(1)} %fusion.82), channel_id=1, source_target_pairs={{0,4},{2,6},{4,8},{6,10},{8,12},{10,14},{12,16},{14,18},{16,20},{1... | collective-permute-start | bytes 294920 | tf_op jit(solution)/shard_map/ppermute | solution.py:17
  197.8 8.1 %collective-permute-done.12 = bf16[1,384,128]{2,1,0:T(8,128)(2,1)S(1)} collective-permute-done((bf16[1,384,128]{2,1,0:T(8,128)(2,1)S(1)}, bf16[1,384,128]{2,1,0:T(8,128)(2,1)S(1)}, u32[]{:S(2)}, u32[]{:S(2)}) %collective-permute-start.12) | collective-permute-done | bytes 98336 | tf_op jit(solution)/shard_map/ppermute | solution.py:17
  208.4 1.9 collective-permute-start.19
  210.3 1.9 collective-permute-start.18
  212.3 3.6 %collective-permute-start.17 = (bf16[1,384,128]{2,1,0:T(8,128)(2,1)S(1)}, bf16[1,384,128]{2,1,0:T(8,128)(2,1)S(1)}, u32[]{:S(2)}, u32[]{:S(2)}) collective-permute-start(bf16[1,384,128]{2,1,0:T(8,128)(2,1)S(1)} %get-tuple-element.73), channel_id=1, source_target_pairs={{0,2},{2,4},{4,6},{6,8},{8,10},{10,12},{12,14},{14,16},{16,18},{18... | collective-permute-start | bytes 294920 | tf_op jit(solution)/shard_map/ppermute | solution.py:17
  215.9 3.4 %collective-permute-start.16 = (bf16[1,384,128]{2,1,0:T(8,128)(2,1)S(1)}, bf16[1,384,128]{2,1,0:T(8,128)(2,1)S(1)}, u32[]{:S(2)}, u32[]{:S(2)}) collective-permute-start(bf16[1,384,128]{2,1,0:T(8,128)(2,1)S(1)} %get-tuple-element.73), channel_id=1, source_target_pairs={{0,4},{2,6},{4,8},{6,10},{8,12},{10,14},{12,16},{14,18},{16,20},{1... | collective-permute-start | bytes 294920 | tf_op jit(solution)/shard_map/ppermute | solution.py:17
  219.7 7.6 %collective-permute-done.16 = bf16[1,384,128]{2,1,0:T(8,128)(2,1)S(1)} collective-permute-done((bf16[1,384,128]{2,1,0:T(8,128)(2,1)S(1)}, bf16[1,384,128]{2,1,0:T(8,128)(2,1)S(1)}, u32[]{:S(2)}, u32[]{:S(2)}) %collective-permute-start.16) | collective-permute-done | bytes 98336 | tf_op jit(solution)/shard_map/ppermute | solution.py:17
  228.0 1.9 collective-permute-start.23
  229.9 1.9 collective-permute-start.22
  231.9 3.6 %collective-permute-start.21 = (bf16[1,384,128]{2,1,0:T(8,128)(2,1)S(1)}, bf16[1,384,128]{2,1,0:T(8,128)(2,1)S(1)}, u32[]{:S(2)}, u32[]{:S(2)}) collective-permute-start(bf16[1,384,128]{2,1,0:T(8,128)(2,1)S(1)} %fusion.80), channel_id=1, source_target_pairs={{0,2},{2,4},{4,6},{6,8},{8,10},{10,12},{12,14},{14,16},{16,18},{18... | collective-permute-start | bytes 294920 | tf_op jit(solution)/shard_map/ppermute | solution.py:17
  235.5 3.4 %collective-permute-start.20 = (bf16[1,384,128]{2,1,0:T(8,128)(2,1)S(1)}, bf16[1,384,128]{2,1,0:T(8,128)(2,1)S(1)}, u32[]{:S(2)}, u32[]{:S(2)}) collective-permute-start(bf16[1,384,128]{2,1,0:T(8,128)(2,1)S(1)} %fusion.80), channel_id=1, source_target_pairs={{0,4},{2,6},{4,8},{6,10},{8,12},{10,14},{12,16},{14,18},{16,20},{1... | collective-permute-start | bytes 294920 | tf_op jit(solution)/shard_map/ppermute | solution.py:17
  239.2 7.7 %collective-permute-done.20 = bf16[1,384,128]{2,1,0:T(8,128)(2,1)S(1)} collective-permute-done((bf16[1,384,128]{2,1,0:T(8,128)(2,1)S(1)}, bf16[1,384,128]{2,1,0:T(8,128)(2,1)S(1)}, u32[]{:S(2)}, u32[]{:S(2)}) %collective-permute-start.20) | collective-permute-done | bytes 98336 | tf_op jit(solution)/shard_map/ppermute | solution.py:17
  (178 shorter events, 46.5 us)
Async XLA Ops:
  1.7 24.2 %copy-start.15 = (bf16[48,256]{1,0:T(8,128)(2,1)}, bf16[48,256]{1,0:T(8,128)(2,1)S(1)}, u32[]{:S(2)}) copy-start(bf16[48,256]{1,0:T(8,128)(2,1)S(1)} %multiply_convert_fusion.s_ref) | copy-start | bytes 73732
  1.7 31.0 %collective-permute-start = (bf16[48,256]{1,0:T(8,128)(2,1)S(1)}, bf16[48,256]{1,0:T(8,128)(2,1)S(1)}, u32[]{:S(2)}, u32[]{:S(2)}) collective-permute-start(bf16[48,256]{1,0:T(8,128)(2,1)S(1)} %multiply_convert_fusion.s_ref), channel_id=1, source_target_pairs={{0,32},{2,34},{4,36},{6,38},{8,40},{10,42},{12,44},{14,46},{16,48}... | collective-permute-start | bytes 73736 | tf_op jit(solution)/shard_map/ppermute | solution.py:266
  28.8 23.8 %copy-start.18 = (f32[3,128]{1,0:T(4,128)S(1)}, f32[3,128]{1,0:T(4,128)}, u32[]{:S(2)}) copy-start(f32[3,128]{1,0:T(4,128)} %param.24) | copy-start | bytes 4612
  32.7 5.5 %copy-start.17 = (bf16[48,256]{1,0:T(8,128)(2,1)}, bf16[48,256]{1,0:T(8,128)(2,1)S(1)}, u32[]{:S(2)}) copy-start(bf16[48,256]{1,0:T(8,128)(2,1)S(1)} %collective-permute-done.s_ref) | copy-start | bytes 73732
  33.5 8.7 %collective-permute-start.1 = (bf16[96,256]{1,0:T(8,128)(2,1)S(1)}, bf16[96,256]{1,0:T(8,128)(2,1)S(1)}, u32[]{:S(2)}, u32[]{:S(2)}) collective-permute-start(bf16[96,256]{1,0:T(8,128)(2,1)S(1)} %pad_maximum_fusion.8), channel_id=1, source_target_pairs={{0,16},{2,18},{4,20},{6,22},{8,24},{10,26},{12,28},{14,30},{16,0},... | collective-permute-start | bytes 147464 | tf_op jit(solution)/shard_map/ppermute | solution.py:266
  42.2 4.0 %copy-start.16 = (bf16[96,256]{1,0:T(8,128)(2,1)}, bf16[96,256]{1,0:T(8,128)(2,1)S(1)}, u32[]{:S(2)}) copy-start(bf16[96,256]{1,0:T(8,128)(2,1)S(1)} %collective-permute-done.1.s_ref) | copy-start | bytes 147460
  42.2 7.3 %collective-permute-start.2 = (bf16[192,256]{1,0:T(8,128)(2,1)S(1)}, bf16[192,256]{1,0:T(8,128)(2,1)S(1)}, u32[]{:S(2)}, u32[]{:S(2)}) collective-permute-start(bf16[192,256]{1,0:T(8,128)(2,1)S(1)} %pad_maximum_fusion.7), channel_id=1, source_target_pairs={{0,8},{2,10},{4,12},{6,14},{8,0},{10,2},{12,4},{14,6},{16,24},{18,... | collective-permute-start | bytes 294920 | tf_op jit(solution)/shard_map/ppermute | solution.py:266
  49.6 3.1 %copy-start.14 = (bf16[192,256]{1,0:T(8,128)(2,1)}, bf16[192,256]{1,0:T(8,128)(2,1)S(1)}, u32[]{:S(2)}) copy-start(bf16[192,256]{1,0:T(8,128)(2,1)S(1)} %collective-permute-done.2.s_ref) | copy-start | bytes 294916
  49.6 7.9 %collective-permute-start.3 = (bf16[384,256]{1,0:T(8,128)(2,1)S(1)}, bf16[384,256]{1,0:T(8,128)(2,1)S(1)}, u32[]{:S(2)}, u32[]{:S(2)}) collective-permute-start(bf16[384,256]{1,0:T(8,128)(2,1)S(1)} %pad_maximum_fusion.5), channel_id=1, source_target_pairs={{0,256},{2,258},{4,260},{6,262},{8,264},{10,266},{12,268},{14,270}... | collective-permute-start | bytes 589832 | tf_op jit(solution)/shard_map/ppermute | solution.py:266
  57.5 6.7 %copy-start.12 = (bf16[384,256]{1,0:T(8,128)(2,1)}, bf16[384,256]{1,0:T(8,128)(2,1)S(1)}, u32[]{:S(2)}) copy-start(bf16[384,256]{1,0:T(8,128)(2,1)S(1)} %collective-permute-done.3.s_ref) | copy-start | bytes 589828
  57.5 10.0 %collective-permute-start.4 = (bf16[768,256]{1,0:T(8,128)(2,1)S(1)}, bf16[768,256]{1,0:T(8,128)(2,1)S(1)}, u32[]{:S(2)}, u32[]{:S(2)}) collective-permute-start(bf16[768,256]{1,0:T(8,128)(2,1)S(1)} %pad_maximum_fusion.3), channel_id=1, source_target_pairs={{0,128},{2,130},{4,132},{6,134},{8,136},{10,138},{12,140},{14,142}... | collective-permute-start | bytes 1179656 | tf_op jit(solution)/shard_map/ppermute | solution.py:266
  67.6 6.6 %copy-start.8 = (bf16[768,256]{1,0:T(8,128)(2,1)}, bf16[768,256]{1,0:T(8,128)(2,1)S(1)}, u32[]{:S(2)}) copy-start(bf16[768,256]{1,0:T(8,128)(2,1)S(1)} %collective-permute-done.4.s_ref) | copy-start | bytes 1179652
  67.6 17.4 %collective-permute-start.5 = (bf16[1536,256]{1,0:T(8,128)(2,1)S(1)}, bf16[1536,256]{1,0:T(8,128)(2,1)}, u32[]{:S(2)}, u32[]{:S(2)}) collective-permute-start(bf16[1536,256]{1,0:T(8,128)(2,1)S(1)} %pad_maximum_fusion.2), channel_id=1, source_target_pairs={{0,64},{2,66},{4,68},{6,70},{8,72},{10,74},{12,76},{14,78},{16,80}... | collective-permute-start | bytes 2359304 | tf_op jit(solution)/shard_map/ppermute | solution.py:266
  72.4 5.6 %copy-start.3 = (bf16[1,384,128]{2,1,0:T(8,128)(2,1)S(1)}, bf16[1,384,128]{2,1,0:T(8,128)(2,1)}, u32[]{:S(2)}) copy-start(bf16[1,384,128]{2,1,0:T(8,128)(2,1)} %param.22) | copy-start | bytes 294916
  83.1 14.5 %copy-start.9 = (f32[384,256]{1,0:T(8,128)S(1)}, f32[384,256]{1,0:T(8,128)}, u32[]{:S(2)}) copy-start(f32[384,256]{1,0:T(8,128)} %fusion.178) | copy-start | bytes 1179652
  86.3 16.9 %copy-start.2 = (bf16[3072,256]{1,0:T(8,128)(2,1)}, bf16[3072,256]{1,0:T(8,128)(2,1)S(1)}, u32[]{:S(2)}) copy-start(bf16[3072,256]{1,0:T(8,128)(2,1)S(1)} %pad_maximum_fusion.1) | copy-start | bytes 4718596
  86.3 29.1 %collective-permute-start.6 = (bf16[3072,256]{1,0:T(8,128)(2,1)S(1)}, bf16[3072,256]{1,0:T(8,128)(2,1)}, u32[]{:S(2)}, u32[]{:S(2)}) collective-permute-start(bf16[3072,256]{1,0:T(8,128)(2,1)S(1)} %pad_maximum_fusion.1), channel_id=1, source_target_pairs={{0,4},{2,62},{4,0},{6,10},{8,12},{10,6},{12,8},{14,18},{16,20},{18... | collective-permute-start | bytes 4718600 | tf_op jit(solution)/shard_map/ppermute | solution.py:266
  106.9 13.2 %copy-start.10 = (f32[384,256]{1,0:T(8,128)S(1)}, f32[384,256]{1,0:T(8,128)}, u32[]{:S(2)}) copy-start(f32[384,256]{1,0:T(8,128)} %convolution_add_fusion.16) | copy-start | bytes 1179652
  115.3 6.5 %copy-start.5 = (bf16[3072,1]{1,0:T(8,128)(2,1)S(1)}, bf16[3072,1]{1,0:T(8,128)(2,1)}, u32[]{:S(2)}) copy-start(bf16[3072,1]{1,0:T(8,128)(2,1)} %fusion.6) | copy-start | bytes 18436
  117.5 4.4 %copy-start.4 = (bf16[3072,1]{1,0:T(8,128)(2,1)S(1)}, bf16[3072,1]{1,0:T(8,128)(2,1)}, u32[]{:S(2)}) copy-start(bf16[3072,1]{1,0:T(8,128)(2,1)} %convert_element_type.419) | copy-start | bytes 18436
  117.5 17.8 %collective-permute-start.7 = (bf16[6144,256]{1,0:T(8,128)(2,1)S(1)}, bf16[6144,256]{1,0:T(8,128)(2,1)}, u32[]{:S(2)}, u32[]{:S(2)}) collective-permute-start(bf16[6144,256]{1,0:T(8,128)(2,1)S(1)} %pad_maximum_fusion), channel_id=1, source_target_pairs={{0,2},{2,0},{4,6},{6,4},{8,10},{10,8},{12,14},{14,12},{16,18},{18,... | collective-permute-start | bytes 9437192 | tf_op jit(solution)/shard_map/ppermute | solution.py:266
  121.9 3.4 %copy-start.1 = (bf16[6144,1]{1,0:T(8,128)(2,1)S(1)}, bf16[6144,1]{1,0:T(8,128)(2,1)}, u32[]{:S(2)}) copy-start(bf16[6144,1]{1,0:T(8,128)(2,1)} %convert_element_type.418) | copy-start | bytes 36868
  144.0 5.6 %copy-start = (bf16[1,384,256]{2,1,0:T(8,128)(2,1)S(1)}, bf16[1,384,256]{2,1,0:T(8,128)(2,1)}, u32[]{:S(2)}) copy-start(bf16[1,384,256]{2,1,0:T(8,128)(2,1)} %param.19) | copy-start | bytes 589828
  144.0 6.2 %copy-start.11 = (bf16[1,384,128]{2,1,0:T(8,128)(2,1)S(1)}, bf16[1,384,128]{2,1,0:T(8,128)(2,1)}, u32[]{:S(2)}) copy-start(bf16[1,384,128]{2,1,0:T(8,128)(2,1)} %param.21) | copy-start | bytes 294916
  145.5 4.7 %copy-start.7 = (bf16[5,384,384]{2,1,0:T(8,128)(2,1)S(1)}, bf16[5,384,384]{2,1,0:T(8,128)(2,1)}, u32[]{:S(2)}) copy-start(bf16[5,384,384]{2,1,0:T(8,128)(2,1)} %param.25) | copy-start | bytes 4423684
  151.1 1.0 copy-start.13
  152.7 18.7 %copy-start.6 = (bf16[5,384,384]{2,1,0:T(8,128)(2,1)S(1)}, bf16[5,384,384]{2,1,0:T(8,128)(2,1)}, u32[]{:S(2)}) copy-start(bf16[5,384,384]{2,1,0:T(8,128)(2,1)} %param.26) | copy-start | bytes 4423684
  153.3 20.7 %collective-permute-start.11 = (bf16[1,384,384]{2,1,0:T(8,128)(2,1)S(1)}, bf16[1,384,384]{2,1,0:T(8,128)(2,1)S(1)}, u32[]{:S(2)}, u32[]{:S(2)}) collective-permute-start(bf16[1,384,384]{2,1,0:T(8,128)(2,1)S(1)} %pad_maximum_fusion.4), channel_id=1, source_target_pairs={{4,0},{6,2},{8,4},{10,6},{12,8},{14,10},{16,12},{18,14},{20,16},{2... | collective-permute-start | bytes 884744 | tf_op jit(solution)/shard_map/ppermute | solution.py:17
  163.6 22.4 %collective-permute-start.10 = (bf16[1,384,384]{2,1,0:T(8,128)(2,1)S(1)}, bf16[1,384,384]{2,1,0:T(8,128)(2,1)S(1)}, u32[]{:S(2)}, u32[]{:S(2)}) collective-permute-start(bf16[1,384,384]{2,1,0:T(8,128)(2,1)S(1)} %pad_maximum_fusion.4), channel_id=1, source_target_pairs={{2,0},{4,2},{6,4},{8,6},{10,8},{12,10},{14,12},{16,14},{18,16},{20... | collective-permute-start | bytes 884744 | tf_op jit(solution)/shard_map/ppermute | solution.py:17
  165.9 7.7 %collective-permute-start.9 = (bf16[1,384,384]{2,1,0:T(8,128)(2,1)S(1)}, bf16[1,384,384]{2,1,0:T(8,128)(2,1)S(1)}, u32[]{:S(2)}, u32[]{:S(2)}) collective-permute-start(bf16[1,384,384]{2,1,0:T(8,128)(2,1)S(1)} %pad_maximum_fusion.4), channel_id=1, source_target_pairs={{0,2},{2,4},{4,6},{6,8},{8,10},{10,12},{12,14},{14,16},{16,18},{18... | collective-permute-start | bytes 884744 | tf_op jit(solution)/shard_map/ppermute | solution.py:17
  169.2 16.2 %collective-permute-start.8 = (bf16[1,384,384]{2,1,0:T(8,128)(2,1)S(1)}, bf16[1,384,384]{2,1,0:T(8,128)(2,1)S(1)}, u32[]{:S(2)}, u32[]{:S(2)}) collective-permute-start(bf16[1,384,384]{2,1,0:T(8,128)(2,1)S(1)} %pad_maximum_fusion.4), channel_id=1, source_target_pairs={{0,4},{2,6},{4,8},{6,10},{8,12},{10,14},{12,16},{14,18},{16,20},{1... | collective-permute-start | bytes 884744 | tf_op jit(solution)/shard_map/ppermute | solution.py:17
  186.6 19.4 %collective-permute-start.15 = (bf16[1,384,128]{2,1,0:T(8,128)(2,1)S(1)}, bf16[1,384,128]{2,1,0:T(8,128)(2,1)S(1)}, u32[]{:S(2)}, u32[]{:S(2)}) collective-permute-start(bf16[1,384,128]{2,1,0:T(8,128)(2,1)S(1)} %fusion.82), channel_id=1, source_target_pairs={{4,0},{6,2},{8,4},{10,6},{12,8},{14,10},{16,12},{18,14},{20,16},{2... | collective-permute-start | bytes 294920 | tf_op jit(solution)/shard_map/ppermute | solution.py:17
  188.5 17.7 %collective-permute-start.14 = (bf16[1,384,128]{2,1,0:T(8,128)(2,1)S(1)}, bf16[1,384,128]{2,1,0:T(8,128)(2,1)S(1)}, u32[]{:S(2)}, u32[]{:S(2)}) collective-permute-start(bf16[1,384,128]{2,1,0:T(8,128)(2,1)S(1)} %fusion.82), channel_id=1, source_target_pairs={{2,0},{4,2},{6,4},{8,6},{10,8},{12,10},{14,12},{16,14},{18,16},{20... | collective-permute-start | bytes 294920 | tf_op jit(solution)/shard_map/ppermute | solution.py:17
  190.9 6.8 %collective-permute-start.13 = (bf16[1,384,128]{2,1,0:T(8,128)(2,1)S(1)}, bf16[1,384,128]{2,1,0:T(8,128)(2,1)S(1)}, u32[]{:S(2)}, u32[]{:S(2)}) collective-permute-start(bf16[1,384,128]{2,1,0:T(8,128)(2,1)S(1)} %fusion.82), channel_id=1, source_target_pairs={{0,2},{2,4},{4,6},{6,8},{8,10},{10,12},{12,14},{14,16},{16,18},{18... | collective-permute-start | bytes 294920 | tf_op jit(solution)/shard_map/ppermute | solution.py:17
  194.4 11.5 %collective-permute-start.12 = (bf16[1,384,128]{2,1,0:T(8,128)(2,1)S(1)}, bf16[1,384,128]{2,1,0:T(8,128)(2,1)S(1)}, u32[]{:S(2)}, u32[]{:S(2)}) collective-permute-start(bf16[1,384,128]{2,1,0:T(8,128)(2,1)S(1)} %fusion.82), channel_id=1, source_target_pairs={{0,4},{2,6},{4,8},{6,10},{8,12},{10,14},{12,16},{14,18},{16,20},{1... | collective-permute-start | bytes 294920 | tf_op jit(solution)/shard_map/ppermute | solution.py:17
  208.4 19.1 %collective-permute-start.19 = (bf16[1,384,128]{2,1,0:T(8,128)(2,1)S(1)}, bf16[1,384,128]{2,1,0:T(8,128)(2,1)S(1)}, u32[]{:S(2)}, u32[]{:S(2)}) collective-permute-start(bf16[1,384,128]{2,1,0:T(8,128)(2,1)S(1)} %get-tuple-element.73), channel_id=1, source_target_pairs={{4,0},{6,2},{8,4},{10,6},{12,8},{14,10},{16,12},{18,14},{20,16},{2... | collective-permute-start | bytes 294920 | tf_op jit(solution)/shard_map/ppermute | solution.py:17
  210.3 17.4 %collective-permute-start.18 = (bf16[1,384,128]{2,1,0:T(8,128)(2,1)S(1)}, bf16[1,384,128]{2,1,0:T(8,128)(2,1)S(1)}, u32[]{:S(2)}, u32[]{:S(2)}) collective-permute-start(bf16[1,384,128]{2,1,0:T(8,128)(2,1)S(1)} %get-tuple-element.73), channel_id=1, source_target_pairs={{2,0},{4,2},{6,4},{8,6},{10,8},{12,10},{14,12},{16,14},{18,16},{20... | collective-permute-start | bytes 294920 | tf_op jit(solution)/shard_map/ppermute | solution.py:17
  212.3 7.2 %collective-permute-start.17 = (bf16[1,384,128]{2,1,0:T(8,128)(2,1)S(1)}, bf16[1,384,128]{2,1,0:T(8,128)(2,1)S(1)}, u32[]{:S(2)}, u32[]{:S(2)}) collective-permute-start(bf16[1,384,128]{2,1,0:T(8,128)(2,1)S(1)} %get-tuple-element.73), channel_id=1, source_target_pairs={{0,2},{2,4},{4,6},{6,8},{8,10},{10,12},{12,14},{14,16},{16,18},{18... | collective-permute-start | bytes 294920 | tf_op jit(solution)/shard_map/ppermute | solution.py:17
  215.9 11.4 %collective-permute-start.16 = (bf16[1,384,128]{2,1,0:T(8,128)(2,1)S(1)}, bf16[1,384,128]{2,1,0:T(8,128)(2,1)S(1)}, u32[]{:S(2)}, u32[]{:S(2)}) collective-permute-start(bf16[1,384,128]{2,1,0:T(8,128)(2,1)S(1)} %get-tuple-element.73), channel_id=1, source_target_pairs={{0,4},{2,6},{4,8},{6,10},{8,12},{10,14},{12,16},{14,18},{16,20},{1... | collective-permute-start | bytes 294920 | tf_op jit(solution)/shard_map/ppermute | solution.py:17
  228.0 19.0 %collective-permute-start.23 = (bf16[1,384,128]{2,1,0:T(8,128)(2,1)S(1)}, bf16[1,384,128]{2,1,0:T(8,128)(2,1)S(1)}, u32[]{:S(2)}, u32[]{:S(2)}) collective-permute-start(bf16[1,384,128]{2,1,0:T(8,128)(2,1)S(1)} %fusion.80), channel_id=1, source_target_pairs={{4,0},{6,2},{8,4},{10,6},{12,8},{14,10},{16,12},{18,14},{20,16},{2... | collective-permute-start | bytes 294920 | tf_op jit(solution)/shard_map/ppermute | solution.py:17
  229.9 17.3 %collective-permute-start.22 = (bf16[1,384,128]{2,1,0:T(8,128)(2,1)S(1)}, bf16[1,384,128]{2,1,0:T(8,128)(2,1)S(1)}, u32[]{:S(2)}, u32[]{:S(2)}) collective-permute-start(bf16[1,384,128]{2,1,0:T(8,128)(2,1)S(1)} %fusion.80), channel_id=1, source_target_pairs={{2,0},{4,2},{6,4},{8,6},{10,8},{12,10},{14,12},{16,14},{18,16},{20... | collective-permute-start | bytes 294920 | tf_op jit(solution)/shard_map/ppermute | solution.py:17
  231.9 7.2 %collective-permute-start.21 = (bf16[1,384,128]{2,1,0:T(8,128)(2,1)S(1)}, bf16[1,384,128]{2,1,0:T(8,128)(2,1)S(1)}, u32[]{:S(2)}, u32[]{:S(2)}) collective-permute-start(bf16[1,384,128]{2,1,0:T(8,128)(2,1)S(1)} %fusion.80), channel_id=1, source_target_pairs={{0,2},{2,4},{4,6},{6,8},{8,10},{10,12},{12,14},{14,16},{16,18},{18... | collective-permute-start | bytes 294920 | tf_op jit(solution)/shard_map/ppermute | solution.py:17
  235.5 11.4 %collective-permute-start.20 = (bf16[1,384,128]{2,1,0:T(8,128)(2,1)S(1)}, bf16[1,384,128]{2,1,0:T(8,128)(2,1)S(1)}, u32[]{:S(2)}, u32[]{:S(2)}) collective-permute-start(bf16[1,384,128]{2,1,0:T(8,128)(2,1)S(1)} %fusion.80), channel_id=1, source_target_pairs={{0,4},{2,6},{4,8},{6,10},{8,12},{10,14},{12,16},{14,18},{16,20},{1... | collective-permute-start | bytes 294920 | tf_op jit(solution)/shard_map/ppermute | solution.py:17

commit v8 on v7

--- a/solution.py
+++ b/solution.py
@@ -260,10 +260,17 @@
         jnp.zeros((pixel_count, 128), jnp.float32),
     )
     held = strips.reshape(band_rows * grid_cols, channels)
-    state = match_block(state, features, held, band[None], grid_cols)
+    merged = 3
+    own_rows = lax.dynamic_index_in_dim(jnp.asarray(row_table), band, 0, keepdims=False)
     for step, bit in enumerate(GATHER_BITS):
         pairs = [(i, int(gather_partner(i, step, np.where))) for i in range(bands)]
         got = lax.ppermute(held, "band", pairs)
+        if step < merged:
+            held = jnp.concatenate([held, got], axis=0)
+            if step == merged - 1:
+                start_rows = own_rows[: 1 << merged].astype(jnp.int32)
+                state = match_block(state, features, held, start_rows, grid_cols)
+            continue
         partner = gather_partner(band, step, jnp.where)
         got_rows = lax.dynamic_index_in_dim(
             jnp.asarray(row_table[:, : 1 << step]), partner, 0, keepdims=False

time: 250 us -> 241 us (0.964)
  Pallas kernels: 33.9 us -> 26.4 us
  waiting for transfers between devices: 51 us -> 56.4 us
  other arithmetic: 28.9 us -> 24.1 us
    pallas_call x9 -> x6, Pallas kernels: 33.9 us -> 26.4 us  [match_block(): pl.pallas_call(match_kernel, grid=(count // tile,), in_specs=[pl.BlockSpe...]
    ppermute x8, waiting for transfers between devices: 15.4 us -> 20.7 us  [per_device(): got = lax.ppermute(held, 'band', pairs)]
    concatenate x9 -> x5, other arithmetic: 8.97 us -> 6.9 us  [match_block(): jnp.concatenate([jnp.ones((count, 1), jnp.float32), strip_row[:, None], s...]
    another operation x15 -> x11, other arithmetic: 9.01 us -> 8.25 us
    convert_element_type x7 -> x6, local copies, waits for them, and re-layouts: 5.7 us -> 5.59 us  [match_block(): strip_row = jnp.repeat(block_rows, grid_cols).astype(jnp.float32)]
  transfers between devices with their start and end apart: 24 -> 24, of which waited for: 11 -> 11; matrix products, arithmetic and copies ran while one was open for 18% -> 17% of each run, Pallas kernels for 10% -> 7%
where the time goes in v8:
time: 241 us; the launch traced here: 239 us
  starting transfers between devices  97.1 us (40%)
  waiting for transfers between devices  56.4 us (23%)
  Pallas kernels  26.4 us (11%)
  other arithmetic  24.1 us (10%)
  local copies, waits for them, and re-layouts  17.2 us (7%)
  matrix products  16.3 us (7%)
    ppermute x16, starting transfers between devices, passed_along(): return lax.ppermute(array, axis, pairs)  49.4 us
    ppermute x8, starting transfers between devices, per_device(): got = lax.ppermute(held, 'band', pairs)  47.7 us
    ppermute x16, waiting for transfers between devices, passed_along(): return lax.ppermute(array, axis, pairs)  35.6 us
    pallas_call x6, Pallas kernels, match_block(): pl.pallas_call(match_kernel, grid=(count // tile,), in_specs=[pl.BlockSpe...  26.4 us
    ppermute x8, waiting for transfers between devices, per_device(): got = lax.ppermute(held, 'band', pairs)  20.7 us
    dot_general x50, matrix products, conv_valid(): jnp.dot(tap_slice.reshape(-1, tap_slice.shape[-1]), weight[kernel_tap], p...  16.3 us
    another operation x11, other arithmetic  8.25 us
    concatenate x5, other arithmetic, match_block(): jnp.concatenate([jnp.ones((count, 1), jnp.float32), strip_row[:, None], s...  6.9 us
  transfers between devices with their start and end apart: 24, of which 11 were waited for; matrix products, arithmetic and copies ran while one was open for 17% of the time, Pallas kernels for 7%

profile of v8, /device:TPU:7, one launch (start us, length us, event | category | flops | bytes accessed | tf_op | source)
XLA Modules:
  0.0 239.1 jit_solution(13966583744979099194)
XLA Ops:
  1.7 15.4 %collective-permute-start = (bf16[48,256]{1,0:T(8,128)(2,1)S(1)}, bf16[48,256]{1,0:T(8,128)(2,1)S(1)}, u32[]{:S(2)}, u32[]{:S(2)}) collective-permute-start(bf16[48,256]{1,0:T(8,128)(2,1)S(1)} %get-tuple-element.41), channel_id=1, source_target_pairs={{0,32},{2,34},{4,36},{6,38},{8,40},{10,42},{12,44},{14,46},{16,48}... | collective-permute-start | bytes 73736 | tf_op jit(solution)/shard_map/ppermute | solution.py:267
  21.1 2.8 %gather_fusion = s32[384]{0:T(512)S(1)} fusion(s32[256]{0:T(256)S(1)} %bitcast.416, s32[1024]{0:T(1024)S(1)} %pad_clamp_fusion.2), kind=kCustom, calls=%fused_computation.2 | custom fusion | bytes 4608 | tf_op jit(solution)/shard_map/gather | solution.py:295
  25.5 4.0 %collective-permute-start.1 = (bf16[96,256]{1,0:T(8,128)(2,1)S(1)}, bf16[96,256]{1,0:T(8,128)(2,1)S(1)}, u32[]{:S(2)}, u32[]{:S(2)}) collective-permute-start(bf16[96,256]{1,0:T(8,128)(2,1)S(1)} %pad_maximum_fusion.7), channel_id=1, source_target_pairs={{0,16},{2,18},{4,20},{6,22},{8,24},{10,26},{12,28},{14,30},{16,0},... | collective-permute-start | bytes 147464 | tf_op jit(solution)/shard_map/ppermute | solution.py:267
  30.2 4.0 %collective-permute-done.1 = bf16[96,256]{1,0:T(8,128)(2,1)S(1)} collective-permute-done((bf16[96,256]{1,0:T(8,128)(2,1)S(1)}, bf16[96,256]{1,0:T(8,128)(2,1)S(1)}, u32[]{:S(2)}, u32[]{:S(2)}) %collective-permute-start.1) | collective-permute-done | bytes 49184 | tf_op jit(solution)/shard_map/ppermute | solution.py:267
  34.3 3.3 %collective-permute-start.2 = (bf16[192,256]{1,0:T(8,128)(2,1)S(1)}, bf16[192,256]{1,0:T(8,128)(2,1)S(1)}, u32[]{:S(2)}, u32[]{:S(2)}) collective-permute-start(bf16[192,256]{1,0:T(8,128)(2,1)S(1)} %pad_maximum_fusion.6), channel_id=1, source_target_pairs={{0,8},{2,10},{4,12},{6,14},{8,0},{10,2},{12,4},{14,6},{16,24},{18,... | collective-permute-start | bytes 294920 | tf_op jit(solution)/shard_map/ppermute | solution.py:267
  37.5 4.0 %collective-permute-done.2 = bf16[192,256]{1,0:T(8,128)(2,1)S(1)} collective-permute-done((bf16[192,256]{1,0:T(8,128)(2,1)S(1)}, bf16[192,256]{1,0:T(8,128)(2,1)S(1)}, u32[]{:S(2)}, u32[]{:S(2)}) %collective-permute-start.2) | collective-permute-done | bytes 98336 | tf_op jit(solution)/shard_map/ppermute | solution.py:267
  41.6 3.0 %collective-permute-start.3 = (bf16[384,256]{1,0:T(8,128)(2,1)S(1)}, bf16[384,256]{1,0:T(8,128)(2,1)S(1)}, u32[]{:S(2)}, u32[]{:S(2)}) collective-permute-start(bf16[384,256]{1,0:T(8,128)(2,1)S(1)} %pad_maximum_fusion.4.s_ref), channel_id=1, source_target_pairs={{0,256},{2,258},{4,260},{6,262},{8,264},{10,266},{12,268},{14,270}... | collective-permute-start | bytes 589832 | tf_op jit(solution)/shard_map/ppermute | solution.py:267
  46.0 2.8 %shard_map.158 = (f32[384,128]{1,0:T(8,128)}, f32[384,128]{1,0:T(8,128)}) custom-call(bf16[384,256]{1,0:T(8,128)(2,1)} %bitcast.417, bf16[384,256]{1,0:T(8,128)(2,1)} %copy-done.13, bf16[384,128]{1,0:T(8,128)(2,1)} %get-tuple-element.43.w_ref, f32[384,128]{1,0:T(8,128)} %broadcast_in_dim.93.m_in, f32[384,128]{1,0:T(8,128)} %broadcast_in_dim.94.a_in), custom_call_target="tpu_custom_call" | custom-call | flops 150994944 | bytes 1277952 | tf_op jit(solution)/shard_map/pallas_call | solution.py:197
  49.5 4.8 %collective-permute-start.4 = (bf16[768,256]{1,0:T(8,128)(2,1)S(1)}, bf16[768,256]{1,0:T(8,128)(2,1)S(1)}, u32[]{:S(2)}, u32[]{:S(2)}) collective-permute-start(bf16[768,256]{1,0:T(8,128)(2,1)S(1)} %constant_dynamic-update-slice_fusion), channel_id=1, source_target_pairs={{0,128},{2,130},{4,132},{6,134},{8,136},{10,138},{12,140},{14,142}... | collective-permute-start | bytes 1179656 | tf_op jit(solution)/shard_map/ppermute | solution.py:267
  55.3 2.8 %shard_map.159 = (f32[384,128]{1,0:T(8,128)}, f32[384,128]{1,0:T(8,128)}) custom-call(bf16[384,256]{1,0:T(8,128)(2,1)} %bitcast.418, bf16[384,256]{1,0:T(8,128)(2,1)} %copy-done.12, bf16[384,128]{1,0:T(8,128)(2,1)} %get-tuple-element.42.w_ref, f32[384,128]{1,0:T(8,128)} %get-tuple-element.18.m_in, f32[384,128]{1,0:T(8,128)} %get-tuple-element.19.a_in), custom_call_target="tpu_custom_call" | custom-call | flops 150994944 | bytes 1277952 | tf_op jit(solution)/shard_map/pallas_call | solution.py:197
  59.6 3.2 %collective-permute-start.5 = (bf16[1536,256]{1,0:T(8,128)(2,1)S(1)}, bf16[1536,256]{1,0:T(8,128)(2,1)}, u32[]{:S(2)}, u32[]{:S(2)}) collective-permute-start(bf16[1536,256]{1,0:T(8,128)(2,1)S(1)} %pad_maximum_fusion.2), channel_id=1, source_target_pairs={{0,64},{2,66},{4,68},{6,70},{8,72},{10,74},{12,76},{14,78},{16,80}... | collective-permute-start | bytes 2359304 | tf_op jit(solution)/shard_map/ppermute | solution.py:267
  66.3 2.9 %convert_element_type.337 = bf16[6144,1]{1,0:T(8,128)(2,1)} reshape(bf16[128,48]{1,0:T(8,128)(2,1)S(1)} %broadcast_in_dim.103) | data formatting | bytes 24576 | tf_op jit(solution)/shard_map/convert_element_type | solution.py:185
  70.1 1.8 fusion.176
  72.2 3.0 %shard_map.160 = (f32[384,128]{1,0:T(8,128)}, f32[384,128]{1,0:T(8,128)}) custom-call(bf16[384,256]{1,0:T(8,128)(2,1)} %bitcast.419, bf16[768,256]{1,0:T(8,128)(2,1)} %copy-done.8, bf16[768,128]{1,0:T(8,128)(2,1)} %maximum_maximum_fusion.3.w_ref, f32[384,128]{1,0:T(8,128)} %get-tuple-element.21.m_in, f32[384,128]{1,0:T(8,128)} %get-tuple-element.22.a_in), custom_call_target="tpu_custom_call" | custom-call | flops 301989888 | bytes 1572864 | tf_op jit(solution)/shard_map/pallas_call | solution.py:197
  75.2 1.8 collective-permute-done.5.s_ref
  78.3 9.5 %collective-permute-start.6 = (bf16[3072,256]{1,0:T(8,128)(2,1)S(1)}, bf16[3072,256]{1,0:T(8,128)(2,1)}, u32[]{:S(2)}, u32[]{:S(2)}) collective-permute-start(bf16[3072,256]{1,0:T(8,128)(2,1)S(1)} %pad_maximum_fusion.1), channel_id=1, source_target_pairs={{0,4},{2,62},{4,0},{6,10},{8,12},{10,6},{12,8},{14,18},{16,20},{18... | collective-permute-start | bytes 4718600 | tf_op jit(solution)/shard_map/ppermute | solution.py:267
  88.9 1.8 convolution_add_fusion.16
  93.4 3.7 %shard_map.161 = (f32[384,128]{1,0:T(8,128)}, f32[384,128]{1,0:T(8,128)}) custom-call(bf16[384,256]{1,0:T(8,128)(2,1)} %bitcast.420, bf16[1536,256]{1,0:T(8,128)(2,1)} %collective-permute-done.5.s_ref, bf16[1536,128]{1,0:T(8,128)(2,1)} %maximum_maximum_fusion.2.w_ref, f32[384,128]{1,0:T(8,128)} %get-tuple-element.24.m_in, f32[384,128]{1,0:T(8,128)} %get-tuple-element.25.a_in), custom_call_target="tpu_custom_call" | custom-call | flops 603979776 | bytes 2162688 | tf_op jit(solution)/shard_map/pallas_call | solution.py:197
  97.1 8.6 %collective-permute-done.6.s_ref = bf16[3072,256]{1,0:T(8,128)(2,1)} collective-permute-done((bf16[3072,256]{1,0:T(8,128)(2,1)S(1)}, bf16[3072,256]{1,0:T(8,128)(2,1)}, u32[]{:S(2)}, u32[]{:S(2)}) %collective-permute-start.6) | collective-permute-done | bytes 1572896 | tf_op jit(solution)/shard_map/ppermute | solution.py:267
  105.7 2.2 pad_maximum_fusion
  107.9 4.4 %collective-permute-start.7 = (bf16[6144,256]{1,0:T(8,128)(2,1)S(1)}, bf16[6144,256]{1,0:T(8,128)(2,1)}, u32[]{:S(2)}, u32[]{:S(2)}) collective-permute-start(bf16[6144,256]{1,0:T(8,128)(2,1)S(1)} %pad_maximum_fusion), channel_id=1, source_target_pairs={{0,2},{2,0},{4,6},{6,4},{8,10},{10,8},{12,14},{14,12},{16,18},{18,... | collective-permute-start | bytes 9437192 | tf_op jit(solution)/shard_map/ppermute | solution.py:267
  112.3 1.8 convolution_add_fusion.15
  115.6 1.9 fusion.1
  117.5 2.5 %maximum_maximum_fusion.w_ref = bf16[6144,128]{1,0:T(8,128)(2,1)} fusion(bf16[6144,1]{1,0:T(8,128)(2,1)S(1)} %fusion.1, bf16[6144,1]{1,0:T(8,128)(2,1)S(1)} %copy-done, bf16[128]{0:T(256)(128)(2,1)S(1)} %pad.58.clone, bf16[128]{0:T(256)(128)(2,1)S(1)} %pad.55.clone), kind=kLoop, calls=%fused_computation.15 | loop fusion | flops 6291456 | bytes 1597952 | tf_op jit(solution)/shard_map/concatenate | solution.py:187
  120.0 2.0 gather_fusion.1
  122.1 5.4 %shard_map.162 = (f32[384,128]{1,0:T(8,128)}, f32[384,128]{1,0:T(8,128)}) custom-call(bf16[384,256]{1,0:T(8,128)(2,1)} %bitcast.421, bf16[3072,256]{1,0:T(8,128)(2,1)} %collective-permute-done.6.s_ref, bf16[3072,128]{1,0:T(8,128)(2,1)} %maximum_maximum_fusion.1.w_ref, f32[384,128]{1,0:T(8,128)} %get-tuple-element.27.m_in, f32[384,128]{1,0:T(8,128)} %get-tuple-element.28.a_in), custom_call_target="tpu_custom_call" | custom-call | flops 1207959552 | bytes 3342336 | tf_op jit(solution)/shard_map/pallas_call | solution.py:197
  127.5 8.7 %shard_map.163 = (f32[384,128]{1,0:T(8,128)}, f32[384,128]{1,0:T(8,128)}) custom-call(bf16[384,256]{1,0:T(8,128)(2,1)} %bitcast.422, bf16[6144,256]{1,0:T(8,128)(2,1)} %collective-permute-done.7.s_ref, bf16[6144,128]{1,0:T(8,128)(2,1)} %maximum_maximum_fusion.w_ref, f32[384,128]{1,0:T(8,128)} %get-tuple-element.30.m_in, f32[384,128]{1,0:T(8,128)} %get-tuple-element.31.a_in), custom_call_target="tpu_custom_call" | custom-call | flops 2415919104 | bytes 5701632 | tf_op jit(solution)/shard_map/pallas_call | solution.py:197
  137.8 4.1 %gather_fusion.2 = bf16[384,256]{1,0:T(8,128)(2,1)S(1)} fusion(bf16[6144,256]{1,0:T(8,128)(2,1)} %collective-permute-done.7.s_ref, s32[1024]{0:T(1024)S(1)} %get-tuple-element.59), kind=kCustom, calls=%fused_computation.1.clone | custom fusion | bytes 394752 | tf_op jit(solution)/shard_map/jit(_take)/gather | solution.py:302
  145.5 9.2 %collective-permute-start.11 = (bf16[1,384,384]{2,1,0:T(8,128)(2,1)S(1)}, bf16[1,384,384]{2,1,0:T(8,128)(2,1)S(1)}, u32[]{:S(2)}, u32[]{:S(2)}) collective-permute-start(bf16[1,384,384]{2,1,0:T(8,128)(2,1)S(1)} %pad_maximum_fusion.3), channel_id=1, source_target_pairs={{4,0},{6,2},{8,4},{10,6},{12,8},{14,10},{16,12},{18,14},{20,16},{2... | collective-permute-start | bytes 884744 | tf_op jit(solution)/shard_map/ppermute | solution.py:17
  154.7 2.2 collective-permute-start.10
  156.9 3.4 %collective-permute-start.9 = (bf16[1,384,384]{2,1,0:T(8,128)(2,1)S(1)}, bf16[1,384,384]{2,1,0:T(8,128)(2,1)S(1)}, u32[]{:S(2)}, u32[]{:S(2)}) collective-permute-start(bf16[1,384,384]{2,1,0:T(8,128)(2,1)S(1)} %pad_maximum_fusion.3), channel_id=1, source_target_pairs={{0,2},{2,4},{4,6},{6,8},{8,10},{10,12},{12,14},{14,16},{16,18},{18... | collective-permute-start | bytes 884744 | tf_op jit(solution)/shard_map/ppermute | solution.py:17
  160.3 2.1 collective-permute-start.8
  165.3 11.1 %collective-permute-done.8 = bf16[1,384,384]{2,1,0:T(8,128)(2,1)S(1)} collective-permute-done((bf16[1,384,384]{2,1,0:T(8,128)(2,1)S(1)}, bf16[1,384,384]{2,1,0:T(8,128)(2,1)S(1)}, u32[]{:S(2)}, u32[]{:S(2)}) %collective-permute-start.8) | collective-permute-done | bytes 294944 | tf_op jit(solution)/shard_map/ppermute | solution.py:17
  177.6 1.9 collective-permute-start.15
  179.6 2.3 collective-permute-start.14
  181.9 3.5 %collective-permute-start.13 = (bf16[1,384,128]{2,1,0:T(8,128)(2,1)S(1)}, bf16[1,384,128]{2,1,0:T(8,128)(2,1)S(1)}, u32[]{:S(2)}, u32[]{:S(2)}) collective-permute-start(bf16[1,384,128]{2,1,0:T(8,128)(2,1)S(1)} %fusion.82), channel_id=1, source_target_pairs={{0,2},{2,4},{4,6},{6,8},{8,10},{10,12},{12,14},{14,16},{16,18},{18... | collective-permute-start | bytes 294920 | tf_op jit(solution)/shard_map/ppermute | solution.py:17
  185.4 3.1 %collective-permute-start.12 = (bf16[1,384,128]{2,1,0:T(8,128)(2,1)S(1)}, bf16[1,384,128]{2,1,0:T(8,128)(2,1)S(1)}, u32[]{:S(2)}, u32[]{:S(2)}) collective-permute-start(bf16[1,384,128]{2,1,0:T(8,128)(2,1)S(1)} %fusion.82), channel_id=1, source_target_pairs={{0,4},{2,6},{4,8},{6,10},{8,12},{10,14},{12,16},{14,18},{16,20},{1... | collective-permute-start | bytes 294920 | tf_op jit(solution)/shard_map/ppermute | solution.py:17
  188.8 8.1 %collective-permute-done.12 = bf16[1,384,128]{2,1,0:T(8,128)(2,1)S(1)} collective-permute-done((bf16[1,384,128]{2,1,0:T(8,128)(2,1)S(1)}, bf16[1,384,128]{2,1,0:T(8,128)(2,1)S(1)}, u32[]{:S(2)}, u32[]{:S(2)}) %collective-permute-start.12) | collective-permute-done | bytes 98336 | tf_op jit(solution)/shard_map/ppermute | solution.py:17
  199.4 1.9 collective-permute-start.19
  201.4 1.9 collective-permute-start.18
  203.3 3.6 %collective-permute-start.17 = (bf16[1,384,128]{2,1,0:T(8,128)(2,1)S(1)}, bf16[1,384,128]{2,1,0:T(8,128)(2,1)S(1)}, u32[]{:S(2)}, u32[]{:S(2)}) collective-permute-start(bf16[1,384,128]{2,1,0:T(8,128)(2,1)S(1)} %get-tuple-element.57), channel_id=1, source_target_pairs={{0,2},{2,4},{4,6},{6,8},{8,10},{10,12},{12,14},{14,16},{16,18},{18... | collective-permute-start | bytes 294920 | tf_op jit(solution)/shard_map/ppermute | solution.py:17
  206.9 3.4 %collective-permute-start.16 = (bf16[1,384,128]{2,1,0:T(8,128)(2,1)S(1)}, bf16[1,384,128]{2,1,0:T(8,128)(2,1)S(1)}, u32[]{:S(2)}, u32[]{:S(2)}) collective-permute-start(bf16[1,384,128]{2,1,0:T(8,128)(2,1)S(1)} %get-tuple-element.57), channel_id=1, source_target_pairs={{0,4},{2,6},{4,8},{6,10},{8,12},{10,14},{12,16},{14,18},{16,20},{1... | collective-permute-start | bytes 294920 | tf_op jit(solution)/shard_map/ppermute | solution.py:17
  210.7 7.6 %collective-permute-done.16 = bf16[1,384,128]{2,1,0:T(8,128)(2,1)S(1)} collective-permute-done((bf16[1,384,128]{2,1,0:T(8,128)(2,1)S(1)}, bf16[1,384,128]{2,1,0:T(8,128)(2,1)S(1)}, u32[]{:S(2)}, u32[]{:S(2)}) %collective-permute-start.16) | collective-permute-done | bytes 98336 | tf_op jit(solution)/shard_map/ppermute | solution.py:17
  219.0 1.9 collective-permute-start.23
  221.0 1.9 collective-permute-start.22
  222.9 3.6 %collective-permute-start.21 = (bf16[1,384,128]{2,1,0:T(8,128)(2,1)S(1)}, bf16[1,384,128]{2,1,0:T(8,128)(2,1)S(1)}, u32[]{:S(2)}, u32[]{:S(2)}) collective-permute-start(bf16[1,384,128]{2,1,0:T(8,128)(2,1)S(1)} %fusion.80), channel_id=1, source_target_pairs={{0,2},{2,4},{4,6},{6,8},{8,10},{10,12},{12,14},{14,16},{16,18},{18... | collective-permute-start | bytes 294920 | tf_op jit(solution)/shard_map/ppermute | solution.py:17
  226.5 3.4 %collective-permute-start.20 = (bf16[1,384,128]{2,1,0:T(8,128)(2,1)S(1)}, bf16[1,384,128]{2,1,0:T(8,128)(2,1)S(1)}, u32[]{:S(2)}, u32[]{:S(2)}) collective-permute-start(bf16[1,384,128]{2,1,0:T(8,128)(2,1)S(1)} %fusion.80), channel_id=1, source_target_pairs={{0,4},{2,6},{4,8},{6,10},{8,12},{10,14},{12,16},{14,18},{16,20},{1... | collective-permute-start | bytes 294920 | tf_op jit(solution)/shard_map/ppermute | solution.py:17
  230.2 7.7 %collective-permute-done.20 = bf16[1,384,128]{2,1,0:T(8,128)(2,1)S(1)} collective-permute-done((bf16[1,384,128]{2,1,0:T(8,128)(2,1)S(1)}, bf16[1,384,128]{2,1,0:T(8,128)(2,1)S(1)}, u32[]{:S(2)}, u32[]{:S(2)}) %collective-permute-start.20) | collective-permute-done | bytes 98336 | tf_op jit(solution)/shard_map/ppermute | solution.py:17
  (161 shorter events, 37.3 us)
Async XLA Ops:
  1.7 23.8 %collective-permute-start = (bf16[48,256]{1,0:T(8,128)(2,1)S(1)}, bf16[48,256]{1,0:T(8,128)(2,1)S(1)}, u32[]{:S(2)}, u32[]{:S(2)}) collective-permute-start(bf16[48,256]{1,0:T(8,128)(2,1)S(1)} %get-tuple-element.41), channel_id=1, source_target_pairs={{0,32},{2,34},{4,36},{6,38},{8,40},{10,42},{12,44},{14,46},{16,48}... | collective-permute-start | bytes 73736 | tf_op jit(solution)/shard_map/ppermute | solution.py:267
  25.5 29.8 %copy-start.15 = (f32[3,128]{1,0:T(4,128)S(1)}, f32[3,128]{1,0:T(4,128)}, u32[]{:S(2)}) copy-start(f32[3,128]{1,0:T(4,128)} %param.22) | copy-start | bytes 4612
  25.5 8.8 %collective-permute-start.1 = (bf16[96,256]{1,0:T(8,128)(2,1)S(1)}, bf16[96,256]{1,0:T(8,128)(2,1)S(1)}, u32[]{:S(2)}, u32[]{:S(2)}) collective-permute-start(bf16[96,256]{1,0:T(8,128)(2,1)S(1)} %pad_maximum_fusion.7), channel_id=1, source_target_pairs={{0,16},{2,18},{4,20},{6,22},{8,24},{10,26},{12,28},{14,30},{16,0},... | collective-permute-start | bytes 147464 | tf_op jit(solution)/shard_map/ppermute | solution.py:267
  34.3 7.3 %collective-permute-start.2 = (bf16[192,256]{1,0:T(8,128)(2,1)S(1)}, bf16[192,256]{1,0:T(8,128)(2,1)S(1)}, u32[]{:S(2)}, u32[]{:S(2)}) collective-permute-start(bf16[192,256]{1,0:T(8,128)(2,1)S(1)} %pad_maximum_fusion.6), channel_id=1, source_target_pairs={{0,8},{2,10},{4,12},{6,14},{8,0},{10,2},{12,4},{14,6},{16,24},{18,... | collective-permute-start | bytes 294920 | tf_op jit(solution)/shard_map/ppermute | solution.py:267
  41.6 4.5 %copy-start.13 = (bf16[384,256]{1,0:T(8,128)(2,1)}, bf16[384,256]{1,0:T(8,128)(2,1)S(1)}, u32[]{:S(2)}) copy-start(bf16[384,256]{1,0:T(8,128)(2,1)S(1)} %pad_maximum_fusion.4.s_ref) | copy-start | bytes 589828
  41.6 7.9 %collective-permute-start.3 = (bf16[384,256]{1,0:T(8,128)(2,1)S(1)}, bf16[384,256]{1,0:T(8,128)(2,1)S(1)}, u32[]{:S(2)}, u32[]{:S(2)}) collective-permute-start(bf16[384,256]{1,0:T(8,128)(2,1)S(1)} %pad_maximum_fusion.4.s_ref), channel_id=1, source_target_pairs={{0,256},{2,258},{4,260},{6,262},{8,264},{10,266},{12,268},{14,270}... | collective-permute-start | bytes 589832 | tf_op jit(solution)/shard_map/ppermute | solution.py:267
  49.5 5.7 %copy-start.12 = (bf16[384,256]{1,0:T(8,128)(2,1)}, bf16[384,256]{1,0:T(8,128)(2,1)S(1)}, u32[]{:S(2)}) copy-start(bf16[384,256]{1,0:T(8,128)(2,1)S(1)} %collective-permute-done.3.s_ref) | copy-start | bytes 589828
  49.5 10.0 %collective-permute-start.4 = (bf16[768,256]{1,0:T(8,128)(2,1)S(1)}, bf16[768,256]{1,0:T(8,128)(2,1)S(1)}, u32[]{:S(2)}, u32[]{:S(2)}) collective-permute-start(bf16[768,256]{1,0:T(8,128)(2,1)S(1)} %constant_dynamic-update-slice_fusion), channel_id=1, source_target_pairs={{0,128},{2,130},{4,132},{6,134},{8,136},{10,138},{12,140},{14,142}... | collective-permute-start | bytes 1179656 | tf_op jit(solution)/shard_map/ppermute | solution.py:267
  59.6 6.6 %copy-start.8 = (bf16[768,256]{1,0:T(8,128)(2,1)}, bf16[768,256]{1,0:T(8,128)(2,1)S(1)}, u32[]{:S(2)}) copy-start(bf16[768,256]{1,0:T(8,128)(2,1)S(1)} %collective-permute-done.4.s_ref) | copy-start | bytes 1179652
  59.6 17.4 %collective-permute-start.5 = (bf16[1536,256]{1,0:T(8,128)(2,1)S(1)}, bf16[1536,256]{1,0:T(8,128)(2,1)}, u32[]{:S(2)}, u32[]{:S(2)}) collective-permute-start(bf16[1536,256]{1,0:T(8,128)(2,1)S(1)} %pad_maximum_fusion.2), channel_id=1, source_target_pairs={{0,64},{2,66},{4,68},{6,70},{8,72},{10,74},{12,76},{14,78},{16,80}... | collective-permute-start | bytes 2359304 | tf_op jit(solution)/shard_map/ppermute | solution.py:267
  64.4 5.6 %copy-start.2 = (bf16[1,384,128]{2,1,0:T(8,128)(2,1)S(1)}, bf16[1,384,128]{2,1,0:T(8,128)(2,1)}, u32[]{:S(2)}) copy-start(bf16[1,384,128]{2,1,0:T(8,128)(2,1)} %param.20) | copy-start | bytes 294916
  75.2 12.6 %copy-start.9 = (f32[384,256]{1,0:T(8,128)S(1)}, f32[384,256]{1,0:T(8,128)}, u32[]{:S(2)}) copy-start(f32[384,256]{1,0:T(8,128)} %fusion.176) | copy-start | bytes 1179652
  78.3 15.1 %copy-start.1 = (bf16[3072,256]{1,0:T(8,128)(2,1)}, bf16[3072,256]{1,0:T(8,128)(2,1)S(1)}, u32[]{:S(2)}) copy-start(bf16[3072,256]{1,0:T(8,128)(2,1)S(1)} %pad_maximum_fusion.1) | copy-start | bytes 4718596
  78.3 27.4 %collective-permute-start.6 = (bf16[3072,256]{1,0:T(8,128)(2,1)S(1)}, bf16[3072,256]{1,0:T(8,128)(2,1)}, u32[]{:S(2)}, u32[]{:S(2)}) collective-permute-start(bf16[3072,256]{1,0:T(8,128)(2,1)S(1)} %pad_maximum_fusion.1), channel_id=1, source_target_pairs={{0,4},{2,62},{4,0},{6,10},{8,12},{10,6},{12,8},{14,18},{16,20},{18... | collective-permute-start | bytes 4718600 | tf_op jit(solution)/shard_map/ppermute | solution.py:267
  97.1 15.2 %copy-start.10 = (f32[384,256]{1,0:T(8,128)S(1)}, f32[384,256]{1,0:T(8,128)}, u32[]{:S(2)}) copy-start(f32[384,256]{1,0:T(8,128)} %convolution_add_fusion.16) | copy-start | bytes 1179652
  105.7 8.4 %copy-start.5 = (bf16[3072,1]{1,0:T(8,128)(2,1)S(1)}, bf16[3072,1]{1,0:T(8,128)(2,1)}, u32[]{:S(2)}) copy-start(bf16[3072,1]{1,0:T(8,128)(2,1)} %fusion.6) | copy-start | bytes 18436
  107.9 6.2 %copy-start.4 = (bf16[3072,1]{1,0:T(8,128)(2,1)S(1)}, bf16[3072,1]{1,0:T(8,128)(2,1)}, u32[]{:S(2)}) copy-start(bf16[3072,1]{1,0:T(8,128)(2,1)} %convert_element_type.338) | copy-start | bytes 18436
  107.9 19.6 %collective-permute-start.7 = (bf16[6144,256]{1,0:T(8,128)(2,1)S(1)}, bf16[6144,256]{1,0:T(8,128)(2,1)}, u32[]{:S(2)}, u32[]{:S(2)}) collective-permute-start(bf16[6144,256]{1,0:T(8,128)(2,1)S(1)} %pad_maximum_fusion), channel_id=1, source_target_pairs={{0,2},{2,0},{4,6},{6,4},{8,10},{10,8},{12,14},{14,12},{16,18},{18,... | collective-permute-start | bytes 9437192 | tf_op jit(solution)/shard_map/ppermute | solution.py:267
  114.1 3.4 %copy-start = (bf16[6144,1]{1,0:T(8,128)(2,1)S(1)}, bf16[6144,1]{1,0:T(8,128)(2,1)}, u32[]{:S(2)}) copy-start(bf16[6144,1]{1,0:T(8,128)(2,1)} %convert_element_type.337) | copy-start | bytes 36868
  136.2 5.6 %copy-start.3 = (bf16[1,384,256]{2,1,0:T(8,128)(2,1)S(1)}, bf16[1,384,256]{2,1,0:T(8,128)(2,1)}, u32[]{:S(2)}) copy-start(bf16[1,384,256]{2,1,0:T(8,128)(2,1)} %param.17) | copy-start | bytes 589828
  136.2 6.2 %copy-start.11 = (bf16[1,384,128]{2,1,0:T(8,128)(2,1)S(1)}, bf16[1,384,128]{2,1,0:T(8,128)(2,1)}, u32[]{:S(2)}) copy-start(bf16[1,384,128]{2,1,0:T(8,128)(2,1)} %param.19) | copy-start | bytes 294916
  137.7 4.7 %copy-start.7 = (bf16[5,384,384]{2,1,0:T(8,128)(2,1)S(1)}, bf16[5,384,384]{2,1,0:T(8,128)(2,1)}, u32[]{:S(2)}) copy-start(bf16[5,384,384]{2,1,0:T(8,128)(2,1)} %param.23) | copy-start | bytes 4423684
  143.3 1.0 copy-start.14
  144.9 17.5 %copy-start.6 = (bf16[5,384,384]{2,1,0:T(8,128)(2,1)S(1)}, bf16[5,384,384]{2,1,0:T(8,128)(2,1)}, u32[]{:S(2)}) copy-start(bf16[5,384,384]{2,1,0:T(8,128)(2,1)} %param.24) | copy-start | bytes 4423684
  145.5 19.5 %collective-permute-start.11 = (bf16[1,384,384]{2,1,0:T(8,128)(2,1)S(1)}, bf16[1,384,384]{2,1,0:T(8,128)(2,1)S(1)}, u32[]{:S(2)}, u32[]{:S(2)}) collective-permute-start(bf16[1,384,384]{2,1,0:T(8,128)(2,1)S(1)} %pad_maximum_fusion.3), channel_id=1, source_target_pairs={{4,0},{6,2},{8,4},{10,6},{12,8},{14,10},{16,12},{18,14},{20,16},{2... | collective-permute-start | bytes 884744 | tf_op jit(solution)/shard_map/ppermute | solution.py:17
  154.7 22.4 %collective-permute-start.10 = (bf16[1,384,384]{2,1,0:T(8,128)(2,1)S(1)}, bf16[1,384,384]{2,1,0:T(8,128)(2,1)S(1)}, u32[]{:S(2)}, u32[]{:S(2)}) collective-permute-start(bf16[1,384,384]{2,1,0:T(8,128)(2,1)S(1)} %pad_maximum_fusion.3), channel_id=1, source_target_pairs={{2,0},{4,2},{6,4},{8,6},{10,8},{12,10},{14,12},{16,14},{18,16},{20... | collective-permute-start | bytes 884744 | tf_op jit(solution)/shard_map/ppermute | solution.py:17
  156.9 7.7 %collective-permute-start.9 = (bf16[1,384,384]{2,1,0:T(8,128)(2,1)S(1)}, bf16[1,384,384]{2,1,0:T(8,128)(2,1)S(1)}, u32[]{:S(2)}, u32[]{:S(2)}) collective-permute-start(bf16[1,384,384]{2,1,0:T(8,128)(2,1)S(1)} %pad_maximum_fusion.3), channel_id=1, source_target_pairs={{0,2},{2,4},{4,6},{6,8},{8,10},{10,12},{12,14},{14,16},{16,18},{18... | collective-permute-start | bytes 884744 | tf_op jit(solution)/shard_map/ppermute | solution.py:17
  160.3 16.2 %collective-permute-start.8 = (bf16[1,384,384]{2,1,0:T(8,128)(2,1)S(1)}, bf16[1,384,384]{2,1,0:T(8,128)(2,1)S(1)}, u32[]{:S(2)}, u32[]{:S(2)}) collective-permute-start(bf16[1,384,384]{2,1,0:T(8,128)(2,1)S(1)} %pad_maximum_fusion.3), channel_id=1, source_target_pairs={{0,4},{2,6},{4,8},{6,10},{8,12},{10,14},{12,16},{14,18},{16,20},{1... | collective-permute-start | bytes 884744 | tf_op jit(solution)/shard_map/ppermute | solution.py:17
  177.6 19.4 %collective-permute-start.15 = (bf16[1,384,128]{2,1,0:T(8,128)(2,1)S(1)}, bf16[1,384,128]{2,1,0:T(8,128)(2,1)S(1)}, u32[]{:S(2)}, u32[]{:S(2)}) collective-permute-start(bf16[1,384,128]{2,1,0:T(8,128)(2,1)S(1)} %fusion.82), channel_id=1, source_target_pairs={{4,0},{6,2},{8,4},{10,6},{12,8},{14,10},{16,12},{18,14},{20,16},{2... | collective-permute-start | bytes 294920 | tf_op jit(solution)/shard_map/ppermute | solution.py:17
  179.6 17.7 %collective-permute-start.14 = (bf16[1,384,128]{2,1,0:T(8,128)(2,1)S(1)}, bf16[1,384,128]{2,1,0:T(8,128)(2,1)S(1)}, u32[]{:S(2)}, u32[]{:S(2)}) collective-permute-start(bf16[1,384,128]{2,1,0:T(8,128)(2,1)S(1)} %fusion.82), channel_id=1, source_target_pairs={{2,0},{4,2},{6,4},{8,6},{10,8},{12,10},{14,12},{16,14},{18,16},{20... | collective-permute-start | bytes 294920 | tf_op jit(solution)/shard_map/ppermute | solution.py:17
  181.9 6.8 %collective-permute-start.13 = (bf16[1,384,128]{2,1,0:T(8,128)(2,1)S(1)}, bf16[1,384,128]{2,1,0:T(8,128)(2,1)S(1)}, u32[]{:S(2)}, u32[]{:S(2)}) collective-permute-start(bf16[1,384,128]{2,1,0:T(8,128)(2,1)S(1)} %fusion.82), channel_id=1, source_target_pairs={{0,2},{2,4},{4,6},{6,8},{8,10},{10,12},{12,14},{14,16},{16,18},{18... | collective-permute-start | bytes 294920 | tf_op jit(solution)/shard_map/ppermute | solution.py:17
  185.4 11.5 %collective-permute-start.12 = (bf16[1,384,128]{2,1,0:T(8,128)(2,1)S(1)}, bf16[1,384,128]{2,1,0:T(8,128)(2,1)S(1)}, u32[]{:S(2)}, u32[]{:S(2)}) collective-permute-start(bf16[1,384,128]{2,1,0:T(8,128)(2,1)S(1)} %fusion.82), channel_id=1, source_target_pairs={{0,4},{2,6},{4,8},{6,10},{8,12},{10,14},{12,16},{14,18},{16,20},{1... | collective-permute-start | bytes 294920 | tf_op jit(solution)/shard_map/ppermute | solution.py:17
  199.4 19.1 %collective-permute-start.19 = (bf16[1,384,128]{2,1,0:T(8,128)(2,1)S(1)}, bf16[1,384,128]{2,1,0:T(8,128)(2,1)S(1)}, u32[]{:S(2)}, u32[]{:S(2)}) collective-permute-start(bf16[1,384,128]{2,1,0:T(8,128)(2,1)S(1)} %get-tuple-element.57), channel_id=1, source_target_pairs={{4,0},{6,2},{8,4},{10,6},{12,8},{14,10},{16,12},{18,14},{20,16},{2... | collective-permute-start | bytes 294920 | tf_op jit(solution)/shard_map/ppermute | solution.py:17
  201.4 17.4 %collective-permute-start.18 = (bf16[1,384,128]{2,1,0:T(8,128)(2,1)S(1)}, bf16[1,384,128]{2,1,0:T(8,128)(2,1)S(1)}, u32[]{:S(2)}, u32[]{:S(2)}) collective-permute-start(bf16[1,384,128]{2,1,0:T(8,128)(2,1)S(1)} %get-tuple-element.57), channel_id=1, source_target_pairs={{2,0},{4,2},{6,4},{8,6},{10,8},{12,10},{14,12},{16,14},{18,16},{20... | collective-permute-start | bytes 294920 | tf_op jit(solution)/shard_map/ppermute | solution.py:17
  203.3 7.2 %collective-permute-start.17 = (bf16[1,384,128]{2,1,0:T(8,128)(2,1)S(1)}, bf16[1,384,128]{2,1,0:T(8,128)(2,1)S(1)}, u32[]{:S(2)}, u32[]{:S(2)}) collective-permute-start(bf16[1,384,128]{2,1,0:T(8,128)(2,1)S(1)} %get-tuple-element.57), channel_id=1, source_target_pairs={{0,2},{2,4},{4,6},{6,8},{8,10},{10,12},{12,14},{14,16},{16,18},{18... | collective-permute-start | bytes 294920 | tf_op jit(solution)/shard_map/ppermute | solution.py:17
  206.9 11.4 %collective-permute-start.16 = (bf16[1,384,128]{2,1,0:T(8,128)(2,1)S(1)}, bf16[1,384,128]{2,1,0:T(8,128)(2,1)S(1)}, u32[]{:S(2)}, u32[]{:S(2)}) collective-permute-start(bf16[1,384,128]{2,1,0:T(8,128)(2,1)S(1)} %get-tuple-element.57), channel_id=1, source_target_pairs={{0,4},{2,6},{4,8},{6,10},{8,12},{10,14},{12,16},{14,18},{16,20},{1... | collective-permute-start | bytes 294920 | tf_op jit(solution)/shard_map/ppermute | solution.py:17
  219.0 19.0 %collective-permute-start.23 = (bf16[1,384,128]{2,1,0:T(8,128)(2,1)S(1)}, bf16[1,384,128]{2,1,0:T(8,128)(2,1)S(1)}, u32[]{:S(2)}, u32[]{:S(2)}) collective-permute-start(bf16[1,384,128]{2,1,0:T(8,128)(2,1)S(1)} %fusion.80), channel_id=1, source_target_pairs={{4,0},{6,2},{8,4},{10,6},{12,8},{14,10},{16,12},{18,14},{20,16},{2... | collective-permute-start | bytes 294920 | tf_op jit(solution)/shard_map/ppermute | solution.py:17
  221.0 17.3 %collective-permute-start.22 = (bf16[1,384,128]{2,1,0:T(8,128)(2,1)S(1)}, bf16[1,384,128]{2,1,0:T(8,128)(2,1)S(1)}, u32[]{:S(2)}, u32[]{:S(2)}) collective-permute-start(bf16[1,384,128]{2,1,0:T(8,128)(2,1)S(1)} %fusion.80), channel_id=1, source_target_pairs={{2,0},{4,2},{6,4},{8,6},{10,8},{12,10},{14,12},{16,14},{18,16},{20... | collective-permute-start | bytes 294920 | tf_op jit(solution)/shard_map/ppermute | solution.py:17
  222.9 7.2 %collective-permute-start.21 = (bf16[1,384,128]{2,1,0:T(8,128)(2,1)S(1)}, bf16[1,384,128]{2,1,0:T(8,128)(2,1)S(1)}, u32[]{:S(2)}, u32[]{:S(2)}) collective-permute-start(bf16[1,384,128]{2,1,0:T(8,128)(2,1)S(1)} %fusion.80), channel_id=1, source_target_pairs={{0,2},{2,4},{4,6},{6,8},{8,10},{10,12},{12,14},{14,16},{16,18},{18... | collective-permute-start | bytes 294920 | tf_op jit(solution)/shard_map/ppermute | solution.py:17
  226.5 11.4 %collective-permute-start.20 = (bf16[1,384,128]{2,1,0:T(8,128)(2,1)S(1)}, bf16[1,384,128]{2,1,0:T(8,128)(2,1)S(1)}, u32[]{:S(2)}, u32[]{:S(2)}) collective-permute-start(bf16[1,384,128]{2,1,0:T(8,128)(2,1)S(1)} %fusion.80), channel_id=1, source_target_pairs={{0,4},{2,6},{4,8},{6,10},{8,12},{10,14},{12,16},{14,18},{16,20},{1... | collective-permute-start | bytes 294920 | tf_op jit(solution)/shard_map/ppermute | solution.py:17

commit v9 on v8

--- a/solution.py
+++ b/solution.py
@@ -260,7 +260,7 @@
         jnp.zeros((pixel_count, 128), jnp.float32),
     )
     held = strips.reshape(band_rows * grid_cols, channels)
-    merged = 3
+    merged = 5
     own_rows = lax.dynamic_index_in_dim(jnp.asarray(row_table), band, 0, keepdims=False)
     for step, bit in enumerate(GATHER_BITS):
         pairs = [(i, int(gather_partner(i, step, np.where))) for i in range(bands)]

time: 241 us -> 237 us (0.983)
  waiting for transfers between devices: 56.4 us -> 61.2 us
  Pallas kernels: 26.4 us -> 21.6 us
  local copies, waits for them, and re-layouts: 17.2 us -> 21.3 us
  starting transfers between devices: 97.1 us -> 93.9 us
  other arithmetic: 24.1 us -> 21 us
    ppermute x8, waiting for transfers between devices: 20.7 us -> 25.5 us  [per_device(): got = lax.ppermute(held, 'band', pairs)]
    pallas_call x6 -> x4, Pallas kernels: 26.4 us -> 21.6 us  [match_block(): pl.pallas_call(match_kernel, grid=(count // tile,), in_specs=[pl.BlockSpe...]
    ppermute x16, starting transfers between devices: 49.4 us -> 46.8 us  [passed_along(): return lax.ppermute(array, axis, pairs)]
    unnamed x35 -> x29, local copies, waits for them, and re-layouts: 0.52 us -> 3.1 us
    another operation x11 -> x7, other arithmetic: 8.25 us -> 6.6 us
    concatenate x5 -> x3, other arithmetic: 6.9 us -> 5.56 us  [match_block(): jnp.concatenate([jnp.ones((count, 1), jnp.float32), strip_row[:, None], s...]
    convert_element_type x6 -> x4, local copies, waits for them, and re-layouts: 5.59 us -> 5.53 us  [match_block(): strip_row = jnp.repeat(block_rows, grid_cols).astype(jnp.float32)]
  transfers between devices with their start and end apart: 24 -> 24, of which waited for: 11 -> 10; matrix products, arithmetic and copies ran while one was open for 17% -> 16% of each run, Pallas kernels for 7% -> 5%
where the time goes in v9:
time: 237 us; the launch traced here: 236 us
  starting transfers between devices  93.9 us (40%)
  waiting for transfers between devices  61.2 us (26%)
  Pallas kernels  21.6 us (9%)
  local copies, waits for them, and re-layouts  21.3 us (9%)
  other arithmetic  21 us (9%)
  matrix products  15.6 us (7%)
    ppermute x8, starting transfers between devices, per_device(): got = lax.ppermute(held, 'band', pairs)  47 us
    ppermute x16, starting transfers between devices, passed_along(): return lax.ppermute(array, axis, pairs)  46.8 us
    ppermute x16, waiting for transfers between devices, passed_along(): return lax.ppermute(array, axis, pairs)  35.6 us
    ppermute x8, waiting for transfers between devices, per_device(): got = lax.ppermute(held, 'band', pairs)  25.5 us
    pallas_call x4, Pallas kernels, match_block(): pl.pallas_call(match_kernel, grid=(count // tile,), in_specs=[pl.BlockSpe...  21.6 us
    dot_general x50, matrix products, conv_valid(): jnp.dot(tap_slice.reshape(-1, tap_slice.shape[-1]), weight[kernel_tap], p...  15.6 us
    another operation x7, other arithmetic  6.6 us
    concatenate x3, other arithmetic, match_block(): jnp.concatenate([jnp.ones((count, 1), jnp.float32), strip_row[:, None], s...  5.56 us
  transfers between devices with their start and end apart: 24, of which 10 were waited for; matrix products, arithmetic and copies ran while one was open for 16% of the time, Pallas kernels for 5%

profile of v9, /device:TPU:7, one launch (start us, length us, event | category | flops | bytes accessed | tf_op | source)
XLA Modules:
  0.0 236.0 jit_solution(11693935505351207764)
XLA Ops:
  2.3 15.4 %collective-permute-start = (bf16[48,256]{1,0:T(8,128)(2,1)S(1)}, bf16[48,256]{1,0:T(8,128)(2,1)S(1)}, u32[]{:S(2)}, u32[]{:S(2)}) collective-permute-start(bf16[48,256]{1,0:T(8,128)(2,1)S(1)} %get-tuple-element.29), channel_id=1, source_target_pairs={{0,32},{2,34},{4,36},{6,38},{8,40},{10,42},{12,44},{14,46},{16,48}... | collective-permute-start | bytes 73736 | tf_op jit(solution)/shard_map/ppermute | solution.py:267
  19.9 2.8 %gather_fusion = s32[384]{0:T(512)S(1)} fusion(s32[256]{0:T(256)S(1)} %bitcast.414, s32[1024]{0:T(1024)S(1)} %pad_clamp_fusion.2), kind=kCustom, calls=%fused_computation.2 | custom fusion | bytes 4608 | tf_op jit(solution)/shard_map/gather | solution.py:295
  23.4 4.0 %collective-permute-start.1 = (bf16[96,256]{1,0:T(8,128)(2,1)S(1)}, bf16[96,256]{1,0:T(8,128)(2,1)S(1)}, u32[]{:S(2)}, u32[]{:S(2)}) collective-permute-start(bf16[96,256]{1,0:T(8,128)(2,1)S(1)} %pad_maximum_fusion.5), channel_id=1, source_target_pairs={{0,16},{2,18},{4,20},{6,22},{8,24},{10,26},{12,28},{14,30},{16,0},... | collective-permute-start | bytes 147464 | tf_op jit(solution)/shard_map/ppermute | solution.py:267
  28.2 4.0 %collective-permute-done.1 = bf16[96,256]{1,0:T(8,128)(2,1)S(1)} collective-permute-done((bf16[96,256]{1,0:T(8,128)(2,1)S(1)}, bf16[96,256]{1,0:T(8,128)(2,1)S(1)}, u32[]{:S(2)}, u32[]{:S(2)}) %collective-permute-start.1) | collective-permute-done | bytes 49184 | tf_op jit(solution)/shard_map/ppermute | solution.py:267
  32.2 3.3 %collective-permute-start.2 = (bf16[192,256]{1,0:T(8,128)(2,1)S(1)}, bf16[192,256]{1,0:T(8,128)(2,1)S(1)}, u32[]{:S(2)}, u32[]{:S(2)}) collective-permute-start(bf16[192,256]{1,0:T(8,128)(2,1)S(1)} %pad_maximum_fusion.4), channel_id=1, source_target_pairs={{0,8},{2,10},{4,12},{6,14},{8,0},{10,2},{12,4},{14,6},{16,24},{18,... | collective-permute-start | bytes 294920 | tf_op jit(solution)/shard_map/ppermute | solution.py:267
  36.1 3.4 %collective-permute-done.2 = bf16[192,256]{1,0:T(8,128)(2,1)S(1)} collective-permute-done((bf16[192,256]{1,0:T(8,128)(2,1)S(1)}, bf16[192,256]{1,0:T(8,128)(2,1)S(1)}, u32[]{:S(2)}, u32[]{:S(2)}) %collective-permute-start.2) | collective-permute-done | bytes 98336 | tf_op jit(solution)/shard_map/ppermute | solution.py:267
  39.5 3.0 %collective-permute-start.3 = (bf16[384,256]{1,0:T(8,128)(2,1)S(1)}, bf16[384,256]{1,0:T(8,128)(2,1)S(1)}, u32[]{:S(2)}, u32[]{:S(2)}) collective-permute-start(bf16[384,256]{1,0:T(8,128)(2,1)S(1)} %pad_maximum_fusion.2), channel_id=1, source_target_pairs={{0,256},{2,258},{4,260},{6,262},{8,264},{10,266},{12,268},{14,270}... | collective-permute-start | bytes 589832 | tf_op jit(solution)/shard_map/ppermute | solution.py:267
  43.9 3.6 %collective-permute-done.3 = bf16[384,256]{1,0:T(8,128)(2,1)S(1)} collective-permute-done((bf16[384,256]{1,0:T(8,128)(2,1)S(1)}, bf16[384,256]{1,0:T(8,128)(2,1)S(1)}, u32[]{:S(2)}, u32[]{:S(2)}) %collective-permute-start.3) | collective-permute-done | bytes 196640 | tf_op jit(solution)/shard_map/ppermute | solution.py:267
  48.2 4.8 %collective-permute-start.4 = (bf16[768,256]{1,0:T(8,128)(2,1)S(1)}, bf16[768,256]{1,0:T(8,128)(2,1)S(1)}, u32[]{:S(2)}, u32[]{:S(2)}) collective-permute-start(bf16[768,256]{1,0:T(8,128)(2,1)S(1)} %get-tuple-element.36), channel_id=1, source_target_pairs={{0,128},{2,130},{4,132},{6,134},{8,136},{10,138},{12,140},{14,142}... | collective-permute-start | bytes 1179656 | tf_op jit(solution)/shard_map/ppermute | solution.py:267
  53.7 4.5 %collective-permute-done.4 = bf16[768,256]{1,0:T(8,128)(2,1)S(1)} collective-permute-done((bf16[768,256]{1,0:T(8,128)(2,1)S(1)}, bf16[768,256]{1,0:T(8,128)(2,1)S(1)}, u32[]{:S(2)}, u32[]{:S(2)}) %collective-permute-start.4) | collective-permute-done | bytes 393248 | tf_op jit(solution)/shard_map/ppermute | solution.py:267
  59.0 3.2 %collective-permute-start.5 = (bf16[1536,256]{1,0:T(8,128)(2,1)}, bf16[1536,256]{1,0:T(8,128)(2,1)}, u32[]{:S(2)}, u32[]{:S(2)}) collective-permute-start(bf16[1536,256]{1,0:T(8,128)(2,1)} %get-tuple-element.32.s_ref), channel_id=1, source_target_pairs={{0,64},{2,66},{4,68},{6,70},{8,72},{10,74},{12,76},{14,78},{16,80}... | collective-permute-start | bytes 2359304 | tf_op jit(solution)/shard_map/ppermute | solution.py:267
  64.1 1.8 convert_element_type.262
  65.9 2.9 %convert_element_type.261 = bf16[6144,1]{1,0:T(8,128)(2,1)} reshape(bf16[128,48]{1,0:T(8,128)(2,1)S(1)} %broadcast_in_dim.75) | data formatting | bytes 24576 | tf_op jit(solution)/shard_map/convert_element_type | solution.py:185
  72.0 3.7 %shard_map.140 = (f32[384,128]{1,0:T(8,128)}, f32[384,128]{1,0:T(8,128)}) custom-call(bf16[384,256]{1,0:T(8,128)(2,1)} %bitcast.415, bf16[1536,256]{1,0:T(8,128)(2,1)} %get-tuple-element.32.s_ref, bf16[1536,128]{1,0:T(8,128)(2,1)} %get-tuple-element.31.w_ref, f32[384,128]{1,0:T(8,128)} %broadcast_in_dim.71.m_in, f32[384,128]{1,0:T(8,128)} %broadcast_in_dim.72.a_in), custom_call_target="tpu_custom_call" | custom-call | flops 603979776 | bytes 2162688 | tf_op jit(solution)/shard_map/pallas_call | solution.py:197
  77.0 3.2 %collective-permute-start.6 = (bf16[3072,256]{1,0:T(8,128)(2,1)S(1)}, bf16[3072,256]{1,0:T(8,128)(2,1)}, u32[]{:S(2)}, u32[]{:S(2)}) collective-permute-start(bf16[3072,256]{1,0:T(8,128)(2,1)S(1)} %constant_dynamic-update-slice_fusion.11), channel_id=1, source_target_pairs={{0,4},{2,62},{4,0},{6,10},{8,12},{10,6},{12,8},{14,18},{16,20},{18... | collective-permute-start | bytes 4718600 | tf_op jit(solution)/shard_map/ppermute | solution.py:267
  82.3 1.8 convolution_add_fusion.16
  84.1 1.6 fusion.6
  85.7 3.7 %shard_map.141 = (f32[384,128]{1,0:T(8,128)}, f32[384,128]{1,0:T(8,128)}) custom-call(bf16[384,256]{1,0:T(8,128)(2,1)} %bitcast.416, bf16[1536,256]{1,0:T(8,128)(2,1)} %collective-permute-done.5.s_ref, bf16[1536,128]{1,0:T(8,128)(2,1)} %get-tuple-element.30.w_ref, f32[384,128]{1,0:T(8,128)} %get-tuple-element.12.m_in, f32[384,128]{1,0:T(8,128)} %get-tuple-element.13.a_in), custom_call_target="tpu_custom_call" | custom-call | flops 603979776 | bytes 2162688 | tf_op jit(solution)/shard_map/pallas_call | solution.py:197
  89.4 10.0 %collective-permute-done.6.s_ref = bf16[3072,256]{1,0:T(8,128)(2,1)} collective-permute-done((bf16[3072,256]{1,0:T(8,128)(2,1)S(1)}, bf16[3072,256]{1,0:T(8,128)(2,1)}, u32[]{:S(2)}, u32[]{:S(2)}) %collective-permute-start.6) | collective-permute-done | bytes 1572896 | tf_op jit(solution)/shard_map/ppermute | solution.py:267
  99.4 2.2 pad_maximum_fusion
  101.6 10.1 %collective-permute-start.7 = (bf16[6144,256]{1,0:T(8,128)(2,1)S(1)}, bf16[6144,256]{1,0:T(8,128)(2,1)}, u32[]{:S(2)}, u32[]{:S(2)}) collective-permute-start(bf16[6144,256]{1,0:T(8,128)(2,1)S(1)} %pad_maximum_fusion), channel_id=1, source_target_pairs={{0,2},{2,0},{4,6},{6,4},{8,10},{10,8},{12,14},{14,12},{16,18},{18,... | collective-permute-start | bytes 9437192 | tf_op jit(solution)/shard_map/ppermute | solution.py:267
  111.7 1.8 convolution_add_fusion.15
  115.0 1.9 fusion.1
  116.9 2.5 %maximum_maximum_fusion.w_ref = bf16[6144,128]{1,0:T(8,128)(2,1)} fusion(bf16[6144,1]{1,0:T(8,128)(2,1)S(1)} %fusion.1, bf16[6144,1]{1,0:T(8,128)(2,1)S(1)} %copy-done, bf16[128]{0:T(256)(128)(2,1)S(1)} %pad.46.clone, bf16[128]{0:T(256)(128)(2,1)S(1)} %pad.43.clone), kind=kLoop, calls=%fused_computation.14 | loop fusion | flops 6291456 | bytes 1597952 | tf_op jit(solution)/shard_map/concatenate | solution.py:187
  119.4 2.0 gather_fusion.1
  121.5 5.4 %shard_map.142 = (f32[384,128]{1,0:T(8,128)}, f32[384,128]{1,0:T(8,128)}) custom-call(bf16[384,256]{1,0:T(8,128)(2,1)} %bitcast.417, bf16[3072,256]{1,0:T(8,128)(2,1)} %collective-permute-done.6.s_ref, bf16[3072,128]{1,0:T(8,128)(2,1)} %maximum_maximum_fusion.1.w_ref, f32[384,128]{1,0:T(8,128)} %get-tuple-element.15.m_in, f32[384,128]{1,0:T(8,128)} %get-tuple-element.16.a_in), custom_call_target="tpu_custom_call" | custom-call | flops 1207959552 | bytes 3342336 | tf_op jit(solution)/shard_map/pallas_call | solution.py:197
  126.9 8.7 %shard_map.143 = (f32[384,128]{1,0:T(8,128)}, f32[384,128]{1,0:T(8,128)}) custom-call(bf16[384,256]{1,0:T(8,128)(2,1)} %bitcast.418, bf16[6144,256]{1,0:T(8,128)(2,1)} %collective-permute-done.7.s_ref, bf16[6144,128]{1,0:T(8,128)(2,1)} %maximum_maximum_fusion.w_ref, f32[384,128]{1,0:T(8,128)} %get-tuple-element.18.m_in, f32[384,128]{1,0:T(8,128)} %get-tuple-element.19.a_in), custom_call_target="tpu_custom_call" | custom-call | flops 2415919104 | bytes 5701632 | tf_op jit(solution)/shard_map/pallas_call | solution.py:197
  137.2 4.1 %gather_fusion.2 = bf16[384,256]{1,0:T(8,128)(2,1)S(1)} fusion(bf16[6144,256]{1,0:T(8,128)(2,1)} %collective-permute-done.7.s_ref, s32[1024]{0:T(1024)S(1)} %get-tuple-element.61), kind=kCustom, calls=%fused_computation.1.clone | custom fusion | bytes 394752 | tf_op jit(solution)/shard_map/jit(_take)/gather | solution.py:302
  144.9 6.6 %collective-permute-start.11 = (bf16[1,384,384]{2,1,0:T(8,128)(2,1)S(1)}, bf16[1,384,384]{2,1,0:T(8,128)(2,1)S(1)}, u32[]{:S(2)}, u32[]{:S(2)}) collective-permute-start(bf16[1,384,384]{2,1,0:T(8,128)(2,1)S(1)} %pad_maximum_fusion.1), channel_id=1, source_target_pairs={{4,0},{6,2},{8,4},{10,6},{12,8},{14,10},{16,12},{18,14},{20,16},{2... | collective-permute-start | bytes 884744 | tf_op jit(solution)/shard_map/ppermute | solution.py:17
  151.5 2.2 collective-permute-start.10
  153.7 3.4 %collective-permute-start.9 = (bf16[1,384,384]{2,1,0:T(8,128)(2,1)S(1)}, bf16[1,384,384]{2,1,0:T(8,128)(2,1)S(1)}, u32[]{:S(2)}, u32[]{:S(2)}) collective-permute-start(bf16[1,384,384]{2,1,0:T(8,128)(2,1)S(1)} %pad_maximum_fusion.1), channel_id=1, source_target_pairs={{0,2},{2,4},{4,6},{6,8},{8,10},{10,12},{12,14},{14,16},{16,18},{18... | collective-permute-start | bytes 884744 | tf_op jit(solution)/shard_map/ppermute | solution.py:17
  157.1 2.1 collective-permute-start.8
  162.1 11.1 %collective-permute-done.8 = bf16[1,384,384]{2,1,0:T(8,128)(2,1)S(1)} collective-permute-done((bf16[1,384,384]{2,1,0:T(8,128)(2,1)S(1)}, bf16[1,384,384]{2,1,0:T(8,128)(2,1)S(1)}, u32[]{:S(2)}, u32[]{:S(2)}) %collective-permute-start.8) | collective-permute-done | bytes 294944 | tf_op jit(solution)/shard_map/ppermute | solution.py:17
  174.5 1.9 collective-permute-start.15
  176.4 2.3 collective-permute-start.14
  178.7 3.5 %collective-permute-start.13 = (bf16[1,384,128]{2,1,0:T(8,128)(2,1)S(1)}, bf16[1,384,128]{2,1,0:T(8,128)(2,1)S(1)}, u32[]{:S(2)}, u32[]{:S(2)}) collective-permute-start(bf16[1,384,128]{2,1,0:T(8,128)(2,1)S(1)} %fusion.71), channel_id=1, source_target_pairs={{0,2},{2,4},{4,6},{6,8},{8,10},{10,12},{12,14},{14,16},{16,18},{18... | collective-permute-start | bytes 294920 | tf_op jit(solution)/shard_map/ppermute | solution.py:17
  182.3 3.1 %collective-permute-start.12 = (bf16[1,384,128]{2,1,0:T(8,128)(2,1)S(1)}, bf16[1,384,128]{2,1,0:T(8,128)(2,1)S(1)}, u32[]{:S(2)}, u32[]{:S(2)}) collective-permute-start(bf16[1,384,128]{2,1,0:T(8,128)(2,1)S(1)} %fusion.71), channel_id=1, source_target_pairs={{0,4},{2,6},{4,8},{6,10},{8,12},{10,14},{12,16},{14,18},{16,20},{1... | collective-permute-start | bytes 294920 | tf_op jit(solution)/shard_map/ppermute | solution.py:17
  185.7 8.1 %collective-permute-done.12 = bf16[1,384,128]{2,1,0:T(8,128)(2,1)S(1)} collective-permute-done((bf16[1,384,128]{2,1,0:T(8,128)(2,1)S(1)}, bf16[1,384,128]{2,1,0:T(8,128)(2,1)S(1)}, u32[]{:S(2)}, u32[]{:S(2)}) %collective-permute-start.12) | collective-permute-done | bytes 98336 | tf_op jit(solution)/shard_map/ppermute | solution.py:17
  196.3 1.9 collective-permute-start.19
  198.2 1.9 collective-permute-start.18
  200.1 3.6 %collective-permute-start.17 = (bf16[1,384,128]{2,1,0:T(8,128)(2,1)S(1)}, bf16[1,384,128]{2,1,0:T(8,128)(2,1)S(1)}, u32[]{:S(2)}, u32[]{:S(2)}) collective-permute-start(bf16[1,384,128]{2,1,0:T(8,128)(2,1)S(1)} %get-tuple-element.59), channel_id=1, source_target_pairs={{0,2},{2,4},{4,6},{6,8},{8,10},{10,12},{12,14},{14,16},{16,18},{18... | collective-permute-start | bytes 294920 | tf_op jit(solution)/shard_map/ppermute | solution.py:17
  203.8 3.4 %collective-permute-start.16 = (bf16[1,384,128]{2,1,0:T(8,128)(2,1)S(1)}, bf16[1,384,128]{2,1,0:T(8,128)(2,1)S(1)}, u32[]{:S(2)}, u32[]{:S(2)}) collective-permute-start(bf16[1,384,128]{2,1,0:T(8,128)(2,1)S(1)} %get-tuple-element.59), channel_id=1, source_target_pairs={{0,4},{2,6},{4,8},{6,10},{8,12},{10,14},{12,16},{14,18},{16,20},{1... | collective-permute-start | bytes 294920 | tf_op jit(solution)/shard_map/ppermute | solution.py:17
  207.5 7.6 %collective-permute-done.16 = bf16[1,384,128]{2,1,0:T(8,128)(2,1)S(1)} collective-permute-done((bf16[1,384,128]{2,1,0:T(8,128)(2,1)S(1)}, bf16[1,384,128]{2,1,0:T(8,128)(2,1)S(1)}, u32[]{:S(2)}, u32[]{:S(2)}) %collective-permute-start.16) | collective-permute-done | bytes 98336 | tf_op jit(solution)/shard_map/ppermute | solution.py:17
  215.9 1.9 collective-permute-start.23
  217.8 1.9 collective-permute-start.22
  219.7 3.6 %collective-permute-start.21 = (bf16[1,384,128]{2,1,0:T(8,128)(2,1)S(1)}, bf16[1,384,128]{2,1,0:T(8,128)(2,1)S(1)}, u32[]{:S(2)}, u32[]{:S(2)}) collective-permute-start(bf16[1,384,128]{2,1,0:T(8,128)(2,1)S(1)} %fusion.69), channel_id=1, source_target_pairs={{0,2},{2,4},{4,6},{6,8},{8,10},{10,12},{12,14},{14,16},{16,18},{18... | collective-permute-start | bytes 294920 | tf_op jit(solution)/shard_map/ppermute | solution.py:17
  223.4 3.4 %collective-permute-start.20 = (bf16[1,384,128]{2,1,0:T(8,128)(2,1)S(1)}, bf16[1,384,128]{2,1,0:T(8,128)(2,1)S(1)}, u32[]{:S(2)}, u32[]{:S(2)}) collective-permute-start(bf16[1,384,128]{2,1,0:T(8,128)(2,1)S(1)} %fusion.69), channel_id=1, source_target_pairs={{0,4},{2,6},{4,8},{6,10},{8,12},{10,14},{12,16},{14,18},{16,20},{1... | collective-permute-start | bytes 294920 | tf_op jit(solution)/shard_map/ppermute | solution.py:17
  227.1 7.7 %collective-permute-done.20 = bf16[1,384,128]{2,1,0:T(8,128)(2,1)S(1)} collective-permute-done((bf16[1,384,128]{2,1,0:T(8,128)(2,1)S(1)}, bf16[1,384,128]{2,1,0:T(8,128)(2,1)S(1)}, u32[]{:S(2)}, u32[]{:S(2)}) %collective-permute-start.20) | collective-permute-done | bytes 98336 | tf_op jit(solution)/shard_map/ppermute | solution.py:17
  (140 shorter events, 33.7 us)
Async XLA Ops:
  2.3 21.1 %collective-permute-start = (bf16[48,256]{1,0:T(8,128)(2,1)S(1)}, bf16[48,256]{1,0:T(8,128)(2,1)S(1)}, u32[]{:S(2)}, u32[]{:S(2)}) collective-permute-start(bf16[48,256]{1,0:T(8,128)(2,1)S(1)} %get-tuple-element.29), channel_id=1, source_target_pairs={{0,32},{2,34},{4,36},{6,38},{8,40},{10,42},{12,44},{14,46},{16,48}... | collective-permute-start | bytes 73736 | tf_op jit(solution)/shard_map/ppermute | solution.py:267
  23.4 8.8 %collective-permute-start.1 = (bf16[96,256]{1,0:T(8,128)(2,1)S(1)}, bf16[96,256]{1,0:T(8,128)(2,1)S(1)}, u32[]{:S(2)}, u32[]{:S(2)}) collective-permute-start(bf16[96,256]{1,0:T(8,128)(2,1)S(1)} %pad_maximum_fusion.5), channel_id=1, source_target_pairs={{0,16},{2,18},{4,20},{6,22},{8,24},{10,26},{12,28},{14,30},{16,0},... | collective-permute-start | bytes 147464 | tf_op jit(solution)/shard_map/ppermute | solution.py:267
  32.2 7.3 %collective-permute-start.2 = (bf16[192,256]{1,0:T(8,128)(2,1)S(1)}, bf16[192,256]{1,0:T(8,128)(2,1)S(1)}, u32[]{:S(2)}, u32[]{:S(2)}) collective-permute-start(bf16[192,256]{1,0:T(8,128)(2,1)S(1)} %pad_maximum_fusion.4), channel_id=1, source_target_pairs={{0,8},{2,10},{4,12},{6,14},{8,0},{10,2},{12,4},{14,6},{16,24},{18,... | collective-permute-start | bytes 294920 | tf_op jit(solution)/shard_map/ppermute | solution.py:267
  39.5 7.9 %collective-permute-start.3 = (bf16[384,256]{1,0:T(8,128)(2,1)S(1)}, bf16[384,256]{1,0:T(8,128)(2,1)S(1)}, u32[]{:S(2)}, u32[]{:S(2)}) collective-permute-start(bf16[384,256]{1,0:T(8,128)(2,1)S(1)} %pad_maximum_fusion.2), channel_id=1, source_target_pairs={{0,256},{2,258},{4,260},{6,262},{8,264},{10,266},{12,268},{14,270}... | collective-permute-start | bytes 589832 | tf_op jit(solution)/shard_map/ppermute | solution.py:267
  48.2 10.0 %collective-permute-start.4 = (bf16[768,256]{1,0:T(8,128)(2,1)S(1)}, bf16[768,256]{1,0:T(8,128)(2,1)S(1)}, u32[]{:S(2)}, u32[]{:S(2)}) collective-permute-start(bf16[768,256]{1,0:T(8,128)(2,1)S(1)} %get-tuple-element.36), channel_id=1, source_target_pairs={{0,128},{2,130},{4,132},{6,134},{8,136},{10,138},{12,140},{14,142}... | collective-permute-start | bytes 1179656 | tf_op jit(solution)/shard_map/ppermute | solution.py:267
  59.0 16.8 %collective-permute-start.5 = (bf16[1536,256]{1,0:T(8,128)(2,1)}, bf16[1536,256]{1,0:T(8,128)(2,1)}, u32[]{:S(2)}, u32[]{:S(2)}) collective-permute-start(bf16[1536,256]{1,0:T(8,128)(2,1)} %get-tuple-element.32.s_ref), channel_id=1, source_target_pairs={{0,64},{2,66},{4,68},{6,70},{8,72},{10,74},{12,76},{14,78},{16,80}... | collective-permute-start | bytes 2359304 | tf_op jit(solution)/shard_map/ppermute | solution.py:267
  72.0 8.2 %copy-start.11 = (f32[3,128]{1,0:T(4,128)S(1)}, f32[3,128]{1,0:T(4,128)}, u32[]{:S(2)}) copy-start(f32[3,128]{1,0:T(4,128)} %param.20) | copy-start | bytes 4612
  72.0 8.2 %copy-start.1 = (bf16[1,384,128]{2,1,0:T(8,128)(2,1)S(1)}, bf16[1,384,128]{2,1,0:T(8,128)(2,1)}, u32[]{:S(2)}) copy-start(bf16[1,384,128]{2,1,0:T(8,128)(2,1)} %param.18) | copy-start | bytes 294916
  76.9 12.5 %copy-start.6 = (bf16[3072,256]{1,0:T(8,128)(2,1)}, bf16[3072,256]{1,0:T(8,128)(2,1)S(1)}, u32[]{:S(2)}) copy-start(bf16[3072,256]{1,0:T(8,128)(2,1)S(1)} %constant_dynamic-update-slice_fusion.11) | copy-start | bytes 4718596
  77.0 22.5 %collective-permute-start.6 = (bf16[3072,256]{1,0:T(8,128)(2,1)S(1)}, bf16[3072,256]{1,0:T(8,128)(2,1)}, u32[]{:S(2)}, u32[]{:S(2)}) collective-permute-start(bf16[3072,256]{1,0:T(8,128)(2,1)S(1)} %constant_dynamic-update-slice_fusion.11), channel_id=1, source_target_pairs={{0,4},{2,62},{4,0},{6,10},{8,12},{10,6},{12,8},{14,18},{16,20},{18... | collective-permute-start | bytes 4718600 | tf_op jit(solution)/shard_map/ppermute | solution.py:267
  89.4 22.2 %copy-start.7 = (f32[384,256]{1,0:T(8,128)S(1)}, f32[384,256]{1,0:T(8,128)}, u32[]{:S(2)}) copy-start(f32[384,256]{1,0:T(8,128)} %convolution_add_fusion.16) | copy-start | bytes 1179652
  99.4 14.0 %copy-start.3 = (bf16[3072,1]{1,0:T(8,128)(2,1)S(1)}, bf16[3072,1]{1,0:T(8,128)(2,1)}, u32[]{:S(2)}) copy-start(bf16[3072,1]{1,0:T(8,128)(2,1)} %fusion.6) | copy-start | bytes 18436
  101.6 11.9 %copy-start.2 = (bf16[3072,1]{1,0:T(8,128)(2,1)S(1)}, bf16[3072,1]{1,0:T(8,128)(2,1)}, u32[]{:S(2)}) copy-start(bf16[3072,1]{1,0:T(8,128)(2,1)} %convert_element_type.262) | copy-start | bytes 18436
  101.6 25.3 %collective-permute-start.7 = (bf16[6144,256]{1,0:T(8,128)(2,1)S(1)}, bf16[6144,256]{1,0:T(8,128)(2,1)}, u32[]{:S(2)}, u32[]{:S(2)}) collective-permute-start(bf16[6144,256]{1,0:T(8,128)(2,1)S(1)} %pad_maximum_fusion), channel_id=1, source_target_pairs={{0,2},{2,0},{4,6},{6,4},{8,10},{10,8},{12,14},{14,12},{16,18},{18,... | collective-permute-start | bytes 9437192 | tf_op jit(solution)/shard_map/ppermute | solution.py:267
  113.5 3.4 %copy-start = (bf16[6144,1]{1,0:T(8,128)(2,1)S(1)}, bf16[6144,1]{1,0:T(8,128)(2,1)}, u32[]{:S(2)}) copy-start(bf16[6144,1]{1,0:T(8,128)(2,1)} %convert_element_type.261) | copy-start | bytes 36868
  135.6 5.6 %copy-start.10 = (bf16[1,384,256]{2,1,0:T(8,128)(2,1)S(1)}, bf16[1,384,256]{2,1,0:T(8,128)(2,1)}, u32[]{:S(2)}) copy-start(bf16[1,384,256]{2,1,0:T(8,128)(2,1)} %param.15) | copy-start | bytes 589828
  135.6 6.2 %copy-start.8 = (bf16[1,384,128]{2,1,0:T(8,128)(2,1)S(1)}, bf16[1,384,128]{2,1,0:T(8,128)(2,1)}, u32[]{:S(2)}) copy-start(bf16[1,384,128]{2,1,0:T(8,128)(2,1)} %param.17) | copy-start | bytes 294916
  137.1 4.7 %copy-start.5 = (bf16[5,384,384]{2,1,0:T(8,128)(2,1)S(1)}, bf16[5,384,384]{2,1,0:T(8,128)(2,1)}, u32[]{:S(2)}) copy-start(bf16[5,384,384]{2,1,0:T(8,128)(2,1)} %param.21) | copy-start | bytes 4423684
  142.7 1.0 copy-start.9
  144.3 14.9 %copy-start.4 = (bf16[5,384,384]{2,1,0:T(8,128)(2,1)S(1)}, bf16[5,384,384]{2,1,0:T(8,128)(2,1)}, u32[]{:S(2)}) copy-start(bf16[5,384,384]{2,1,0:T(8,128)(2,1)} %param.22) | copy-start | bytes 4423684
  144.9 16.9 %collective-permute-start.11 = (bf16[1,384,384]{2,1,0:T(8,128)(2,1)S(1)}, bf16[1,384,384]{2,1,0:T(8,128)(2,1)S(1)}, u32[]{:S(2)}, u32[]{:S(2)}) collective-permute-start(bf16[1,384,384]{2,1,0:T(8,128)(2,1)S(1)} %pad_maximum_fusion.1), channel_id=1, source_target_pairs={{4,0},{6,2},{8,4},{10,6},{12,8},{14,10},{16,12},{18,14},{20,16},{2... | collective-permute-start | bytes 884744 | tf_op jit(solution)/shard_map/ppermute | solution.py:17
  151.5 22.4 %collective-permute-start.10 = (bf16[1,384,384]{2,1,0:T(8,128)(2,1)S(1)}, bf16[1,384,384]{2,1,0:T(8,128)(2,1)S(1)}, u32[]{:S(2)}, u32[]{:S(2)}) collective-permute-start(bf16[1,384,384]{2,1,0:T(8,128)(2,1)S(1)} %pad_maximum_fusion.1), channel_id=1, source_target_pairs={{2,0},{4,2},{6,4},{8,6},{10,8},{12,10},{14,12},{16,14},{18,16},{20... | collective-permute-start | bytes 884744 | tf_op jit(solution)/shard_map/ppermute | solution.py:17
  153.7 7.7 %collective-permute-start.9 = (bf16[1,384,384]{2,1,0:T(8,128)(2,1)S(1)}, bf16[1,384,384]{2,1,0:T(8,128)(2,1)S(1)}, u32[]{:S(2)}, u32[]{:S(2)}) collective-permute-start(bf16[1,384,384]{2,1,0:T(8,128)(2,1)S(1)} %pad_maximum_fusion.1), channel_id=1, source_target_pairs={{0,2},{2,4},{4,6},{6,8},{8,10},{10,12},{12,14},{14,16},{16,18},{18... | collective-permute-start | bytes 884744 | tf_op jit(solution)/shard_map/ppermute | solution.py:17
  157.1 16.2 %collective-permute-start.8 = (bf16[1,384,384]{2,1,0:T(8,128)(2,1)S(1)}, bf16[1,384,384]{2,1,0:T(8,128)(2,1)S(1)}, u32[]{:S(2)}, u32[]{:S(2)}) collective-permute-start(bf16[1,384,384]{2,1,0:T(8,128)(2,1)S(1)} %pad_maximum_fusion.1), channel_id=1, source_target_pairs={{0,4},{2,6},{4,8},{6,10},{8,12},{10,14},{12,16},{14,18},{16,20},{1... | collective-permute-start | bytes 884744 | tf_op jit(solution)/shard_map/ppermute | solution.py:17
  174.5 19.4 %collective-permute-start.15 = (bf16[1,384,128]{2,1,0:T(8,128)(2,1)S(1)}, bf16[1,384,128]{2,1,0:T(8,128)(2,1)S(1)}, u32[]{:S(2)}, u32[]{:S(2)}) collective-permute-start(bf16[1,384,128]{2,1,0:T(8,128)(2,1)S(1)} %fusion.71), channel_id=1, source_target_pairs={{4,0},{6,2},{8,4},{10,6},{12,8},{14,10},{16,12},{18,14},{20,16},{2... | collective-permute-start | bytes 294920 | tf_op jit(solution)/shard_map/ppermute | solution.py:17
  176.4 17.7 %collective-permute-start.14 = (bf16[1,384,128]{2,1,0:T(8,128)(2,1)S(1)}, bf16[1,384,128]{2,1,0:T(8,128)(2,1)S(1)}, u32[]{:S(2)}, u32[]{:S(2)}) collective-permute-start(bf16[1,384,128]{2,1,0:T(8,128)(2,1)S(1)} %fusion.71), channel_id=1, source_target_pairs={{2,0},{4,2},{6,4},{8,6},{10,8},{12,10},{14,12},{16,14},{18,16},{20... | collective-permute-start | bytes 294920 | tf_op jit(solution)/shard_map/ppermute | solution.py:17
  178.7 6.8 %collective-permute-start.13 = (bf16[1,384,128]{2,1,0:T(8,128)(2,1)S(1)}, bf16[1,384,128]{2,1,0:T(8,128)(2,1)S(1)}, u32[]{:S(2)}, u32[]{:S(2)}) collective-permute-start(bf16[1,384,128]{2,1,0:T(8,128)(2,1)S(1)} %fusion.71), channel_id=1, source_target_pairs={{0,2},{2,4},{4,6},{6,8},{8,10},{10,12},{12,14},{14,16},{16,18},{18... | collective-permute-start | bytes 294920 | tf_op jit(solution)/shard_map/ppermute | solution.py:17
  182.3 11.5 %collective-permute-start.12 = (bf16[1,384,128]{2,1,0:T(8,128)(2,1)S(1)}, bf16[1,384,128]{2,1,0:T(8,128)(2,1)S(1)}, u32[]{:S(2)}, u32[]{:S(2)}) collective-permute-start(bf16[1,384,128]{2,1,0:T(8,128)(2,1)S(1)} %fusion.71), channel_id=1, source_target_pairs={{0,4},{2,6},{4,8},{6,10},{8,12},{10,14},{12,16},{14,18},{16,20},{1... | collective-permute-start | bytes 294920 | tf_op jit(solution)/shard_map/ppermute | solution.py:17
  196.3 19.1 %collective-permute-start.19 = (bf16[1,384,128]{2,1,0:T(8,128)(2,1)S(1)}, bf16[1,384,128]{2,1,0:T(8,128)(2,1)S(1)}, u32[]{:S(2)}, u32[]{:S(2)}) collective-permute-start(bf16[1,384,128]{2,1,0:T(8,128)(2,1)S(1)} %get-tuple-element.59), channel_id=1, source_target_pairs={{4,0},{6,2},{8,4},{10,6},{12,8},{14,10},{16,12},{18,14},{20,16},{2... | collective-permute-start | bytes 294920 | tf_op jit(solution)/shard_map/ppermute | solution.py:17
  198.2 17.4 %collective-permute-start.18 = (bf16[1,384,128]{2,1,0:T(8,128)(2,1)S(1)}, bf16[1,384,128]{2,1,0:T(8,128)(2,1)S(1)}, u32[]{:S(2)}, u32[]{:S(2)}) collective-permute-start(bf16[1,384,128]{2,1,0:T(8,128)(2,1)S(1)} %get-tuple-element.59), channel_id=1, source_target_pairs={{2,0},{4,2},{6,4},{8,6},{10,8},{12,10},{14,12},{16,14},{18,16},{20... | collective-permute-start | bytes 294920 | tf_op jit(solution)/shard_map/ppermute | solution.py:17
  200.1 7.2 %collective-permute-start.17 = (bf16[1,384,128]{2,1,0:T(8,128)(2,1)S(1)}, bf16[1,384,128]{2,1,0:T(8,128)(2,1)S(1)}, u32[]{:S(2)}, u32[]{:S(2)}) collective-permute-start(bf16[1,384,128]{2,1,0:T(8,128)(2,1)S(1)} %get-tuple-element.59), channel_id=1, source_target_pairs={{0,2},{2,4},{4,6},{6,8},{8,10},{10,12},{12,14},{14,16},{16,18},{18... | collective-permute-start | bytes 294920 | tf_op jit(solution)/shard_map/ppermute | solution.py:17
  203.8 11.4 %collective-permute-start.16 = (bf16[1,384,128]{2,1,0:T(8,128)(2,1)S(1)}, bf16[1,384,128]{2,1,0:T(8,128)(2,1)S(1)}, u32[]{:S(2)}, u32[]{:S(2)}) collective-permute-start(bf16[1,384,128]{2,1,0:T(8,128)(2,1)S(1)} %get-tuple-element.59), channel_id=1, source_target_pairs={{0,4},{2,6},{4,8},{6,10},{8,12},{10,14},{12,16},{14,18},{16,20},{1... | collective-permute-start | bytes 294920 | tf_op jit(solution)/shard_map/ppermute | solution.py:17
  215.9 19.0 %collective-permute-start.23 = (bf16[1,384,128]{2,1,0:T(8,128)(2,1)S(1)}, bf16[1,384,128]{2,1,0:T(8,128)(2,1)S(1)}, u32[]{:S(2)}, u32[]{:S(2)}) collective-permute-start(bf16[1,384,128]{2,1,0:T(8,128)(2,1)S(1)} %fusion.69), channel_id=1, source_target_pairs={{4,0},{6,2},{8,4},{10,6},{12,8},{14,10},{16,12},{18,14},{20,16},{2... | collective-permute-start | bytes 294920 | tf_op jit(solution)/shard_map/ppermute | solution.py:17
  217.8 17.3 %collective-permute-start.22 = (bf16[1,384,128]{2,1,0:T(8,128)(2,1)S(1)}, bf16[1,384,128]{2,1,0:T(8,128)(2,1)S(1)}, u32[]{:S(2)}, u32[]{:S(2)}) collective-permute-start(bf16[1,384,128]{2,1,0:T(8,128)(2,1)S(1)} %fusion.69), channel_id=1, source_target_pairs={{2,0},{4,2},{6,4},{8,6},{10,8},{12,10},{14,12},{16,14},{18,16},{20... | collective-permute-start | bytes 294920 | tf_op jit(solution)/shard_map/ppermute | solution.py:17
  219.7 7.2 %collective-permute-start.21 = (bf16[1,384,128]{2,1,0:T(8,128)(2,1)S(1)}, bf16[1,384,128]{2,1,0:T(8,128)(2,1)S(1)}, u32[]{:S(2)}, u32[]{:S(2)}) collective-permute-start(bf16[1,384,128]{2,1,0:T(8,128)(2,1)S(1)} %fusion.69), channel_id=1, source_target_pairs={{0,2},{2,4},{4,6},{6,8},{8,10},{10,12},{12,14},{14,16},{16,18},{18... | collective-permute-start | bytes 294920 | tf_op jit(solution)/shard_map/ppermute | solution.py:17
  223.4 11.4 %collective-permute-start.20 = (bf16[1,384,128]{2,1,0:T(8,128)(2,1)S(1)}, bf16[1,384,128]{2,1,0:T(8,128)(2,1)S(1)}, u32[]{:S(2)}, u32[]{:S(2)}) collective-permute-start(bf16[1,384,128]{2,1,0:T(8,128)(2,1)S(1)} %fusion.69), channel_id=1, source_target_pairs={{0,4},{2,6},{4,8},{6,10},{8,12},{10,14},{12,16},{14,18},{16,20},{1... | collective-permute-start | bytes 294920 | tf_op jit(solution)/shard_map/ppermute | solution.py:17

commit v10 on v9

--- a/solution.py
+++ b/solution.py
@@ -181,7 +181,7 @@
 def match_block(state, features, block, block_rows, grid_cols):
     count, channels = block.shape
     pixels = features.shape[0]
-    tile = min(count, 1536)
+    tile = min(count, 3072)
     strip_row = jnp.repeat(block_rows, grid_cols).astype(jnp.float32)
     strip_col = (jnp.arange(count, dtype=jnp.int32) % grid_cols).astype(jnp.float32)
     weights = jnp.concatenate(

time: 237 us -> 236 us (level)
  no operation moved by 1% of the time
where the time goes in v10:
time: 236 us; the launch traced here: 235 us
  starting transfers between devices  93.7 us (40%)
  waiting for transfers between devices  61 us (26%)
  local copies, waits for them, and re-layouts  21.3 us (9%)
  other arithmetic  21 us (9%)
  Pallas kernels  20.6 us (9%)
  matrix products  15.6 us (7%)
    ppermute x8, starting transfers between devices, per_device(): got = lax.ppermute(held, 'band', pairs)  46.9 us
    ppermute x16, starting transfers between devices, passed_along(): return lax.ppermute(array, axis, pairs)  46.8 us
    ppermute x16, waiting for transfers between devices, passed_along(): return lax.ppermute(array, axis, pairs)  35.5 us
    ppermute x8, waiting for transfers between devices, per_device(): got = lax.ppermute(held, 'band', pairs)  25.5 us
    pallas_call x4, Pallas kernels, match_block(): pl.pallas_call(match_kernel, grid=(count // tile,), in_specs=[pl.BlockSpe...  20.6 us
    dot_general x50, matrix products, conv_valid(): jnp.dot(tap_slice.reshape(-1, tap_slice.shape[-1]), weight[kernel_tap], p...  15.6 us
    another operation x7, other arithmetic  6.6 us
    concatenate x3, other arithmetic, match_block(): jnp.concatenate([jnp.ones((count, 1), jnp.float32), strip_row[:, None], s...  5.56 us
  transfers between devices with their start and end apart: 24, of which 10 were waited for; matrix products, arithmetic and copies ran while one was open for 16% of the time, Pallas kernels for 5%

profile of v10, /device:TPU:7, one launch (start us, length us, event | category | flops | bytes accessed | tf_op | source)
XLA Modules:
  0.0 234.6 jit_solution(8681399852005014500)
XLA Ops:
  2.3 15.4 %collective-permute-start = (bf16[48,256]{1,0:T(8,128)(2,1)S(1)}, bf16[48,256]{1,0:T(8,128)(2,1)S(1)}, u32[]{:S(2)}, u32[]{:S(2)}) collective-permute-start(bf16[48,256]{1,0:T(8,128)(2,1)S(1)} %get-tuple-element.29), channel_id=1, source_target_pairs={{0,32},{2,34},{4,36},{6,38},{8,40},{10,42},{12,44},{14,46},{16,48}... | collective-permute-start | bytes 73736 | tf_op jit(solution)/shard_map/ppermute | solution.py:267
  19.9 2.8 %gather_fusion = s32[384]{0:T(512)S(1)} fusion(s32[256]{0:T(256)S(1)} %bitcast.414, s32[1024]{0:T(1024)S(1)} %pad_clamp_fusion.2), kind=kCustom, calls=%fused_computation.2 | custom fusion | bytes 4608 | tf_op jit(solution)/shard_map/gather | solution.py:295
  23.4 4.0 %collective-permute-start.1 = (bf16[96,256]{1,0:T(8,128)(2,1)S(1)}, bf16[96,256]{1,0:T(8,128)(2,1)S(1)}, u32[]{:S(2)}, u32[]{:S(2)}) collective-permute-start(bf16[96,256]{1,0:T(8,128)(2,1)S(1)} %pad_maximum_fusion.5), channel_id=1, source_target_pairs={{0,16},{2,18},{4,20},{6,22},{8,24},{10,26},{12,28},{14,30},{16,0},... | collective-permute-start | bytes 147464 | tf_op jit(solution)/shard_map/ppermute | solution.py:267
  28.2 4.0 %collective-permute-done.1 = bf16[96,256]{1,0:T(8,128)(2,1)S(1)} collective-permute-done((bf16[96,256]{1,0:T(8,128)(2,1)S(1)}, bf16[96,256]{1,0:T(8,128)(2,1)S(1)}, u32[]{:S(2)}, u32[]{:S(2)}) %collective-permute-start.1) | collective-permute-done | bytes 49184 | tf_op jit(solution)/shard_map/ppermute | solution.py:267
  32.2 3.3 %collective-permute-start.2 = (bf16[192,256]{1,0:T(8,128)(2,1)S(1)}, bf16[192,256]{1,0:T(8,128)(2,1)S(1)}, u32[]{:S(2)}, u32[]{:S(2)}) collective-permute-start(bf16[192,256]{1,0:T(8,128)(2,1)S(1)} %pad_maximum_fusion.4), channel_id=1, source_target_pairs={{0,8},{2,10},{4,12},{6,14},{8,0},{10,2},{12,4},{14,6},{16,24},{18,... | collective-permute-start | bytes 294920 | tf_op jit(solution)/shard_map/ppermute | solution.py:267
  36.1 3.4 %collective-permute-done.2 = bf16[192,256]{1,0:T(8,128)(2,1)S(1)} collective-permute-done((bf16[192,256]{1,0:T(8,128)(2,1)S(1)}, bf16[192,256]{1,0:T(8,128)(2,1)S(1)}, u32[]{:S(2)}, u32[]{:S(2)}) %collective-permute-start.2) | collective-permute-done | bytes 98336 | tf_op jit(solution)/shard_map/ppermute | solution.py:267
  39.5 3.0 %collective-permute-start.3 = (bf16[384,256]{1,0:T(8,128)(2,1)S(1)}, bf16[384,256]{1,0:T(8,128)(2,1)S(1)}, u32[]{:S(2)}, u32[]{:S(2)}) collective-permute-start(bf16[384,256]{1,0:T(8,128)(2,1)S(1)} %pad_maximum_fusion.2), channel_id=1, source_target_pairs={{0,256},{2,258},{4,260},{6,262},{8,264},{10,266},{12,268},{14,270}... | collective-permute-start | bytes 589832 | tf_op jit(solution)/shard_map/ppermute | solution.py:267
  43.9 3.6 %collective-permute-done.3 = bf16[384,256]{1,0:T(8,128)(2,1)S(1)} collective-permute-done((bf16[384,256]{1,0:T(8,128)(2,1)S(1)}, bf16[384,256]{1,0:T(8,128)(2,1)S(1)}, u32[]{:S(2)}, u32[]{:S(2)}) %collective-permute-start.3) | collective-permute-done | bytes 196640 | tf_op jit(solution)/shard_map/ppermute | solution.py:267
  48.2 4.8 %collective-permute-start.4 = (bf16[768,256]{1,0:T(8,128)(2,1)S(1)}, bf16[768,256]{1,0:T(8,128)(2,1)S(1)}, u32[]{:S(2)}, u32[]{:S(2)}) collective-permute-start(bf16[768,256]{1,0:T(8,128)(2,1)S(1)} %get-tuple-element.36), channel_id=1, source_target_pairs={{0,128},{2,130},{4,132},{6,134},{8,136},{10,138},{12,140},{14,142}... | collective-permute-start | bytes 1179656 | tf_op jit(solution)/shard_map/ppermute | solution.py:267
  53.7 4.5 %collective-permute-done.4 = bf16[768,256]{1,0:T(8,128)(2,1)S(1)} collective-permute-done((bf16[768,256]{1,0:T(8,128)(2,1)S(1)}, bf16[768,256]{1,0:T(8,128)(2,1)S(1)}, u32[]{:S(2)}, u32[]{:S(2)}) %collective-permute-start.4) | collective-permute-done | bytes 393248 | tf_op jit(solution)/shard_map/ppermute | solution.py:267
  59.0 3.2 %collective-permute-start.5 = (bf16[1536,256]{1,0:T(8,128)(2,1)}, bf16[1536,256]{1,0:T(8,128)(2,1)}, u32[]{:S(2)}, u32[]{:S(2)}) collective-permute-start(bf16[1536,256]{1,0:T(8,128)(2,1)} %get-tuple-element.32.s_ref), channel_id=1, source_target_pairs={{0,64},{2,66},{4,68},{6,70},{8,72},{10,74},{12,76},{14,78},{16,80}... | collective-permute-start | bytes 2359304 | tf_op jit(solution)/shard_map/ppermute | solution.py:267
  64.1 1.8 convert_element_type.262
  65.9 2.9 %convert_element_type.261 = bf16[6144,1]{1,0:T(8,128)(2,1)} reshape(bf16[128,48]{1,0:T(8,128)(2,1)S(1)} %broadcast_in_dim.75) | data formatting | bytes 24576 | tf_op jit(solution)/shard_map/convert_element_type | solution.py:185
  72.0 3.7 %shard_map.140 = (f32[384,128]{1,0:T(8,128)}, f32[384,128]{1,0:T(8,128)}) custom-call(bf16[384,256]{1,0:T(8,128)(2,1)} %bitcast.415, bf16[1536,256]{1,0:T(8,128)(2,1)} %get-tuple-element.32.s_ref, bf16[1536,128]{1,0:T(8,128)(2,1)} %get-tuple-element.31.w_ref, f32[384,128]{1,0:T(8,128)} %broadcast_in_dim.71.m_in, f32[384,128]{1,0:T(8,128)} %broadcast_in_dim.72.a_in), custom_call_target="tpu_custom_call" | custom-call | flops 603979776 | bytes 2162688 | tf_op jit(solution)/shard_map/pallas_call | solution.py:197
  77.0 3.2 %collective-permute-start.6 = (bf16[3072,256]{1,0:T(8,128)(2,1)S(1)}, bf16[3072,256]{1,0:T(8,128)(2,1)}, u32[]{:S(2)}, u32[]{:S(2)}) collective-permute-start(bf16[3072,256]{1,0:T(8,128)(2,1)S(1)} %constant_dynamic-update-slice_fusion.11), channel_id=1, source_target_pairs={{0,4},{2,62},{4,0},{6,10},{8,12},{10,6},{12,8},{14,18},{16,20},{18... | collective-permute-start | bytes 4718600 | tf_op jit(solution)/shard_map/ppermute | solution.py:267
  82.3 1.8 convolution_add_fusion.16
  84.1 1.6 fusion.6
  85.7 3.7 %shard_map.141 = (f32[384,128]{1,0:T(8,128)}, f32[384,128]{1,0:T(8,128)}) custom-call(bf16[384,256]{1,0:T(8,128)(2,1)} %bitcast.416, bf16[1536,256]{1,0:T(8,128)(2,1)} %collective-permute-done.5.s_ref, bf16[1536,128]{1,0:T(8,128)(2,1)} %get-tuple-element.30.w_ref, f32[384,128]{1,0:T(8,128)} %get-tuple-element.12.m_in, f32[384,128]{1,0:T(8,128)} %get-tuple-element.13.a_in), custom_call_target="tpu_custom_call" | custom-call | flops 603979776 | bytes 2162688 | tf_op jit(solution)/shard_map/pallas_call | solution.py:197
  89.4 10.0 %collective-permute-done.6.s_ref = bf16[3072,256]{1,0:T(8,128)(2,1)} collective-permute-done((bf16[3072,256]{1,0:T(8,128)(2,1)S(1)}, bf16[3072,256]{1,0:T(8,128)(2,1)}, u32[]{:S(2)}, u32[]{:S(2)}) %collective-permute-start.6) | collective-permute-done | bytes 1572896 | tf_op jit(solution)/shard_map/ppermute | solution.py:267
  99.4 2.2 pad_maximum_fusion
  101.6 9.9 %collective-permute-start.7 = (bf16[6144,256]{1,0:T(8,128)(2,1)S(1)}, bf16[6144,256]{1,0:T(8,128)(2,1)}, u32[]{:S(2)}, u32[]{:S(2)}) collective-permute-start(bf16[6144,256]{1,0:T(8,128)(2,1)S(1)} %pad_maximum_fusion), channel_id=1, source_target_pairs={{0,2},{2,0},{4,6},{6,4},{8,10},{10,8},{12,14},{14,12},{16,18},{18,... | collective-permute-start | bytes 9437192 | tf_op jit(solution)/shard_map/ppermute | solution.py:267
  111.5 1.8 convolution_add_fusion.15
  114.9 1.9 fusion.1
  116.7 2.5 %maximum_maximum_fusion.w_ref = bf16[6144,128]{1,0:T(8,128)(2,1)} fusion(bf16[6144,1]{1,0:T(8,128)(2,1)S(1)} %fusion.1, bf16[6144,1]{1,0:T(8,128)(2,1)S(1)} %copy-done, bf16[128]{0:T(256)(128)(2,1)S(1)} %pad.46.clone, bf16[128]{0:T(256)(128)(2,1)S(1)} %pad.43.clone), kind=kLoop, calls=%fused_computation.14 | loop fusion | flops 6291456 | bytes 1597952 | tf_op jit(solution)/shard_map/concatenate | solution.py:187
  119.3 2.0 gather_fusion.1
  121.3 5.2 %shard_map.142 = (f32[384,128]{1,0:T(8,128)}, f32[384,128]{1,0:T(8,128)}) custom-call(bf16[384,256]{1,0:T(8,128)(2,1)} %bitcast.417, bf16[3072,256]{1,0:T(8,128)(2,1)} %collective-permute-done.6.s_ref, bf16[3072,128]{1,0:T(8,128)(2,1)} %maximum_maximum_fusion.1.w_ref, f32[384,128]{1,0:T(8,128)} %get-tuple-element.15.m_in, f32[384,128]{1,0:T(8,128)} %get-tuple-element.16.a_in), custom_call_target="tpu_custom_call" | custom-call | flops 1207959552 | bytes 3342336 | tf_op jit(solution)/shard_map/pallas_call | solution.py:197
  126.5 8.0 %shard_map.143 = (f32[384,128]{1,0:T(8,128)}, f32[384,128]{1,0:T(8,128)}) custom-call(bf16[384,256]{1,0:T(8,128)(2,1)} %bitcast.418, bf16[6144,256]{1,0:T(8,128)(2,1)} %collective-permute-done.7.s_ref, bf16[6144,128]{1,0:T(8,128)(2,1)} %maximum_maximum_fusion.w_ref, f32[384,128]{1,0:T(8,128)} %get-tuple-element.18.m_in, f32[384,128]{1,0:T(8,128)} %get-tuple-element.19.a_in), custom_call_target="tpu_custom_call" | custom-call | flops 2415919104 | bytes 5701632 | tf_op jit(solution)/shard_map/pallas_call | solution.py:197
  136.0 4.1 %gather_fusion.2 = bf16[384,256]{1,0:T(8,128)(2,1)S(1)} fusion(bf16[6144,256]{1,0:T(8,128)(2,1)} %collective-permute-done.7.s_ref, s32[1024]{0:T(1024)S(1)} %get-tuple-element.61), kind=kCustom, calls=%fused_computation.1.clone | custom fusion | bytes 394752 | tf_op jit(solution)/shard_map/jit(_take)/gather | solution.py:302
  143.7 6.6 %collective-permute-start.11 = (bf16[1,384,384]{2,1,0:T(8,128)(2,1)S(1)}, bf16[1,384,384]{2,1,0:T(8,128)(2,1)S(1)}, u32[]{:S(2)}, u32[]{:S(2)}) collective-permute-start(bf16[1,384,384]{2,1,0:T(8,128)(2,1)S(1)} %pad_maximum_fusion.1), channel_id=1, source_target_pairs={{4,0},{6,2},{8,4},{10,6},{12,8},{14,10},{16,12},{18,14},{20,16},{2... | collective-permute-start | bytes 884744 | tf_op jit(solution)/shard_map/ppermute | solution.py:17
  150.3 2.2 collective-permute-start.10
  152.5 3.6 %collective-permute-start.9 = (bf16[1,384,384]{2,1,0:T(8,128)(2,1)S(1)}, bf16[1,384,384]{2,1,0:T(8,128)(2,1)S(1)}, u32[]{:S(2)}, u32[]{:S(2)}) collective-permute-start(bf16[1,384,384]{2,1,0:T(8,128)(2,1)S(1)} %pad_maximum_fusion.1), channel_id=1, source_target_pairs={{0,2},{2,4},{4,6},{6,8},{8,10},{10,12},{12,14},{14,16},{16,18},{18... | collective-permute-start | bytes 884744 | tf_op jit(solution)/shard_map/ppermute | solution.py:17
  156.1 1.9 collective-permute-start.8
  160.7 11.3 %collective-permute-done.8 = bf16[1,384,384]{2,1,0:T(8,128)(2,1)S(1)} collective-permute-done((bf16[1,384,384]{2,1,0:T(8,128)(2,1)S(1)}, bf16[1,384,384]{2,1,0:T(8,128)(2,1)S(1)}, u32[]{:S(2)}, u32[]{:S(2)}) %collective-permute-start.8) | collective-permute-done | bytes 294944 | tf_op jit(solution)/shard_map/ppermute | solution.py:17
  173.3 1.9 collective-permute-start.15
  175.2 2.2 collective-permute-start.14
  177.4 3.5 %collective-permute-start.13 = (bf16[1,384,128]{2,1,0:T(8,128)(2,1)S(1)}, bf16[1,384,128]{2,1,0:T(8,128)(2,1)S(1)}, u32[]{:S(2)}, u32[]{:S(2)}) collective-permute-start(bf16[1,384,128]{2,1,0:T(8,128)(2,1)S(1)} %fusion.71), channel_id=1, source_target_pairs={{0,2},{2,4},{4,6},{6,8},{8,10},{10,12},{12,14},{14,16},{16,18},{18... | collective-permute-start | bytes 294920 | tf_op jit(solution)/shard_map/ppermute | solution.py:17
  180.9 3.2 %collective-permute-start.12 = (bf16[1,384,128]{2,1,0:T(8,128)(2,1)S(1)}, bf16[1,384,128]{2,1,0:T(8,128)(2,1)S(1)}, u32[]{:S(2)}, u32[]{:S(2)}) collective-permute-start(bf16[1,384,128]{2,1,0:T(8,128)(2,1)S(1)} %fusion.71), channel_id=1, source_target_pairs={{0,4},{2,6},{4,8},{6,10},{8,12},{10,14},{12,16},{14,18},{16,20},{1... | collective-permute-start | bytes 294920 | tf_op jit(solution)/shard_map/ppermute | solution.py:17
  184.5 7.9 %collective-permute-done.12 = bf16[1,384,128]{2,1,0:T(8,128)(2,1)S(1)} collective-permute-done((bf16[1,384,128]{2,1,0:T(8,128)(2,1)S(1)}, bf16[1,384,128]{2,1,0:T(8,128)(2,1)S(1)}, u32[]{:S(2)}, u32[]{:S(2)}) %collective-permute-start.12) | collective-permute-done | bytes 98336 | tf_op jit(solution)/shard_map/ppermute | solution.py:17
  194.9 1.9 collective-permute-start.19
  196.9 1.9 collective-permute-start.18
  198.8 3.6 %collective-permute-start.17 = (bf16[1,384,128]{2,1,0:T(8,128)(2,1)S(1)}, bf16[1,384,128]{2,1,0:T(8,128)(2,1)S(1)}, u32[]{:S(2)}, u32[]{:S(2)}) collective-permute-start(bf16[1,384,128]{2,1,0:T(8,128)(2,1)S(1)} %get-tuple-element.59), channel_id=1, source_target_pairs={{0,2},{2,4},{4,6},{6,8},{8,10},{10,12},{12,14},{14,16},{16,18},{18... | collective-permute-start | bytes 294920 | tf_op jit(solution)/shard_map/ppermute | solution.py:17
  202.4 3.4 %collective-permute-start.16 = (bf16[1,384,128]{2,1,0:T(8,128)(2,1)S(1)}, bf16[1,384,128]{2,1,0:T(8,128)(2,1)S(1)}, u32[]{:S(2)}, u32[]{:S(2)}) collective-permute-start(bf16[1,384,128]{2,1,0:T(8,128)(2,1)S(1)} %get-tuple-element.59), channel_id=1, source_target_pairs={{0,4},{2,6},{4,8},{6,10},{8,12},{10,14},{12,16},{14,18},{16,20},{1... | collective-permute-start | bytes 294920 | tf_op jit(solution)/shard_map/ppermute | solution.py:17
  206.2 7.6 %collective-permute-done.16 = bf16[1,384,128]{2,1,0:T(8,128)(2,1)S(1)} collective-permute-done((bf16[1,384,128]{2,1,0:T(8,128)(2,1)S(1)}, bf16[1,384,128]{2,1,0:T(8,128)(2,1)S(1)}, u32[]{:S(2)}, u32[]{:S(2)}) %collective-permute-start.16) | collective-permute-done | bytes 98336 | tf_op jit(solution)/shard_map/ppermute | solution.py:17
  214.5 1.9 collective-permute-start.23
  216.5 1.9 collective-permute-start.22
  218.4 3.6 %collective-permute-start.21 = (bf16[1,384,128]{2,1,0:T(8,128)(2,1)S(1)}, bf16[1,384,128]{2,1,0:T(8,128)(2,1)S(1)}, u32[]{:S(2)}, u32[]{:S(2)}) collective-permute-start(bf16[1,384,128]{2,1,0:T(8,128)(2,1)S(1)} %fusion.69), channel_id=1, source_target_pairs={{0,2},{2,4},{4,6},{6,8},{8,10},{10,12},{12,14},{14,16},{16,18},{18... | collective-permute-start | bytes 294920 | tf_op jit(solution)/shard_map/ppermute | solution.py:17
  222.0 3.4 %collective-permute-start.20 = (bf16[1,384,128]{2,1,0:T(8,128)(2,1)S(1)}, bf16[1,384,128]{2,1,0:T(8,128)(2,1)S(1)}, u32[]{:S(2)}, u32[]{:S(2)}) collective-permute-start(bf16[1,384,128]{2,1,0:T(8,128)(2,1)S(1)} %fusion.69), channel_id=1, source_target_pairs={{0,4},{2,6},{4,8},{6,10},{8,12},{10,14},{12,16},{14,18},{16,20},{1... | collective-permute-start | bytes 294920 | tf_op jit(solution)/shard_map/ppermute | solution.py:17
  225.7 7.7 %collective-permute-done.20 = bf16[1,384,128]{2,1,0:T(8,128)(2,1)S(1)} collective-permute-done((bf16[1,384,128]{2,1,0:T(8,128)(2,1)S(1)}, bf16[1,384,128]{2,1,0:T(8,128)(2,1)S(1)}, u32[]{:S(2)}, u32[]{:S(2)}) %collective-permute-start.20) | collective-permute-done | bytes 98336 | tf_op jit(solution)/shard_map/ppermute | solution.py:17
  (140 shorter events, 33.4 us)
Async XLA Ops:
  2.3 21.1 %collective-permute-start = (bf16[48,256]{1,0:T(8,128)(2,1)S(1)}, bf16[48,256]{1,0:T(8,128)(2,1)S(1)}, u32[]{:S(2)}, u32[]{:S(2)}) collective-permute-start(bf16[48,256]{1,0:T(8,128)(2,1)S(1)} %get-tuple-element.29), channel_id=1, source_target_pairs={{0,32},{2,34},{4,36},{6,38},{8,40},{10,42},{12,44},{14,46},{16,48}... | collective-permute-start | bytes 73736 | tf_op jit(solution)/shard_map/ppermute | solution.py:267
  23.4 8.8 %collective-permute-start.1 = (bf16[96,256]{1,0:T(8,128)(2,1)S(1)}, bf16[96,256]{1,0:T(8,128)(2,1)S(1)}, u32[]{:S(2)}, u32[]{:S(2)}) collective-permute-start(bf16[96,256]{1,0:T(8,128)(2,1)S(1)} %pad_maximum_fusion.5), channel_id=1, source_target_pairs={{0,16},{2,18},{4,20},{6,22},{8,24},{10,26},{12,28},{14,30},{16,0},... | collective-permute-start | bytes 147464 | tf_op jit(solution)/shard_map/ppermute | solution.py:267
  32.2 7.3 %collective-permute-start.2 = (bf16[192,256]{1,0:T(8,128)(2,1)S(1)}, bf16[192,256]{1,0:T(8,128)(2,1)S(1)}, u32[]{:S(2)}, u32[]{:S(2)}) collective-permute-start(bf16[192,256]{1,0:T(8,128)(2,1)S(1)} %pad_maximum_fusion.4), channel_id=1, source_target_pairs={{0,8},{2,10},{4,12},{6,14},{8,0},{10,2},{12,4},{14,6},{16,24},{18,... | collective-permute-start | bytes 294920 | tf_op jit(solution)/shard_map/ppermute | solution.py:267
  39.5 7.9 %collective-permute-start.3 = (bf16[384,256]{1,0:T(8,128)(2,1)S(1)}, bf16[384,256]{1,0:T(8,128)(2,1)S(1)}, u32[]{:S(2)}, u32[]{:S(2)}) collective-permute-start(bf16[384,256]{1,0:T(8,128)(2,1)S(1)} %pad_maximum_fusion.2), channel_id=1, source_target_pairs={{0,256},{2,258},{4,260},{6,262},{8,264},{10,266},{12,268},{14,270}... | collective-permute-start | bytes 589832 | tf_op jit(solution)/shard_map/ppermute | solution.py:267
  48.2 10.0 %collective-permute-start.4 = (bf16[768,256]{1,0:T(8,128)(2,1)S(1)}, bf16[768,256]{1,0:T(8,128)(2,1)S(1)}, u32[]{:S(2)}, u32[]{:S(2)}) collective-permute-start(bf16[768,256]{1,0:T(8,128)(2,1)S(1)} %get-tuple-element.36), channel_id=1, source_target_pairs={{0,128},{2,130},{4,132},{6,134},{8,136},{10,138},{12,140},{14,142}... | collective-permute-start | bytes 1179656 | tf_op jit(solution)/shard_map/ppermute | solution.py:267
  59.0 16.8 %collective-permute-start.5 = (bf16[1536,256]{1,0:T(8,128)(2,1)}, bf16[1536,256]{1,0:T(8,128)(2,1)}, u32[]{:S(2)}, u32[]{:S(2)}) collective-permute-start(bf16[1536,256]{1,0:T(8,128)(2,1)} %get-tuple-element.32.s_ref), channel_id=1, source_target_pairs={{0,64},{2,66},{4,68},{6,70},{8,72},{10,74},{12,76},{14,78},{16,80}... | collective-permute-start | bytes 2359304 | tf_op jit(solution)/shard_map/ppermute | solution.py:267
  72.0 8.2 %copy-start.11 = (f32[3,128]{1,0:T(4,128)S(1)}, f32[3,128]{1,0:T(4,128)}, u32[]{:S(2)}) copy-start(f32[3,128]{1,0:T(4,128)} %param.20) | copy-start | bytes 4612
  72.0 8.2 %copy-start.1 = (bf16[1,384,128]{2,1,0:T(8,128)(2,1)S(1)}, bf16[1,384,128]{2,1,0:T(8,128)(2,1)}, u32[]{:S(2)}) copy-start(bf16[1,384,128]{2,1,0:T(8,128)(2,1)} %param.18) | copy-start | bytes 294916
  76.9 12.5 %copy-start.6 = (bf16[3072,256]{1,0:T(8,128)(2,1)}, bf16[3072,256]{1,0:T(8,128)(2,1)S(1)}, u32[]{:S(2)}) copy-start(bf16[3072,256]{1,0:T(8,128)(2,1)S(1)} %constant_dynamic-update-slice_fusion.11) | copy-start | bytes 4718596
  77.0 22.5 %collective-permute-start.6 = (bf16[3072,256]{1,0:T(8,128)(2,1)S(1)}, bf16[3072,256]{1,0:T(8,128)(2,1)}, u32[]{:S(2)}, u32[]{:S(2)}) collective-permute-start(bf16[3072,256]{1,0:T(8,128)(2,1)S(1)} %constant_dynamic-update-slice_fusion.11), channel_id=1, source_target_pairs={{0,4},{2,62},{4,0},{6,10},{8,12},{10,6},{12,8},{14,18},{16,20},{18... | collective-permute-start | bytes 4718600 | tf_op jit(solution)/shard_map/ppermute | solution.py:267
  89.4 22.0 %copy-start.7 = (f32[384,256]{1,0:T(8,128)S(1)}, f32[384,256]{1,0:T(8,128)}, u32[]{:S(2)}) copy-start(f32[384,256]{1,0:T(8,128)} %convolution_add_fusion.16) | copy-start | bytes 1179652
  99.4 13.8 %copy-start.3 = (bf16[3072,1]{1,0:T(8,128)(2,1)S(1)}, bf16[3072,1]{1,0:T(8,128)(2,1)}, u32[]{:S(2)}) copy-start(bf16[3072,1]{1,0:T(8,128)(2,1)} %fusion.6) | copy-start | bytes 18436
  101.6 11.7 %copy-start.2 = (bf16[3072,1]{1,0:T(8,128)(2,1)S(1)}, bf16[3072,1]{1,0:T(8,128)(2,1)}, u32[]{:S(2)}) copy-start(bf16[3072,1]{1,0:T(8,128)(2,1)} %convert_element_type.262) | copy-start | bytes 18436
  101.6 24.9 %collective-permute-start.7 = (bf16[6144,256]{1,0:T(8,128)(2,1)S(1)}, bf16[6144,256]{1,0:T(8,128)(2,1)}, u32[]{:S(2)}, u32[]{:S(2)}) collective-permute-start(bf16[6144,256]{1,0:T(8,128)(2,1)S(1)} %pad_maximum_fusion), channel_id=1, source_target_pairs={{0,2},{2,0},{4,6},{6,4},{8,10},{10,8},{12,14},{14,12},{16,18},{18,... | collective-permute-start | bytes 9437192 | tf_op jit(solution)/shard_map/ppermute | solution.py:267
  113.3 3.4 %copy-start = (bf16[6144,1]{1,0:T(8,128)(2,1)S(1)}, bf16[6144,1]{1,0:T(8,128)(2,1)}, u32[]{:S(2)}) copy-start(bf16[6144,1]{1,0:T(8,128)(2,1)} %convert_element_type.261) | copy-start | bytes 36868
  134.5 5.6 %copy-start.10 = (bf16[1,384,256]{2,1,0:T(8,128)(2,1)S(1)}, bf16[1,384,256]{2,1,0:T(8,128)(2,1)}, u32[]{:S(2)}) copy-start(bf16[1,384,256]{2,1,0:T(8,128)(2,1)} %param.15) | copy-start | bytes 589828
  134.5 6.2 %copy-start.8 = (bf16[1,384,128]{2,1,0:T(8,128)(2,1)S(1)}, bf16[1,384,128]{2,1,0:T(8,128)(2,1)}, u32[]{:S(2)}) copy-start(bf16[1,384,128]{2,1,0:T(8,128)(2,1)} %param.17) | copy-start | bytes 294916
  135.9 4.7 %copy-start.5 = (bf16[5,384,384]{2,1,0:T(8,128)(2,1)S(1)}, bf16[5,384,384]{2,1,0:T(8,128)(2,1)}, u32[]{:S(2)}) copy-start(bf16[5,384,384]{2,1,0:T(8,128)(2,1)} %param.21) | copy-start | bytes 4423684
  141.5 1.0 copy-start.9
  143.1 14.9 %copy-start.4 = (bf16[5,384,384]{2,1,0:T(8,128)(2,1)S(1)}, bf16[5,384,384]{2,1,0:T(8,128)(2,1)}, u32[]{:S(2)}) copy-start(bf16[5,384,384]{2,1,0:T(8,128)(2,1)} %param.22) | copy-start | bytes 4423684
  143.7 16.7 %collective-permute-start.11 = (bf16[1,384,384]{2,1,0:T(8,128)(2,1)S(1)}, bf16[1,384,384]{2,1,0:T(8,128)(2,1)S(1)}, u32[]{:S(2)}, u32[]{:S(2)}) collective-permute-start(bf16[1,384,384]{2,1,0:T(8,128)(2,1)S(1)} %pad_maximum_fusion.1), channel_id=1, source_target_pairs={{4,0},{6,2},{8,4},{10,6},{12,8},{14,10},{16,12},{18,14},{20,16},{2... | collective-permute-start | bytes 884744 | tf_op jit(solution)/shard_map/ppermute | solution.py:17
  150.3 22.4 %collective-permute-start.10 = (bf16[1,384,384]{2,1,0:T(8,128)(2,1)S(1)}, bf16[1,384,384]{2,1,0:T(8,128)(2,1)S(1)}, u32[]{:S(2)}, u32[]{:S(2)}) collective-permute-start(bf16[1,384,384]{2,1,0:T(8,128)(2,1)S(1)} %pad_maximum_fusion.1), channel_id=1, source_target_pairs={{2,0},{4,2},{6,4},{8,6},{10,8},{12,10},{14,12},{16,14},{18,16},{20... | collective-permute-start | bytes 884744 | tf_op jit(solution)/shard_map/ppermute | solution.py:17
  152.5 7.5 %collective-permute-start.9 = (bf16[1,384,384]{2,1,0:T(8,128)(2,1)S(1)}, bf16[1,384,384]{2,1,0:T(8,128)(2,1)S(1)}, u32[]{:S(2)}, u32[]{:S(2)}) collective-permute-start(bf16[1,384,384]{2,1,0:T(8,128)(2,1)S(1)} %pad_maximum_fusion.1), channel_id=1, source_target_pairs={{0,2},{2,4},{4,6},{6,8},{8,10},{10,12},{12,14},{14,16},{16,18},{18... | collective-permute-start | bytes 884744 | tf_op jit(solution)/shard_map/ppermute | solution.py:17
  156.1 15.9 %collective-permute-start.8 = (bf16[1,384,384]{2,1,0:T(8,128)(2,1)S(1)}, bf16[1,384,384]{2,1,0:T(8,128)(2,1)S(1)}, u32[]{:S(2)}, u32[]{:S(2)}) collective-permute-start(bf16[1,384,384]{2,1,0:T(8,128)(2,1)S(1)} %pad_maximum_fusion.1), channel_id=1, source_target_pairs={{0,4},{2,6},{4,8},{6,10},{8,12},{10,14},{12,16},{14,18},{16,20},{1... | collective-permute-start | bytes 884744 | tf_op jit(solution)/shard_map/ppermute | solution.py:17
  173.3 19.3 %collective-permute-start.15 = (bf16[1,384,128]{2,1,0:T(8,128)(2,1)S(1)}, bf16[1,384,128]{2,1,0:T(8,128)(2,1)S(1)}, u32[]{:S(2)}, u32[]{:S(2)}) collective-permute-start(bf16[1,384,128]{2,1,0:T(8,128)(2,1)S(1)} %fusion.71), channel_id=1, source_target_pairs={{4,0},{6,2},{8,4},{10,6},{12,8},{14,10},{16,12},{18,14},{20,16},{2... | collective-permute-start | bytes 294920 | tf_op jit(solution)/shard_map/ppermute | solution.py:17
  175.2 17.5 %collective-permute-start.14 = (bf16[1,384,128]{2,1,0:T(8,128)(2,1)S(1)}, bf16[1,384,128]{2,1,0:T(8,128)(2,1)S(1)}, u32[]{:S(2)}, u32[]{:S(2)}) collective-permute-start(bf16[1,384,128]{2,1,0:T(8,128)(2,1)S(1)} %fusion.71), channel_id=1, source_target_pairs={{2,0},{4,2},{6,4},{8,6},{10,8},{12,10},{14,12},{16,14},{18,16},{20... | collective-permute-start | bytes 294920 | tf_op jit(solution)/shard_map/ppermute | solution.py:17
  177.4 6.9 %collective-permute-start.13 = (bf16[1,384,128]{2,1,0:T(8,128)(2,1)S(1)}, bf16[1,384,128]{2,1,0:T(8,128)(2,1)S(1)}, u32[]{:S(2)}, u32[]{:S(2)}) collective-permute-start(bf16[1,384,128]{2,1,0:T(8,128)(2,1)S(1)} %fusion.71), channel_id=1, source_target_pairs={{0,2},{2,4},{4,6},{6,8},{8,10},{10,12},{12,14},{14,16},{16,18},{18... | collective-permute-start | bytes 294920 | tf_op jit(solution)/shard_map/ppermute | solution.py:17
  180.9 11.5 %collective-permute-start.12 = (bf16[1,384,128]{2,1,0:T(8,128)(2,1)S(1)}, bf16[1,384,128]{2,1,0:T(8,128)(2,1)S(1)}, u32[]{:S(2)}, u32[]{:S(2)}) collective-permute-start(bf16[1,384,128]{2,1,0:T(8,128)(2,1)S(1)} %fusion.71), channel_id=1, source_target_pairs={{0,4},{2,6},{4,8},{6,10},{8,12},{10,14},{12,16},{14,18},{16,20},{1... | collective-permute-start | bytes 294920 | tf_op jit(solution)/shard_map/ppermute | solution.py:17
  194.9 19.1 %collective-permute-start.19 = (bf16[1,384,128]{2,1,0:T(8,128)(2,1)S(1)}, bf16[1,384,128]{2,1,0:T(8,128)(2,1)S(1)}, u32[]{:S(2)}, u32[]{:S(2)}) collective-permute-start(bf16[1,384,128]{2,1,0:T(8,128)(2,1)S(1)} %get-tuple-element.59), channel_id=1, source_target_pairs={{4,0},{6,2},{8,4},{10,6},{12,8},{14,10},{16,12},{18,14},{20,16},{2... | collective-permute-start | bytes 294920 | tf_op jit(solution)/shard_map/ppermute | solution.py:17
  196.9 17.4 %collective-permute-start.18 = (bf16[1,384,128]{2,1,0:T(8,128)(2,1)S(1)}, bf16[1,384,128]{2,1,0:T(8,128)(2,1)S(1)}, u32[]{:S(2)}, u32[]{:S(2)}) collective-permute-start(bf16[1,384,128]{2,1,0:T(8,128)(2,1)S(1)} %get-tuple-element.59), channel_id=1, source_target_pairs={{2,0},{4,2},{6,4},{8,6},{10,8},{12,10},{14,12},{16,14},{18,16},{20... | collective-permute-start | bytes 294920 | tf_op jit(solution)/shard_map/ppermute | solution.py:17
  198.8 7.2 %collective-permute-start.17 = (bf16[1,384,128]{2,1,0:T(8,128)(2,1)S(1)}, bf16[1,384,128]{2,1,0:T(8,128)(2,1)S(1)}, u32[]{:S(2)}, u32[]{:S(2)}) collective-permute-start(bf16[1,384,128]{2,1,0:T(8,128)(2,1)S(1)} %get-tuple-element.59), channel_id=1, source_target_pairs={{0,2},{2,4},{4,6},{6,8},{8,10},{10,12},{12,14},{14,16},{16,18},{18... | collective-permute-start | bytes 294920 | tf_op jit(solution)/shard_map/ppermute | solution.py:17
  202.4 11.4 %collective-permute-start.16 = (bf16[1,384,128]{2,1,0:T(8,128)(2,1)S(1)}, bf16[1,384,128]{2,1,0:T(8,128)(2,1)S(1)}, u32[]{:S(2)}, u32[]{:S(2)}) collective-permute-start(bf16[1,384,128]{2,1,0:T(8,128)(2,1)S(1)} %get-tuple-element.59), channel_id=1, source_target_pairs={{0,4},{2,6},{4,8},{6,10},{8,12},{10,14},{12,16},{14,18},{16,20},{1... | collective-permute-start | bytes 294920 | tf_op jit(solution)/shard_map/ppermute | solution.py:17
  214.5 19.0 %collective-permute-start.23 = (bf16[1,384,128]{2,1,0:T(8,128)(2,1)S(1)}, bf16[1,384,128]{2,1,0:T(8,128)(2,1)S(1)}, u32[]{:S(2)}, u32[]{:S(2)}) collective-permute-start(bf16[1,384,128]{2,1,0:T(8,128)(2,1)S(1)} %fusion.69), channel_id=1, source_target_pairs={{4,0},{6,2},{8,4},{10,6},{12,8},{14,10},{16,12},{18,14},{20,16},{2... | collective-permute-start | bytes 294920 | tf_op jit(solution)/shard_map/ppermute | solution.py:17
  216.5 17.3 %collective-permute-start.22 = (bf16[1,384,128]{2,1,0:T(8,128)(2,1)S(1)}, bf16[1,384,128]{2,1,0:T(8,128)(2,1)S(1)}, u32[]{:S(2)}, u32[]{:S(2)}) collective-permute-start(bf16[1,384,128]{2,1,0:T(8,128)(2,1)S(1)} %fusion.69), channel_id=1, source_target_pairs={{2,0},{4,2},{6,4},{8,6},{10,8},{12,10},{14,12},{16,14},{18,16},{20... | collective-permute-start | bytes 294920 | tf_op jit(solution)/shard_map/ppermute | solution.py:17
  218.4 7.2 %collective-permute-start.21 = (bf16[1,384,128]{2,1,0:T(8,128)(2,1)S(1)}, bf16[1,384,128]{2,1,0:T(8,128)(2,1)S(1)}, u32[]{:S(2)}, u32[]{:S(2)}) collective-permute-start(bf16[1,384,128]{2,1,0:T(8,128)(2,1)S(1)} %fusion.69), channel_id=1, source_target_pairs={{0,2},{2,4},{4,6},{6,8},{8,10},{10,12},{12,14},{14,16},{16,18},{18... | collective-permute-start | bytes 294920 | tf_op jit(solution)/shard_map/ppermute | solution.py:17
  222.0 11.4 %collective-permute-start.20 = (bf16[1,384,128]{2,1,0:T(8,128)(2,1)S(1)}, bf16[1,384,128]{2,1,0:T(8,128)(2,1)S(1)}, u32[]{:S(2)}, u32[]{:S(2)}) collective-permute-start(bf16[1,384,128]{2,1,0:T(8,128)(2,1)S(1)} %fusion.69), channel_id=1, source_target_pairs={{0,4},{2,6},{4,8},{6,10},{8,12},{10,14},{12,16},{14,18},{16,20},{1... | collective-permute-start | bytes 294920 | tf_op jit(solution)/shard_map/ppermute | solution.py:17

commit v11 on v10

--- a/solution.py
+++ b/solution.py
@@ -260,7 +260,7 @@
         jnp.zeros((pixel_count, 128), jnp.float32),
     )
     held = strips.reshape(band_rows * grid_cols, channels)
-    merged = 5
+    merged = 6
     own_rows = lax.dynamic_index_in_dim(jnp.asarray(row_table), band, 0, keepdims=False)
     for step, bit in enumerate(GATHER_BITS):
         pairs = [(i, int(gather_partner(i, step, np.where))) for i in range(bands)]

time: 236 us -> 226 us (0.958)
  waiting for transfers between devices: 61 us -> 36.6 us
  starting transfers between devices: 93.7 us -> 114 us
  other arithmetic: 21 us -> 15.8 us
  local copies, waits for them, and re-layouts: 21.3 us -> 25.4 us
  matrix products: 15.6 us -> 12.4 us
    ppermute x16, waiting for transfers between devices: 35.5 us -> 10.5 us  [passed_along(): return lax.ppermute(array, axis, pairs)]
    ppermute x16, starting transfers between devices: 46.8 us -> 66.8 us  [passed_along(): return lax.ppermute(array, axis, pairs)]
    dot_general x50, matrix products: 15.6 us -> 12.4 us  [conv_valid(): jnp.dot(tap_slice.reshape(-1, tap_slice.shape[-1]), weight[kernel_tap], p...]
    pallas_call x4 -> x3, Pallas kernels: 20.6 us -> 18.3 us  [match_block(): pl.pallas_call(match_kernel, grid=(count // tile,), in_specs=[pl.BlockSpe...]
    convert_element_type x4 -> x3, local copies, waits for them, and re-layouts: 5.53 us -> 3.48 us  [match_block(): strip_row = jnp.repeat(block_rows, grid_cols).astype(jnp.float32)]
    another operation x7 -> x5, other arithmetic: 6.6 us -> 4.62 us
    concatenate x3 -> x2, other arithmetic: 5.56 us -> 4.81 us  [match_block(): jnp.concatenate([jnp.ones((count, 1), jnp.float32), strip_row[:, None], s...]
  transfers between devices with their start and end apart: 24 -> 24, of which waited for: 10 -> 13; matrix products, arithmetic and copies ran while one was open for 16% -> 15% of each run, Pallas kernels for 5% -> 5%
where the time goes in v11:
time: 226 us; the launch traced here: 224 us
  starting transfers between devices  114 us (50%)
  waiting for transfers between devices  36.6 us (16%)
  local copies, waits for them, and re-layouts  25.4 us (11%)
  Pallas kernels  18.3 us (8%)
  other arithmetic  15.8 us (7%)
  matrix products  12.4 us (5%)
    ppermute x16, starting transfers between devices, passed_along(): return lax.ppermute(array, axis, pairs)  66.8 us
    ppermute x8, starting transfers between devices, per_device(): got = lax.ppermute(held, 'band', pairs)  47.6 us
    ppermute x8, waiting for transfers between devices, per_device(): got = lax.ppermute(held, 'band', pairs)  26.2 us
    pallas_call x3, Pallas kernels, match_block(): pl.pallas_call(match_kernel, grid=(count // tile,), in_specs=[pl.BlockSpe...  18.3 us
    dot_general x50, matrix products, conv_valid(): jnp.dot(tap_slice.reshape(-1, tap_slice.shape[-1]), weight[kernel_tap], p...  12.4 us
    ppermute x16, waiting for transfers between devices, passed_along(): return lax.ppermute(array, axis, pairs)  10.5 us
    concatenate x2, other arithmetic, match_block(): jnp.concatenate([jnp.ones((count, 1), jnp.float32), strip_row[:, None], s...  4.81 us
    another operation x5, other arithmetic  4.62 us
  transfers between devices with their start and end apart: 24, of which 13 were waited for; matrix products, arithmetic and copies ran while one was open for 15% of the time, Pallas kernels for 5%

profile of v11, /device:TPU:7, one launch (start us, length us, event | category | flops | bytes accessed | tf_op | source)
XLA Modules:
  0.0 224.5 jit_solution(4440561904515088273)
XLA Ops:
  2.3 15.4 %collective-permute-start = (bf16[48,256]{1,0:T(8,128)(2,1)S(1)}, bf16[48,256]{1,0:T(8,128)(2,1)S(1)}, u32[]{:S(2)}, u32[]{:S(2)}) collective-permute-start(bf16[48,256]{1,0:T(8,128)(2,1)S(1)} %get-tuple-element.23), channel_id=1, source_target_pairs={{0,32},{2,34},{4,36},{6,38},{8,40},{10,42},{12,44},{14,46},{16,48}... | collective-permute-start | bytes 73736 | tf_op jit(solution)/shard_map/ppermute | solution.py:267
  17.7 1.3 collective-permute-done
  19.0 5.3 %collective-permute-start.1 = (bf16[96,256]{1,0:T(8,128)(2,1)S(1)}, bf16[96,256]{1,0:T(8,128)(2,1)S(1)}, u32[]{:S(2)}, u32[]{:S(2)}) collective-permute-start(bf16[96,256]{1,0:T(8,128)(2,1)S(1)} %pad_maximum_fusion.4), channel_id=1, source_target_pairs={{0,16},{2,18},{4,20},{6,22},{8,24},{10,26},{12,28},{14,30},{16,0},... | collective-permute-start | bytes 147464 | tf_op jit(solution)/shard_map/ppermute | solution.py:267
  25.0 3.3 %collective-permute-done.1 = bf16[96,256]{1,0:T(8,128)(2,1)S(1)} collective-permute-done((bf16[96,256]{1,0:T(8,128)(2,1)S(1)}, bf16[96,256]{1,0:T(8,128)(2,1)S(1)}, u32[]{:S(2)}, u32[]{:S(2)}) %collective-permute-start.1) | collective-permute-done | bytes 49184 | tf_op jit(solution)/shard_map/ppermute | solution.py:267
  28.3 2.8 %collective-permute-start.2 = (bf16[192,256]{1,0:T(8,128)(2,1)S(1)}, bf16[192,256]{1,0:T(8,128)(2,1)S(1)}, u32[]{:S(2)}, u32[]{:S(2)}) collective-permute-start(bf16[192,256]{1,0:T(8,128)(2,1)S(1)} %pad_maximum_fusion.3), channel_id=1, source_target_pairs={{0,8},{2,10},{4,12},{6,14},{8,0},{10,2},{12,4},{14,6},{16,24},{18,... | collective-permute-start | bytes 294920 | tf_op jit(solution)/shard_map/ppermute | solution.py:267
  31.7 3.8 %collective-permute-done.2 = bf16[192,256]{1,0:T(8,128)(2,1)S(1)} collective-permute-done((bf16[192,256]{1,0:T(8,128)(2,1)S(1)}, bf16[192,256]{1,0:T(8,128)(2,1)S(1)}, u32[]{:S(2)}, u32[]{:S(2)}) %collective-permute-start.2) | collective-permute-done | bytes 98336 | tf_op jit(solution)/shard_map/ppermute | solution.py:267
  35.6 3.0 %collective-permute-start.3 = (bf16[384,256]{1,0:T(8,128)(2,1)S(1)}, bf16[384,256]{1,0:T(8,128)(2,1)S(1)}, u32[]{:S(2)}, u32[]{:S(2)}) collective-permute-start(bf16[384,256]{1,0:T(8,128)(2,1)S(1)} %pad_maximum_fusion.1), channel_id=1, source_target_pairs={{0,256},{2,258},{4,260},{6,262},{8,264},{10,266},{12,268},{14,270}... | collective-permute-start | bytes 589832 | tf_op jit(solution)/shard_map/ppermute | solution.py:267
  40.0 3.5 %collective-permute-done.3 = bf16[384,256]{1,0:T(8,128)(2,1)S(1)} collective-permute-done((bf16[384,256]{1,0:T(8,128)(2,1)S(1)}, bf16[384,256]{1,0:T(8,128)(2,1)S(1)}, u32[]{:S(2)}, u32[]{:S(2)}) %collective-permute-start.3) | collective-permute-done | bytes 196640 | tf_op jit(solution)/shard_map/ppermute | solution.py:267
  44.3 4.8 %collective-permute-start.4 = (bf16[768,256]{1,0:T(8,128)(2,1)S(1)}, bf16[768,256]{1,0:T(8,128)(2,1)S(1)}, u32[]{:S(2)}, u32[]{:S(2)}) collective-permute-start(bf16[768,256]{1,0:T(8,128)(2,1)S(1)} %get-tuple-element.34), channel_id=1, source_target_pairs={{0,128},{2,130},{4,132},{6,134},{8,136},{10,138},{12,140},{14,142}... | collective-permute-start | bytes 1179656 | tf_op jit(solution)/shard_map/ppermute | solution.py:267
  50.6 3.8 %collective-permute-done.4 = bf16[768,256]{1,0:T(8,128)(2,1)S(1)} collective-permute-done((bf16[768,256]{1,0:T(8,128)(2,1)S(1)}, bf16[768,256]{1,0:T(8,128)(2,1)S(1)}, u32[]{:S(2)}, u32[]{:S(2)}) %collective-permute-start.4) | collective-permute-done | bytes 393248 | tf_op jit(solution)/shard_map/ppermute | solution.py:267
  55.3 3.2 %collective-permute-start.5 = (bf16[1536,256]{1,0:T(8,128)(2,1)S(1)}, bf16[1536,256]{1,0:T(8,128)(2,1)S(1)}, u32[]{:S(2)}, u32[]{:S(2)}) collective-permute-start(bf16[1536,256]{1,0:T(8,128)(2,1)S(1)} %get-tuple-element.30), channel_id=1, source_target_pairs={{0,64},{2,66},{4,68},{6,70},{8,72},{10,74},{12,76},{14,78},{16,80}... | collective-permute-start | bytes 2359304 | tf_op jit(solution)/shard_map/ppermute | solution.py:267
  59.2 2.8 %gather_fusion = s32[384]{0:T(512)S(1)} fusion(s32[256]{0:T(256)S(1)} %bitcast.411, s32[1024]{0:T(1024)S(1)} %pad_clamp_fusion.2), kind=kCustom, calls=%fused_computation.2 | custom fusion | bytes 4608 | tf_op jit(solution)/shard_map/gather | solution.py:295
  63.2 8.3 %collective-permute-done.5 = bf16[1536,256]{1,0:T(8,128)(2,1)S(1)} collective-permute-done((bf16[1536,256]{1,0:T(8,128)(2,1)S(1)}, bf16[1536,256]{1,0:T(8,128)(2,1)S(1)}, u32[]{:S(2)}, u32[]{:S(2)}) %collective-permute-start.5) | collective-permute-done | bytes 786464 | tf_op jit(solution)/shard_map/ppermute | solution.py:267
  72.8 7.4 %collective-permute-start.6 = (bf16[3072,256]{1,0:T(8,128)(2,1)}, bf16[3072,256]{1,0:T(8,128)(2,1)}, u32[]{:S(2)}, u32[]{:S(2)}) collective-permute-start(bf16[3072,256]{1,0:T(8,128)(2,1)} %get-tuple-element.26.s_ref), channel_id=1, source_target_pairs={{0,4},{2,62},{4,0},{6,10},{8,12},{10,6},{12,8},{14,18},{16,20},{18... | collective-permute-start | bytes 4718600 | tf_op jit(solution)/shard_map/ppermute | solution.py:267
  83.0 1.8 convert_element_type.223
  84.8 1.8 fusion.156
  87.2 2.3 %maximum_maximum_fusion.2 = (bf16[3072,128]{1,0:T(8,128)(2,1)}, bf16[3072,128]{1,0:T(8,128)(2,1)}) fusion(bf16[3072,1]{1,0:T(8,128)(2,1)S(1)} %convert_element_type.224, bf16[3072,1]{1,0:T(8,128)(2,1)S(1)} %fusion.6, bf16[128]{0:T(256)(128)(2,1)S(1)} %pad.40.clone, bf16[128]{0:T(256)(128)(2,1)S(1)} %pad.37.clone, bf16[3072,1]{1,0:T(8,128)(2,1)S(1)} %convert_element_type.222), kind=kLoop, calls=%fused_computation.103 | loop fusion | flops 5111808 | bytes 1591808 | tf_op jit(solution)/shard_map/concatenate | solution.py:187
  90.9 5.2 %shard_map.131 = (f32[384,128]{1,0:T(8,128)}, f32[384,128]{1,0:T(8,128)}) custom-call(bf16[384,256]{1,0:T(8,128)(2,1)} %bitcast.412, bf16[3072,256]{1,0:T(8,128)(2,1)} %get-tuple-element.26.s_ref, bf16[3072,128]{1,0:T(8,128)(2,1)} %get-tuple-element.25.w_ref, f32[384,128]{1,0:T(8,128)} %broadcast_in_dim.60.m_in, f32[384,128]{1,0:T(8,128)} %broadcast_in_dim.61.a_in), custom_call_target="tpu_custom_call" | custom-call | flops 1207959552 | bytes 3342336 | tf_op jit(solution)/shard_map/pallas_call | solution.py:197
  96.1 2.2 collective-permute-done.6.s_ref
  98.3 2.9 %constant_dynamic-update-slice_fusion.18 = bf16[6144,256]{1,0:T(8,128)(2,1)} fusion(bf16[6144,256]{1,0:T(8,128)(2,1)} %get-tuple-element.27, bf16[3072,256]{1,0:T(8,128)(2,1)} %collective-permute-done.6.s_ref), kind=kLoop, calls=%fused_computation.312 | loop fusion | bytes 3145728 | tf_op jit(solution)/shard_map/concatenate | solution.py:281
  101.2 5.6 %collective-permute-start.7 = (bf16[6144,256]{1,0:T(8,128)(2,1)}, bf16[6144,256]{1,0:T(8,128)(2,1)}, u32[]{:S(2)}, u32[]{:S(2)}) collective-permute-start(bf16[6144,256]{1,0:T(8,128)(2,1)} %constant_dynamic-update-slice_fusion.18), channel_id=1, source_target_pairs={{0,2},{2,0},{4,6},{6,4},{8,10},{10,8},{12,14},{14,12},{16,18},{18,... | collective-permute-start | bytes 9437192 | tf_op jit(solution)/shard_map/ppermute | solution.py:267
  108.0 1.9 fusion.1
  109.9 2.5 %maximum_maximum_fusion.w_ref = bf16[6144,128]{1,0:T(8,128)(2,1)} fusion(bf16[6144,1]{1,0:T(8,128)(2,1)S(1)} %fusion.1, bf16[6144,1]{1,0:T(8,128)(2,1)S(1)} %convert_element_type.223, bf16[128]{0:T(256)(128)(2,1)S(1)} %pad.40.clone, bf16[128]{0:T(256)(128)(2,1)S(1)} %pad.37.clone), kind=kLoop, calls=%fused_computation.13 | loop fusion | flops 6291456 | bytes 1597952 | tf_op jit(solution)/shard_map/concatenate | solution.py:187
  112.4 4.0 %gather_fusion.1 = bf16[384,256]{1,0:T(8,128)(2,1)S(1)} fusion(bf16[6144,256]{1,0:T(8,128)(2,1)} %constant_dynamic-update-slice_fusion.18, s32[1024]{0:T(1024)S(1)} %get-tuple-element.64), kind=kCustom, calls=%fused_computation.clone | custom fusion | bytes 394752 | tf_op jit(solution)/shard_map/jit(_take)/gather | solution.py:301
  116.4 5.2 %shard_map.132 = (f32[384,128]{1,0:T(8,128)}, f32[384,128]{1,0:T(8,128)}) custom-call(bf16[384,256]{1,0:T(8,128)(2,1)} %bitcast.413, bf16[3072,256]{1,0:T(8,128)(2,1)} %collective-permute-done.6.s_ref, bf16[3072,128]{1,0:T(8,128)(2,1)} %get-tuple-element.24.w_ref, f32[384,128]{1,0:T(8,128)} %get-tuple-element.9.m_in, f32[384,128]{1,0:T(8,128)} %get-tuple-element.10.a_in), custom_call_target="tpu_custom_call" | custom-call | flops 1207959552 | bytes 3342336 | tf_op jit(solution)/shard_map/pallas_call | solution.py:197
  121.6 8.0 %shard_map.133 = (f32[384,128]{1,0:T(8,128)}, f32[384,128]{1,0:T(8,128)}) custom-call(bf16[384,256]{1,0:T(8,128)(2,1)} %bitcast.414, bf16[6144,256]{1,0:T(8,128)(2,1)} %collective-permute-done.7.s_ref, bf16[6144,128]{1,0:T(8,128)(2,1)} %maximum_maximum_fusion.w_ref, f32[384,128]{1,0:T(8,128)} %get-tuple-element.12.m_in, f32[384,128]{1,0:T(8,128)} %get-tuple-element.13.a_in), custom_call_target="tpu_custom_call" | custom-call | flops 2415919104 | bytes 5701632 | tf_op jit(solution)/shard_map/pallas_call | solution.py:197
  129.6 1.5 subtract_reduce_fusion
  131.2 4.2 %gather_fusion.2 = bf16[384,256]{1,0:T(8,128)(2,1)S(1)} fusion(bf16[6144,256]{1,0:T(8,128)(2,1)} %collective-permute-done.7.s_ref, s32[1024]{0:T(1024)S(1)} %get-tuple-element.63), kind=kCustom, calls=%fused_computation.1.clone | custom fusion | bytes 394752 | tf_op jit(solution)/shard_map/jit(_take)/gather | solution.py:302
  138.6 1.9 collective-permute-start.9
  140.5 2.3 %collective-permute-start.8 = (bf16[1,384,384]{2,1,0:T(8,128)(2,1)S(1)}, bf16[1,384,384]{2,1,0:T(8,128)(2,1)S(1)}, u32[]{:S(2)}, u32[]{:S(2)}) collective-permute-start(bf16[1,384,384]{2,1,0:T(8,128)(2,1)S(1)} %pad_maximum_fusion), channel_id=1, source_target_pairs={{0,4},{2,6},{4,8},{6,10},{8,12},{10,14},{12,16},{14,18},{16,20},{1... | collective-permute-start | bytes 884744 | tf_op jit(solution)/shard_map/ppermute | solution.py:17
  142.9 10.1 %collective-permute-start.11 = (bf16[1,384,384]{2,1,0:T(8,128)(2,1)S(1)}, bf16[1,384,384]{2,1,0:T(8,128)(2,1)S(1)}, u32[]{:S(2)}, u32[]{:S(2)}) collective-permute-start(bf16[1,384,384]{2,1,0:T(8,128)(2,1)S(1)} %pad_maximum_fusion), channel_id=1, source_target_pairs={{4,0},{6,2},{8,4},{10,6},{12,8},{14,10},{16,12},{18,14},{20,16},{2... | collective-permute-start | bytes 884744 | tf_op jit(solution)/shard_map/ppermute | solution.py:17
  153.0 2.7 %collective-permute-start.10 = (bf16[1,384,384]{2,1,0:T(8,128)(2,1)S(1)}, bf16[1,384,384]{2,1,0:T(8,128)(2,1)S(1)}, u32[]{:S(2)}, u32[]{:S(2)}) collective-permute-start(bf16[1,384,384]{2,1,0:T(8,128)(2,1)S(1)} %pad_maximum_fusion), channel_id=1, source_target_pairs={{2,0},{4,2},{6,4},{8,6},{10,8},{12,10},{14,12},{16,14},{18,16},{20... | collective-permute-start | bytes 884744 | tf_op jit(solution)/shard_map/ppermute | solution.py:17
  157.2 1.6 collective-permute-done.11
  161.6 1.9 collective-permute-start.13
  163.7 1.9 collective-permute-start.12
  165.6 11.4 %collective-permute-start.15 = (bf16[1,384,128]{2,1,0:T(8,128)(2,1)S(1)}, bf16[1,384,128]{2,1,0:T(8,128)(2,1)S(1)}, u32[]{:S(2)}, u32[]{:S(2)}) collective-permute-start(bf16[1,384,128]{2,1,0:T(8,128)(2,1)S(1)} %fusion.66), channel_id=1, source_target_pairs={{4,0},{6,2},{8,4},{10,6},{12,8},{14,10},{16,12},{18,14},{20,16},{2... | collective-permute-start | bytes 294920 | tf_op jit(solution)/shard_map/ppermute | solution.py:17
  177.1 2.7 %collective-permute-start.14 = (bf16[1,384,128]{2,1,0:T(8,128)(2,1)S(1)}, bf16[1,384,128]{2,1,0:T(8,128)(2,1)S(1)}, u32[]{:S(2)}, u32[]{:S(2)}) collective-permute-start(bf16[1,384,128]{2,1,0:T(8,128)(2,1)S(1)} %fusion.66), channel_id=1, source_target_pairs={{2,0},{4,2},{6,4},{8,6},{10,8},{12,10},{14,12},{16,14},{18,16},{20... | collective-permute-start | bytes 294920 | tf_op jit(solution)/shard_map/ppermute | solution.py:17
  180.3 2.7 %collective-permute-done.14 = bf16[1,384,128]{2,1,0:T(8,128)(2,1)S(1)} collective-permute-done((bf16[1,384,128]{2,1,0:T(8,128)(2,1)S(1)}, bf16[1,384,128]{2,1,0:T(8,128)(2,1)S(1)}, u32[]{:S(2)}, u32[]{:S(2)}) %collective-permute-start.14) | collective-permute-done | bytes 98336 | tf_op jit(solution)/shard_map/ppermute | solution.py:17
  185.2 1.9 collective-permute-start.17
  187.3 1.9 collective-permute-start.16
  189.2 9.1 %collective-permute-start.19 = (bf16[1,384,128]{2,1,0:T(8,128)(2,1)S(1)}, bf16[1,384,128]{2,1,0:T(8,128)(2,1)S(1)}, u32[]{:S(2)}, u32[]{:S(2)}) collective-permute-start(bf16[1,384,128]{2,1,0:T(8,128)(2,1)S(1)} %get-tuple-element.61), channel_id=1, source_target_pairs={{4,0},{6,2},{8,4},{10,6},{12,8},{14,10},{16,12},{18,14},{20,16},{2... | collective-permute-start | bytes 294920 | tf_op jit(solution)/shard_map/ppermute | solution.py:17
  198.3 3.0 %collective-permute-start.18 = (bf16[1,384,128]{2,1,0:T(8,128)(2,1)S(1)}, bf16[1,384,128]{2,1,0:T(8,128)(2,1)S(1)}, u32[]{:S(2)}, u32[]{:S(2)}) collective-permute-start(bf16[1,384,128]{2,1,0:T(8,128)(2,1)S(1)} %get-tuple-element.61), channel_id=1, source_target_pairs={{2,0},{4,2},{6,4},{8,6},{10,8},{12,10},{14,12},{16,14},{18,16},{20... | collective-permute-start | bytes 294920 | tf_op jit(solution)/shard_map/ppermute | solution.py:17
  201.9 2.4 %collective-permute-done.18 = bf16[1,384,128]{2,1,0:T(8,128)(2,1)S(1)} collective-permute-done((bf16[1,384,128]{2,1,0:T(8,128)(2,1)S(1)}, bf16[1,384,128]{2,1,0:T(8,128)(2,1)S(1)}, u32[]{:S(2)}, u32[]{:S(2)}) %collective-permute-start.18) | collective-permute-done | bytes 98336 | tf_op jit(solution)/shard_map/ppermute | solution.py:17
  204.6 1.9 collective-permute-start.21
  206.7 1.9 collective-permute-start.20
  208.6 9.1 %collective-permute-start.23 = (bf16[1,384,128]{2,1,0:T(8,128)(2,1)S(1)}, bf16[1,384,128]{2,1,0:T(8,128)(2,1)S(1)}, u32[]{:S(2)}, u32[]{:S(2)}) collective-permute-start(bf16[1,384,128]{2,1,0:T(8,128)(2,1)S(1)} %fusion.64), channel_id=1, source_target_pairs={{4,0},{6,2},{8,4},{10,6},{12,8},{14,10},{16,12},{18,14},{20,16},{2... | collective-permute-start | bytes 294920 | tf_op jit(solution)/shard_map/ppermute | solution.py:17
  217.7 3.0 %collective-permute-start.22 = (bf16[1,384,128]{2,1,0:T(8,128)(2,1)S(1)}, bf16[1,384,128]{2,1,0:T(8,128)(2,1)S(1)}, u32[]{:S(2)}, u32[]{:S(2)}) collective-permute-start(bf16[1,384,128]{2,1,0:T(8,128)(2,1)S(1)} %fusion.64), channel_id=1, source_target_pairs={{2,0},{4,2},{6,4},{8,6},{10,8},{12,10},{14,12},{16,14},{18,16},{20... | collective-permute-start | bytes 294920 | tf_op jit(solution)/shard_map/ppermute | solution.py:17
  221.2 2.5 %collective-permute-done.22 = bf16[1,384,128]{2,1,0:T(8,128)(2,1)S(1)} collective-permute-done((bf16[1,384,128]{2,1,0:T(8,128)(2,1)S(1)}, bf16[1,384,128]{2,1,0:T(8,128)(2,1)S(1)}, u32[]{:S(2)}, u32[]{:S(2)}) %collective-permute-start.22) | collective-permute-done | bytes 98336 | tf_op jit(solution)/shard_map/ppermute | solution.py:17
  (140 shorter events, 29.4 us)
Async XLA Ops:
  1.7 48.8 %copy-start.6 = (s32[2,1,384]{2,1,0:T(1,128)S(1)}, s32[2,1,384]{2,1,0:T(1,128)}, u32[]{:S(2)}) copy-start(s32[2,1,384]{2,1,0:T(1,128)} %param.18) | copy-start | bytes 9220
  2.3 16.7 %collective-permute-start = (bf16[48,256]{1,0:T(8,128)(2,1)S(1)}, bf16[48,256]{1,0:T(8,128)(2,1)S(1)}, u32[]{:S(2)}, u32[]{:S(2)}) collective-permute-start(bf16[48,256]{1,0:T(8,128)(2,1)S(1)} %get-tuple-element.23), channel_id=1, source_target_pairs={{0,32},{2,34},{4,36},{6,38},{8,40},{10,42},{12,44},{14,46},{16,48}... | collective-permute-start | bytes 73736 | tf_op jit(solution)/shard_map/ppermute | solution.py:267
  19.0 9.3 %collective-permute-start.1 = (bf16[96,256]{1,0:T(8,128)(2,1)S(1)}, bf16[96,256]{1,0:T(8,128)(2,1)S(1)}, u32[]{:S(2)}, u32[]{:S(2)}) collective-permute-start(bf16[96,256]{1,0:T(8,128)(2,1)S(1)} %pad_maximum_fusion.4), channel_id=1, source_target_pairs={{0,16},{2,18},{4,20},{6,22},{8,24},{10,26},{12,28},{14,30},{16,0},... | collective-permute-start | bytes 147464 | tf_op jit(solution)/shard_map/ppermute | solution.py:267
  28.3 7.2 %collective-permute-start.2 = (bf16[192,256]{1,0:T(8,128)(2,1)S(1)}, bf16[192,256]{1,0:T(8,128)(2,1)S(1)}, u32[]{:S(2)}, u32[]{:S(2)}) collective-permute-start(bf16[192,256]{1,0:T(8,128)(2,1)S(1)} %pad_maximum_fusion.3), channel_id=1, source_target_pairs={{0,8},{2,10},{4,12},{6,14},{8,0},{10,2},{12,4},{14,6},{16,24},{18,... | collective-permute-start | bytes 294920 | tf_op jit(solution)/shard_map/ppermute | solution.py:267
  35.6 7.9 %collective-permute-start.3 = (bf16[384,256]{1,0:T(8,128)(2,1)S(1)}, bf16[384,256]{1,0:T(8,128)(2,1)S(1)}, u32[]{:S(2)}, u32[]{:S(2)}) collective-permute-start(bf16[384,256]{1,0:T(8,128)(2,1)S(1)} %pad_maximum_fusion.1), channel_id=1, source_target_pairs={{0,256},{2,258},{4,260},{6,262},{8,264},{10,266},{12,268},{14,270}... | collective-permute-start | bytes 589832 | tf_op jit(solution)/shard_map/ppermute | solution.py:267
  44.3 10.0 %collective-permute-start.4 = (bf16[768,256]{1,0:T(8,128)(2,1)S(1)}, bf16[768,256]{1,0:T(8,128)(2,1)S(1)}, u32[]{:S(2)}, u32[]{:S(2)}) collective-permute-start(bf16[768,256]{1,0:T(8,128)(2,1)S(1)} %get-tuple-element.34), channel_id=1, source_target_pairs={{0,128},{2,130},{4,132},{6,134},{8,136},{10,138},{12,140},{14,142}... | collective-permute-start | bytes 1179656 | tf_op jit(solution)/shard_map/ppermute | solution.py:267
  54.3 7.7 %copy-start.14 = (f32[3,128]{1,0:T(4,128)S(1)}, f32[3,128]{1,0:T(4,128)}, u32[]{:S(2)}) copy-start(f32[3,128]{1,0:T(4,128)} %param.19) | copy-start | bytes 4612
  55.3 16.2 %collective-permute-start.5 = (bf16[1536,256]{1,0:T(8,128)(2,1)S(1)}, bf16[1536,256]{1,0:T(8,128)(2,1)S(1)}, u32[]{:S(2)}, u32[]{:S(2)}) collective-permute-start(bf16[1536,256]{1,0:T(8,128)(2,1)S(1)} %get-tuple-element.30), channel_id=1, source_target_pairs={{0,64},{2,66},{4,68},{6,70},{8,72},{10,74},{12,76},{14,78},{16,80}... | collective-permute-start | bytes 2359304 | tf_op jit(solution)/shard_map/ppermute | solution.py:267
  72.8 25.5 %collective-permute-start.6 = (bf16[3072,256]{1,0:T(8,128)(2,1)}, bf16[3072,256]{1,0:T(8,128)(2,1)}, u32[]{:S(2)}, u32[]{:S(2)}) collective-permute-start(bf16[3072,256]{1,0:T(8,128)(2,1)} %get-tuple-element.26.s_ref), channel_id=1, source_target_pairs={{0,4},{2,62},{4,0},{6,10},{8,12},{10,6},{12,8},{14,18},{16,20},{18... | collective-permute-start | bytes 4718600 | tf_op jit(solution)/shard_map/ppermute | solution.py:267
  81.0 3.8 %copy-start = (bf16[1,384,128]{2,1,0:T(8,128)(2,1)S(1)}, bf16[1,384,128]{2,1,0:T(8,128)(2,1)}, u32[]{:S(2)}) copy-start(bf16[1,384,128]{2,1,0:T(8,128)(2,1)} %param.17) | copy-start | bytes 294916
  98.3 9.1 %copy-start.2 = (bf16[5,384,384]{2,1,0:T(8,128)(2,1)S(1)}, bf16[5,384,384]{2,1,0:T(8,128)(2,1)}, u32[]{:S(2)}) copy-start(bf16[5,384,384]{2,1,0:T(8,128)(2,1)} %param.20) | copy-start | bytes 4423684
  98.3 9.1 %copy-start.3 = (f32[384,256]{1,0:T(8,128)S(1)}, f32[384,256]{1,0:T(8,128)}, u32[]{:S(2)}) copy-start(f32[384,256]{1,0:T(8,128)} %fusion.156) | copy-start | bytes 1179652
  101.2 20.4 %collective-permute-start.7 = (bf16[6144,256]{1,0:T(8,128)(2,1)}, bf16[6144,256]{1,0:T(8,128)(2,1)}, u32[]{:S(2)}, u32[]{:S(2)}) collective-permute-start(bf16[6144,256]{1,0:T(8,128)(2,1)} %constant_dynamic-update-slice_fusion.18), channel_id=1, source_target_pairs={{0,2},{2,0},{4,6},{6,4},{8,10},{10,8},{12,14},{14,12},{16,18},{18,... | collective-permute-start | bytes 9437192 | tf_op jit(solution)/shard_map/ppermute | solution.py:267
  129.5 5.8 %copy-start.5 = (bf16[1,384,256]{2,1,0:T(8,128)(2,1)S(1)}, bf16[1,384,256]{2,1,0:T(8,128)(2,1)}, u32[]{:S(2)}) copy-start(bf16[1,384,256]{2,1,0:T(8,128)(2,1)} %param.14) | copy-start | bytes 589828
  129.5 5.8 %copy-start.11 = (pred[384]{0:T(512)(128)(4,1)S(1)}, pred[384]{0:T(512)(128)(4,1)}, u32[]{:S(2)}) copy-start(pred[384]{0:T(512)(128)(4,1)} %get-tuple-element.19) | copy-start | bytes 1156
  129.5 5.8 %copy-start.12 = (pred[384]{0:T(512)(128)(4,1)S(1)}, pred[384]{0:T(512)(128)(4,1)}, u32[]{:S(2)}) copy-start(pred[384]{0:T(512)(128)(4,1)} %get-tuple-element.53) | copy-start | bytes 1156
  129.5 5.8 %copy-start.13 = (pred[384]{0:T(512)(128)(4,1)S(1)}, pred[384]{0:T(512)(128)(4,1)}, u32[]{:S(2)}) copy-start(pred[384]{0:T(512)(128)(4,1)} %get-tuple-element.54) | copy-start | bytes 1156
  129.6 6.1 %copy-start.10 = (pred[384]{0:T(512)(128)(4,1)S(1)}, pred[384]{0:T(512)(128)(4,1)}, u32[]{:S(2)}) copy-start(pred[384]{0:T(512)(128)(4,1)} %get-tuple-element.21) | copy-start | bytes 1156
  129.6 6.2 %copy-start.7 = (f32[128]{0:T(128)S(1)}, f32[128]{0:T(128)}, u32[]{:S(2)}) copy-start(f32[128]{0:T(128)} %get-tuple-element.50) | copy-start | bytes 1540
  129.6 6.2 %copy-start.8 = (f32[128]{0:T(128)S(1)}, f32[128]{0:T(128)}, u32[]{:S(2)}) copy-start(f32[128]{0:T(128)} %get-tuple-element.51) | copy-start | bytes 1540
  129.6 6.2 %copy-start.9 = (f32[128]{0:T(128)S(1)}, f32[128]{0:T(128)}, u32[]{:S(2)}) copy-start(f32[128]{0:T(128)} %get-tuple-element.52) | copy-start | bytes 1540
  129.6 6.4 %copy-start.4 = (bf16[1,384,128]{2,1,0:T(8,128)(2,1)S(1)}, bf16[1,384,128]{2,1,0:T(8,128)(2,1)}, u32[]{:S(2)}) copy-start(bf16[1,384,128]{2,1,0:T(8,128)(2,1)} %param.16) | copy-start | bytes 294916
  138.0 17.7 %copy-start.1 = (bf16[5,384,384]{2,1,0:T(8,128)(2,1)S(1)}, bf16[5,384,384]{2,1,0:T(8,128)(2,1)}, u32[]{:S(2)}) copy-start(bf16[5,384,384]{2,1,0:T(8,128)(2,1)} %param.21) | copy-start | bytes 4423684
  138.6 18.1 %collective-permute-start.9 = (bf16[1,384,384]{2,1,0:T(8,128)(2,1)S(1)}, bf16[1,384,384]{2,1,0:T(8,128)(2,1)S(1)}, u32[]{:S(2)}, u32[]{:S(2)}) collective-permute-start(bf16[1,384,384]{2,1,0:T(8,128)(2,1)S(1)} %pad_maximum_fusion), channel_id=1, source_target_pairs={{0,2},{2,4},{4,6},{6,8},{8,10},{10,12},{12,14},{14,16},{16,18},{18... | collective-permute-start | bytes 884744 | tf_op jit(solution)/shard_map/ppermute | solution.py:17
  140.5 19.0 %collective-permute-start.8 = (bf16[1,384,384]{2,1,0:T(8,128)(2,1)S(1)}, bf16[1,384,384]{2,1,0:T(8,128)(2,1)S(1)}, u32[]{:S(2)}, u32[]{:S(2)}) collective-permute-start(bf16[1,384,384]{2,1,0:T(8,128)(2,1)S(1)} %pad_maximum_fusion), channel_id=1, source_target_pairs={{0,4},{2,6},{4,8},{6,10},{8,12},{10,14},{12,16},{14,18},{16,20},{1... | collective-permute-start | bytes 884744 | tf_op jit(solution)/shard_map/ppermute | solution.py:17
  142.9 16.0 %collective-permute-start.11 = (bf16[1,384,384]{2,1,0:T(8,128)(2,1)S(1)}, bf16[1,384,384]{2,1,0:T(8,128)(2,1)S(1)}, u32[]{:S(2)}, u32[]{:S(2)}) collective-permute-start(bf16[1,384,384]{2,1,0:T(8,128)(2,1)S(1)} %pad_maximum_fusion), channel_id=1, source_target_pairs={{4,0},{6,2},{8,4},{10,6},{12,8},{14,10},{16,12},{18,14},{20,16},{2... | collective-permute-start | bytes 884744 | tf_op jit(solution)/shard_map/ppermute | solution.py:17
  153.0 8.0 %collective-permute-start.10 = (bf16[1,384,384]{2,1,0:T(8,128)(2,1)S(1)}, bf16[1,384,384]{2,1,0:T(8,128)(2,1)S(1)}, u32[]{:S(2)}, u32[]{:S(2)}) collective-permute-start(bf16[1,384,384]{2,1,0:T(8,128)(2,1)S(1)} %pad_maximum_fusion), channel_id=1, source_target_pairs={{2,0},{4,2},{6,4},{8,6},{10,8},{12,10},{14,12},{16,14},{18,16},{20... | collective-permute-start | bytes 884744 | tf_op jit(solution)/shard_map/ppermute | solution.py:17
  161.6 18.2 %collective-permute-start.13 = (bf16[1,384,128]{2,1,0:T(8,128)(2,1)S(1)}, bf16[1,384,128]{2,1,0:T(8,128)(2,1)S(1)}, u32[]{:S(2)}, u32[]{:S(2)}) collective-permute-start(bf16[1,384,128]{2,1,0:T(8,128)(2,1)S(1)} %fusion.66), channel_id=1, source_target_pairs={{0,2},{2,4},{4,6},{6,8},{8,10},{10,12},{12,14},{14,16},{16,18},{18... | collective-permute-start | bytes 294920 | tf_op jit(solution)/shard_map/ppermute | solution.py:17
  163.7 16.2 %collective-permute-start.12 = (bf16[1,384,128]{2,1,0:T(8,128)(2,1)S(1)}, bf16[1,384,128]{2,1,0:T(8,128)(2,1)S(1)}, u32[]{:S(2)}, u32[]{:S(2)}) collective-permute-start(bf16[1,384,128]{2,1,0:T(8,128)(2,1)S(1)} %fusion.66), channel_id=1, source_target_pairs={{0,4},{2,6},{4,8},{6,10},{8,12},{10,14},{12,16},{14,18},{16,20},{1... | collective-permute-start | bytes 294920 | tf_op jit(solution)/shard_map/ppermute | solution.py:17
  165.6 14.5 %collective-permute-start.15 = (bf16[1,384,128]{2,1,0:T(8,128)(2,1)S(1)}, bf16[1,384,128]{2,1,0:T(8,128)(2,1)S(1)}, u32[]{:S(2)}, u32[]{:S(2)}) collective-permute-start(bf16[1,384,128]{2,1,0:T(8,128)(2,1)S(1)} %fusion.66), channel_id=1, source_target_pairs={{4,0},{6,2},{8,4},{10,6},{12,8},{14,10},{16,12},{18,14},{20,16},{2... | collective-permute-start | bytes 294920 | tf_op jit(solution)/shard_map/ppermute | solution.py:17
  177.1 5.9 %collective-permute-start.14 = (bf16[1,384,128]{2,1,0:T(8,128)(2,1)S(1)}, bf16[1,384,128]{2,1,0:T(8,128)(2,1)S(1)}, u32[]{:S(2)}, u32[]{:S(2)}) collective-permute-start(bf16[1,384,128]{2,1,0:T(8,128)(2,1)S(1)} %fusion.66), channel_id=1, source_target_pairs={{2,0},{4,2},{6,4},{8,6},{10,8},{12,10},{14,12},{16,14},{18,16},{20... | collective-permute-start | bytes 294920 | tf_op jit(solution)/shard_map/ppermute | solution.py:17
  185.2 16.1 %collective-permute-start.17 = (bf16[1,384,128]{2,1,0:T(8,128)(2,1)S(1)}, bf16[1,384,128]{2,1,0:T(8,128)(2,1)S(1)}, u32[]{:S(2)}, u32[]{:S(2)}) collective-permute-start(bf16[1,384,128]{2,1,0:T(8,128)(2,1)S(1)} %get-tuple-element.61), channel_id=1, source_target_pairs={{0,2},{2,4},{4,6},{6,8},{8,10},{10,12},{12,14},{14,16},{16,18},{18... | collective-permute-start | bytes 294920 | tf_op jit(solution)/shard_map/ppermute | solution.py:17
  187.3 14.2 %collective-permute-start.16 = (bf16[1,384,128]{2,1,0:T(8,128)(2,1)S(1)}, bf16[1,384,128]{2,1,0:T(8,128)(2,1)S(1)}, u32[]{:S(2)}, u32[]{:S(2)}) collective-permute-start(bf16[1,384,128]{2,1,0:T(8,128)(2,1)S(1)} %get-tuple-element.61), channel_id=1, source_target_pairs={{0,4},{2,6},{4,8},{6,10},{8,12},{10,14},{12,16},{14,18},{16,20},{1... | collective-permute-start | bytes 294920 | tf_op jit(solution)/shard_map/ppermute | solution.py:17
  189.2 12.5 %collective-permute-start.19 = (bf16[1,384,128]{2,1,0:T(8,128)(2,1)S(1)}, bf16[1,384,128]{2,1,0:T(8,128)(2,1)S(1)}, u32[]{:S(2)}, u32[]{:S(2)}) collective-permute-start(bf16[1,384,128]{2,1,0:T(8,128)(2,1)S(1)} %get-tuple-element.61), channel_id=1, source_target_pairs={{4,0},{6,2},{8,4},{10,6},{12,8},{14,10},{16,12},{18,14},{20,16},{2... | collective-permute-start | bytes 294920 | tf_op jit(solution)/shard_map/ppermute | solution.py:17
  198.3 5.9 %collective-permute-start.18 = (bf16[1,384,128]{2,1,0:T(8,128)(2,1)S(1)}, bf16[1,384,128]{2,1,0:T(8,128)(2,1)S(1)}, u32[]{:S(2)}, u32[]{:S(2)}) collective-permute-start(bf16[1,384,128]{2,1,0:T(8,128)(2,1)S(1)} %get-tuple-element.61), channel_id=1, source_target_pairs={{2,0},{4,2},{6,4},{8,6},{10,8},{12,10},{14,12},{16,14},{18,16},{20... | collective-permute-start | bytes 294920 | tf_op jit(solution)/shard_map/ppermute | solution.py:17
  204.6 16.1 %collective-permute-start.21 = (bf16[1,384,128]{2,1,0:T(8,128)(2,1)S(1)}, bf16[1,384,128]{2,1,0:T(8,128)(2,1)S(1)}, u32[]{:S(2)}, u32[]{:S(2)}) collective-permute-start(bf16[1,384,128]{2,1,0:T(8,128)(2,1)S(1)} %fusion.64), channel_id=1, source_target_pairs={{0,2},{2,4},{4,6},{6,8},{8,10},{10,12},{12,14},{14,16},{16,18},{18... | collective-permute-start | bytes 294920 | tf_op jit(solution)/shard_map/ppermute | solution.py:17
  206.7 14.2 %collective-permute-start.20 = (bf16[1,384,128]{2,1,0:T(8,128)(2,1)S(1)}, bf16[1,384,128]{2,1,0:T(8,128)(2,1)S(1)}, u32[]{:S(2)}, u32[]{:S(2)}) collective-permute-start(bf16[1,384,128]{2,1,0:T(8,128)(2,1)S(1)} %fusion.64), channel_id=1, source_target_pairs={{0,4},{2,6},{4,8},{6,10},{8,12},{10,14},{12,16},{14,18},{16,20},{1... | collective-permute-start | bytes 294920 | tf_op jit(solution)/shard_map/ppermute | solution.py:17
  208.6 12.4 %collective-permute-start.23 = (bf16[1,384,128]{2,1,0:T(8,128)(2,1)S(1)}, bf16[1,384,128]{2,1,0:T(8,128)(2,1)S(1)}, u32[]{:S(2)}, u32[]{:S(2)}) collective-permute-start(bf16[1,384,128]{2,1,0:T(8,128)(2,1)S(1)} %fusion.64), channel_id=1, source_target_pairs={{4,0},{6,2},{8,4},{10,6},{12,8},{14,10},{16,12},{18,14},{20,16},{2... | collective-permute-start | bytes 294920 | tf_op jit(solution)/shard_map/ppermute | solution.py:17
  217.7 5.9 %collective-permute-start.22 = (bf16[1,384,128]{2,1,0:T(8,128)(2,1)S(1)}, bf16[1,384,128]{2,1,0:T(8,128)(2,1)S(1)}, u32[]{:S(2)}, u32[]{:S(2)}) collective-permute-start(bf16[1,384,128]{2,1,0:T(8,128)(2,1)S(1)} %fusion.64), channel_id=1, source_target_pairs={{2,0},{4,2},{6,4},{8,6},{10,8},{12,10},{14,12},{16,14},{18,16},{20... | collective-permute-start | bytes 294920 | tf_op jit(solution)/shard_map/ppermute | solution.py:17

commit v12 on v11

--- a/solution.py
+++ b/solution.py
@@ -260,7 +260,7 @@
         jnp.zeros((pixel_count, 128), jnp.float32),
     )
     held = strips.reshape(band_rows * grid_cols, channels)
-    merged = 6
+    merged = 7
     own_rows = lax.dynamic_index_in_dim(jnp.asarray(row_table), band, 0, keepdims=False)
     for step, bit in enumerate(GATHER_BITS):
         pairs = [(i, int(gather_partner(i, step, np.where))) for i in range(bands)]

time: 226 us -> 237 us (1.049)
  waiting for transfers between devices: 36.6 us -> 52.4 us
  other arithmetic: 15.8 us -> 12.3 us
  matrix products: 12.4 us -> 15.8 us
    ppermute x8, waiting for transfers between devices: 26.2 us -> 41.9 us  [per_device(): got = lax.ppermute(held, 'band', pairs)]
    dot_general x50, matrix products: 12.4 us -> 15.8 us  [conv_valid(): jnp.dot(tap_slice.reshape(-1, tap_slice.shape[-1]), weight[kernel_tap], p...]
    pallas_call x3 -> x2, Pallas kernels: 18.3 us -> 16 us  [match_block(): pl.pallas_call(match_kernel, grid=(count // tile,), in_specs=[pl.BlockSpe...]
    concatenate x2 -> x1, other arithmetic: 4.81 us -> 3.84 us  [match_block(): jnp.concatenate([jnp.ones((count, 1), jnp.float32), strip_row[:, None], s...]
    unnamed x36 -> x22, local copies, waits for them, and re-layouts: 4.48 us -> 4.82 us
  transfers between devices with their start and end apart: 24 -> 24, of which waited for: 13 -> 13; matrix products, arithmetic and copies ran while one was open for 15% -> 14% of each run, Pallas kernels for 5% -> 3%
where the time goes in v12:
time: 237 us; the launch traced here: 236 us
  starting transfers between devices  114 us (48%)
  waiting for transfers between devices  52.4 us (22%)
  local copies, waits for them, and re-layouts  23.7 us (10%)
  Pallas kernels  16 us (7%)
  matrix products  15.8 us (7%)
  other arithmetic  12.3 us (5%)
    ppermute x16, starting transfers between devices, passed_along(): return lax.ppermute(array, axis, pairs)  66.8 us
    ppermute x8, starting transfers between devices, per_device(): got = lax.ppermute(held, 'band', pairs)  47.6 us
    ppermute x8, waiting for transfers between devices, per_device(): got = lax.ppermute(held, 'band', pairs)  41.9 us
    pallas_call x2, Pallas kernels, match_block(): pl.pallas_call(match_kernel, grid=(count // tile,), in_specs=[pl.BlockSpe...  16 us
    dot_general x50, matrix products, conv_valid(): jnp.dot(tap_slice.reshape(-1, tap_slice.shape[-1]), weight[kernel_tap], p...  15.8 us
    ppermute x16, waiting for transfers between devices, passed_along(): return lax.ppermute(array, axis, pairs)  10.5 us
    unnamed x22, local copies, waits for them, and re-layouts  4.82 us
  transfers between devices with their start and end apart: 24, of which 13 were waited for; matrix products, arithmetic and copies ran while one was open for 14% of the time, Pallas kernels for 3%

profile of v12, /device:TPU:7, one launch (start us, length us, event | category | flops | bytes accessed | tf_op | source)
XLA Modules:
  0.0 236.0 jit_solution(14370397360901273697)
XLA Ops:
  2.3 15.4 %collective-permute-start = (bf16[48,256]{1,0:T(8,128)(2,1)S(1)}, bf16[48,256]{1,0:T(8,128)(2,1)S(1)}, u32[]{:S(2)}, u32[]{:S(2)}) collective-permute-start(bf16[48,256]{1,0:T(8,128)(2,1)S(1)} %get-tuple-element.17), channel_id=1, source_target_pairs={{0,32},{2,34},{4,36},{6,38},{8,40},{10,42},{12,44},{14,46},{16,48}... | collective-permute-start | bytes 73736 | tf_op jit(solution)/shard_map/ppermute | solution.py:267
  17.7 1.3 collective-permute-done
  19.0 5.3 %collective-permute-start.1 = (bf16[96,256]{1,0:T(8,128)(2,1)S(1)}, bf16[96,256]{1,0:T(8,128)(2,1)S(1)}, u32[]{:S(2)}, u32[]{:S(2)}) collective-permute-start(bf16[96,256]{1,0:T(8,128)(2,1)S(1)} %pad_maximum_fusion.4), channel_id=1, source_target_pairs={{0,16},{2,18},{4,20},{6,22},{8,24},{10,26},{12,28},{14,30},{16,0},... | collective-permute-start | bytes 147464 | tf_op jit(solution)/shard_map/ppermute | solution.py:267
  25.0 3.3 %collective-permute-done.1 = bf16[96,256]{1,0:T(8,128)(2,1)S(1)} collective-permute-done((bf16[96,256]{1,0:T(8,128)(2,1)S(1)}, bf16[96,256]{1,0:T(8,128)(2,1)S(1)}, u32[]{:S(2)}, u32[]{:S(2)}) %collective-permute-start.1) | collective-permute-done | bytes 49184 | tf_op jit(solution)/shard_map/ppermute | solution.py:267
  28.3 2.8 %collective-permute-start.2 = (bf16[192,256]{1,0:T(8,128)(2,1)S(1)}, bf16[192,256]{1,0:T(8,128)(2,1)S(1)}, u32[]{:S(2)}, u32[]{:S(2)}) collective-permute-start(bf16[192,256]{1,0:T(8,128)(2,1)S(1)} %pad_maximum_fusion.3), channel_id=1, source_target_pairs={{0,8},{2,10},{4,12},{6,14},{8,0},{10,2},{12,4},{14,6},{16,24},{18,... | collective-permute-start | bytes 294920 | tf_op jit(solution)/shard_map/ppermute | solution.py:267
  31.7 3.8 %collective-permute-done.2 = bf16[192,256]{1,0:T(8,128)(2,1)S(1)} collective-permute-done((bf16[192,256]{1,0:T(8,128)(2,1)S(1)}, bf16[192,256]{1,0:T(8,128)(2,1)S(1)}, u32[]{:S(2)}, u32[]{:S(2)}) %collective-permute-start.2) | collective-permute-done | bytes 98336 | tf_op jit(solution)/shard_map/ppermute | solution.py:267
  35.6 3.0 %collective-permute-start.3 = (bf16[384,256]{1,0:T(8,128)(2,1)S(1)}, bf16[384,256]{1,0:T(8,128)(2,1)S(1)}, u32[]{:S(2)}, u32[]{:S(2)}) collective-permute-start(bf16[384,256]{1,0:T(8,128)(2,1)S(1)} %pad_maximum_fusion.1), channel_id=1, source_target_pairs={{0,256},{2,258},{4,260},{6,262},{8,264},{10,266},{12,268},{14,270}... | collective-permute-start | bytes 589832 | tf_op jit(solution)/shard_map/ppermute | solution.py:267
  40.0 3.5 %collective-permute-done.3 = bf16[384,256]{1,0:T(8,128)(2,1)S(1)} collective-permute-done((bf16[384,256]{1,0:T(8,128)(2,1)S(1)}, bf16[384,256]{1,0:T(8,128)(2,1)S(1)}, u32[]{:S(2)}, u32[]{:S(2)}) %collective-permute-start.3) | collective-permute-done | bytes 196640 | tf_op jit(solution)/shard_map/ppermute | solution.py:267
  44.3 4.8 %collective-permute-start.4 = (bf16[768,256]{1,0:T(8,128)(2,1)S(1)}, bf16[768,256]{1,0:T(8,128)(2,1)S(1)}, u32[]{:S(2)}, u32[]{:S(2)}) collective-permute-start(bf16[768,256]{1,0:T(8,128)(2,1)S(1)} %get-tuple-element.28), channel_id=1, source_target_pairs={{0,128},{2,130},{4,132},{6,134},{8,136},{10,138},{12,140},{14,142}... | collective-permute-start | bytes 1179656 | tf_op jit(solution)/shard_map/ppermute | solution.py:267
  49.1 5.2 %collective-permute-done.4 = bf16[768,256]{1,0:T(8,128)(2,1)S(1)} collective-permute-done((bf16[768,256]{1,0:T(8,128)(2,1)S(1)}, bf16[768,256]{1,0:T(8,128)(2,1)S(1)}, u32[]{:S(2)}, u32[]{:S(2)}) %collective-permute-start.4) | collective-permute-done | bytes 393248 | tf_op jit(solution)/shard_map/ppermute | solution.py:267
  55.2 3.2 %collective-permute-start.5 = (bf16[1536,256]{1,0:T(8,128)(2,1)S(1)}, bf16[1536,256]{1,0:T(8,128)(2,1)S(1)}, u32[]{:S(2)}, u32[]{:S(2)}) collective-permute-start(bf16[1536,256]{1,0:T(8,128)(2,1)S(1)} %get-tuple-element.24), channel_id=1, source_target_pairs={{0,64},{2,66},{4,68},{6,70},{8,72},{10,74},{12,76},{14,78},{16,80}... | collective-permute-start | bytes 2359304 | tf_op jit(solution)/shard_map/ppermute | solution.py:267
  58.5 12.9 %collective-permute-done.5 = bf16[1536,256]{1,0:T(8,128)(2,1)S(1)} collective-permute-done((bf16[1536,256]{1,0:T(8,128)(2,1)S(1)}, bf16[1536,256]{1,0:T(8,128)(2,1)S(1)}, u32[]{:S(2)}, u32[]{:S(2)}) %collective-permute-start.5) | collective-permute-done | bytes 786464 | tf_op jit(solution)/shard_map/ppermute | solution.py:267
  71.4 1.3 constant_dynamic-update-slice_fusion.11
  72.8 7.5 %collective-permute-start.6 = (bf16[3072,256]{1,0:T(8,128)(2,1)}, bf16[3072,256]{1,0:T(8,128)(2,1)S(1)}, u32[]{:S(2)}, u32[]{:S(2)}) collective-permute-start(bf16[3072,256]{1,0:T(8,128)(2,1)} %get-tuple-element.20), channel_id=1, source_target_pairs={{0,4},{2,62},{4,0},{6,10},{8,12},{10,6},{12,8},{14,18},{16,20},{18... | collective-permute-start | bytes 4718600 | tf_op jit(solution)/shard_map/ppermute | solution.py:267
  81.0 2.8 %gather_fusion = s32[384]{0:T(512)S(1)} fusion(s32[256]{0:T(256)S(1)} %bitcast.408, s32[1024]{0:T(1024)S(1)} %pad_clamp_fusion.2), kind=kCustom, calls=%fused_computation.2 | custom fusion | bytes 4608 | tf_op jit(solution)/shard_map/gather | solution.py:295
  84.7 1.8 fusion.151
  86.5 11.9 %collective-permute-done.6 = bf16[3072,256]{1,0:T(8,128)(2,1)S(1)} collective-permute-done((bf16[3072,256]{1,0:T(8,128)(2,1)}, bf16[3072,256]{1,0:T(8,128)(2,1)S(1)}, u32[]{:S(2)}, u32[]{:S(2)}) %collective-permute-start.6) | collective-permute-done | bytes 1572896 | tf_op jit(solution)/shard_map/ppermute | solution.py:267
  99.6 5.5 %collective-permute-start.7 = (bf16[6144,256]{1,0:T(8,128)(2,1)}, bf16[6144,256]{1,0:T(8,128)(2,1)}, u32[]{:S(2)}, u32[]{:S(2)}) collective-permute-start(bf16[6144,256]{1,0:T(8,128)(2,1)} %constant_dynamic-update-slice_fusion.18.s_ref), channel_id=1, source_target_pairs={{0,2},{2,0},{4,6},{6,4},{8,10},{10,8},{12,14},{14,12},{16,18},{18,... | collective-permute-start | bytes 9437192 | tf_op jit(solution)/shard_map/ppermute | solution.py:267
  105.9 1.8 convert_element_type.185
  107.7 1.8 convert_element_type.186
  111.9 1.8 convolution_add_fusion.15
  113.6 1.9 fusion.1
  115.5 3.8 %maximum_maximum_fusion.1 = (bf16[6144,128]{1,0:T(8,128)(2,1)}, bf16[6144,128]{1,0:T(8,128)(2,1)}) fusion(bf16[6144,1]{1,0:T(8,128)(2,1)S(1)} %convert_element_type.186, bf16[6144,1]{1,0:T(8,128)(2,1)S(1)} %fusion.1, bf16[128]{0:T(256)(128)(2,1)S(1)} %pad.36.clone, bf16[128]{0:T(256)(128)(2,1)S(1)} %pad.33.clone, bf16[6144,1]{1,0:T(8,128)(2,1)S(1)} %convert_element_type.185), kind=kLoop, calls=%fused_computation.11 | loop fusion | flops 10223616 | bytes 3183104 | tf_op jit(solution)/shard_map/concatenate | solution.py:187
  119.3 4.0 %gather_fusion.1 = bf16[384,256]{1,0:T(8,128)(2,1)S(1)} fusion(bf16[6144,256]{1,0:T(8,128)(2,1)} %constant_dynamic-update-slice_fusion.18.s_ref, s32[1024]{0:T(1024)S(1)} %get-tuple-element.58), kind=kCustom, calls=%fused_computation.clone | custom fusion | bytes 394752 | tf_op jit(solution)/shard_map/jit(_take)/gather | solution.py:301
  124.7 8.0 %shard_map.122 = (f32[384,128]{1,0:T(8,128)}, f32[384,128]{1,0:T(8,128)}) custom-call(bf16[384,256]{1,0:T(8,128)(2,1)} %bitcast.409, bf16[6144,256]{1,0:T(8,128)(2,1)} %constant_dynamic-update-slice_fusion.18.s_ref, bf16[6144,128]{1,0:T(8,128)(2,1)} %get-tuple-element.18.w_ref, f32[384,128]{1,0:T(8,128)} %broadcast_in_dim.50.m_in, ...), custom_call_target="tpu_custom_call" | custom-call | flops 2415919104 | bytes 5701632 | tf_op jit(solution)/shard_map/pallas_call | solution.py:197
  132.7 8.0 %shard_map.123 = (f32[384,128]{1,0:T(8,128)}, f32[384,128]{1,0:T(8,128)}) custom-call(bf16[384,256]{1,0:T(8,128)(2,1)} %bitcast.410, bf16[6144,256]{1,0:T(8,128)(2,1)} %collective-permute-done.7.s_ref, bf16[6144,128]{1,0:T(8,128)(2,1)} %get-tuple-element.19.w_ref, f32[384,128]{1,0:T(8,128)} %get-tuple-element.6.m_in, f32[384,128]{1,0:T(8,128)} %get-tuple-element.7.a_in), custom_call_target="tpu_custom_call" | custom-call | flops 2415919104 | bytes 5701632 | tf_op jit(solution)/shard_map/pallas_call | solution.py:197
  140.7 1.5 subtract_reduce_fusion
  142.2 4.3 %gather_fusion.2 = bf16[384,256]{1,0:T(8,128)(2,1)S(1)} fusion(bf16[6144,256]{1,0:T(8,128)(2,1)} %collective-permute-done.7.s_ref, s32[1024]{0:T(1024)S(1)} %get-tuple-element.57), kind=kCustom, calls=%fused_computation.1.clone | custom fusion | bytes 394752 | tf_op jit(solution)/shard_map/jit(_take)/gather | solution.py:302
  150.2 1.9 collective-permute-start.9
  152.1 2.3 collective-permute-start.8
  154.4 10.1 %collective-permute-start.11 = (bf16[1,384,384]{2,1,0:T(8,128)(2,1)S(1)}, bf16[1,384,384]{2,1,0:T(8,128)(2,1)S(1)}, u32[]{:S(2)}, u32[]{:S(2)}) collective-permute-start(bf16[1,384,384]{2,1,0:T(8,128)(2,1)S(1)} %pad_maximum_fusion), channel_id=1, source_target_pairs={{4,0},{6,2},{8,4},{10,6},{12,8},{14,10},{16,12},{18,14},{20,16},{2... | collective-permute-start | bytes 884744 | tf_op jit(solution)/shard_map/ppermute | solution.py:17
  164.5 2.7 %collective-permute-start.10 = (bf16[1,384,384]{2,1,0:T(8,128)(2,1)S(1)}, bf16[1,384,384]{2,1,0:T(8,128)(2,1)S(1)}, u32[]{:S(2)}, u32[]{:S(2)}) collective-permute-start(bf16[1,384,384]{2,1,0:T(8,128)(2,1)S(1)} %pad_maximum_fusion), channel_id=1, source_target_pairs={{2,0},{4,2},{6,4},{8,6},{10,8},{12,10},{14,12},{16,14},{18,16},{20... | collective-permute-start | bytes 884744 | tf_op jit(solution)/shard_map/ppermute | solution.py:17
  168.7 1.6 collective-permute-done.11
  173.1 1.9 collective-permute-start.13
  175.2 1.9 collective-permute-start.12
  177.1 11.5 %collective-permute-start.15 = (bf16[1,384,128]{2,1,0:T(8,128)(2,1)S(1)}, bf16[1,384,128]{2,1,0:T(8,128)(2,1)S(1)}, u32[]{:S(2)}, u32[]{:S(2)}) collective-permute-start(bf16[1,384,128]{2,1,0:T(8,128)(2,1)S(1)} %fusion.61), channel_id=1, source_target_pairs={{4,0},{6,2},{8,4},{10,6},{12,8},{14,10},{16,12},{18,14},{20,16},{2... | collective-permute-start | bytes 294920 | tf_op jit(solution)/shard_map/ppermute | solution.py:17
  188.6 2.7 %collective-permute-start.14 = (bf16[1,384,128]{2,1,0:T(8,128)(2,1)S(1)}, bf16[1,384,128]{2,1,0:T(8,128)(2,1)S(1)}, u32[]{:S(2)}, u32[]{:S(2)}) collective-permute-start(bf16[1,384,128]{2,1,0:T(8,128)(2,1)S(1)} %fusion.61), channel_id=1, source_target_pairs={{2,0},{4,2},{6,4},{8,6},{10,8},{12,10},{14,12},{16,14},{18,16},{20... | collective-permute-start | bytes 294920 | tf_op jit(solution)/shard_map/ppermute | solution.py:17
  191.8 2.7 %collective-permute-done.14 = bf16[1,384,128]{2,1,0:T(8,128)(2,1)S(1)} collective-permute-done((bf16[1,384,128]{2,1,0:T(8,128)(2,1)S(1)}, bf16[1,384,128]{2,1,0:T(8,128)(2,1)S(1)}, u32[]{:S(2)}, u32[]{:S(2)}) %collective-permute-start.14) | collective-permute-done | bytes 98336 | tf_op jit(solution)/shard_map/ppermute | solution.py:17
  196.7 1.9 collective-permute-start.17
  198.8 1.9 collective-permute-start.16
  200.8 9.1 %collective-permute-start.19 = (bf16[1,384,128]{2,1,0:T(8,128)(2,1)S(1)}, bf16[1,384,128]{2,1,0:T(8,128)(2,1)S(1)}, u32[]{:S(2)}, u32[]{:S(2)}) collective-permute-start(bf16[1,384,128]{2,1,0:T(8,128)(2,1)S(1)} %get-tuple-element.55), channel_id=1, source_target_pairs={{4,0},{6,2},{8,4},{10,6},{12,8},{14,10},{16,12},{18,14},{20,16},{2... | collective-permute-start | bytes 294920 | tf_op jit(solution)/shard_map/ppermute | solution.py:17
  209.9 3.0 %collective-permute-start.18 = (bf16[1,384,128]{2,1,0:T(8,128)(2,1)S(1)}, bf16[1,384,128]{2,1,0:T(8,128)(2,1)S(1)}, u32[]{:S(2)}, u32[]{:S(2)}) collective-permute-start(bf16[1,384,128]{2,1,0:T(8,128)(2,1)S(1)} %get-tuple-element.55), channel_id=1, source_target_pairs={{2,0},{4,2},{6,4},{8,6},{10,8},{12,10},{14,12},{16,14},{18,16},{20... | collective-permute-start | bytes 294920 | tf_op jit(solution)/shard_map/ppermute | solution.py:17
  213.5 2.4 collective-permute-done.18
  216.1 1.9 collective-permute-start.21
  218.2 1.9 collective-permute-start.20
  220.1 9.1 %collective-permute-start.23 = (bf16[1,384,128]{2,1,0:T(8,128)(2,1)S(1)}, bf16[1,384,128]{2,1,0:T(8,128)(2,1)S(1)}, u32[]{:S(2)}, u32[]{:S(2)}) collective-permute-start(bf16[1,384,128]{2,1,0:T(8,128)(2,1)S(1)} %fusion.59), channel_id=1, source_target_pairs={{4,0},{6,2},{8,4},{10,6},{12,8},{14,10},{16,12},{18,14},{20,16},{2... | collective-permute-start | bytes 294920 | tf_op jit(solution)/shard_map/ppermute | solution.py:17
  229.2 3.0 %collective-permute-start.22 = (bf16[1,384,128]{2,1,0:T(8,128)(2,1)S(1)}, bf16[1,384,128]{2,1,0:T(8,128)(2,1)S(1)}, u32[]{:S(2)}, u32[]{:S(2)}) collective-permute-start(bf16[1,384,128]{2,1,0:T(8,128)(2,1)S(1)} %fusion.59), channel_id=1, source_target_pairs={{2,0},{4,2},{6,4},{8,6},{10,8},{12,10},{14,12},{16,14},{18,16},{20... | collective-permute-start | bytes 294920 | tf_op jit(solution)/shard_map/ppermute | solution.py:17
  232.7 2.5 %collective-permute-done.22 = bf16[1,384,128]{2,1,0:T(8,128)(2,1)S(1)} collective-permute-done((bf16[1,384,128]{2,1,0:T(8,128)(2,1)S(1)}, bf16[1,384,128]{2,1,0:T(8,128)(2,1)S(1)}, u32[]{:S(2)}, u32[]{:S(2)}) %collective-permute-start.22) | collective-permute-done | bytes 98336 | tf_op jit(solution)/shard_map/ppermute | solution.py:17
  (120 shorter events, 26.5 us)
Async XLA Ops:
  2.3 16.7 %collective-permute-start = (bf16[48,256]{1,0:T(8,128)(2,1)S(1)}, bf16[48,256]{1,0:T(8,128)(2,1)S(1)}, u32[]{:S(2)}, u32[]{:S(2)}) collective-permute-start(bf16[48,256]{1,0:T(8,128)(2,1)S(1)} %get-tuple-element.17), channel_id=1, source_target_pairs={{0,32},{2,34},{4,36},{6,38},{8,40},{10,42},{12,44},{14,46},{16,48}... | collective-permute-start | bytes 73736 | tf_op jit(solution)/shard_map/ppermute | solution.py:267
  19.0 9.3 %collective-permute-start.1 = (bf16[96,256]{1,0:T(8,128)(2,1)S(1)}, bf16[96,256]{1,0:T(8,128)(2,1)S(1)}, u32[]{:S(2)}, u32[]{:S(2)}) collective-permute-start(bf16[96,256]{1,0:T(8,128)(2,1)S(1)} %pad_maximum_fusion.4), channel_id=1, source_target_pairs={{0,16},{2,18},{4,20},{6,22},{8,24},{10,26},{12,28},{14,30},{16,0},... | collective-permute-start | bytes 147464 | tf_op jit(solution)/shard_map/ppermute | solution.py:267
  28.3 7.2 %collective-permute-start.2 = (bf16[192,256]{1,0:T(8,128)(2,1)S(1)}, bf16[192,256]{1,0:T(8,128)(2,1)S(1)}, u32[]{:S(2)}, u32[]{:S(2)}) collective-permute-start(bf16[192,256]{1,0:T(8,128)(2,1)S(1)} %pad_maximum_fusion.3), channel_id=1, source_target_pairs={{0,8},{2,10},{4,12},{6,14},{8,0},{10,2},{12,4},{14,6},{16,24},{18,... | collective-permute-start | bytes 294920 | tf_op jit(solution)/shard_map/ppermute | solution.py:267
  35.6 7.9 %collective-permute-start.3 = (bf16[384,256]{1,0:T(8,128)(2,1)S(1)}, bf16[384,256]{1,0:T(8,128)(2,1)S(1)}, u32[]{:S(2)}, u32[]{:S(2)}) collective-permute-start(bf16[384,256]{1,0:T(8,128)(2,1)S(1)} %pad_maximum_fusion.1), channel_id=1, source_target_pairs={{0,256},{2,258},{4,260},{6,262},{8,264},{10,266},{12,268},{14,270}... | collective-permute-start | bytes 589832 | tf_op jit(solution)/shard_map/ppermute | solution.py:267
  39.3 19.2 %copy-start.6 = (s32[2,1,384]{2,1,0:T(1,128)S(1)}, s32[2,1,384]{2,1,0:T(1,128)}, u32[]{:S(2)}) copy-start(s32[2,1,384]{2,1,0:T(1,128)} %param.17) | copy-start | bytes 9220
  44.3 10.0 %collective-permute-start.4 = (bf16[768,256]{1,0:T(8,128)(2,1)S(1)}, bf16[768,256]{1,0:T(8,128)(2,1)S(1)}, u32[]{:S(2)}, u32[]{:S(2)}) collective-permute-start(bf16[768,256]{1,0:T(8,128)(2,1)S(1)} %get-tuple-element.28), channel_id=1, source_target_pairs={{0,128},{2,130},{4,132},{6,134},{8,136},{10,138},{12,140},{14,142}... | collective-permute-start | bytes 1179656 | tf_op jit(solution)/shard_map/ppermute | solution.py:267
  55.2 16.2 %collective-permute-start.5 = (bf16[1536,256]{1,0:T(8,128)(2,1)S(1)}, bf16[1536,256]{1,0:T(8,128)(2,1)S(1)}, u32[]{:S(2)}, u32[]{:S(2)}) collective-permute-start(bf16[1536,256]{1,0:T(8,128)(2,1)S(1)} %get-tuple-element.24), channel_id=1, source_target_pairs={{0,64},{2,66},{4,68},{6,70},{8,72},{10,74},{12,76},{14,78},{16,80}... | collective-permute-start | bytes 2359304 | tf_op jit(solution)/shard_map/ppermute | solution.py:267
  72.8 11.8 %copy-start.7 = (f32[3,128]{1,0:T(4,128)S(1)}, f32[3,128]{1,0:T(4,128)}, u32[]{:S(2)}) copy-start(f32[3,128]{1,0:T(4,128)} %param.18) | copy-start | bytes 4612
  72.8 11.9 %copy-start = (bf16[1,384,128]{2,1,0:T(8,128)(2,1)S(1)}, bf16[1,384,128]{2,1,0:T(8,128)(2,1)}, u32[]{:S(2)}) copy-start(bf16[1,384,128]{2,1,0:T(8,128)(2,1)} %param.16) | copy-start | bytes 294916
  72.8 25.5 %collective-permute-start.6 = (bf16[3072,256]{1,0:T(8,128)(2,1)}, bf16[3072,256]{1,0:T(8,128)(2,1)S(1)}, u32[]{:S(2)}, u32[]{:S(2)}) collective-permute-start(bf16[3072,256]{1,0:T(8,128)(2,1)} %get-tuple-element.20), channel_id=1, source_target_pairs={{0,4},{2,62},{4,0},{6,10},{8,12},{10,6},{12,8},{14,18},{16,20},{18... | collective-permute-start | bytes 4718600 | tf_op jit(solution)/shard_map/ppermute | solution.py:267
  99.6 33.1 %collective-permute-start.7 = (bf16[6144,256]{1,0:T(8,128)(2,1)}, bf16[6144,256]{1,0:T(8,128)(2,1)}, u32[]{:S(2)}, u32[]{:S(2)}) collective-permute-start(bf16[6144,256]{1,0:T(8,128)(2,1)} %constant_dynamic-update-slice_fusion.18.s_ref), channel_id=1, source_target_pairs={{0,2},{2,0},{4,6},{6,4},{8,10},{10,8},{12,14},{14,12},{16,18},{18,... | collective-permute-start | bytes 9437192 | tf_op jit(solution)/shard_map/ppermute | solution.py:267
  140.7 5.8 %copy-start.5 = (bf16[1,384,256]{2,1,0:T(8,128)(2,1)S(1)}, bf16[1,384,256]{2,1,0:T(8,128)(2,1)}, u32[]{:S(2)}) copy-start(bf16[1,384,256]{2,1,0:T(8,128)(2,1)} %param.13) | copy-start | bytes 589828
  140.7 6.4 %copy-start.3 = (bf16[1,384,128]{2,1,0:T(8,128)(2,1)S(1)}, bf16[1,384,128]{2,1,0:T(8,128)(2,1)}, u32[]{:S(2)}) copy-start(bf16[1,384,128]{2,1,0:T(8,128)(2,1)} %param.15) | copy-start | bytes 294916
  142.1 5.0 %copy-start.2 = (bf16[5,384,384]{2,1,0:T(8,128)(2,1)S(1)}, bf16[5,384,384]{2,1,0:T(8,128)(2,1)}, u32[]{:S(2)}) copy-start(bf16[5,384,384]{2,1,0:T(8,128)(2,1)} %param.19) | copy-start | bytes 4423684
  147.9 1.0 copy-start.4
  149.6 17.7 %copy-start.1 = (bf16[5,384,384]{2,1,0:T(8,128)(2,1)S(1)}, bf16[5,384,384]{2,1,0:T(8,128)(2,1)}, u32[]{:S(2)}) copy-start(bf16[5,384,384]{2,1,0:T(8,128)(2,1)} %param.20) | copy-start | bytes 4423684
  150.2 18.1 %collective-permute-start.9 = (bf16[1,384,384]{2,1,0:T(8,128)(2,1)S(1)}, bf16[1,384,384]{2,1,0:T(8,128)(2,1)S(1)}, u32[]{:S(2)}, u32[]{:S(2)}) collective-permute-start(bf16[1,384,384]{2,1,0:T(8,128)(2,1)S(1)} %pad_maximum_fusion), channel_id=1, source_target_pairs={{0,2},{2,4},{4,6},{6,8},{8,10},{10,12},{12,14},{14,16},{16,18},{18... | collective-permute-start | bytes 884744 | tf_op jit(solution)/shard_map/ppermute | solution.py:17
  152.1 19.0 %collective-permute-start.8 = (bf16[1,384,384]{2,1,0:T(8,128)(2,1)S(1)}, bf16[1,384,384]{2,1,0:T(8,128)(2,1)S(1)}, u32[]{:S(2)}, u32[]{:S(2)}) collective-permute-start(bf16[1,384,384]{2,1,0:T(8,128)(2,1)S(1)} %pad_maximum_fusion), channel_id=1, source_target_pairs={{0,4},{2,6},{4,8},{6,10},{8,12},{10,14},{12,16},{14,18},{16,20},{1... | collective-permute-start | bytes 884744 | tf_op jit(solution)/shard_map/ppermute | solution.py:17
  154.4 16.0 %collective-permute-start.11 = (bf16[1,384,384]{2,1,0:T(8,128)(2,1)S(1)}, bf16[1,384,384]{2,1,0:T(8,128)(2,1)S(1)}, u32[]{:S(2)}, u32[]{:S(2)}) collective-permute-start(bf16[1,384,384]{2,1,0:T(8,128)(2,1)S(1)} %pad_maximum_fusion), channel_id=1, source_target_pairs={{4,0},{6,2},{8,4},{10,6},{12,8},{14,10},{16,12},{18,14},{20,16},{2... | collective-permute-start | bytes 884744 | tf_op jit(solution)/shard_map/ppermute | solution.py:17
  164.5 8.0 %collective-permute-start.10 = (bf16[1,384,384]{2,1,0:T(8,128)(2,1)S(1)}, bf16[1,384,384]{2,1,0:T(8,128)(2,1)S(1)}, u32[]{:S(2)}, u32[]{:S(2)}) collective-permute-start(bf16[1,384,384]{2,1,0:T(8,128)(2,1)S(1)} %pad_maximum_fusion), channel_id=1, source_target_pairs={{2,0},{4,2},{6,4},{8,6},{10,8},{12,10},{14,12},{16,14},{18,16},{20... | collective-permute-start | bytes 884744 | tf_op jit(solution)/shard_map/ppermute | solution.py:17
  173.1 18.2 %collective-permute-start.13 = (bf16[1,384,128]{2,1,0:T(8,128)(2,1)S(1)}, bf16[1,384,128]{2,1,0:T(8,128)(2,1)S(1)}, u32[]{:S(2)}, u32[]{:S(2)}) collective-permute-start(bf16[1,384,128]{2,1,0:T(8,128)(2,1)S(1)} %fusion.61), channel_id=1, source_target_pairs={{0,2},{2,4},{4,6},{6,8},{8,10},{10,12},{12,14},{14,16},{16,18},{18... | collective-permute-start | bytes 294920 | tf_op jit(solution)/shard_map/ppermute | solution.py:17
  175.2 16.3 %collective-permute-start.12 = (bf16[1,384,128]{2,1,0:T(8,128)(2,1)S(1)}, bf16[1,384,128]{2,1,0:T(8,128)(2,1)S(1)}, u32[]{:S(2)}, u32[]{:S(2)}) collective-permute-start(bf16[1,384,128]{2,1,0:T(8,128)(2,1)S(1)} %fusion.61), channel_id=1, source_target_pairs={{0,4},{2,6},{4,8},{6,10},{8,12},{10,14},{12,16},{14,18},{16,20},{1... | collective-permute-start | bytes 294920 | tf_op jit(solution)/shard_map/ppermute | solution.py:17
  177.1 14.5 %collective-permute-start.15 = (bf16[1,384,128]{2,1,0:T(8,128)(2,1)S(1)}, bf16[1,384,128]{2,1,0:T(8,128)(2,1)S(1)}, u32[]{:S(2)}, u32[]{:S(2)}) collective-permute-start(bf16[1,384,128]{2,1,0:T(8,128)(2,1)S(1)} %fusion.61), channel_id=1, source_target_pairs={{4,0},{6,2},{8,4},{10,6},{12,8},{14,10},{16,12},{18,14},{20,16},{2... | collective-permute-start | bytes 294920 | tf_op jit(solution)/shard_map/ppermute | solution.py:17
  188.6 5.9 %collective-permute-start.14 = (bf16[1,384,128]{2,1,0:T(8,128)(2,1)S(1)}, bf16[1,384,128]{2,1,0:T(8,128)(2,1)S(1)}, u32[]{:S(2)}, u32[]{:S(2)}) collective-permute-start(bf16[1,384,128]{2,1,0:T(8,128)(2,1)S(1)} %fusion.61), channel_id=1, source_target_pairs={{2,0},{4,2},{6,4},{8,6},{10,8},{12,10},{14,12},{16,14},{18,16},{20... | collective-permute-start | bytes 294920 | tf_op jit(solution)/shard_map/ppermute | solution.py:17
  196.7 16.1 %collective-permute-start.17 = (bf16[1,384,128]{2,1,0:T(8,128)(2,1)S(1)}, bf16[1,384,128]{2,1,0:T(8,128)(2,1)S(1)}, u32[]{:S(2)}, u32[]{:S(2)}) collective-permute-start(bf16[1,384,128]{2,1,0:T(8,128)(2,1)S(1)} %get-tuple-element.55), channel_id=1, source_target_pairs={{0,2},{2,4},{4,6},{6,8},{8,10},{10,12},{12,14},{14,16},{16,18},{18... | collective-permute-start | bytes 294920 | tf_op jit(solution)/shard_map/ppermute | solution.py:17
  198.8 14.2 %collective-permute-start.16 = (bf16[1,384,128]{2,1,0:T(8,128)(2,1)S(1)}, bf16[1,384,128]{2,1,0:T(8,128)(2,1)S(1)}, u32[]{:S(2)}, u32[]{:S(2)}) collective-permute-start(bf16[1,384,128]{2,1,0:T(8,128)(2,1)S(1)} %get-tuple-element.55), channel_id=1, source_target_pairs={{0,4},{2,6},{4,8},{6,10},{8,12},{10,14},{12,16},{14,18},{16,20},{1... | collective-permute-start | bytes 294920 | tf_op jit(solution)/shard_map/ppermute | solution.py:17
  200.8 12.5 %collective-permute-start.19 = (bf16[1,384,128]{2,1,0:T(8,128)(2,1)S(1)}, bf16[1,384,128]{2,1,0:T(8,128)(2,1)S(1)}, u32[]{:S(2)}, u32[]{:S(2)}) collective-permute-start(bf16[1,384,128]{2,1,0:T(8,128)(2,1)S(1)} %get-tuple-element.55), channel_id=1, source_target_pairs={{4,0},{6,2},{8,4},{10,6},{12,8},{14,10},{16,12},{18,14},{20,16},{2... | collective-permute-start | bytes 294920 | tf_op jit(solution)/shard_map/ppermute | solution.py:17
  209.9 5.9 %collective-permute-start.18 = (bf16[1,384,128]{2,1,0:T(8,128)(2,1)S(1)}, bf16[1,384,128]{2,1,0:T(8,128)(2,1)S(1)}, u32[]{:S(2)}, u32[]{:S(2)}) collective-permute-start(bf16[1,384,128]{2,1,0:T(8,128)(2,1)S(1)} %get-tuple-element.55), channel_id=1, source_target_pairs={{2,0},{4,2},{6,4},{8,6},{10,8},{12,10},{14,12},{16,14},{18,16},{20... | collective-permute-start | bytes 294920 | tf_op jit(solution)/shard_map/ppermute | solution.py:17
  216.1 16.1 %collective-permute-start.21 = (bf16[1,384,128]{2,1,0:T(8,128)(2,1)S(1)}, bf16[1,384,128]{2,1,0:T(8,128)(2,1)S(1)}, u32[]{:S(2)}, u32[]{:S(2)}) collective-permute-start(bf16[1,384,128]{2,1,0:T(8,128)(2,1)S(1)} %fusion.59), channel_id=1, source_target_pairs={{0,2},{2,4},{4,6},{6,8},{8,10},{10,12},{12,14},{14,16},{16,18},{18... | collective-permute-start | bytes 294920 | tf_op jit(solution)/shard_map/ppermute | solution.py:17
  218.2 14.2 %collective-permute-start.20 = (bf16[1,384,128]{2,1,0:T(8,128)(2,1)S(1)}, bf16[1,384,128]{2,1,0:T(8,128)(2,1)S(1)}, u32[]{:S(2)}, u32[]{:S(2)}) collective-permute-start(bf16[1,384,128]{2,1,0:T(8,128)(2,1)S(1)} %fusion.59), channel_id=1, source_target_pairs={{0,4},{2,6},{4,8},{6,10},{8,12},{10,14},{12,16},{14,18},{16,20},{1... | collective-permute-start | bytes 294920 | tf_op jit(solution)/shard_map/ppermute | solution.py:17
  220.1 12.4 %collective-permute-start.23 = (bf16[1,384,128]{2,1,0:T(8,128)(2,1)S(1)}, bf16[1,384,128]{2,1,0:T(8,128)(2,1)S(1)}, u32[]{:S(2)}, u32[]{:S(2)}) collective-permute-start(bf16[1,384,128]{2,1,0:T(8,128)(2,1)S(1)} %fusion.59), channel_id=1, source_target_pairs={{4,0},{6,2},{8,4},{10,6},{12,8},{14,10},{16,12},{18,14},{20,16},{2... | collective-permute-start | bytes 294920 | tf_op jit(solution)/shard_map/ppermute | solution.py:17
  229.2 5.9 %collective-permute-start.22 = (bf16[1,384,128]{2,1,0:T(8,128)(2,1)S(1)}, bf16[1,384,128]{2,1,0:T(8,128)(2,1)S(1)}, u32[]{:S(2)}, u32[]{:S(2)}) collective-permute-start(bf16[1,384,128]{2,1,0:T(8,128)(2,1)S(1)} %fusion.59), channel_id=1, source_target_pairs={{2,0},{4,2},{6,4},{8,6},{10,8},{12,10},{14,12},{16,14},{18,16},{20... | collective-permute-start | bytes 294920 | tf_op jit(solution)/shard_map/ppermute | solution.py:17

commit v13 on v11

--- a/solution.py
+++ b/solution.py
@@ -181,7 +181,7 @@
 def match_block(state, features, block, block_rows, grid_cols):
     count, channels = block.shape
     pixels = features.shape[0]
-    tile = min(count, 3072)
+    tile = min(count, 6144)
     strip_row = jnp.repeat(block_rows, grid_cols).astype(jnp.float32)
     strip_col = (jnp.arange(count, dtype=jnp.int32) % grid_cols).astype(jnp.float32)
     weights = jnp.concatenate(

time: 226 us -> 226 us (level)
  no operation moved by 1% of the time
where the time goes in v13:
time: 226 us; the launch traced here: 225 us
  starting transfers between devices  114 us (50%)
  waiting for transfers between devices  36.6 us (16%)
  local copies, waits for them, and re-layouts  25.4 us (11%)
  Pallas kernels  18.5 us (8%)
  other arithmetic  15.8 us (7%)
  matrix products  12.4 us (5%)
    ppermute x16, starting transfers between devices, passed_along(): return lax.ppermute(array, axis, pairs)  66.8 us
    ppermute x8, starting transfers between devices, per_device(): got = lax.ppermute(held, 'band', pairs)  47.6 us
    ppermute x8, waiting for transfers between devices, per_device(): got = lax.ppermute(held, 'band', pairs)  26.2 us
    pallas_call x3, Pallas kernels, match_block(): pl.pallas_call(match_kernel, grid=(count // tile,), in_specs=[pl.BlockSpe...  18.5 us
    dot_general x50, matrix products, conv_valid(): jnp.dot(tap_slice.reshape(-1, tap_slice.shape[-1]), weight[kernel_tap], p...  12.4 us
    ppermute x16, waiting for transfers between devices, passed_along(): return lax.ppermute(array, axis, pairs)  10.5 us
    concatenate x2, other arithmetic, match_block(): jnp.concatenate([jnp.ones((count, 1), jnp.float32), strip_row[:, None], s...  4.81 us
    another operation x5, other arithmetic  4.62 us
  transfers between devices with their start and end apart: 24, of which 13 were waited for; matrix products, arithmetic and copies ran while one was open for 15% of the time, Pallas kernels for 5%

profile of v13, /device:TPU:7, one launch (start us, length us, event | category | flops | bytes accessed | tf_op | source)
XLA Modules:
  0.0 224.6 jit_solution(12029282582438596270)
XLA Ops:
  2.3 15.4 %collective-permute-start = (bf16[48,256]{1,0:T(8,128)(2,1)S(1)}, bf16[48,256]{1,0:T(8,128)(2,1)S(1)}, u32[]{:S(2)}, u32[]{:S(2)}) collective-permute-start(bf16[48,256]{1,0:T(8,128)(2,1)S(1)} %get-tuple-element.23), channel_id=1, source_target_pairs={{0,32},{2,34},{4,36},{6,38},{8,40},{10,42},{12,44},{14,46},{16,48}... | collective-permute-start | bytes 73736 | tf_op jit(solution)/shard_map/ppermute | solution.py:267
  17.7 1.3 collective-permute-done
  19.0 5.3 %collective-permute-start.1 = (bf16[96,256]{1,0:T(8,128)(2,1)S(1)}, bf16[96,256]{1,0:T(8,128)(2,1)S(1)}, u32[]{:S(2)}, u32[]{:S(2)}) collective-permute-start(bf16[96,256]{1,0:T(8,128)(2,1)S(1)} %pad_maximum_fusion.4), channel_id=1, source_target_pairs={{0,16},{2,18},{4,20},{6,22},{8,24},{10,26},{12,28},{14,30},{16,0},... | collective-permute-start | bytes 147464 | tf_op jit(solution)/shard_map/ppermute | solution.py:267
  25.0 3.3 %collective-permute-done.1 = bf16[96,256]{1,0:T(8,128)(2,1)S(1)} collective-permute-done((bf16[96,256]{1,0:T(8,128)(2,1)S(1)}, bf16[96,256]{1,0:T(8,128)(2,1)S(1)}, u32[]{:S(2)}, u32[]{:S(2)}) %collective-permute-start.1) | collective-permute-done | bytes 49184 | tf_op jit(solution)/shard_map/ppermute | solution.py:267
  28.3 2.8 %collective-permute-start.2 = (bf16[192,256]{1,0:T(8,128)(2,1)S(1)}, bf16[192,256]{1,0:T(8,128)(2,1)S(1)}, u32[]{:S(2)}, u32[]{:S(2)}) collective-permute-start(bf16[192,256]{1,0:T(8,128)(2,1)S(1)} %pad_maximum_fusion.3), channel_id=1, source_target_pairs={{0,8},{2,10},{4,12},{6,14},{8,0},{10,2},{12,4},{14,6},{16,24},{18,... | collective-permute-start | bytes 294920 | tf_op jit(solution)/shard_map/ppermute | solution.py:267
  31.7 3.8 %collective-permute-done.2 = bf16[192,256]{1,0:T(8,128)(2,1)S(1)} collective-permute-done((bf16[192,256]{1,0:T(8,128)(2,1)S(1)}, bf16[192,256]{1,0:T(8,128)(2,1)S(1)}, u32[]{:S(2)}, u32[]{:S(2)}) %collective-permute-start.2) | collective-permute-done | bytes 98336 | tf_op jit(solution)/shard_map/ppermute | solution.py:267
  35.6 3.0 %collective-permute-start.3 = (bf16[384,256]{1,0:T(8,128)(2,1)S(1)}, bf16[384,256]{1,0:T(8,128)(2,1)S(1)}, u32[]{:S(2)}, u32[]{:S(2)}) collective-permute-start(bf16[384,256]{1,0:T(8,128)(2,1)S(1)} %pad_maximum_fusion.1), channel_id=1, source_target_pairs={{0,256},{2,258},{4,260},{6,262},{8,264},{10,266},{12,268},{14,270}... | collective-permute-start | bytes 589832 | tf_op jit(solution)/shard_map/ppermute | solution.py:267
  40.0 3.5 %collective-permute-done.3 = bf16[384,256]{1,0:T(8,128)(2,1)S(1)} collective-permute-done((bf16[384,256]{1,0:T(8,128)(2,1)S(1)}, bf16[384,256]{1,0:T(8,128)(2,1)S(1)}, u32[]{:S(2)}, u32[]{:S(2)}) %collective-permute-start.3) | collective-permute-done | bytes 196640 | tf_op jit(solution)/shard_map/ppermute | solution.py:267
  44.3 4.8 %collective-permute-start.4 = (bf16[768,256]{1,0:T(8,128)(2,1)S(1)}, bf16[768,256]{1,0:T(8,128)(2,1)S(1)}, u32[]{:S(2)}, u32[]{:S(2)}) collective-permute-start(bf16[768,256]{1,0:T(8,128)(2,1)S(1)} %get-tuple-element.34), channel_id=1, source_target_pairs={{0,128},{2,130},{4,132},{6,134},{8,136},{10,138},{12,140},{14,142}... | collective-permute-start | bytes 1179656 | tf_op jit(solution)/shard_map/ppermute | solution.py:267
  50.6 3.8 %collective-permute-done.4 = bf16[768,256]{1,0:T(8,128)(2,1)S(1)} collective-permute-done((bf16[768,256]{1,0:T(8,128)(2,1)S(1)}, bf16[768,256]{1,0:T(8,128)(2,1)S(1)}, u32[]{:S(2)}, u32[]{:S(2)}) %collective-permute-start.4) | collective-permute-done | bytes 393248 | tf_op jit(solution)/shard_map/ppermute | solution.py:267
  55.3 3.2 %collective-permute-start.5 = (bf16[1536,256]{1,0:T(8,128)(2,1)S(1)}, bf16[1536,256]{1,0:T(8,128)(2,1)S(1)}, u32[]{:S(2)}, u32[]{:S(2)}) collective-permute-start(bf16[1536,256]{1,0:T(8,128)(2,1)S(1)} %get-tuple-element.30), channel_id=1, source_target_pairs={{0,64},{2,66},{4,68},{6,70},{8,72},{10,74},{12,76},{14,78},{16,80}... | collective-permute-start | bytes 2359304 | tf_op jit(solution)/shard_map/ppermute | solution.py:267
  59.2 2.8 %gather_fusion = s32[384]{0:T(512)S(1)} fusion(s32[256]{0:T(256)S(1)} %bitcast.411, s32[1024]{0:T(1024)S(1)} %pad_clamp_fusion.2), kind=kCustom, calls=%fused_computation.2 | custom fusion | bytes 4608 | tf_op jit(solution)/shard_map/gather | solution.py:295
  63.2 8.3 %collective-permute-done.5 = bf16[1536,256]{1,0:T(8,128)(2,1)S(1)} collective-permute-done((bf16[1536,256]{1,0:T(8,128)(2,1)S(1)}, bf16[1536,256]{1,0:T(8,128)(2,1)S(1)}, u32[]{:S(2)}, u32[]{:S(2)}) %collective-permute-start.5) | collective-permute-done | bytes 786464 | tf_op jit(solution)/shard_map/ppermute | solution.py:267
  72.8 7.4 %collective-permute-start.6 = (bf16[3072,256]{1,0:T(8,128)(2,1)}, bf16[3072,256]{1,0:T(8,128)(2,1)}, u32[]{:S(2)}, u32[]{:S(2)}) collective-permute-start(bf16[3072,256]{1,0:T(8,128)(2,1)} %get-tuple-element.26.s_ref), channel_id=1, source_target_pairs={{0,4},{2,62},{4,0},{6,10},{8,12},{10,6},{12,8},{14,18},{16,20},{18... | collective-permute-start | bytes 4718600 | tf_op jit(solution)/shard_map/ppermute | solution.py:267
  83.0 1.8 convert_element_type.223
  84.8 1.8 fusion.156
  87.2 2.3 %maximum_maximum_fusion.2 = (bf16[3072,128]{1,0:T(8,128)(2,1)}, bf16[3072,128]{1,0:T(8,128)(2,1)}) fusion(bf16[3072,1]{1,0:T(8,128)(2,1)S(1)} %convert_element_type.224, bf16[3072,1]{1,0:T(8,128)(2,1)S(1)} %fusion.6, bf16[128]{0:T(256)(128)(2,1)S(1)} %pad.40.clone, bf16[128]{0:T(256)(128)(2,1)S(1)} %pad.37.clone, bf16[3072,1]{1,0:T(8,128)(2,1)S(1)} %convert_element_type.222), kind=kLoop, calls=%fused_computation.103 | loop fusion | flops 5111808 | bytes 1591808 | tf_op jit(solution)/shard_map/concatenate | solution.py:187
  90.9 5.2 %shard_map.131 = (f32[384,128]{1,0:T(8,128)}, f32[384,128]{1,0:T(8,128)}) custom-call(bf16[384,256]{1,0:T(8,128)(2,1)} %bitcast.412, bf16[3072,256]{1,0:T(8,128)(2,1)} %get-tuple-element.26.s_ref, bf16[3072,128]{1,0:T(8,128)(2,1)} %get-tuple-element.25.w_ref, f32[384,128]{1,0:T(8,128)} %broadcast_in_dim.60.m_in, f32[384,128]{1,0:T(8,128)} %broadcast_in_dim.61.a_in), custom_call_target="tpu_custom_call" | custom-call | flops 1207959552 | bytes 3342336 | tf_op jit(solution)/shard_map/pallas_call | solution.py:197
  96.1 2.2 collective-permute-done.6.s_ref
  98.3 2.9 %constant_dynamic-update-slice_fusion.18 = bf16[6144,256]{1,0:T(8,128)(2,1)} fusion(bf16[6144,256]{1,0:T(8,128)(2,1)} %get-tuple-element.27, bf16[3072,256]{1,0:T(8,128)(2,1)} %collective-permute-done.6.s_ref), kind=kLoop, calls=%fused_computation.312 | loop fusion | bytes 3145728 | tf_op jit(solution)/shard_map/concatenate | solution.py:281
  101.2 5.6 %collective-permute-start.7 = (bf16[6144,256]{1,0:T(8,128)(2,1)}, bf16[6144,256]{1,0:T(8,128)(2,1)}, u32[]{:S(2)}, u32[]{:S(2)}) collective-permute-start(bf16[6144,256]{1,0:T(8,128)(2,1)} %constant_dynamic-update-slice_fusion.18), channel_id=1, source_target_pairs={{0,2},{2,0},{4,6},{6,4},{8,10},{10,8},{12,14},{14,12},{16,18},{18,... | collective-permute-start | bytes 9437192 | tf_op jit(solution)/shard_map/ppermute | solution.py:267
  108.0 1.9 fusion.1
  109.9 2.5 %maximum_maximum_fusion.w_ref = bf16[6144,128]{1,0:T(8,128)(2,1)} fusion(bf16[6144,1]{1,0:T(8,128)(2,1)S(1)} %fusion.1, bf16[6144,1]{1,0:T(8,128)(2,1)S(1)} %convert_element_type.223, bf16[128]{0:T(256)(128)(2,1)S(1)} %pad.40.clone, bf16[128]{0:T(256)(128)(2,1)S(1)} %pad.37.clone), kind=kLoop, calls=%fused_computation.13 | loop fusion | flops 6291456 | bytes 1597952 | tf_op jit(solution)/shard_map/concatenate | solution.py:187
  112.4 4.0 %gather_fusion.1 = bf16[384,256]{1,0:T(8,128)(2,1)S(1)} fusion(bf16[6144,256]{1,0:T(8,128)(2,1)} %constant_dynamic-update-slice_fusion.18, s32[1024]{0:T(1024)S(1)} %get-tuple-element.64), kind=kCustom, calls=%fused_computation.clone | custom fusion | bytes 394752 | tf_op jit(solution)/shard_map/jit(_take)/gather | solution.py:301
  116.4 5.2 %shard_map.132 = (f32[384,128]{1,0:T(8,128)}, f32[384,128]{1,0:T(8,128)}) custom-call(bf16[384,256]{1,0:T(8,128)(2,1)} %bitcast.413, bf16[3072,256]{1,0:T(8,128)(2,1)} %collective-permute-done.6.s_ref, bf16[3072,128]{1,0:T(8,128)(2,1)} %get-tuple-element.24.w_ref, f32[384,128]{1,0:T(8,128)} %get-tuple-element.9.m_in, f32[384,128]{1,0:T(8,128)} %get-tuple-element.10.a_in), custom_call_target="tpu_custom_call" | custom-call | flops 1207959552 | bytes 3342336 | tf_op jit(solution)/shard_map/pallas_call | solution.py:197
  121.6 8.1 %shard_map.133 = (f32[384,128]{1,0:T(8,128)}, f32[384,128]{1,0:T(8,128)}) custom-call(bf16[384,256]{1,0:T(8,128)(2,1)} %bitcast.414, bf16[6144,256]{1,0:T(8,128)(2,1)} %collective-permute-done.7.s_ref, bf16[6144,128]{1,0:T(8,128)(2,1)} %maximum_maximum_fusion.w_ref, f32[384,128]{1,0:T(8,128)} %get-tuple-element.12.m_in, f32[384,128]{1,0:T(8,128)} %get-tuple-element.13.a_in), custom_call_target="tpu_custom_call" | custom-call | flops 2415919104 | bytes 5701632 | tf_op jit(solution)/shard_map/pallas_call | solution.py:197
  129.7 1.5 subtract_reduce_fusion
  131.3 4.2 %gather_fusion.2 = bf16[384,256]{1,0:T(8,128)(2,1)S(1)} fusion(bf16[6144,256]{1,0:T(8,128)(2,1)} %collective-permute-done.7.s_ref, s32[1024]{0:T(1024)S(1)} %get-tuple-element.63), kind=kCustom, calls=%fused_computation.1.clone | custom fusion | bytes 394752 | tf_op jit(solution)/shard_map/jit(_take)/gather | solution.py:302
  138.7 1.9 collective-permute-start.9
  140.7 2.3 %collective-permute-start.8 = (bf16[1,384,384]{2,1,0:T(8,128)(2,1)S(1)}, bf16[1,384,384]{2,1,0:T(8,128)(2,1)S(1)}, u32[]{:S(2)}, u32[]{:S(2)}) collective-permute-start(bf16[1,384,384]{2,1,0:T(8,128)(2,1)S(1)} %pad_maximum_fusion), channel_id=1, source_target_pairs={{0,4},{2,6},{4,8},{6,10},{8,12},{10,14},{12,16},{14,18},{16,20},{1... | collective-permute-start | bytes 884744 | tf_op jit(solution)/shard_map/ppermute | solution.py:17
  143.0 10.1 %collective-permute-start.11 = (bf16[1,384,384]{2,1,0:T(8,128)(2,1)S(1)}, bf16[1,384,384]{2,1,0:T(8,128)(2,1)S(1)}, u32[]{:S(2)}, u32[]{:S(2)}) collective-permute-start(bf16[1,384,384]{2,1,0:T(8,128)(2,1)S(1)} %pad_maximum_fusion), channel_id=1, source_target_pairs={{4,0},{6,2},{8,4},{10,6},{12,8},{14,10},{16,12},{18,14},{20,16},{2... | collective-permute-start | bytes 884744 | tf_op jit(solution)/shard_map/ppermute | solution.py:17
  153.1 2.7 %collective-permute-start.10 = (bf16[1,384,384]{2,1,0:T(8,128)(2,1)S(1)}, bf16[1,384,384]{2,1,0:T(8,128)(2,1)S(1)}, u32[]{:S(2)}, u32[]{:S(2)}) collective-permute-start(bf16[1,384,384]{2,1,0:T(8,128)(2,1)S(1)} %pad_maximum_fusion), channel_id=1, source_target_pairs={{2,0},{4,2},{6,4},{8,6},{10,8},{12,10},{14,12},{16,14},{18,16},{20... | collective-permute-start | bytes 884744 | tf_op jit(solution)/shard_map/ppermute | solution.py:17
  157.3 1.6 collective-permute-done.11
  161.7 1.9 collective-permute-start.13
  163.8 1.9 collective-permute-start.12
  165.8 11.4 %collective-permute-start.15 = (bf16[1,384,128]{2,1,0:T(8,128)(2,1)S(1)}, bf16[1,384,128]{2,1,0:T(8,128)(2,1)S(1)}, u32[]{:S(2)}, u32[]{:S(2)}) collective-permute-start(bf16[1,384,128]{2,1,0:T(8,128)(2,1)S(1)} %fusion.66), channel_id=1, source_target_pairs={{4,0},{6,2},{8,4},{10,6},{12,8},{14,10},{16,12},{18,14},{20,16},{2... | collective-permute-start | bytes 294920 | tf_op jit(solution)/shard_map/ppermute | solution.py:17
  177.2 2.7 %collective-permute-start.14 = (bf16[1,384,128]{2,1,0:T(8,128)(2,1)S(1)}, bf16[1,384,128]{2,1,0:T(8,128)(2,1)S(1)}, u32[]{:S(2)}, u32[]{:S(2)}) collective-permute-start(bf16[1,384,128]{2,1,0:T(8,128)(2,1)S(1)} %fusion.66), channel_id=1, source_target_pairs={{2,0},{4,2},{6,4},{8,6},{10,8},{12,10},{14,12},{16,14},{18,16},{20... | collective-permute-start | bytes 294920 | tf_op jit(solution)/shard_map/ppermute | solution.py:17
  180.4 2.7 %collective-permute-done.14 = bf16[1,384,128]{2,1,0:T(8,128)(2,1)S(1)} collective-permute-done((bf16[1,384,128]{2,1,0:T(8,128)(2,1)S(1)}, bf16[1,384,128]{2,1,0:T(8,128)(2,1)S(1)}, u32[]{:S(2)}, u32[]{:S(2)}) %collective-permute-start.14) | collective-permute-done | bytes 98336 | tf_op jit(solution)/shard_map/ppermute | solution.py:17
  185.3 1.9 collective-permute-start.17
  187.4 1.9 collective-permute-start.16
  189.4 9.1 %collective-permute-start.19 = (bf16[1,384,128]{2,1,0:T(8,128)(2,1)S(1)}, bf16[1,384,128]{2,1,0:T(8,128)(2,1)S(1)}, u32[]{:S(2)}, u32[]{:S(2)}) collective-permute-start(bf16[1,384,128]{2,1,0:T(8,128)(2,1)S(1)} %get-tuple-element.61), channel_id=1, source_target_pairs={{4,0},{6,2},{8,4},{10,6},{12,8},{14,10},{16,12},{18,14},{20,16},{2... | collective-permute-start | bytes 294920 | tf_op jit(solution)/shard_map/ppermute | solution.py:17
  198.5 3.0 %collective-permute-start.18 = (bf16[1,384,128]{2,1,0:T(8,128)(2,1)S(1)}, bf16[1,384,128]{2,1,0:T(8,128)(2,1)S(1)}, u32[]{:S(2)}, u32[]{:S(2)}) collective-permute-start(bf16[1,384,128]{2,1,0:T(8,128)(2,1)S(1)} %get-tuple-element.61), channel_id=1, source_target_pairs={{2,0},{4,2},{6,4},{8,6},{10,8},{12,10},{14,12},{16,14},{18,16},{20... | collective-permute-start | bytes 294920 | tf_op jit(solution)/shard_map/ppermute | solution.py:17
  202.1 2.4 %collective-permute-done.18 = bf16[1,384,128]{2,1,0:T(8,128)(2,1)S(1)} collective-permute-done((bf16[1,384,128]{2,1,0:T(8,128)(2,1)S(1)}, bf16[1,384,128]{2,1,0:T(8,128)(2,1)S(1)}, u32[]{:S(2)}, u32[]{:S(2)}) %collective-permute-start.18) | collective-permute-done | bytes 98336 | tf_op jit(solution)/shard_map/ppermute | solution.py:17
  204.7 1.9 collective-permute-start.21
  206.8 1.9 collective-permute-start.20
  208.7 9.1 %collective-permute-start.23 = (bf16[1,384,128]{2,1,0:T(8,128)(2,1)S(1)}, bf16[1,384,128]{2,1,0:T(8,128)(2,1)S(1)}, u32[]{:S(2)}, u32[]{:S(2)}) collective-permute-start(bf16[1,384,128]{2,1,0:T(8,128)(2,1)S(1)} %fusion.64), channel_id=1, source_target_pairs={{4,0},{6,2},{8,4},{10,6},{12,8},{14,10},{16,12},{18,14},{20,16},{2... | collective-permute-start | bytes 294920 | tf_op jit(solution)/shard_map/ppermute | solution.py:17
  217.8 3.0 %collective-permute-start.22 = (bf16[1,384,128]{2,1,0:T(8,128)(2,1)S(1)}, bf16[1,384,128]{2,1,0:T(8,128)(2,1)S(1)}, u32[]{:S(2)}, u32[]{:S(2)}) collective-permute-start(bf16[1,384,128]{2,1,0:T(8,128)(2,1)S(1)} %fusion.64), channel_id=1, source_target_pairs={{2,0},{4,2},{6,4},{8,6},{10,8},{12,10},{14,12},{16,14},{18,16},{20... | collective-permute-start | bytes 294920 | tf_op jit(solution)/shard_map/ppermute | solution.py:17
  221.3 2.5 %collective-permute-done.22 = bf16[1,384,128]{2,1,0:T(8,128)(2,1)S(1)} collective-permute-done((bf16[1,384,128]{2,1,0:T(8,128)(2,1)S(1)}, bf16[1,384,128]{2,1,0:T(8,128)(2,1)S(1)}, u32[]{:S(2)}, u32[]{:S(2)}) %collective-permute-start.22) | collective-permute-done | bytes 98336 | tf_op jit(solution)/shard_map/ppermute | solution.py:17
  (140 shorter events, 29.4 us)
Async XLA Ops:
  1.7 48.8 %copy-start.6 = (s32[2,1,384]{2,1,0:T(1,128)S(1)}, s32[2,1,384]{2,1,0:T(1,128)}, u32[]{:S(2)}) copy-start(s32[2,1,384]{2,1,0:T(1,128)} %param.18) | copy-start | bytes 9220
  2.3 16.7 %collective-permute-start = (bf16[48,256]{1,0:T(8,128)(2,1)S(1)}, bf16[48,256]{1,0:T(8,128)(2,1)S(1)}, u32[]{:S(2)}, u32[]{:S(2)}) collective-permute-start(bf16[48,256]{1,0:T(8,128)(2,1)S(1)} %get-tuple-element.23), channel_id=1, source_target_pairs={{0,32},{2,34},{4,36},{6,38},{8,40},{10,42},{12,44},{14,46},{16,48}... | collective-permute-start | bytes 73736 | tf_op jit(solution)/shard_map/ppermute | solution.py:267
  19.0 9.3 %collective-permute-start.1 = (bf16[96,256]{1,0:T(8,128)(2,1)S(1)}, bf16[96,256]{1,0:T(8,128)(2,1)S(1)}, u32[]{:S(2)}, u32[]{:S(2)}) collective-permute-start(bf16[96,256]{1,0:T(8,128)(2,1)S(1)} %pad_maximum_fusion.4), channel_id=1, source_target_pairs={{0,16},{2,18},{4,20},{6,22},{8,24},{10,26},{12,28},{14,30},{16,0},... | collective-permute-start | bytes 147464 | tf_op jit(solution)/shard_map/ppermute | solution.py:267
  28.3 7.2 %collective-permute-start.2 = (bf16[192,256]{1,0:T(8,128)(2,1)S(1)}, bf16[192,256]{1,0:T(8,128)(2,1)S(1)}, u32[]{:S(2)}, u32[]{:S(2)}) collective-permute-start(bf16[192,256]{1,0:T(8,128)(2,1)S(1)} %pad_maximum_fusion.3), channel_id=1, source_target_pairs={{0,8},{2,10},{4,12},{6,14},{8,0},{10,2},{12,4},{14,6},{16,24},{18,... | collective-permute-start | bytes 294920 | tf_op jit(solution)/shard_map/ppermute | solution.py:267
  35.6 7.9 %collective-permute-start.3 = (bf16[384,256]{1,0:T(8,128)(2,1)S(1)}, bf16[384,256]{1,0:T(8,128)(2,1)S(1)}, u32[]{:S(2)}, u32[]{:S(2)}) collective-permute-start(bf16[384,256]{1,0:T(8,128)(2,1)S(1)} %pad_maximum_fusion.1), channel_id=1, source_target_pairs={{0,256},{2,258},{4,260},{6,262},{8,264},{10,266},{12,268},{14,270}... | collective-permute-start | bytes 589832 | tf_op jit(solution)/shard_map/ppermute | solution.py:267
  44.3 10.0 %collective-permute-start.4 = (bf16[768,256]{1,0:T(8,128)(2,1)S(1)}, bf16[768,256]{1,0:T(8,128)(2,1)S(1)}, u32[]{:S(2)}, u32[]{:S(2)}) collective-permute-start(bf16[768,256]{1,0:T(8,128)(2,1)S(1)} %get-tuple-element.34), channel_id=1, source_target_pairs={{0,128},{2,130},{4,132},{6,134},{8,136},{10,138},{12,140},{14,142}... | collective-permute-start | bytes 1179656 | tf_op jit(solution)/shard_map/ppermute | solution.py:267
  54.3 7.7 %copy-start.14 = (f32[3,128]{1,0:T(4,128)S(1)}, f32[3,128]{1,0:T(4,128)}, u32[]{:S(2)}) copy-start(f32[3,128]{1,0:T(4,128)} %param.19) | copy-start | bytes 4612
  55.3 16.2 %collective-permute-start.5 = (bf16[1536,256]{1,0:T(8,128)(2,1)S(1)}, bf16[1536,256]{1,0:T(8,128)(2,1)S(1)}, u32[]{:S(2)}, u32[]{:S(2)}) collective-permute-start(bf16[1536,256]{1,0:T(8,128)(2,1)S(1)} %get-tuple-element.30), channel_id=1, source_target_pairs={{0,64},{2,66},{4,68},{6,70},{8,72},{10,74},{12,76},{14,78},{16,80}... | collective-permute-start | bytes 2359304 | tf_op jit(solution)/shard_map/ppermute | solution.py:267
  72.8 25.5 %collective-permute-start.6 = (bf16[3072,256]{1,0:T(8,128)(2,1)}, bf16[3072,256]{1,0:T(8,128)(2,1)}, u32[]{:S(2)}, u32[]{:S(2)}) collective-permute-start(bf16[3072,256]{1,0:T(8,128)(2,1)} %get-tuple-element.26.s_ref), channel_id=1, source_target_pairs={{0,4},{2,62},{4,0},{6,10},{8,12},{10,6},{12,8},{14,18},{16,20},{18... | collective-permute-start | bytes 4718600 | tf_op jit(solution)/shard_map/ppermute | solution.py:267
  81.0 3.8 %copy-start = (bf16[1,384,128]{2,1,0:T(8,128)(2,1)S(1)}, bf16[1,384,128]{2,1,0:T(8,128)(2,1)}, u32[]{:S(2)}) copy-start(bf16[1,384,128]{2,1,0:T(8,128)(2,1)} %param.17) | copy-start | bytes 294916
  98.3 9.1 %copy-start.2 = (bf16[5,384,384]{2,1,0:T(8,128)(2,1)S(1)}, bf16[5,384,384]{2,1,0:T(8,128)(2,1)}, u32[]{:S(2)}) copy-start(bf16[5,384,384]{2,1,0:T(8,128)(2,1)} %param.20) | copy-start | bytes 4423684
  98.3 9.1 %copy-start.3 = (f32[384,256]{1,0:T(8,128)S(1)}, f32[384,256]{1,0:T(8,128)}, u32[]{:S(2)}) copy-start(f32[384,256]{1,0:T(8,128)} %fusion.156) | copy-start | bytes 1179652
  101.2 20.4 %collective-permute-start.7 = (bf16[6144,256]{1,0:T(8,128)(2,1)}, bf16[6144,256]{1,0:T(8,128)(2,1)}, u32[]{:S(2)}, u32[]{:S(2)}) collective-permute-start(bf16[6144,256]{1,0:T(8,128)(2,1)} %constant_dynamic-update-slice_fusion.18), channel_id=1, source_target_pairs={{0,2},{2,0},{4,6},{6,4},{8,10},{10,8},{12,14},{14,12},{16,18},{18,... | collective-permute-start | bytes 9437192 | tf_op jit(solution)/shard_map/ppermute | solution.py:267
  129.7 5.8 %copy-start.5 = (bf16[1,384,256]{2,1,0:T(8,128)(2,1)S(1)}, bf16[1,384,256]{2,1,0:T(8,128)(2,1)}, u32[]{:S(2)}) copy-start(bf16[1,384,256]{2,1,0:T(8,128)(2,1)} %param.14) | copy-start | bytes 589828
  129.7 5.8 %copy-start.11 = (pred[384]{0:T(512)(128)(4,1)S(1)}, pred[384]{0:T(512)(128)(4,1)}, u32[]{:S(2)}) copy-start(pred[384]{0:T(512)(128)(4,1)} %get-tuple-element.19) | copy-start | bytes 1156
  129.7 5.8 %copy-start.12 = (pred[384]{0:T(512)(128)(4,1)S(1)}, pred[384]{0:T(512)(128)(4,1)}, u32[]{:S(2)}) copy-start(pred[384]{0:T(512)(128)(4,1)} %get-tuple-element.53) | copy-start | bytes 1156
  129.7 5.8 %copy-start.13 = (pred[384]{0:T(512)(128)(4,1)S(1)}, pred[384]{0:T(512)(128)(4,1)}, u32[]{:S(2)}) copy-start(pred[384]{0:T(512)(128)(4,1)} %get-tuple-element.54) | copy-start | bytes 1156
  129.7 6.1 %copy-start.10 = (pred[384]{0:T(512)(128)(4,1)S(1)}, pred[384]{0:T(512)(128)(4,1)}, u32[]{:S(2)}) copy-start(pred[384]{0:T(512)(128)(4,1)} %get-tuple-element.21) | copy-start | bytes 1156
  129.7 6.2 %copy-start.7 = (f32[128]{0:T(128)S(1)}, f32[128]{0:T(128)}, u32[]{:S(2)}) copy-start(f32[128]{0:T(128)} %get-tuple-element.50) | copy-start | bytes 1540
  129.7 6.2 %copy-start.8 = (f32[128]{0:T(128)S(1)}, f32[128]{0:T(128)}, u32[]{:S(2)}) copy-start(f32[128]{0:T(128)} %get-tuple-element.51) | copy-start | bytes 1540
  129.7 6.2 %copy-start.9 = (f32[128]{0:T(128)S(1)}, f32[128]{0:T(128)}, u32[]{:S(2)}) copy-start(f32[128]{0:T(128)} %get-tuple-element.52) | copy-start | bytes 1540
  129.7 6.4 %copy-start.4 = (bf16[1,384,128]{2,1,0:T(8,128)(2,1)S(1)}, bf16[1,384,128]{2,1,0:T(8,128)(2,1)}, u32[]{:S(2)}) copy-start(bf16[1,384,128]{2,1,0:T(8,128)(2,1)} %param.16) | copy-start | bytes 294916
  138.1 17.7 %copy-start.1 = (bf16[5,384,384]{2,1,0:T(8,128)(2,1)S(1)}, bf16[5,384,384]{2,1,0:T(8,128)(2,1)}, u32[]{:S(2)}) copy-start(bf16[5,384,384]{2,1,0:T(8,128)(2,1)} %param.21) | copy-start | bytes 4423684
  138.7 18.1 %collective-permute-start.9 = (bf16[1,384,384]{2,1,0:T(8,128)(2,1)S(1)}, bf16[1,384,384]{2,1,0:T(8,128)(2,1)S(1)}, u32[]{:S(2)}, u32[]{:S(2)}) collective-permute-start(bf16[1,384,384]{2,1,0:T(8,128)(2,1)S(1)} %pad_maximum_fusion), channel_id=1, source_target_pairs={{0,2},{2,4},{4,6},{6,8},{8,10},{10,12},{12,14},{14,16},{16,18},{18... | collective-permute-start | bytes 884744 | tf_op jit(solution)/shard_map/ppermute | solution.py:17
  140.7 19.0 %collective-permute-start.8 = (bf16[1,384,384]{2,1,0:T(8,128)(2,1)S(1)}, bf16[1,384,384]{2,1,0:T(8,128)(2,1)S(1)}, u32[]{:S(2)}, u32[]{:S(2)}) collective-permute-start(bf16[1,384,384]{2,1,0:T(8,128)(2,1)S(1)} %pad_maximum_fusion), channel_id=1, source_target_pairs={{0,4},{2,6},{4,8},{6,10},{8,12},{10,14},{12,16},{14,18},{16,20},{1... | collective-permute-start | bytes 884744 | tf_op jit(solution)/shard_map/ppermute | solution.py:17
  143.0 16.0 %collective-permute-start.11 = (bf16[1,384,384]{2,1,0:T(8,128)(2,1)S(1)}, bf16[1,384,384]{2,1,0:T(8,128)(2,1)S(1)}, u32[]{:S(2)}, u32[]{:S(2)}) collective-permute-start(bf16[1,384,384]{2,1,0:T(8,128)(2,1)S(1)} %pad_maximum_fusion), channel_id=1, source_target_pairs={{4,0},{6,2},{8,4},{10,6},{12,8},{14,10},{16,12},{18,14},{20,16},{2... | collective-permute-start | bytes 884744 | tf_op jit(solution)/shard_map/ppermute | solution.py:17
  153.1 8.0 %collective-permute-start.10 = (bf16[1,384,384]{2,1,0:T(8,128)(2,1)S(1)}, bf16[1,384,384]{2,1,0:T(8,128)(2,1)S(1)}, u32[]{:S(2)}, u32[]{:S(2)}) collective-permute-start(bf16[1,384,384]{2,1,0:T(8,128)(2,1)S(1)} %pad_maximum_fusion), channel_id=1, source_target_pairs={{2,0},{4,2},{6,4},{8,6},{10,8},{12,10},{14,12},{16,14},{18,16},{20... | collective-permute-start | bytes 884744 | tf_op jit(solution)/shard_map/ppermute | solution.py:17
  161.7 18.2 %collective-permute-start.13 = (bf16[1,384,128]{2,1,0:T(8,128)(2,1)S(1)}, bf16[1,384,128]{2,1,0:T(8,128)(2,1)S(1)}, u32[]{:S(2)}, u32[]{:S(2)}) collective-permute-start(bf16[1,384,128]{2,1,0:T(8,128)(2,1)S(1)} %fusion.66), channel_id=1, source_target_pairs={{0,2},{2,4},{4,6},{6,8},{8,10},{10,12},{12,14},{14,16},{16,18},{18... | collective-permute-start | bytes 294920 | tf_op jit(solution)/shard_map/ppermute | solution.py:17
  163.8 16.2 %collective-permute-start.12 = (bf16[1,384,128]{2,1,0:T(8,128)(2,1)S(1)}, bf16[1,384,128]{2,1,0:T(8,128)(2,1)S(1)}, u32[]{:S(2)}, u32[]{:S(2)}) collective-permute-start(bf16[1,384,128]{2,1,0:T(8,128)(2,1)S(1)} %fusion.66), channel_id=1, source_target_pairs={{0,4},{2,6},{4,8},{6,10},{8,12},{10,14},{12,16},{14,18},{16,20},{1... | collective-permute-start | bytes 294920 | tf_op jit(solution)/shard_map/ppermute | solution.py:17
  165.8 14.5 %collective-permute-start.15 = (bf16[1,384,128]{2,1,0:T(8,128)(2,1)S(1)}, bf16[1,384,128]{2,1,0:T(8,128)(2,1)S(1)}, u32[]{:S(2)}, u32[]{:S(2)}) collective-permute-start(bf16[1,384,128]{2,1,0:T(8,128)(2,1)S(1)} %fusion.66), channel_id=1, source_target_pairs={{4,0},{6,2},{8,4},{10,6},{12,8},{14,10},{16,12},{18,14},{20,16},{2... | collective-permute-start | bytes 294920 | tf_op jit(solution)/shard_map/ppermute | solution.py:17
  177.2 5.9 %collective-permute-start.14 = (bf16[1,384,128]{2,1,0:T(8,128)(2,1)S(1)}, bf16[1,384,128]{2,1,0:T(8,128)(2,1)S(1)}, u32[]{:S(2)}, u32[]{:S(2)}) collective-permute-start(bf16[1,384,128]{2,1,0:T(8,128)(2,1)S(1)} %fusion.66), channel_id=1, source_target_pairs={{2,0},{4,2},{6,4},{8,6},{10,8},{12,10},{14,12},{16,14},{18,16},{20... | collective-permute-start | bytes 294920 | tf_op jit(solution)/shard_map/ppermute | solution.py:17
  185.3 16.1 %collective-permute-start.17 = (bf16[1,384,128]{2,1,0:T(8,128)(2,1)S(1)}, bf16[1,384,128]{2,1,0:T(8,128)(2,1)S(1)}, u32[]{:S(2)}, u32[]{:S(2)}) collective-permute-start(bf16[1,384,128]{2,1,0:T(8,128)(2,1)S(1)} %get-tuple-element.61), channel_id=1, source_target_pairs={{0,2},{2,4},{4,6},{6,8},{8,10},{10,12},{12,14},{14,16},{16,18},{18... | collective-permute-start | bytes 294920 | tf_op jit(solution)/shard_map/ppermute | solution.py:17
  187.4 14.2 %collective-permute-start.16 = (bf16[1,384,128]{2,1,0:T(8,128)(2,1)S(1)}, bf16[1,384,128]{2,1,0:T(8,128)(2,1)S(1)}, u32[]{:S(2)}, u32[]{:S(2)}) collective-permute-start(bf16[1,384,128]{2,1,0:T(8,128)(2,1)S(1)} %get-tuple-element.61), channel_id=1, source_target_pairs={{0,4},{2,6},{4,8},{6,10},{8,12},{10,14},{12,16},{14,18},{16,20},{1... | collective-permute-start | bytes 294920 | tf_op jit(solution)/shard_map/ppermute | solution.py:17
  189.4 12.5 %collective-permute-start.19 = (bf16[1,384,128]{2,1,0:T(8,128)(2,1)S(1)}, bf16[1,384,128]{2,1,0:T(8,128)(2,1)S(1)}, u32[]{:S(2)}, u32[]{:S(2)}) collective-permute-start(bf16[1,384,128]{2,1,0:T(8,128)(2,1)S(1)} %get-tuple-element.61), channel_id=1, source_target_pairs={{4,0},{6,2},{8,4},{10,6},{12,8},{14,10},{16,12},{18,14},{20,16},{2... | collective-permute-start | bytes 294920 | tf_op jit(solution)/shard_map/ppermute | solution.py:17
  198.5 5.9 %collective-permute-start.18 = (bf16[1,384,128]{2,1,0:T(8,128)(2,1)S(1)}, bf16[1,384,128]{2,1,0:T(8,128)(2,1)S(1)}, u32[]{:S(2)}, u32[]{:S(2)}) collective-permute-start(bf16[1,384,128]{2,1,0:T(8,128)(2,1)S(1)} %get-tuple-element.61), channel_id=1, source_target_pairs={{2,0},{4,2},{6,4},{8,6},{10,8},{12,10},{14,12},{16,14},{18,16},{20... | collective-permute-start | bytes 294920 | tf_op jit(solution)/shard_map/ppermute | solution.py:17
  204.7 16.1 %collective-permute-start.21 = (bf16[1,384,128]{2,1,0:T(8,128)(2,1)S(1)}, bf16[1,384,128]{2,1,0:T(8,128)(2,1)S(1)}, u32[]{:S(2)}, u32[]{:S(2)}) collective-permute-start(bf16[1,384,128]{2,1,0:T(8,128)(2,1)S(1)} %fusion.64), channel_id=1, source_target_pairs={{0,2},{2,4},{4,6},{6,8},{8,10},{10,12},{12,14},{14,16},{16,18},{18... | collective-permute-start | bytes 294920 | tf_op jit(solution)/shard_map/ppermute | solution.py:17
  206.8 14.2 %collective-permute-start.20 = (bf16[1,384,128]{2,1,0:T(8,128)(2,1)S(1)}, bf16[1,384,128]{2,1,0:T(8,128)(2,1)S(1)}, u32[]{:S(2)}, u32[]{:S(2)}) collective-permute-start(bf16[1,384,128]{2,1,0:T(8,128)(2,1)S(1)} %fusion.64), channel_id=1, source_target_pairs={{0,4},{2,6},{4,8},{6,10},{8,12},{10,14},{12,16},{14,18},{16,20},{1... | collective-permute-start | bytes 294920 | tf_op jit(solution)/shard_map/ppermute | solution.py:17
  208.7 12.4 %collective-permute-start.23 = (bf16[1,384,128]{2,1,0:T(8,128)(2,1)S(1)}, bf16[1,384,128]{2,1,0:T(8,128)(2,1)S(1)}, u32[]{:S(2)}, u32[]{:S(2)}) collective-permute-start(bf16[1,384,128]{2,1,0:T(8,128)(2,1)S(1)} %fusion.64), channel_id=1, source_target_pairs={{4,0},{6,2},{8,4},{10,6},{12,8},{14,10},{16,12},{18,14},{20,16},{2... | collective-permute-start | bytes 294920 | tf_op jit(solution)/shard_map/ppermute | solution.py:17
  217.8 5.9 %collective-permute-start.22 = (bf16[1,384,128]{2,1,0:T(8,128)(2,1)S(1)}, bf16[1,384,128]{2,1,0:T(8,128)(2,1)S(1)}, u32[]{:S(2)}, u32[]{:S(2)}) collective-permute-start(bf16[1,384,128]{2,1,0:T(8,128)(2,1)S(1)} %fusion.64), channel_id=1, source_target_pairs={{2,0},{4,2},{6,4},{8,6},{10,8},{12,10},{14,12},{16,14},{18,16},{20... | collective-permute-start | bytes 294920 | tf_op jit(solution)/shard_map/ppermute | solution.py:17

commit v14 on v13

--- a/solution.py
+++ b/solution.py
@@ -152,7 +152,7 @@
     return ((1.0 - update_gate) * hidden + update_gate * candidate, from_inputs)
 
 
-GATHER_BITS = (4, 3, 2, 7, 6, 5, 1, 0)
+GATHER_BITS = (4, 3, 2, 6, 7, 5, 1, 0)
 
 
 def match_kernel(f1_ref, s_ref, w_ref, m_in, a_in, m_out, a_out):

time: 226 us -> 225 us (level)
  no operation moved by 1% of the time
where the time goes in v14:
time: 225 us; the launch traced here: 224 us
  starting transfers between devices  115 us (51%)
  waiting for transfers between devices  35 us (16%)
  local copies, waits for them, and re-layouts  25.4 us (11%)
  Pallas kernels  18.5 us (8%)
  other arithmetic  15.8 us (7%)
  matrix products  12.4 us (6%)
    ppermute x16, starting transfers between devices, passed_along(): return lax.ppermute(array, axis, pairs)  66.8 us
    ppermute x8, starting transfers between devices, per_device(): got = lax.ppermute(held, 'band', pairs)  48.4 us
    ppermute x8, waiting for transfers between devices, per_device(): got = lax.ppermute(held, 'band', pairs)  24.6 us
    pallas_call x3, Pallas kernels, match_block(): pl.pallas_call(match_kernel, grid=(count // tile,), in_specs=[pl.BlockSpe...  18.5 us
    dot_general x50, matrix products, conv_valid(): jnp.dot(tap_slice.reshape(-1, tap_slice.shape[-1]), weight[kernel_tap], p...  12.4 us
    ppermute x16, waiting for transfers between devices, passed_along(): return lax.ppermute(array, axis, pairs)  10.5 us
    concatenate x2, other arithmetic, match_block(): jnp.concatenate([jnp.ones((count, 1), jnp.float32), strip_row[:, None], s...  4.81 us
    another operation x5, other arithmetic  4.62 us
  transfers between devices with their start and end apart: 24, of which 13 were waited for; matrix products, arithmetic and copies ran while one was open for 15% of the time, Pallas kernels for 5%

profile of v14, /device:TPU:7, one launch (start us, length us, event | category | flops | bytes accessed | tf_op | source)
XLA Modules:
  0.0 223.8 jit_solution(5504644155614750904)
XLA Ops:
  2.3 15.4 %collective-permute-start = (bf16[48,256]{1,0:T(8,128)(2,1)S(1)}, bf16[48,256]{1,0:T(8,128)(2,1)S(1)}, u32[]{:S(2)}, u32[]{:S(2)}) collective-permute-start(bf16[48,256]{1,0:T(8,128)(2,1)S(1)} %get-tuple-element.23), channel_id=1, source_target_pairs={{0,32},{2,34},{4,36},{6,38},{8,40},{10,42},{12,44},{14,46},{16,48}... | collective-permute-start | bytes 73736 | tf_op jit(solution)/shard_map/ppermute | solution.py:267
  17.7 1.3 collective-permute-done
  19.0 5.3 %collective-permute-start.1 = (bf16[96,256]{1,0:T(8,128)(2,1)S(1)}, bf16[96,256]{1,0:T(8,128)(2,1)S(1)}, u32[]{:S(2)}, u32[]{:S(2)}) collective-permute-start(bf16[96,256]{1,0:T(8,128)(2,1)S(1)} %pad_maximum_fusion.4), channel_id=1, source_target_pairs={{0,16},{2,18},{4,20},{6,22},{8,24},{10,26},{12,28},{14,30},{16,0},... | collective-permute-start | bytes 147464 | tf_op jit(solution)/shard_map/ppermute | solution.py:267
  25.0 3.3 %collective-permute-done.1 = bf16[96,256]{1,0:T(8,128)(2,1)S(1)} collective-permute-done((bf16[96,256]{1,0:T(8,128)(2,1)S(1)}, bf16[96,256]{1,0:T(8,128)(2,1)S(1)}, u32[]{:S(2)}, u32[]{:S(2)}) %collective-permute-start.1) | collective-permute-done | bytes 49184 | tf_op jit(solution)/shard_map/ppermute | solution.py:267
  28.3 2.8 %collective-permute-start.2 = (bf16[192,256]{1,0:T(8,128)(2,1)S(1)}, bf16[192,256]{1,0:T(8,128)(2,1)S(1)}, u32[]{:S(2)}, u32[]{:S(2)}) collective-permute-start(bf16[192,256]{1,0:T(8,128)(2,1)S(1)} %pad_maximum_fusion.3), channel_id=1, source_target_pairs={{0,8},{2,10},{4,12},{6,14},{8,0},{10,2},{12,4},{14,6},{16,24},{18,... | collective-permute-start | bytes 294920 | tf_op jit(solution)/shard_map/ppermute | solution.py:267
  31.7 3.8 %collective-permute-done.2 = bf16[192,256]{1,0:T(8,128)(2,1)S(1)} collective-permute-done((bf16[192,256]{1,0:T(8,128)(2,1)S(1)}, bf16[192,256]{1,0:T(8,128)(2,1)S(1)}, u32[]{:S(2)}, u32[]{:S(2)}) %collective-permute-start.2) | collective-permute-done | bytes 98336 | tf_op jit(solution)/shard_map/ppermute | solution.py:267
  35.6 4.8 %collective-permute-start.3 = (bf16[384,256]{1,0:T(8,128)(2,1)S(1)}, bf16[384,256]{1,0:T(8,128)(2,1)S(1)}, u32[]{:S(2)}, u32[]{:S(2)}) collective-permute-start(bf16[384,256]{1,0:T(8,128)(2,1)S(1)} %pad_maximum_fusion.1), channel_id=1, source_target_pairs={{0,128},{2,130},{4,132},{6,134},{8,136},{10,138},{12,140},{14,142}... | collective-permute-start | bytes 589832 | tf_op jit(solution)/shard_map/ppermute | solution.py:267
  41.8 1.7 collective-permute-done.3
  44.3 3.0 %collective-permute-start.4 = (bf16[768,256]{1,0:T(8,128)(2,1)S(1)}, bf16[768,256]{1,0:T(8,128)(2,1)S(1)}, u32[]{:S(2)}, u32[]{:S(2)}) collective-permute-start(bf16[768,256]{1,0:T(8,128)(2,1)S(1)} %get-tuple-element.34), channel_id=1, source_target_pairs={{0,256},{2,258},{4,260},{6,262},{8,264},{10,266},{12,268},{14,270}... | collective-permute-start | bytes 1179656 | tf_op jit(solution)/shard_map/ppermute | solution.py:267
  48.8 5.5 %collective-permute-done.4 = bf16[768,256]{1,0:T(8,128)(2,1)S(1)} collective-permute-done((bf16[768,256]{1,0:T(8,128)(2,1)S(1)}, bf16[768,256]{1,0:T(8,128)(2,1)S(1)}, u32[]{:S(2)}, u32[]{:S(2)}) %collective-permute-start.4) | collective-permute-done | bytes 393248 | tf_op jit(solution)/shard_map/ppermute | solution.py:267
  55.3 3.2 %collective-permute-start.5 = (bf16[1536,256]{1,0:T(8,128)(2,1)S(1)}, bf16[1536,256]{1,0:T(8,128)(2,1)S(1)}, u32[]{:S(2)}, u32[]{:S(2)}) collective-permute-start(bf16[1536,256]{1,0:T(8,128)(2,1)S(1)} %get-tuple-element.30), channel_id=1, source_target_pairs={{0,64},{2,66},{4,68},{6,70},{8,72},{10,74},{12,76},{14,78},{16,80}... | collective-permute-start | bytes 2359304 | tf_op jit(solution)/shard_map/ppermute | solution.py:267
  59.2 2.8 %gather_fusion = s32[384]{0:T(512)S(1)} fusion(s32[256]{0:T(256)S(1)} %bitcast.411, s32[1024]{0:T(1024)S(1)} %pad_clamp_fusion.2), kind=kCustom, calls=%fused_computation.2 | custom fusion | bytes 4608 | tf_op jit(solution)/shard_map/gather | solution.py:295
  63.2 6.7 %collective-permute-done.5 = bf16[1536,256]{1,0:T(8,128)(2,1)S(1)} collective-permute-done((bf16[1536,256]{1,0:T(8,128)(2,1)S(1)}, bf16[1536,256]{1,0:T(8,128)(2,1)S(1)}, u32[]{:S(2)}, u32[]{:S(2)}) %collective-permute-start.5) | collective-permute-done | bytes 786464 | tf_op jit(solution)/shard_map/ppermute | solution.py:267
  71.2 6.4 %collective-permute-start.6 = (bf16[3072,256]{1,0:T(8,128)(2,1)}, bf16[3072,256]{1,0:T(8,128)(2,1)}, u32[]{:S(2)}, u32[]{:S(2)}) collective-permute-start(bf16[3072,256]{1,0:T(8,128)(2,1)} %get-tuple-element.26.s_ref), channel_id=1, source_target_pairs={{0,4},{2,62},{4,0},{6,10},{8,12},{10,6},{12,8},{14,18},{16,20},{18... | collective-permute-start | bytes 4718600 | tf_op jit(solution)/shard_map/ppermute | solution.py:267
  80.4 1.8 convert_element_type.223
  82.2 1.8 fusion.156
  84.6 2.3 %maximum_maximum_fusion.2 = (bf16[3072,128]{1,0:T(8,128)(2,1)}, bf16[3072,128]{1,0:T(8,128)(2,1)}) fusion(bf16[3072,1]{1,0:T(8,128)(2,1)S(1)} %convert_element_type.224, bf16[3072,1]{1,0:T(8,128)(2,1)S(1)} %fusion.6, bf16[128]{0:T(256)(128)(2,1)S(1)} %pad.40.clone, bf16[128]{0:T(256)(128)(2,1)S(1)} %pad.37.clone, bf16[3072,1]{1,0:T(8,128)(2,1)S(1)} %convert_element_type.222), kind=kLoop, calls=%fused_computation.103 | loop fusion | flops 5111808 | bytes 1591808 | tf_op jit(solution)/shard_map/concatenate | solution.py:187
  88.3 5.2 %shard_map.131 = (f32[384,128]{1,0:T(8,128)}, f32[384,128]{1,0:T(8,128)}) custom-call(bf16[384,256]{1,0:T(8,128)(2,1)} %bitcast.412, bf16[3072,256]{1,0:T(8,128)(2,1)} %get-tuple-element.26.s_ref, bf16[3072,128]{1,0:T(8,128)(2,1)} %get-tuple-element.25.w_ref, f32[384,128]{1,0:T(8,128)} %broadcast_in_dim.60.m_in, f32[384,128]{1,0:T(8,128)} %broadcast_in_dim.61.a_in), custom_call_target="tpu_custom_call" | custom-call | flops 1207959552 | bytes 3342336 | tf_op jit(solution)/shard_map/pallas_call | solution.py:197
  93.5 2.2 collective-permute-done.6.s_ref
  95.7 2.9 %constant_dynamic-update-slice_fusion.18 = bf16[6144,256]{1,0:T(8,128)(2,1)} fusion(bf16[6144,256]{1,0:T(8,128)(2,1)} %get-tuple-element.27, bf16[3072,256]{1,0:T(8,128)(2,1)} %collective-permute-done.6.s_ref), kind=kLoop, calls=%fused_computation.312 | loop fusion | bytes 3145728 | tf_op jit(solution)/shard_map/concatenate | solution.py:281
  98.6 7.4 %collective-permute-start.7 = (bf16[6144,256]{1,0:T(8,128)(2,1)}, bf16[6144,256]{1,0:T(8,128)(2,1)}, u32[]{:S(2)}, u32[]{:S(2)}) collective-permute-start(bf16[6144,256]{1,0:T(8,128)(2,1)} %constant_dynamic-update-slice_fusion.18), channel_id=1, source_target_pairs={{0,2},{2,0},{4,6},{6,4},{8,10},{10,8},{12,14},{14,12},{16,18},{18,... | collective-permute-start | bytes 9437192 | tf_op jit(solution)/shard_map/ppermute | solution.py:267
  107.2 1.9 fusion.1
  109.1 2.5 %maximum_maximum_fusion.w_ref = bf16[6144,128]{1,0:T(8,128)(2,1)} fusion(bf16[6144,1]{1,0:T(8,128)(2,1)S(1)} %fusion.1, bf16[6144,1]{1,0:T(8,128)(2,1)S(1)} %convert_element_type.223, bf16[128]{0:T(256)(128)(2,1)S(1)} %pad.40.clone, bf16[128]{0:T(256)(128)(2,1)S(1)} %pad.37.clone), kind=kLoop, calls=%fused_computation.13 | loop fusion | flops 6291456 | bytes 1597952 | tf_op jit(solution)/shard_map/concatenate | solution.py:187
  111.6 4.0 %gather_fusion.1 = bf16[384,256]{1,0:T(8,128)(2,1)S(1)} fusion(bf16[6144,256]{1,0:T(8,128)(2,1)} %constant_dynamic-update-slice_fusion.18, s32[1024]{0:T(1024)S(1)} %get-tuple-element.64), kind=kCustom, calls=%fused_computation.clone | custom fusion | bytes 394752 | tf_op jit(solution)/shard_map/jit(_take)/gather | solution.py:301
  115.6 5.2 %shard_map.132 = (f32[384,128]{1,0:T(8,128)}, f32[384,128]{1,0:T(8,128)}) custom-call(bf16[384,256]{1,0:T(8,128)(2,1)} %bitcast.413, bf16[3072,256]{1,0:T(8,128)(2,1)} %collective-permute-done.6.s_ref, bf16[3072,128]{1,0:T(8,128)(2,1)} %get-tuple-element.24.w_ref, f32[384,128]{1,0:T(8,128)} %get-tuple-element.9.m_in, f32[384,128]{1,0:T(8,128)} %get-tuple-element.10.a_in), custom_call_target="tpu_custom_call" | custom-call | flops 1207959552 | bytes 3342336 | tf_op jit(solution)/shard_map/pallas_call | solution.py:197
  120.8 8.1 %shard_map.133 = (f32[384,128]{1,0:T(8,128)}, f32[384,128]{1,0:T(8,128)}) custom-call(bf16[384,256]{1,0:T(8,128)(2,1)} %bitcast.414, bf16[6144,256]{1,0:T(8,128)(2,1)} %collective-permute-done.7.s_ref, bf16[6144,128]{1,0:T(8,128)(2,1)} %maximum_maximum_fusion.w_ref, f32[384,128]{1,0:T(8,128)} %get-tuple-element.12.m_in, f32[384,128]{1,0:T(8,128)} %get-tuple-element.13.a_in), custom_call_target="tpu_custom_call" | custom-call | flops 2415919104 | bytes 5701632 | tf_op jit(solution)/shard_map/pallas_call | solution.py:197
  128.9 1.5 subtract_reduce_fusion
  130.5 4.2 %gather_fusion.2 = bf16[384,256]{1,0:T(8,128)(2,1)S(1)} fusion(bf16[6144,256]{1,0:T(8,128)(2,1)} %collective-permute-done.7.s_ref, s32[1024]{0:T(1024)S(1)} %get-tuple-element.63), kind=kCustom, calls=%fused_computation.1.clone | custom fusion | bytes 394752 | tf_op jit(solution)/shard_map/jit(_take)/gather | solution.py:302
  137.9 1.9 collective-permute-start.9
  139.9 2.5 %collective-permute-start.8 = (bf16[1,384,384]{2,1,0:T(8,128)(2,1)S(1)}, bf16[1,384,384]{2,1,0:T(8,128)(2,1)S(1)}, u32[]{:S(2)}, u32[]{:S(2)}) collective-permute-start(bf16[1,384,384]{2,1,0:T(8,128)(2,1)S(1)} %pad_maximum_fusion), channel_id=1, source_target_pairs={{0,4},{2,6},{4,8},{6,10},{8,12},{10,14},{12,16},{14,18},{16,20},{1... | collective-permute-start | bytes 884744 | tf_op jit(solution)/shard_map/ppermute | solution.py:17
  142.3 10.0 %collective-permute-start.11 = (bf16[1,384,384]{2,1,0:T(8,128)(2,1)S(1)}, bf16[1,384,384]{2,1,0:T(8,128)(2,1)S(1)}, u32[]{:S(2)}, u32[]{:S(2)}) collective-permute-start(bf16[1,384,384]{2,1,0:T(8,128)(2,1)S(1)} %pad_maximum_fusion), channel_id=1, source_target_pairs={{4,0},{6,2},{8,4},{10,6},{12,8},{14,10},{16,12},{18,14},{20,16},{2... | collective-permute-start | bytes 884744 | tf_op jit(solution)/shard_map/ppermute | solution.py:17
  152.3 2.7 %collective-permute-start.10 = (bf16[1,384,384]{2,1,0:T(8,128)(2,1)S(1)}, bf16[1,384,384]{2,1,0:T(8,128)(2,1)S(1)}, u32[]{:S(2)}, u32[]{:S(2)}) collective-permute-start(bf16[1,384,384]{2,1,0:T(8,128)(2,1)S(1)} %pad_maximum_fusion), channel_id=1, source_target_pairs={{2,0},{4,2},{6,4},{8,6},{10,8},{12,10},{14,12},{16,14},{18,16},{20... | collective-permute-start | bytes 884744 | tf_op jit(solution)/shard_map/ppermute | solution.py:17
  156.5 1.6 collective-permute-done.11
  160.9 1.9 collective-permute-start.13
  163.0 1.9 collective-permute-start.12
  164.9 11.4 %collective-permute-start.15 = (bf16[1,384,128]{2,1,0:T(8,128)(2,1)S(1)}, bf16[1,384,128]{2,1,0:T(8,128)(2,1)S(1)}, u32[]{:S(2)}, u32[]{:S(2)}) collective-permute-start(bf16[1,384,128]{2,1,0:T(8,128)(2,1)S(1)} %fusion.66), channel_id=1, source_target_pairs={{4,0},{6,2},{8,4},{10,6},{12,8},{14,10},{16,12},{18,14},{20,16},{2... | collective-permute-start | bytes 294920 | tf_op jit(solution)/shard_map/ppermute | solution.py:17
  176.4 2.7 %collective-permute-start.14 = (bf16[1,384,128]{2,1,0:T(8,128)(2,1)S(1)}, bf16[1,384,128]{2,1,0:T(8,128)(2,1)S(1)}, u32[]{:S(2)}, u32[]{:S(2)}) collective-permute-start(bf16[1,384,128]{2,1,0:T(8,128)(2,1)S(1)} %fusion.66), channel_id=1, source_target_pairs={{2,0},{4,2},{6,4},{8,6},{10,8},{12,10},{14,12},{16,14},{18,16},{20... | collective-permute-start | bytes 294920 | tf_op jit(solution)/shard_map/ppermute | solution.py:17
  179.6 2.7 %collective-permute-done.14 = bf16[1,384,128]{2,1,0:T(8,128)(2,1)S(1)} collective-permute-done((bf16[1,384,128]{2,1,0:T(8,128)(2,1)S(1)}, bf16[1,384,128]{2,1,0:T(8,128)(2,1)S(1)}, u32[]{:S(2)}, u32[]{:S(2)}) %collective-permute-start.14) | collective-permute-done | bytes 98336 | tf_op jit(solution)/shard_map/ppermute | solution.py:17
  184.5 1.9 collective-permute-start.17
  186.6 1.9 collective-permute-start.16
  188.6 9.1 %collective-permute-start.19 = (bf16[1,384,128]{2,1,0:T(8,128)(2,1)S(1)}, bf16[1,384,128]{2,1,0:T(8,128)(2,1)S(1)}, u32[]{:S(2)}, u32[]{:S(2)}) collective-permute-start(bf16[1,384,128]{2,1,0:T(8,128)(2,1)S(1)} %get-tuple-element.61), channel_id=1, source_target_pairs={{4,0},{6,2},{8,4},{10,6},{12,8},{14,10},{16,12},{18,14},{20,16},{2... | collective-permute-start | bytes 294920 | tf_op jit(solution)/shard_map/ppermute | solution.py:17
  197.7 3.0 %collective-permute-start.18 = (bf16[1,384,128]{2,1,0:T(8,128)(2,1)S(1)}, bf16[1,384,128]{2,1,0:T(8,128)(2,1)S(1)}, u32[]{:S(2)}, u32[]{:S(2)}) collective-permute-start(bf16[1,384,128]{2,1,0:T(8,128)(2,1)S(1)} %get-tuple-element.61), channel_id=1, source_target_pairs={{2,0},{4,2},{6,4},{8,6},{10,8},{12,10},{14,12},{16,14},{18,16},{20... | collective-permute-start | bytes 294920 | tf_op jit(solution)/shard_map/ppermute | solution.py:17
  201.2 2.4 %collective-permute-done.18 = bf16[1,384,128]{2,1,0:T(8,128)(2,1)S(1)} collective-permute-done((bf16[1,384,128]{2,1,0:T(8,128)(2,1)S(1)}, bf16[1,384,128]{2,1,0:T(8,128)(2,1)S(1)}, u32[]{:S(2)}, u32[]{:S(2)}) %collective-permute-start.18) | collective-permute-done | bytes 98336 | tf_op jit(solution)/shard_map/ppermute | solution.py:17
  203.9 1.9 collective-permute-start.21
  206.0 1.9 collective-permute-start.20
  207.9 9.1 %collective-permute-start.23 = (bf16[1,384,128]{2,1,0:T(8,128)(2,1)S(1)}, bf16[1,384,128]{2,1,0:T(8,128)(2,1)S(1)}, u32[]{:S(2)}, u32[]{:S(2)}) collective-permute-start(bf16[1,384,128]{2,1,0:T(8,128)(2,1)S(1)} %fusion.64), channel_id=1, source_target_pairs={{4,0},{6,2},{8,4},{10,6},{12,8},{14,10},{16,12},{18,14},{20,16},{2... | collective-permute-start | bytes 294920 | tf_op jit(solution)/shard_map/ppermute | solution.py:17
  217.0 3.0 %collective-permute-start.22 = (bf16[1,384,128]{2,1,0:T(8,128)(2,1)S(1)}, bf16[1,384,128]{2,1,0:T(8,128)(2,1)S(1)}, u32[]{:S(2)}, u32[]{:S(2)}) collective-permute-start(bf16[1,384,128]{2,1,0:T(8,128)(2,1)S(1)} %fusion.64), channel_id=1, source_target_pairs={{2,0},{4,2},{6,4},{8,6},{10,8},{12,10},{14,12},{16,14},{18,16},{20... | collective-permute-start | bytes 294920 | tf_op jit(solution)/shard_map/ppermute | solution.py:17
  220.5 2.5 %collective-permute-done.22 = bf16[1,384,128]{2,1,0:T(8,128)(2,1)S(1)} collective-permute-done((bf16[1,384,128]{2,1,0:T(8,128)(2,1)S(1)}, bf16[1,384,128]{2,1,0:T(8,128)(2,1)S(1)}, u32[]{:S(2)}, u32[]{:S(2)}) %collective-permute-start.22) | collective-permute-done | bytes 98336 | tf_op jit(solution)/shard_map/ppermute | solution.py:17
  (140 shorter events, 29.4 us)
Async XLA Ops:
  1.7 47.1 %copy-start.6 = (s32[2,1,384]{2,1,0:T(1,128)S(1)}, s32[2,1,384]{2,1,0:T(1,128)}, u32[]{:S(2)}) copy-start(s32[2,1,384]{2,1,0:T(1,128)} %param.18) | copy-start | bytes 9220
  2.3 16.7 %collective-permute-start = (bf16[48,256]{1,0:T(8,128)(2,1)S(1)}, bf16[48,256]{1,0:T(8,128)(2,1)S(1)}, u32[]{:S(2)}, u32[]{:S(2)}) collective-permute-start(bf16[48,256]{1,0:T(8,128)(2,1)S(1)} %get-tuple-element.23), channel_id=1, source_target_pairs={{0,32},{2,34},{4,36},{6,38},{8,40},{10,42},{12,44},{14,46},{16,48}... | collective-permute-start | bytes 73736 | tf_op jit(solution)/shard_map/ppermute | solution.py:267
  19.0 9.3 %collective-permute-start.1 = (bf16[96,256]{1,0:T(8,128)(2,1)S(1)}, bf16[96,256]{1,0:T(8,128)(2,1)S(1)}, u32[]{:S(2)}, u32[]{:S(2)}) collective-permute-start(bf16[96,256]{1,0:T(8,128)(2,1)S(1)} %pad_maximum_fusion.4), channel_id=1, source_target_pairs={{0,16},{2,18},{4,20},{6,22},{8,24},{10,26},{12,28},{14,30},{16,0},... | collective-permute-start | bytes 147464 | tf_op jit(solution)/shard_map/ppermute | solution.py:267
  28.3 7.2 %collective-permute-start.2 = (bf16[192,256]{1,0:T(8,128)(2,1)S(1)}, bf16[192,256]{1,0:T(8,128)(2,1)S(1)}, u32[]{:S(2)}, u32[]{:S(2)}) collective-permute-start(bf16[192,256]{1,0:T(8,128)(2,1)S(1)} %pad_maximum_fusion.3), channel_id=1, source_target_pairs={{0,8},{2,10},{4,12},{6,14},{8,0},{10,2},{12,4},{14,6},{16,24},{18,... | collective-permute-start | bytes 294920 | tf_op jit(solution)/shard_map/ppermute | solution.py:267
  35.6 7.9 %collective-permute-start.3 = (bf16[384,256]{1,0:T(8,128)(2,1)S(1)}, bf16[384,256]{1,0:T(8,128)(2,1)S(1)}, u32[]{:S(2)}, u32[]{:S(2)}) collective-permute-start(bf16[384,256]{1,0:T(8,128)(2,1)S(1)} %pad_maximum_fusion.1), channel_id=1, source_target_pairs={{0,128},{2,130},{4,132},{6,134},{8,136},{10,138},{12,140},{14,142}... | collective-permute-start | bytes 589832 | tf_op jit(solution)/shard_map/ppermute | solution.py:267
  44.3 10.0 %collective-permute-start.4 = (bf16[768,256]{1,0:T(8,128)(2,1)S(1)}, bf16[768,256]{1,0:T(8,128)(2,1)S(1)}, u32[]{:S(2)}, u32[]{:S(2)}) collective-permute-start(bf16[768,256]{1,0:T(8,128)(2,1)S(1)} %get-tuple-element.34), channel_id=1, source_target_pairs={{0,256},{2,258},{4,260},{6,262},{8,264},{10,266},{12,268},{14,270}... | collective-permute-start | bytes 1179656 | tf_op jit(solution)/shard_map/ppermute | solution.py:267
  54.3 7.7 %copy-start.14 = (f32[3,128]{1,0:T(4,128)S(1)}, f32[3,128]{1,0:T(4,128)}, u32[]{:S(2)}) copy-start(f32[3,128]{1,0:T(4,128)} %param.19) | copy-start | bytes 4612
  55.3 14.6 %collective-permute-start.5 = (bf16[1536,256]{1,0:T(8,128)(2,1)S(1)}, bf16[1536,256]{1,0:T(8,128)(2,1)S(1)}, u32[]{:S(2)}, u32[]{:S(2)}) collective-permute-start(bf16[1536,256]{1,0:T(8,128)(2,1)S(1)} %get-tuple-element.30), channel_id=1, source_target_pairs={{0,64},{2,66},{4,68},{6,70},{8,72},{10,74},{12,76},{14,78},{16,80}... | collective-permute-start | bytes 2359304 | tf_op jit(solution)/shard_map/ppermute | solution.py:267
  71.2 24.5 %collective-permute-start.6 = (bf16[3072,256]{1,0:T(8,128)(2,1)}, bf16[3072,256]{1,0:T(8,128)(2,1)}, u32[]{:S(2)}, u32[]{:S(2)}) collective-permute-start(bf16[3072,256]{1,0:T(8,128)(2,1)} %get-tuple-element.26.s_ref), channel_id=1, source_target_pairs={{0,4},{2,62},{4,0},{6,10},{8,12},{10,6},{12,8},{14,18},{16,20},{18... | collective-permute-start | bytes 4718600 | tf_op jit(solution)/shard_map/ppermute | solution.py:267
  78.4 3.8 %copy-start = (bf16[1,384,128]{2,1,0:T(8,128)(2,1)S(1)}, bf16[1,384,128]{2,1,0:T(8,128)(2,1)}, u32[]{:S(2)}) copy-start(bf16[1,384,128]{2,1,0:T(8,128)(2,1)} %param.17) | copy-start | bytes 294916
  95.7 10.9 %copy-start.2 = (bf16[5,384,384]{2,1,0:T(8,128)(2,1)S(1)}, bf16[5,384,384]{2,1,0:T(8,128)(2,1)}, u32[]{:S(2)}) copy-start(bf16[5,384,384]{2,1,0:T(8,128)(2,1)} %param.20) | copy-start | bytes 4423684
  95.7 10.9 %copy-start.3 = (f32[384,256]{1,0:T(8,128)S(1)}, f32[384,256]{1,0:T(8,128)}, u32[]{:S(2)}) copy-start(f32[384,256]{1,0:T(8,128)} %fusion.156) | copy-start | bytes 1179652
  98.6 22.2 %collective-permute-start.7 = (bf16[6144,256]{1,0:T(8,128)(2,1)}, bf16[6144,256]{1,0:T(8,128)(2,1)}, u32[]{:S(2)}, u32[]{:S(2)}) collective-permute-start(bf16[6144,256]{1,0:T(8,128)(2,1)} %constant_dynamic-update-slice_fusion.18), channel_id=1, source_target_pairs={{0,2},{2,0},{4,6},{6,4},{8,10},{10,8},{12,14},{14,12},{16,18},{18,... | collective-permute-start | bytes 9437192 | tf_op jit(solution)/shard_map/ppermute | solution.py:267
  128.9 5.8 %copy-start.5 = (bf16[1,384,256]{2,1,0:T(8,128)(2,1)S(1)}, bf16[1,384,256]{2,1,0:T(8,128)(2,1)}, u32[]{:S(2)}) copy-start(bf16[1,384,256]{2,1,0:T(8,128)(2,1)} %param.14) | copy-start | bytes 589828
  128.9 5.8 %copy-start.11 = (pred[384]{0:T(512)(128)(4,1)S(1)}, pred[384]{0:T(512)(128)(4,1)}, u32[]{:S(2)}) copy-start(pred[384]{0:T(512)(128)(4,1)} %get-tuple-element.19) | copy-start | bytes 1156
  128.9 5.8 %copy-start.12 = (pred[384]{0:T(512)(128)(4,1)S(1)}, pred[384]{0:T(512)(128)(4,1)}, u32[]{:S(2)}) copy-start(pred[384]{0:T(512)(128)(4,1)} %get-tuple-element.53) | copy-start | bytes 1156
  128.9 5.8 %copy-start.13 = (pred[384]{0:T(512)(128)(4,1)S(1)}, pred[384]{0:T(512)(128)(4,1)}, u32[]{:S(2)}) copy-start(pred[384]{0:T(512)(128)(4,1)} %get-tuple-element.54) | copy-start | bytes 1156
  128.9 6.1 %copy-start.10 = (pred[384]{0:T(512)(128)(4,1)S(1)}, pred[384]{0:T(512)(128)(4,1)}, u32[]{:S(2)}) copy-start(pred[384]{0:T(512)(128)(4,1)} %get-tuple-element.21) | copy-start | bytes 1156
  128.9 6.2 %copy-start.7 = (f32[128]{0:T(128)S(1)}, f32[128]{0:T(128)}, u32[]{:S(2)}) copy-start(f32[128]{0:T(128)} %get-tuple-element.50) | copy-start | bytes 1540
  128.9 6.2 %copy-start.8 = (f32[128]{0:T(128)S(1)}, f32[128]{0:T(128)}, u32[]{:S(2)}) copy-start(f32[128]{0:T(128)} %get-tuple-element.51) | copy-start | bytes 1540
  128.9 6.2 %copy-start.9 = (f32[128]{0:T(128)S(1)}, f32[128]{0:T(128)}, u32[]{:S(2)}) copy-start(f32[128]{0:T(128)} %get-tuple-element.52) | copy-start | bytes 1540
  128.9 6.4 %copy-start.4 = (bf16[1,384,128]{2,1,0:T(8,128)(2,1)S(1)}, bf16[1,384,128]{2,1,0:T(8,128)(2,1)}, u32[]{:S(2)}) copy-start(bf16[1,384,128]{2,1,0:T(8,128)(2,1)} %param.16) | copy-start | bytes 294916
  137.3 17.7 %copy-start.1 = (bf16[5,384,384]{2,1,0:T(8,128)(2,1)S(1)}, bf16[5,384,384]{2,1,0:T(8,128)(2,1)}, u32[]{:S(2)}) copy-start(bf16[5,384,384]{2,1,0:T(8,128)(2,1)} %param.21) | copy-start | bytes 4423684
  137.9 18.1 %collective-permute-start.9 = (bf16[1,384,384]{2,1,0:T(8,128)(2,1)S(1)}, bf16[1,384,384]{2,1,0:T(8,128)(2,1)S(1)}, u32[]{:S(2)}, u32[]{:S(2)}) collective-permute-start(bf16[1,384,384]{2,1,0:T(8,128)(2,1)S(1)} %pad_maximum_fusion), channel_id=1, source_target_pairs={{0,2},{2,4},{4,6},{6,8},{8,10},{10,12},{12,14},{14,16},{16,18},{18... | collective-permute-start | bytes 884744 | tf_op jit(solution)/shard_map/ppermute | solution.py:17
  139.9 19.0 %collective-permute-start.8 = (bf16[1,384,384]{2,1,0:T(8,128)(2,1)S(1)}, bf16[1,384,384]{2,1,0:T(8,128)(2,1)S(1)}, u32[]{:S(2)}, u32[]{:S(2)}) collective-permute-start(bf16[1,384,384]{2,1,0:T(8,128)(2,1)S(1)} %pad_maximum_fusion), channel_id=1, source_target_pairs={{0,4},{2,6},{4,8},{6,10},{8,12},{10,14},{12,16},{14,18},{16,20},{1... | collective-permute-start | bytes 884744 | tf_op jit(solution)/shard_map/ppermute | solution.py:17
  142.3 15.8 %collective-permute-start.11 = (bf16[1,384,384]{2,1,0:T(8,128)(2,1)S(1)}, bf16[1,384,384]{2,1,0:T(8,128)(2,1)S(1)}, u32[]{:S(2)}, u32[]{:S(2)}) collective-permute-start(bf16[1,384,384]{2,1,0:T(8,128)(2,1)S(1)} %pad_maximum_fusion), channel_id=1, source_target_pairs={{4,0},{6,2},{8,4},{10,6},{12,8},{14,10},{16,12},{18,14},{20,16},{2... | collective-permute-start | bytes 884744 | tf_op jit(solution)/shard_map/ppermute | solution.py:17
  152.3 8.0 %collective-permute-start.10 = (bf16[1,384,384]{2,1,0:T(8,128)(2,1)S(1)}, bf16[1,384,384]{2,1,0:T(8,128)(2,1)S(1)}, u32[]{:S(2)}, u32[]{:S(2)}) collective-permute-start(bf16[1,384,384]{2,1,0:T(8,128)(2,1)S(1)} %pad_maximum_fusion), channel_id=1, source_target_pairs={{2,0},{4,2},{6,4},{8,6},{10,8},{12,10},{14,12},{16,14},{18,16},{20... | collective-permute-start | bytes 884744 | tf_op jit(solution)/shard_map/ppermute | solution.py:17
  160.9 18.2 %collective-permute-start.13 = (bf16[1,384,128]{2,1,0:T(8,128)(2,1)S(1)}, bf16[1,384,128]{2,1,0:T(8,128)(2,1)S(1)}, u32[]{:S(2)}, u32[]{:S(2)}) collective-permute-start(bf16[1,384,128]{2,1,0:T(8,128)(2,1)S(1)} %fusion.66), channel_id=1, source_target_pairs={{0,2},{2,4},{4,6},{6,8},{8,10},{10,12},{12,14},{14,16},{16,18},{18... | collective-permute-start | bytes 294920 | tf_op jit(solution)/shard_map/ppermute | solution.py:17
  163.0 16.2 %collective-permute-start.12 = (bf16[1,384,128]{2,1,0:T(8,128)(2,1)S(1)}, bf16[1,384,128]{2,1,0:T(8,128)(2,1)S(1)}, u32[]{:S(2)}, u32[]{:S(2)}) collective-permute-start(bf16[1,384,128]{2,1,0:T(8,128)(2,1)S(1)} %fusion.66), channel_id=1, source_target_pairs={{0,4},{2,6},{4,8},{6,10},{8,12},{10,14},{12,16},{14,18},{16,20},{1... | collective-permute-start | bytes 294920 | tf_op jit(solution)/shard_map/ppermute | solution.py:17
  164.9 14.5 %collective-permute-start.15 = (bf16[1,384,128]{2,1,0:T(8,128)(2,1)S(1)}, bf16[1,384,128]{2,1,0:T(8,128)(2,1)S(1)}, u32[]{:S(2)}, u32[]{:S(2)}) collective-permute-start(bf16[1,384,128]{2,1,0:T(8,128)(2,1)S(1)} %fusion.66), channel_id=1, source_target_pairs={{4,0},{6,2},{8,4},{10,6},{12,8},{14,10},{16,12},{18,14},{20,16},{2... | collective-permute-start | bytes 294920 | tf_op jit(solution)/shard_map/ppermute | solution.py:17
  176.4 5.9 %collective-permute-start.14 = (bf16[1,384,128]{2,1,0:T(8,128)(2,1)S(1)}, bf16[1,384,128]{2,1,0:T(8,128)(2,1)S(1)}, u32[]{:S(2)}, u32[]{:S(2)}) collective-permute-start(bf16[1,384,128]{2,1,0:T(8,128)(2,1)S(1)} %fusion.66), channel_id=1, source_target_pairs={{2,0},{4,2},{6,4},{8,6},{10,8},{12,10},{14,12},{16,14},{18,16},{20... | collective-permute-start | bytes 294920 | tf_op jit(solution)/shard_map/ppermute | solution.py:17
  184.5 16.1 %collective-permute-start.17 = (bf16[1,384,128]{2,1,0:T(8,128)(2,1)S(1)}, bf16[1,384,128]{2,1,0:T(8,128)(2,1)S(1)}, u32[]{:S(2)}, u32[]{:S(2)}) collective-permute-start(bf16[1,384,128]{2,1,0:T(8,128)(2,1)S(1)} %get-tuple-element.61), channel_id=1, source_target_pairs={{0,2},{2,4},{4,6},{6,8},{8,10},{10,12},{12,14},{14,16},{16,18},{18... | collective-permute-start | bytes 294920 | tf_op jit(solution)/shard_map/ppermute | solution.py:17
  186.6 14.2 %collective-permute-start.16 = (bf16[1,384,128]{2,1,0:T(8,128)(2,1)S(1)}, bf16[1,384,128]{2,1,0:T(8,128)(2,1)S(1)}, u32[]{:S(2)}, u32[]{:S(2)}) collective-permute-start(bf16[1,384,128]{2,1,0:T(8,128)(2,1)S(1)} %get-tuple-element.61), channel_id=1, source_target_pairs={{0,4},{2,6},{4,8},{6,10},{8,12},{10,14},{12,16},{14,18},{16,20},{1... | collective-permute-start | bytes 294920 | tf_op jit(solution)/shard_map/ppermute | solution.py:17
  188.6 12.5 %collective-permute-start.19 = (bf16[1,384,128]{2,1,0:T(8,128)(2,1)S(1)}, bf16[1,384,128]{2,1,0:T(8,128)(2,1)S(1)}, u32[]{:S(2)}, u32[]{:S(2)}) collective-permute-start(bf16[1,384,128]{2,1,0:T(8,128)(2,1)S(1)} %get-tuple-element.61), channel_id=1, source_target_pairs={{4,0},{6,2},{8,4},{10,6},{12,8},{14,10},{16,12},{18,14},{20,16},{2... | collective-permute-start | bytes 294920 | tf_op jit(solution)/shard_map/ppermute | solution.py:17
  197.7 5.9 %collective-permute-start.18 = (bf16[1,384,128]{2,1,0:T(8,128)(2,1)S(1)}, bf16[1,384,128]{2,1,0:T(8,128)(2,1)S(1)}, u32[]{:S(2)}, u32[]{:S(2)}) collective-permute-start(bf16[1,384,128]{2,1,0:T(8,128)(2,1)S(1)} %get-tuple-element.61), channel_id=1, source_target_pairs={{2,0},{4,2},{6,4},{8,6},{10,8},{12,10},{14,12},{16,14},{18,16},{20... | collective-permute-start | bytes 294920 | tf_op jit(solution)/shard_map/ppermute | solution.py:17
  203.9 16.1 %collective-permute-start.21 = (bf16[1,384,128]{2,1,0:T(8,128)(2,1)S(1)}, bf16[1,384,128]{2,1,0:T(8,128)(2,1)S(1)}, u32[]{:S(2)}, u32[]{:S(2)}) collective-permute-start(bf16[1,384,128]{2,1,0:T(8,128)(2,1)S(1)} %fusion.64), channel_id=1, source_target_pairs={{0,2},{2,4},{4,6},{6,8},{8,10},{10,12},{12,14},{14,16},{16,18},{18... | collective-permute-start | bytes 294920 | tf_op jit(solution)/shard_map/ppermute | solution.py:17
  206.0 14.2 %collective-permute-start.20 = (bf16[1,384,128]{2,1,0:T(8,128)(2,1)S(1)}, bf16[1,384,128]{2,1,0:T(8,128)(2,1)S(1)}, u32[]{:S(2)}, u32[]{:S(2)}) collective-permute-start(bf16[1,384,128]{2,1,0:T(8,128)(2,1)S(1)} %fusion.64), channel_id=1, source_target_pairs={{0,4},{2,6},{4,8},{6,10},{8,12},{10,14},{12,16},{14,18},{16,20},{1... | collective-permute-start | bytes 294920 | tf_op jit(solution)/shard_map/ppermute | solution.py:17
  207.9 12.4 %collective-permute-start.23 = (bf16[1,384,128]{2,1,0:T(8,128)(2,1)S(1)}, bf16[1,384,128]{2,1,0:T(8,128)(2,1)S(1)}, u32[]{:S(2)}, u32[]{:S(2)}) collective-permute-start(bf16[1,384,128]{2,1,0:T(8,128)(2,1)S(1)} %fusion.64), channel_id=1, source_target_pairs={{4,0},{6,2},{8,4},{10,6},{12,8},{14,10},{16,12},{18,14},{20,16},{2... | collective-permute-start | bytes 294920 | tf_op jit(solution)/shard_map/ppermute | solution.py:17
  217.0 5.9 %collective-permute-start.22 = (bf16[1,384,128]{2,1,0:T(8,128)(2,1)S(1)}, bf16[1,384,128]{2,1,0:T(8,128)(2,1)S(1)}, u32[]{:S(2)}, u32[]{:S(2)}) collective-permute-start(bf16[1,384,128]{2,1,0:T(8,128)(2,1)S(1)} %fusion.64), channel_id=1, source_target_pairs={{2,0},{4,2},{6,4},{8,6},{10,8},{12,10},{14,12},{16,14},{18,16},{20... | collective-permute-start | bytes 294920 | tf_op jit(solution)/shard_map/ppermute | solution.py:17
